TPU v7x, 512 devices: a whole 4x4x16 slice. The times are simulated.
512 devices in a mesh: layer: 64 (over y, z_lo, x), batch: 8 (over z_hi, core).
Axes of the slice: x: 4, y: 4, z: 16 (z_hi: 4, z_lo: 4; z = z_hi * 4 + z_lo), core: 2. Of those that a mesh axis runs over, the one named last changes fastest.
Arguments:
- initial_state: float32 [8, 128, 512], P('batch'), may hold values from -6 to 6
- cotangent: float32 [8, 128, 512], P('batch'), may hold values from -6 to 6
- conv_weight: bfloat16 [128, 128, 1152], P('layer'), may hold values from -0.1875 to 0.1875
- conv_bias: float32 [128, 128], P('layer'), may hold values from -3 to 3
- block_gain: float32 [64, 128], P('layer'), may hold values from 0 to 1
- adjoint_gain: float32 [64, 128], P('layer'), may hold values from 0 to 1
Outputs:
- block_ends: float32 [64, 8, 128, 512], P('layer', 'batch')
- adjoint_start: float32 [64, 8, 128, 512], P('layer', 'batch')
- weight_grad: float32 [128, 128, 1152], P('layer')
- bias_grad: float32 [128, 128], P('layer')
All inputs are finite; a program needn't handle non-finite values.
Results may differ from a plain program's by a relative error of at most 0.0085.
Values sent between devices are 32-bit elements; how exact they have to be, the bound alone decides.
No kernel may reach another device: no remote copies, remote signals or barrier semaphores. Data moves between devices by JAX's collectives and lax.ppermute only.
A program may use at most 64 MiB of HBM per device.

v0:
```python
import jax
import jax.numpy as jnp
from jax import lax
from jax.sharding import PartitionSpec as P

HEIGHT = 16
WIDTH = 32
ITERS = 2


step_size = 0.25


def from_behind(value, axis, steps):
    count = lax.axis_size(axis)
    leading, last = (max(0, -steps), min(count, count - steps))
    return lax.ppermute(value, axis, [(source, source + steps) for source in range(leading, last)])


def carried_in(part, axis, combine, identity, reverse):
    count = lax.axis_size(axis)
    place = lax.axis_index(axis)
    ahead = count - 1 - place if reverse else place
    gathered = jax.tree.map(lambda a: lax.all_gather(a, axis), part)
    state = jax.tree.map(lambda a, e: jnp.zeros_like(a) + jnp.asarray(e, a.dtype), part, identity)

    def one(hop, state):
        source = count - 1 - hop if reverse else hop
        return combine(
            state, jax.tree.map(lambda a: lax.dynamic_index_in_dim(a, source, 0, False), gathered)
        )

    return lax.fori_loop(0, ahead, one, state)


def columns(current):
    rounded = current.astype(jnp.bfloat16)
    pixels = HEIGHT * WIDTH
    margin = WIDTH + 1
    padded = jnp.pad(rounded, ((0, 0), (0, 0), (margin, margin)))
    across = jnp.arange(pixels) % WIDTH
    pieces = []
    for offset_y in (-1, 0, 1):
        for offset_x in (-1, 0, 1):
            shift_by = offset_y * WIDTH + offset_x
            inside = (across + offset_x >= 0) & (across + offset_x < WIDTH)
            window = padded[:, :, margin + shift_by : margin + shift_by + pixels]
            pieces.append(jnp.where(inside, window, jnp.zeros_like(window)))
    return jnp.concatenate(pieces, axis=1)


def flip_weight(weight):
    channels = weight.shape[0]
    taps = weight.reshape(channels, 9, channels)[:, ::-1, :]
    return jnp.transpose(taps, (2, 1, 0)).reshape(channels, 9 * channels)


def forward_layer(current, weight, bias_row):
    stacked = columns(current)
    pre_act = (
        jnp.einsum("ok,bkp->bop", weight, stacked, preferred_element_type=jnp.float32)
        + bias_row[None, :, None]
    )
    activity = jnp.tanh(pre_act)
    return (current + step_size * activity, activity, stacked)


def backward_layer(adjoint, activity, flipped):
    scaled = step_size * (1.0 - activity * activity) * adjoint
    rounded = scaled.astype(jnp.bfloat16)
    gathered = columns(rounded)
    back = jnp.einsum("ck,bkp->bcp", flipped, gathered, preferred_element_type=jnp.float32)
    return (adjoint + back, rounded, scaled)


def relax_block(start, weights, biases):
    current = start
    stored = []
    for layer_index in range(weights.shape[0]):
        current, activity, stacked = forward_layer(
            current, weights[layer_index], biases[layer_index]
        )
        stored.append((stacked, activity))
    return (current, stored)


def adjoint_block(finish, stored, flipped_list):
    adjoint = finish
    for layer_index in range(len(stored) - 1, -1, -1):
        adjoint = backward_layer(adjoint, stored[layer_index][1], flipped_list[layer_index])[0]
    return adjoint


def combine_maps(earlier, later):
    return (later[0] * earlier[0], later[0][None, :, None] * earlier[1] + later[1])


def per_device(initial_state, cotangent, conv_weight, conv_bias, block_gain, adjoint_gain):
    position = lax.axis_index("layer")
    blocks = lax.axis_size("layer")
    gain_row = block_gain[0]
    back_row = adjoint_gain[0]
    identity = (jnp.ones_like(gain_row), jnp.zeros_like(initial_state))
    flipped_list = [
        flip_weight(conv_weight[layer_index]) for layer_index in range(conv_weight.shape[0])
    ]
    c_points = initial_state
    for sweep_index in range(ITERS):
        ending = relax_block(c_points, conv_weight, conv_bias)[0]
        following = from_behind(c_points, "layer", -1)
        residual = jnp.where(position == blocks - 1, jnp.zeros_like(ending), ending - following)
        prefix = carried_in((gain_row, residual), "layer", combine_maps, identity, False)
        c_points = c_points + prefix[1]
    ending, stored = relax_block(c_points, conv_weight, conv_bias)
    target = cotangent
    for sweep_index in range(ITERS):
        start_adj = adjoint_block(target, stored, flipped_list)
        previous = from_behind(target, "layer", 1)
        residual = jnp.where(position == 0, jnp.zeros_like(start_adj), start_adj - previous)
        prefix = carried_in((back_row, residual), "layer", combine_maps, identity, True)
        target = target + prefix[1]
    adjoint = target
    weight_parts = []
    bias_parts = []
    for layer_index in range(len(stored) - 1, -1, -1):
        adjoint, rounded, scaled = backward_layer(
            adjoint, stored[layer_index][1], flipped_list[layer_index]
        )
        weight_part = jnp.einsum(
            "bop,bkp->ok", rounded, stored[layer_index][0], preferred_element_type=jnp.float32
        )
        bias_part = jnp.sum(scaled, axis=(0, 2))
        weight_parts.insert(0, weight_part)
        bias_parts.insert(0, bias_part)
    weight_grad = jnp.stack(weight_parts)
    bias_grad = jnp.stack(bias_parts)
    weight_grad, bias_grad = lax.psum((weight_grad, bias_grad), "batch")
    return (ending[None], adjoint[None], weight_grad, bias_grad)


def solution(mesh):
    return jax.shard_map(
        per_device,
        mesh=mesh,
        in_specs=(
            P("batch", None, None),
            P("batch", None, None),
            P("layer", None, None),
            P("layer", None),
            P("layer", None),
            P("layer", None),
        ),
        out_specs=(
            P("layer", "batch", None, None),
            P("layer", "batch", None, None),
            P("layer", None, None),
            P("layer", None),
        ),
        check_vma=False,
    )
```

profile of v0, /device:TPU:1, one launch (start us, length us, event | category | flops | bytes accessed | tf_op | source)
XLA Modules:
  0.0 1995.5 jit_solution(8567619220573073386)
XLA Ops:
  7.2 1.1 copy.66
  8.3 1.3 collective-permute-start
  13.9 2.1 collective-permute-done
  17.4 164.9 %all-gather.4 = f32[64,1,128]{2,1,0:T(1,128)S(1)} all-gather(f32[1,1,128]{2,1,0:T(1,128)S(1)} %bitcast.452), channel_id=1, replica_groups=mesh['layer'=64,'batch'=8] {'layer'}, dimensions={0}, use_global_device_ids=true | all-gather | bytes 33280 | tf_op jit(solution)/shard_map/all_gather | solution.py:24
  182.3 191.2 %all-gather.11.cloned.1.call-done = f32[64,128,512]{2,1,0:T(8,128)} async-done(((f32[1,128,512]{2,1,0:T(8,128)}), f32[64,128,512]{2,1,0:T(8,128)}) %all-gather.11.cloned.1.call-update) | async-done | bytes 16777232 | tf_op jit(solution)/shard_map/all_gather | solution.py:24
  373.7 1.3 collective-permute-start.1
  378.5 3.1 collective-permute-done.1
  383.9 3.3 collective-permute-start.2
  389.5 445.6 %all-gather.13.cloned.1.call-done = f32[64,128,512]{2,1,0:T(8,128)} async-done(((f32[1,128,512]{2,1,0:T(8,128)}), f32[64,128,512]{2,1,0:T(8,128)}) %all-gather.13.cloned.1.call-update) | async-done | bytes 16777232 | tf_op jit(solution)/shard_map/all_gather | solution.py:24
  838.9 1.4 fusion.187
  841.9 1.4 fusion.185
  845.6 1.4 fusion.89
  847.9 228.0 %all-gather.5 = f32[64,1,128]{2,1,0:T(1,128)S(1)} all-gather(f32[1,1,128]{2,1,0:T(1,128)S(1)} %bitcast.453), channel_id=1, replica_groups=mesh['layer'=64,'batch'=8] {'layer'}, dimensions={0}, use_global_device_ids=true | all-gather | bytes 33280 | tf_op jit(solution)/shard_map/all_gather | solution.py:24
  1075.9 224.5 %all-gather.15.cloned.1.call-done = f32[64,128,512]{2,1,0:T(8,128)} async-done(((f32[1,128,512]{2,1,0:T(8,128)}), f32[64,128,512]{2,1,0:T(8,128)}) %all-gather.15.cloned.1.call-update) | async-done | bytes 16777232 | tf_op jit(solution)/shard_map/all_gather | solution.py:24
  1300.4 69.5 %while.54 = (s32[]{:T(128)}, f32[1,128,512]{2,1,0:T(8,128)S(1)}, s32[]{:T(128)}, f32[64,128]{1,0:T(8,128)S(1)}, f32[64,1,128,512]{3,2,1,0:T(8,128)}, /*index=5*/s32[]{:T(128)}, s32[]{:T(128)}, s32[]{:T(128)}, s32[]{:T(128)}) while((s32[]{:T(128)}, f32[1,128,512]{2,1,0:T(8,128)S(1)}, s32[]{:T(128)}, f32[64,128]{1,0:T(8,128)S(1)}, ...), condition=%wide.region_5.6_spmd, body=%wide.region_4.5_spmd.sunk | while | flops 131078 | bytes 788123 | solution.py:33
  1303.8 1.1 bitcast_add_fusion.12
  1304.9 1.1 bitcast_add_fusion.12
  1309.3 1.1 bitcast_add_fusion.12
  1310.4 1.1 bitcast_add_fusion.12
  1314.8 1.1 bitcast_add_fusion.12
  1319.2 1.1 bitcast_add_fusion.12
  1320.3 1.1 bitcast_add_fusion.12
  1324.7 1.1 bitcast_add_fusion.12
  1325.8 1.1 bitcast_add_fusion.12
  1330.2 1.1 bitcast_add_fusion.12
  1331.3 1.1 bitcast_add_fusion.12
  1335.8 1.1 bitcast_add_fusion.12
  1340.2 1.1 bitcast_add_fusion.12
  1341.3 1.1 bitcast_add_fusion.12
  1345.7 1.1 bitcast_add_fusion.12
  1346.8 1.1 bitcast_add_fusion.12
  1351.2 1.1 bitcast_add_fusion.12
  1352.3 1.1 bitcast_add_fusion.12
  1356.7 1.1 bitcast_add_fusion.12
  1361.1 1.1 bitcast_add_fusion.12
  1362.2 1.1 bitcast_add_fusion.12
  1366.7 1.1 bitcast_add_fusion.12
  1367.8 1.1 bitcast_add_fusion.12
  1370.8 1.1 fusion.188
  1371.9 1.3 collective-permute-start.3
  1378.1 381.9 %all-gather.17.cloned.1.call-done = f32[64,128,512]{2,1,0:T(8,128)} async-done(((f32[1,128,512]{2,1,0:T(8,128)}), f32[64,128,512]{2,1,0:T(8,128)}) %all-gather.17.cloned.1.call-update) | async-done | bytes 16777232 | tf_op jit(solution)/shard_map/all_gather | solution.py:24
  1760.0 69.8 %while.55 = (s32[]{:T(128)}, f32[1,128,512]{2,1,0:T(8,128)S(1)}, s32[]{:T(128)}, f32[64,128]{1,0:T(8,128)S(1)}, f32[64,1,128,512]{3,2,1,0:T(8,128)}, /*index=5*/s32[]{:T(128)}, s32[]{:T(128)}, s32[]{:T(128)}, s32[]{:T(128)}) while((s32[]{:T(128)}, f32[1,128,512]{2,1,0:T(8,128)S(1)}, s32[]{:T(128)}, f32[64,128]{1,0:T(8,128)S(1)}, ...), condition=%wide.region_7.8_spmd, body=%wide.region_6.7_spmd.sunk | while | flops 131078 | bytes 788123 | solution.py:33
  1761.1 1.1 bitcast_add_fusion.13
  1763.4 1.1 bitcast_add_fusion.13
  1765.6 1.1 bitcast_add_fusion.13
  1767.8 1.1 bitcast_add_fusion.13
  1775.5 1.1 bitcast_add_fusion.13
  1777.7 1.1 bitcast_add_fusion.13
  1779.9 1.1 bitcast_add_fusion.13
  1782.1 1.1 bitcast_add_fusion.13
  1784.3 1.1 bitcast_add_fusion.13
  1786.5 1.1 bitcast_add_fusion.13
  1788.8 1.1 bitcast_add_fusion.13
  1796.5 1.1 bitcast_add_fusion.13
  1798.7 1.1 bitcast_add_fusion.13
  1800.9 1.1 bitcast_add_fusion.13
  1803.1 1.1 bitcast_add_fusion.13
  1830.6 1.1 fusion.193
  1831.9 1.2 convolution_bitcast_fusion
  1840.6 1.1 pad_maximum_fusion
  1841.7 1.2 copy-done.10
  1845.0 60.9 %psum.15 = f32[2,128]{1,0:T(2,128)} all-reduce(f32[2,128]{1,0:T(2,128)S(1)} %pad_maximum_fusion.1), channel_id=1, replica_groups=mesh['layer'=64,'batch'=8] {'batch'}, use_global_device_ids=true, to_apply=%region_11.12 | all-reduce | flops 256 | bytes 2048 | tf_op jit(solution)/shard_map/psum | solution.py:137
  1905.9 80.7 %all-reduce.14.cloned.1.call-done = f32[2,128,1152]{2,1,0:T(8,128)} async-done(((f32[2,128,1152]{2,1,0:T(8,128)}), f32[2,128,1152]{2,1,0:T(8,128)}) %all-reduce.14.cloned.1.call-update) | async-done | bytes 1179664 | tf_op jit(solution)/shard_map/psum | solution.py:137
  1986.6 2.4 copy.213
  (407 shorter events, 132.1 us)
Async XLA Ops:
  7.2 366.4 %all-gather.11.cloned.1.call-start = ((), (), s32[]{:S(2)}) async-start(), calls=%async_computation.1 | async-start | bytes 17039360 | tf_op jit(solution)/shard_map/all_gather | solution.py:24
  8.3 7.7 collective-permute-start
  10.5 1.4 copy-start
  16.0 1.4 copy-start.13
  17.3 817.7 %all-gather.13.cloned.1.call-start = ((), (), s32[]{:S(2)}) async-start(), calls=%async_computation.2 | async-start | bytes 17039360 | tf_op jit(solution)/shard_map/all_gather | solution.py:24
  373.7 7.9 collective-permute-start.1
  381.6 1.4 copy-start.12
  383.0 917.4 %all-gather.15.cloned.1.call-start = ((), (), s32[]{:S(2)}) async-start(), calls=%async_computation.3 | async-start | bytes 17039360 | tf_op jit(solution)/shard_map/all_gather | solution.py:24
  383.9 461.0 %collective-permute-start.2 = (f32[1,128,512]{1,2,0:T(8,128)}, f32[1,128,512]{1,2,0:T(8,128)S(1)}, u32[]{:S(2)}, u32[]{:S(2)}) collective-permute-start(f32[1,128,512]{1,2,0:T(8,128)} %copy.80), channel_id=1, source_target_pairs={{0,8},{8,16},{16,24},{24,32},{32,40},{40,48},{48,56},{56,64},{64,7... | collective-permute-start | bytes 786440 | tf_op jit(solution)/shard_map/ppermute | solution.py:17
  835.5 1.5 copy-start.6
  837.5 4.4 copy-start.3
  840.4 1.5 copy-start.2
  843.3 2.2 copy-start.1
  844.8 0.7 copy-start.11
  845.6 2.4 copy-start.14
  847.9 912.1 %all-gather.17.cloned.1.call-start = ((), (), s32[]{:S(2)}) async-start(), calls=%async_computation.4 | async-start | bytes 17039360 | tf_op jit(solution)/shard_map/all_gather | solution.py:24
  1371.9 2.8 copy-start.8
  1371.9 4.8 collective-permute-start.3
  1373.2 1.5 copy-start.4
  1378.0 608.5 %all-reduce.14.cloned.1.call-start = ((), (), s32[]{:S(2)}) async-start(), calls=%async_computation | async-start | bytes 2359296 | tf_op jit(solution)/shard_map/psum | solution.py:137
  1834.3 1.0 copy-start.5
  1834.3 1.0 copy-start.7
  1836.6 4.0 copy-start.9
  1841.7 1.3 copy-start.10
Sparse Core Ops, SparseCore 0:
  17.5 356.0 all-gather.10
  383.1 451.9 all-gather.12
  848.0 452.3 all-gather.14
  1378.2 381.7 all-gather.16
  1841.8 144.6 all-reduce.13
where the time goes:
time: 2000 us
  waiting for transfers between devices  1330 us (66%)
  blocking collectives  454 us (23%)
  other arithmetic  157 us (8%)
    all_gather x4, waiting for transfers between devices, carried_in(): gathered = jax.tree.map(lambda a: lax.all_gather(a, axis), part)  1240 us
    all_gather x2, blocking collectives, carried_in(): gathered = jax.tree.map(lambda a: lax.all_gather(a, axis), part)  393 us
    add x126, other arithmetic, combine_maps(): later[0][None, :, None] * earlier[1] + later[1]  133 us
    psum x1, waiting for transfers between devices, per_device(): weight_grad, bias_grad = lax.psum((weight_grad, bias_grad), 'batch')  80.7 us
    psum x1, blocking collectives, per_device(): weight_grad, bias_grad = lax.psum((weight_grad, bias_grad), 'batch')  60.9 us
  transfers between devices with their start and end apart: 9, of which 7 were waited for; matrix products, arithmetic and copies ran while one was open for 1% of the time, Pallas kernels for 0%

commit v1 on v0

--- a/solution.py
+++ b/solution.py
@@ -9,28 +9,6 @@
 
 
 step_size = 0.25
-
-
-def from_behind(value, axis, steps):
-    count = lax.axis_size(axis)
-    leading, last = (max(0, -steps), min(count, count - steps))
-    return lax.ppermute(value, axis, [(source, source + steps) for source in range(leading, last)])
-
-
-def carried_in(part, axis, combine, identity, reverse):
-    count = lax.axis_size(axis)
-    place = lax.axis_index(axis)
-    ahead = count - 1 - place if reverse else place
-    gathered = jax.tree.map(lambda a: lax.all_gather(a, axis), part)
-    state = jax.tree.map(lambda a, e: jnp.zeros_like(a) + jnp.asarray(e, a.dtype), part, identity)
-
-    def one(hop, state):
-        source = count - 1 - hop if reverse else hop
-        return combine(
-            state, jax.tree.map(lambda a: lax.dynamic_index_in_dim(a, source, 0, False), gathered)
-        )
-
-    return lax.fori_loop(0, ahead, one, state)
 
 
 def columns(current):
@@ -91,8 +69,33 @@
     return adjoint
 
 
-def combine_maps(earlier, later):
-    return (later[0] * earlier[0], later[0][None, :, None] * earlier[1] + later[1])
+def window_products(table, place, distances):
+    rows = jnp.arange(table.shape[0])
+    out = []
+    for d in distances:
+        inside = (rows >= place - d + 1) & (rows <= place - 1)
+        out.append(jnp.prod(jnp.where(inside[:, None], table, 1.0), axis=0))
+    return out
+
+
+def exclusive_scan(gain, local, table, place, axis, reverse):
+    count = lax.axis_size(axis)
+    distances = []
+    d = 1
+    while d < count:
+        distances.append(d)
+        d *= 2
+    factors = window_products(table, place, distances)
+    total = jnp.zeros_like(local)
+    for d, factor in zip(distances, factors):
+        sending = gain[None, :, None] * total + local
+        if reverse:
+            pairs = [(k, k - d) for k in range(d, count)]
+        else:
+            pairs = [(k, k + d) for k in range(count - d)]
+        received = lax.ppermute(sending, axis, pairs)
+        total = total + factor[None, :, None] * received
+    return total
 
 
 def per_device(initial_state, cotangent, conv_weight, conv_bias, block_gain, adjoint_gain):
@@ -100,25 +103,30 @@
     blocks = lax.axis_size("layer")
     gain_row = block_gain[0]
     back_row = adjoint_gain[0]
-    identity = (jnp.ones_like(gain_row), jnp.zeros_like(initial_state))
+    gain_table = lax.all_gather(gain_row, "layer")
+    back_table = lax.all_gather(back_row, "layer")[::-1]
     flipped_list = [
         flip_weight(conv_weight[layer_index]) for layer_index in range(conv_weight.shape[0])
     ]
     c_points = initial_state
+    following = initial_state
     for sweep_index in range(ITERS):
         ending = relax_block(c_points, conv_weight, conv_bias)[0]
-        following = from_behind(c_points, "layer", -1)
-        residual = jnp.where(position == blocks - 1, jnp.zeros_like(ending), ending - following)
-        prefix = carried_in((gain_row, residual), "layer", combine_maps, identity, False)
-        c_points = c_points + prefix[1]
+        residual = ending - following
+        error = exclusive_scan(gain_row, residual, gain_table, position, "layer", False)
+        c_points = c_points + error
+        following = following + gain_row[None, :, None] * error + residual
     ending, stored = relax_block(c_points, conv_weight, conv_bias)
     target = cotangent
+    previous = cotangent
     for sweep_index in range(ITERS):
         start_adj = adjoint_block(target, stored, flipped_list)
-        previous = from_behind(target, "layer", 1)
-        residual = jnp.where(position == 0, jnp.zeros_like(start_adj), start_adj - previous)
-        prefix = carried_in((back_row, residual), "layer", combine_maps, identity, True)
-        target = target + prefix[1]
+        residual = start_adj - previous
+        error = exclusive_scan(
+            back_row, residual, back_table, blocks - 1 - position, "layer", True
+        )
+        target = target + error
+        previous = previous + back_row[None, :, None] * error + residual
     adjoint = target
     weight_parts = []
     bias_parts = []

time: 2000 us -> 741 us (0.37)
  waiting for transfers between devices: 1330 us -> 208 us
  other arithmetic: 157 us -> 20.8 us
  starting transfers between devices: 7.36 us -> 76.8 us
  blocking collectives: 454 us -> 404 us
    all_gather x4 -> x0, waiting for transfers between devices: 1240 us -> none  [carried_in(): gathered = jax.tree.map(lambda a: lax.all_gather(a, axis), part)]
    add x126 -> x20, other arithmetic: 133 us -> 1.11 us  [exclusive_scan(): sending = gain[None, :, None] * total + local]
    ppermute x4 -> x24, waiting for transfers between devices: 5.24 us -> 120 us  [exclusive_scan(): received = lax.ppermute(sending, axis, pairs)]
    all_gather x2, blocking collectives: 393 us -> 309 us  [the longest x1 157 us: per_device(): gain_table = lax.all_gather(gain_row, 'layer')]
    ppermute x4 -> x24, starting transfers between devices: 7.16 us -> 76.8 us  [exclusive_scan(): received = lax.ppermute(sending, axis, pairs)]
    psum x1, blocking collectives: 60.9 us -> 95.2 us  [per_device(): weight_grad, bias_grad = lax.psum((weight_grad, bias_grad), 'batch')]
  transfers between devices with their start and end apart: 9 -> 25, of which waited for: 7 -> 23; matrix products, arithmetic and copies ran while one was open for 1% -> 1% of each run, Pallas kernels for 0% -> 0%
where the time goes in v1:
time: 741 us; the launch traced here: 740 us
  blocking collectives  404 us (55%)
  waiting for transfers between devices  208 us (28%)
  starting transfers between devices  76.8 us (10%)
  other arithmetic  20.8 us (3%)
  between operations  15.3 us (2%)
  local copies, waits for them, and re-layouts  7.67 us (1%)
    all_gather x1, blocking collectives, per_device(): gain_table = lax.all_gather(gain_row, 'layer')  157 us
    all_gather x1, blocking collectives, per_device(): back_table = lax.all_gather(back_row, 'layer')[::-1]  152 us
    ppermute x24, waiting for transfers between devices, exclusive_scan(): received = lax.ppermute(sending, axis, pairs)  120 us
    psum x1, blocking collectives, per_device(): weight_grad, bias_grad = lax.psum((weight_grad, bias_grad), 'batch')  95.2 us
    psum x1, waiting for transfers between devices, per_device(): weight_grad, bias_grad = lax.psum((weight_grad, bias_grad), 'batch')  87.8 us
    ppermute x24, starting transfers between devices, exclusive_scan(): received = lax.ppermute(sending, axis, pairs)  76.8 us
    unnamed x96, other arithmetic  15.2 us
  transfers between devices with their start and end apart: 25, of which 23 were waited for; matrix products, arithmetic and copies ran while one was open for 1% of the time, Pallas kernels for 0%

profile of v1, /device:TPU:1, one launch (start us, length us, event | category | flops | bytes accessed | tf_op | source)
XLA Modules:
  0.0 739.6 jit_solution(15187054471448019251)
XLA Ops:
  7.2 0.7 broadcast_multiply_fusion.1
  7.9 0.8 slice_bitcast_fusion
  8.7 1.1 copy.45
  11.3 0.5 fusion.202
  13.7 4.0 collective-permute-start
  17.8 157.1 %all-gather = f32[64,1,128]{2,1,0:T(1,128)S(1)} all-gather(f32[1,1,128]{2,1,0:T(1,128)S(1)} %bitcast.398), channel_id=1, replica_groups=mesh['layer'=64,'batch'=8] {'layer'}, dimensions={0}, use_global_device_ids=true | all-gather | bytes 33280 | tf_op jit(solution)/shard_map/all_gather | solution.py:106
  175.1 1.3 collective-permute-start.1
  176.4 3.3 collective-permute-done.1
  179.8 1.3 collective-permute-start.2
  181.1 3.3 collective-permute-done.2
  184.4 2.2 collective-permute-start.3
  186.6 3.3 collective-permute-done.3
  190.0 3.5 collective-permute-start.4
  193.5 4.0 collective-permute-done.4
  197.6 5.4 collective-permute-start.5
  203.0 5.7 collective-permute-done.5
  210.3 0.5 fusion.203
  212.3 0.5 broadcast_add_fusion.2
  212.8 1.3 collective-permute-start.6
  214.1 3.3 collective-permute-done.6
  217.4 5.8 collective-permute-start.7
  223.2 3.3 collective-permute-done.7
  226.6 9.3 %collective-permute-start.8 = (f32[1,128,512]{1,2,0:T(8,128)S(1)}, f32[1,128,512]{1,2,0:T(8,128)S(1)}, u32[]{:S(2)}, u32[]{:S(2)}) collective-permute-start(f32[1,128,512]{1,2,0:T(8,128)S(1)} %get-tuple-element.45), channel_id=1, source_target_pairs={{0,32},{8,40},{16,48},{24,56},{32,64},{40,72},{48,80},{56,88},{64,... | collective-permute-start | bytes 786440 | tf_op jit(solution)/shard_map/ppermute | solution.py:96
  235.9 3.3 collective-permute-done.8
  239.3 5.5 collective-permute-start.9
  244.7 3.3 collective-permute-done.9
  248.1 10.4 %collective-permute-start.10 = (f32[1,128,512]{1,2,0:T(8,128)S(1)}, f32[1,128,512]{1,2,0:T(8,128)S(1)}, u32[]{:S(2)}, u32[]{:S(2)}) collective-permute-start(f32[1,128,512]{1,2,0:T(8,128)S(1)} %get-tuple-element.43), channel_id=1, source_target_pairs={{0,128},{8,136},{16,144},{24,152},{32,160},{40,168},{48,176},{56,1... | collective-permute-start | bytes 786440 | tf_op jit(solution)/shard_map/ppermute | solution.py:96
  259.1 2.7 collective-permute-done.10
  261.8 10.9 %collective-permute-start.11 = (f32[1,128,512]{1,2,0:T(8,128)S(1)}, f32[1,128,512]{1,2,0:T(8,128)S(1)}, u32[]{:S(2)}, u32[]{:S(2)}) collective-permute-start(f32[1,128,512]{1,2,0:T(8,128)S(1)} %multiply_add_fusion.19), channel_id=1, source_target_pairs={{0,256},{8,264},{16,272},{24,280},{32,288},{40,296},{48,304},{56,3... | collective-permute-start | bytes 786440 | tf_op jit(solution)/shard_map/ppermute | solution.py:96
  273.4 2.5 collective-permute-done.11
  279.4 0.5 fusion.175
  281.7 0.5 fusion.173
  283.7 0.5 broadcast_add_fusion.1
  284.2 1.3 collective-permute-start.12
  285.5 152.1 %all-gather.1 = f32[64,1,128]{2,1,0:T(1,128)S(1)} all-gather(f32[1,1,128]{2,1,0:T(1,128)S(1)} %bitcast.410), channel_id=1, replica_groups=mesh['layer'=64,'batch'=8] {'layer'}, dimensions={0}, use_global_device_ids=true | all-gather | bytes 33280 | tf_op jit(solution)/shard_map/all_gather | solution.py:107
  437.8 1.3 collective-permute-start.13
  439.1 7.3 collective-permute-done.13
  446.5 1.3 collective-permute-start.14
  447.8 6.1 collective-permute-done.14
  453.9 1.3 collective-permute-start.15
  455.2 8.5 %collective-permute-done.15 = f32[1,128,512]{1,2,0:T(8,128)S(1)} collective-permute-done((f32[1,128,512]{1,2,0:T(8,128)S(1)}, f32[1,128,512]{1,2,0:T(8,128)S(1)}, u32[]{:S(2)}, u32[]{:S(2)}) %collective-permute-start.15) | collective-permute-done | bytes 262176 | tf_op jit(solution)/shard_map/ppermute | solution.py:96
  463.8 1.3 collective-permute-start.16
  465.1 6.1 collective-permute-done.16
  471.3 1.3 collective-permute-start.17
  472.6 7.3 collective-permute-done.17
  481.5 0.5 fusion.174
  484.0 1.3 collective-permute-start.18
  485.3 6.1 collective-permute-done.18
  491.4 1.3 collective-permute-start.19
  492.7 7.6 %collective-permute-done.19 = f32[1,128,512]{1,2,0:T(8,128)S(1)} collective-permute-done((f32[1,128,512]{1,2,0:T(8,128)S(1)}, f32[1,128,512]{1,2,0:T(8,128)S(1)}, u32[]{:S(2)}, u32[]{:S(2)}) %collective-permute-start.19) | collective-permute-done | bytes 262176 | tf_op jit(solution)/shard_map/ppermute | solution.py:96
  500.4 1.3 collective-permute-start.20
  501.7 8.0 %collective-permute-done.20 = f32[1,128,512]{1,2,0:T(8,128)S(1)} collective-permute-done((f32[1,128,512]{1,2,0:T(8,128)S(1)}, f32[1,128,512]{1,2,0:T(8,128)S(1)}, u32[]{:S(2)}, u32[]{:S(2)}) %collective-permute-start.20) | collective-permute-done | bytes 262176 | tf_op jit(solution)/shard_map/ppermute | solution.py:96
  509.7 1.3 collective-permute-start.21
  511.0 11.6 %collective-permute-done.21 = f32[1,128,512]{1,2,0:T(8,128)S(1)} collective-permute-done((f32[1,128,512]{1,2,0:T(8,128)S(1)}, f32[1,128,512]{1,2,0:T(8,128)S(1)}, u32[]{:S(2)}, u32[]{:S(2)}) %collective-permute-start.21) | collective-permute-done | bytes 262176 | tf_op jit(solution)/shard_map/ppermute | solution.py:96
  522.7 1.3 collective-permute-start.22
  524.0 5.8 collective-permute-done.22
  529.9 1.6 collective-permute-start.23
  531.6 7.8 %collective-permute-done.23 = f32[1,128,512]{1,2,0:T(8,128)S(1)} collective-permute-done((f32[1,128,512]{1,2,0:T(8,128)S(1)}, f32[1,128,512]{1,2,0:T(8,128)S(1)}, u32[]{:S(2)}, u32[]{:S(2)}) %collective-permute-start.23) | collective-permute-done | bytes 262176 | tf_op jit(solution)/shard_map/ppermute | solution.py:96
  542.8 1.1 pad_maximum_fusion
  543.9 0.8 copy.54
  546.6 0.8 copy.55
  547.4 95.2 %psum.15 = f32[2,128]{1,0:T(2,128)} all-reduce(f32[2,128]{1,0:T(2,128)S(1)} %pad_maximum_fusion.1), channel_id=1, replica_groups=mesh['layer'=64,'batch'=8] {'batch'}, use_global_device_ids=true, to_apply=%region_15.16 | all-reduce | flops 256 | bytes 2048 | tf_op jit(solution)/shard_map/psum | solution.py:145
  642.6 87.8 %all-reduce.14.cloned.1.call-done = f32[2,128,1152]{2,1,0:T(8,128)} async-done(((f32[2,128,1152]{2,1,0:T(8,128)}), f32[2,128,1152]{2,1,0:T(8,128)}) %all-reduce.14.cloned.1.call-update) | async-done | bytes 1179664 | tf_op jit(solution)/shard_map/psum | solution.py:145
  730.4 2.4 copy.155
  (184 shorter events, 24.1 us)
Async XLA Ops:
  7.2 723.2 %all-reduce.14.cloned.1.call-start = ((), (), s32[]{:S(2)}) async-start(), calls=%async_computation | async-start | bytes 2359296 | tf_op jit(solution)/shard_map/psum | solution.py:145
  9.9 1.4 copy-start
  13.2 4.5 copy-start.6
  13.7 161.3 %collective-permute-start = (f32[1,128,512]{1,2,0:T(8,128)S(1)}, f32[1,128,512]{1,2,0:T(8,128)S(1)}, u32[]{:S(2)}, u32[]{:S(2)}) collective-permute-start(f32[1,128,512]{1,2,0:T(8,128)S(1)} %get-tuple-element.63), channel_id=1, source_target_pairs={{0,8},{8,16},{16,24},{24,32},{32,40},{40,48},{48,56},{56,64},{64,7... | collective-permute-start | bytes 786440 | tf_op jit(solution)/shard_map/ppermute | solution.py:96
  175.1 4.6 collective-permute-start.1
  179.8 4.6 collective-permute-start.2
  184.4 5.5 collective-permute-start.3
  190.0 7.5 %collective-permute-start.4 = (f32[1,128,512]{1,2,0:T(8,128)S(1)}, f32[1,128,512]{1,2,0:T(8,128)S(1)}, u32[]{:S(2)}, u32[]{:S(2)}) collective-permute-start(f32[1,128,512]{1,2,0:T(8,128)S(1)} %get-tuple-element.50), channel_id=1, source_target_pairs={{0,128},{8,136},{16,144},{24,152},{32,160},{40,168},{48,176},{56,1... | collective-permute-start | bytes 786440 | tf_op jit(solution)/shard_map/ppermute | solution.py:96
  197.6 11.1 %collective-permute-start.5 = (f32[1,128,512]{1,2,0:T(8,128)S(1)}, f32[1,128,512]{1,2,0:T(8,128)S(1)}, u32[]{:S(2)}, u32[]{:S(2)}) collective-permute-start(f32[1,128,512]{1,2,0:T(8,128)S(1)} %multiply_add_fusion.29), channel_id=1, source_target_pairs={{0,256},{8,264},{16,272},{24,280},{32,288},{40,296},{48,304},{56,3... | collective-permute-start | bytes 786440 | tf_op jit(solution)/shard_map/ppermute | solution.py:96
  212.8 4.6 collective-permute-start.6
  217.4 9.1 %collective-permute-start.7 = (f32[1,128,512]{1,2,0:T(8,128)S(1)}, f32[1,128,512]{1,2,0:T(8,128)S(1)}, u32[]{:S(2)}, u32[]{:S(2)}) collective-permute-start(f32[1,128,512]{1,2,0:T(8,128)S(1)} %multiply_add_fusion.27), channel_id=1, source_target_pairs={{0,16},{8,24},{16,32},{24,40},{32,48},{40,56},{48,64},{56,72},{64,... | collective-permute-start | bytes 786440 | tf_op jit(solution)/shard_map/ppermute | solution.py:96
  226.6 12.6 %collective-permute-start.8 = (f32[1,128,512]{1,2,0:T(8,128)S(1)}, f32[1,128,512]{1,2,0:T(8,128)S(1)}, u32[]{:S(2)}, u32[]{:S(2)}) collective-permute-start(f32[1,128,512]{1,2,0:T(8,128)S(1)} %get-tuple-element.45), channel_id=1, source_target_pairs={{0,32},{8,40},{16,48},{24,56},{32,64},{40,72},{48,80},{56,88},{64,... | collective-permute-start | bytes 786440 | tf_op jit(solution)/shard_map/ppermute | solution.py:96
  239.3 8.8 %collective-permute-start.9 = (f32[1,128,512]{1,2,0:T(8,128)S(1)}, f32[1,128,512]{1,2,0:T(8,128)S(1)}, u32[]{:S(2)}, u32[]{:S(2)}) collective-permute-start(f32[1,128,512]{1,2,0:T(8,128)S(1)} %multiply_add_fusion.23), channel_id=1, source_target_pairs={{0,64},{8,72},{16,80},{24,88},{32,96},{40,104},{48,112},{56,120},{... | collective-permute-start | bytes 786440 | tf_op jit(solution)/shard_map/ppermute | solution.py:96
  248.1 13.7 %collective-permute-start.10 = (f32[1,128,512]{1,2,0:T(8,128)S(1)}, f32[1,128,512]{1,2,0:T(8,128)S(1)}, u32[]{:S(2)}, u32[]{:S(2)}) collective-permute-start(f32[1,128,512]{1,2,0:T(8,128)S(1)} %get-tuple-element.43), channel_id=1, source_target_pairs={{0,128},{8,136},{16,144},{24,152},{32,160},{40,168},{48,176},{56,1... | collective-permute-start | bytes 786440 | tf_op jit(solution)/shard_map/ppermute | solution.py:96
  259.0 13.8 %copy-start.5 = (f32[1,128,512]{2,1,0:T(8,128)S(1)}, f32[1,128,512]{2,1,0:T(8,128)}, u32[]{:S(2)}) copy-start(f32[1,128,512]{2,1,0:T(8,128)} %param.7) | copy-start | bytes 786436
  261.8 11.6 %copy-start.7 = (f32[1,128]{1,0:T(1,128)S(1)}, f32[1,128]{1,0:T(1,128)}, u32[]{:S(2)}) copy-start(f32[1,128]{1,0:T(1,128)} %param.11) | copy-start | bytes 1540
  261.8 14.0 %collective-permute-start.11 = (f32[1,128,512]{1,2,0:T(8,128)S(1)}, f32[1,128,512]{1,2,0:T(8,128)S(1)}, u32[]{:S(2)}, u32[]{:S(2)}) collective-permute-start(f32[1,128,512]{1,2,0:T(8,128)S(1)} %multiply_add_fusion.19), channel_id=1, source_target_pairs={{0,256},{8,264},{16,272},{24,280},{32,288},{40,296},{48,304},{56,3... | collective-permute-start | bytes 786440 | tf_op jit(solution)/shard_map/ppermute | solution.py:96
  275.9 1.5 copy-start.3
  279.4 1.0 copy-start.1
  284.2 153.5 %collective-permute-start.12 = (f32[1,128,512]{1,2,0:T(8,128)S(1)}, f32[1,128,512]{1,2,0:T(8,128)S(1)}, u32[]{:S(2)}, u32[]{:S(2)}) collective-permute-start(f32[1,128,512]{1,2,0:T(8,128)S(1)} %get-tuple-element.75), channel_id=1, source_target_pairs={{8,0},{16,8},{24,16},{32,24},{40,32},{48,40},{56,48},{64,56},{72,6... | collective-permute-start | bytes 786440 | tf_op jit(solution)/shard_map/ppermute | solution.py:96
  437.8 8.6 %collective-permute-start.13 = (f32[1,128,512]{1,2,0:T(8,128)S(1)}, f32[1,128,512]{1,2,0:T(8,128)S(1)}, u32[]{:S(2)}, u32[]{:S(2)}) collective-permute-start(f32[1,128,512]{1,2,0:T(8,128)S(1)} %multiply_add_fusion.18), channel_id=1, source_target_pairs={{16,0},{24,8},{32,16},{40,24},{48,32},{56,40},{64,48},{72,56},{80,... | collective-permute-start | bytes 786440 | tf_op jit(solution)/shard_map/ppermute | solution.py:96
  446.5 7.4 %collective-permute-start.14 = (f32[1,128,512]{1,2,0:T(8,128)S(1)}, f32[1,128,512]{1,2,0:T(8,128)S(1)}, u32[]{:S(2)}, u32[]{:S(2)}) collective-permute-start(f32[1,128,512]{1,2,0:T(8,128)S(1)} %get-tuple-element.39), channel_id=1, source_target_pairs={{32,0},{40,8},{48,16},{56,24},{64,32},{72,40},{80,48},{88,56},{96,... | collective-permute-start | bytes 786440 | tf_op jit(solution)/shard_map/ppermute | solution.py:96
  453.9 9.8 %collective-permute-start.15 = (f32[1,128,512]{1,2,0:T(8,128)S(1)}, f32[1,128,512]{1,2,0:T(8,128)S(1)}, u32[]{:S(2)}, u32[]{:S(2)}) collective-permute-start(f32[1,128,512]{1,2,0:T(8,128)S(1)} %multiply_add_fusion.14), channel_id=1, source_target_pairs={{64,0},{72,8},{80,16},{88,24},{96,32},{104,40},{112,48},{120,56},{... | collective-permute-start | bytes 786440 | tf_op jit(solution)/shard_map/ppermute | solution.py:96
  463.8 7.4 %collective-permute-start.16 = (f32[1,128,512]{1,2,0:T(8,128)S(1)}, f32[1,128,512]{1,2,0:T(8,128)S(1)}, u32[]{:S(2)}, u32[]{:S(2)}) collective-permute-start(f32[1,128,512]{1,2,0:T(8,128)S(1)} %get-tuple-element.37), channel_id=1, source_target_pairs={{128,0},{136,8},{144,16},{152,24},{160,32},{168,40},{176,48},{184,... | collective-permute-start | bytes 786440 | tf_op jit(solution)/shard_map/ppermute | solution.py:96
  471.3 8.6 %collective-permute-start.17 = (f32[1,128,512]{1,2,0:T(8,128)S(1)}, f32[1,128,512]{1,2,0:T(8,128)S(1)}, u32[]{:S(2)}, u32[]{:S(2)}) collective-permute-start(f32[1,128,512]{1,2,0:T(8,128)S(1)} %multiply_add_fusion.10), channel_id=1, source_target_pairs={{256,0},{264,8},{272,16},{280,24},{288,32},{296,40},{304,48},{312,... | collective-permute-start | bytes 786440 | tf_op jit(solution)/shard_map/ppermute | solution.py:96
  484.0 7.4 %collective-permute-start.18 = (f32[1,128,512]{1,2,0:T(8,128)S(1)}, f32[1,128,512]{1,2,0:T(8,128)S(1)}, u32[]{:S(2)}, u32[]{:S(2)}) collective-permute-start(f32[1,128,512]{1,2,0:T(8,128)S(1)} %get-tuple-element.79), channel_id=1, source_target_pairs={{8,0},{16,8},{24,16},{32,24},{40,32},{48,40},{56,48},{64,56},{72,6... | collective-permute-start | bytes 786440 | tf_op jit(solution)/shard_map/ppermute | solution.py:96
  491.4 8.9 %collective-permute-start.19 = (f32[1,128,512]{1,2,0:T(8,128)S(1)}, f32[1,128,512]{1,2,0:T(8,128)S(1)}, u32[]{:S(2)}, u32[]{:S(2)}) collective-permute-start(f32[1,128,512]{1,2,0:T(8,128)S(1)} %multiply_add_fusion.8), channel_id=1, source_target_pairs={{16,0},{24,8},{32,16},{40,24},{48,32},{56,40},{64,48},{72,56},{80,... | collective-permute-start | bytes 786440 | tf_op jit(solution)/shard_map/ppermute | solution.py:96
  500.4 9.3 %collective-permute-start.20 = (f32[1,128,512]{1,2,0:T(8,128)S(1)}, f32[1,128,512]{1,2,0:T(8,128)S(1)}, u32[]{:S(2)}, u32[]{:S(2)}) collective-permute-start(f32[1,128,512]{1,2,0:T(8,128)S(1)} %get-tuple-element.32), channel_id=1, source_target_pairs={{32,0},{40,8},{48,16},{56,24},{64,32},{72,40},{80,48},{88,56},{96,... | collective-permute-start | bytes 786440 | tf_op jit(solution)/shard_map/ppermute | solution.py:96
  509.7 12.9 %collective-permute-start.21 = (f32[1,128,512]{1,2,0:T(8,128)S(1)}, f32[1,128,512]{1,2,0:T(8,128)S(1)}, u32[]{:S(2)}, u32[]{:S(2)}) collective-permute-start(f32[1,128,512]{1,2,0:T(8,128)S(1)} %multiply_add_fusion.4), channel_id=1, source_target_pairs={{64,0},{72,8},{80,16},{88,24},{96,32},{104,40},{112,48},{120,56},{... | collective-permute-start | bytes 786440 | tf_op jit(solution)/shard_map/ppermute | solution.py:96
  522.7 7.1 collective-permute-start.22
  529.9 9.6 %copy-start.2 = (bf16[1,1152,512]{1,2,0:T(8,128)(2,1)S(1)}, bf16[1,1152,512]{1,2,0:T(8,128)(2,1)}, u32[]{:S(2)}) copy-start(bf16[1,1152,512]{1,2,0:T(8,128)(2,1)} %copy-done.1) | copy-start | bytes 3538948
  529.9 9.4 %collective-permute-start.23 = (f32[1,128,512]{1,2,0:T(8,128)S(1)}, f32[1,128,512]{1,2,0:T(8,128)S(1)}, u32[]{:S(2)}, u32[]{:S(2)}) collective-permute-start(f32[1,128,512]{1,2,0:T(8,128)S(1)} %multiply_add_fusion), channel_id=1, source_target_pairs={{256,0},{264,8},{272,16},{280,24},{288,32},{296,40},{304,48},{312,... | collective-permute-start | bytes 786440 | tf_op jit(solution)/shard_map/ppermute | solution.py:96
  541.2 1.0 copy-start.4
Sparse Core Ops, SparseCore 0:
  544.0 186.3 all-reduce.13

commit v2 on v1

--- a/solution.py
+++ b/solution.py
@@ -69,42 +69,51 @@
     return adjoint
 
 
-def window_products(table, place, distances):
-    rows = jnp.arange(table.shape[0])
-    out = []
-    for d in distances:
-        inside = (rows >= place - d + 1) & (rows <= place - 1)
-        out.append(jnp.prod(jnp.where(inside[:, None], table, 1.0), axis=0))
-    return out
-
-
-def exclusive_scan(gain, local, table, place, axis, reverse):
-    count = lax.axis_size(axis)
+def scan_distances(count):
     distances = []
     d = 1
     while d < count:
         distances.append(d)
         d *= 2
-    factors = window_products(table, place, distances)
+    return distances
+
+
+def scan_pairs(count, d, reverse):
+    if reverse:
+        return [(k, k - d) for k in range(d, count)]
+    return [(k, k + d) for k in range(count - d)]
+
+
+def exclusive_scan_first(gain, local, axis, reverse):
+    count = lax.axis_size(axis)
+    channels, pixels = local.shape[1], local.shape[2]
     total = jnp.zeros_like(local)
-    for d, factor in zip(distances, factors):
+    product = jnp.ones_like(gain)
+    factors = []
+    for d in scan_distances(count):
         sending = gain[None, :, None] * total + local
-        if reverse:
-            pairs = [(k, k - d) for k in range(d, count)]
-        else:
-            pairs = [(k, k + d) for k in range(count - d)]
-        received = lax.ppermute(sending, axis, pairs)
+        gain_row = jnp.pad(gain * product, (0, pixels - channels))
+        packed = jnp.concatenate([sending, gain_row[None, None, :]], axis=1)
+        received = lax.ppermute(packed, axis, scan_pairs(count, d, reverse))
+        factors.append(product)
+        total = total + product[None, :, None] * received[:, :channels, :]
+        product = product * received[0, channels, :channels]
+    return total, factors
+
+
+def exclusive_scan_again(gain, local, factors, axis, reverse):
+    count = lax.axis_size(axis)
+    total = jnp.zeros_like(local)
+    for d, factor in zip(scan_distances(count), factors):
+        sending = gain[None, :, None] * total + local
+        received = lax.ppermute(sending, axis, scan_pairs(count, d, reverse))
         total = total + factor[None, :, None] * received
     return total
 
 
 def per_device(initial_state, cotangent, conv_weight, conv_bias, block_gain, adjoint_gain):
-    position = lax.axis_index("layer")
-    blocks = lax.axis_size("layer")
     gain_row = block_gain[0]
     back_row = adjoint_gain[0]
-    gain_table = lax.all_gather(gain_row, "layer")
-    back_table = lax.all_gather(back_row, "layer")[::-1]
     flipped_list = [
         flip_weight(conv_weight[layer_index]) for layer_index in range(conv_weight.shape[0])
     ]
@@ -113,7 +122,10 @@
     for sweep_index in range(ITERS):
         ending = relax_block(c_points, conv_weight, conv_bias)[0]
         residual = ending - following
-        error = exclusive_scan(gain_row, residual, gain_table, position, "layer", False)
+        if sweep_index == 0:
+            error, factors = exclusive_scan_first(gain_row, residual, "layer", False)
+        else:
+            error = exclusive_scan_again(gain_row, residual, factors, "layer", False)
         c_points = c_points + error
         following = following + gain_row[None, :, None] * error + residual
     ending, stored = relax_block(c_points, conv_weight, conv_bias)
@@ -122,9 +134,10 @@
     for sweep_index in range(ITERS):
         start_adj = adjoint_block(target, stored, flipped_list)
         residual = start_adj - previous
-        error = exclusive_scan(
-            back_row, residual, back_table, blocks - 1 - position, "layer", True
-        )
+        if sweep_index == 0:
+            error, factors = exclusive_scan_first(back_row, residual, "layer", True)
+        else:
+            error = exclusive_scan_again(back_row, residual, factors, "layer", True)
         target = target + error
         previous = previous + back_row[None, :, None] * error + residual
     adjoint = target
@@ -140,9 +153,17 @@
         bias_part = jnp.sum(scaled, axis=(0, 2))
         weight_parts.insert(0, weight_part)
         bias_parts.insert(0, bias_part)
-    weight_grad = jnp.stack(weight_parts)
-    bias_grad = jnp.stack(bias_parts)
-    weight_grad, bias_grad = lax.psum((weight_grad, bias_grad), "batch")
+    width = weight_parts[0].shape[1]
+    channels = weight_parts[0].shape[0]
+    packed = jnp.stack(
+        [
+            jnp.concatenate([w, jnp.pad(b, (0, width - channels))[None, :]], axis=0)
+            for w, b in zip(weight_parts, bias_parts)
+        ]
+    )
+    packed = lax.psum(packed, "batch")
+    weight_grad = packed[:, :channels, :]
+    bias_grad = packed[:, channels, :channels]
     return (ending[None], adjoint[None], weight_grad, bias_grad)
 
 

time: 741 us -> 438 us (0.59)
  blocking collectives: 404 us -> 0 us
  waiting for transfers between devices: 208 us -> 286 us
  starting transfers between devices: 76.8 us -> 107 us
    all_gather x2 -> x0, blocking collectives: 309 us -> none  [the longest x1 157 us: per_device(): gain_table = lax.all_gather(gain_row, 'layer')]
    psum x1 -> x0, blocking collectives: 95.2 us -> none  [per_device(): weight_grad, bias_grad = lax.psum((weight_grad, bias_grad), 'batch')]
    psum x1, waiting for transfers between devices: 87.8 us -> 141 us  [per_device(): packed = lax.psum(packed, 'batch')]
    ppermute x24, starting transfers between devices: 76.8 us -> 107 us  [the longest x12 56.9 us: exclusive_scan_first(): received = lax.ppermute(packed, axis, scan_pairs(count, d, reverse))]
    ppermute x24, waiting for transfers between devices: 120 us -> 145 us  [the longest x12 74 us: exclusive_scan_again(): received = lax.ppermute(sending, axis, scan_pairs(count, d, reverse))]
  transfers between devices with their start and end apart: 25 -> 25, of which waited for: 23 -> 25; matrix products, arithmetic and copies ran while one was open for 1% -> 1% of each run, Pallas kernels for 0% -> 0%
where the time goes in v2:
time: 438 us; the launch traced here: 437 us
  waiting for transfers between devices  286 us (65%)
  starting transfers between devices  107 us (24%)
  other arithmetic  17.1 us (4%)
  between operations  15.6 us (4%)
  matrix products  6.22 us (1%)
  local copies, waits for them, and re-layouts  5.7 us (1%)
    psum x1, waiting for transfers between devices, per_device(): packed = lax.psum(packed, 'batch')  141 us
    ppermute x12, waiting for transfers between devices, exclusive_scan_again(): received = lax.ppermute(sending, axis, scan_pairs(count, d, reverse))  74 us
    ppermute x12, waiting for transfers between devices, exclusive_scan_first(): received = lax.ppermute(packed, axis, scan_pairs(count, d, reverse))  70.9 us
    ppermute x12, starting transfers between devices, exclusive_scan_first(): received = lax.ppermute(packed, axis, scan_pairs(count, d, reverse))  56.9 us
    ppermute x12, starting transfers between devices, exclusive_scan_again(): received = lax.ppermute(sending, axis, scan_pairs(count, d, reverse))  49.9 us
    unnamed x96, other arithmetic  9.1 us
  transfers between devices with their start and end apart: 25, of which 25 were waited for; matrix products, arithmetic and copies ran while one was open for 1% of the time, Pallas kernels for 0%

profile of v2, /device:TPU:1, one launch (start us, length us, event | category | flops | bytes accessed | tf_op | source)
XLA Modules:
  0.0 437.1 jit_solution(17419453857398917620)
XLA Ops:
  7.3 0.7 broadcast_multiply_fusion.1
  7.9 0.8 slice_bitcast_fusion.10
  8.7 1.0 convert_element_type.65
  12.6 4.0 collective-permute-start
  16.5 3.5 collective-permute-done
  20.1 7.5 %collective-permute-start.1 = (f32[1,129,512]{2,1,0:T(8,128)S(1)}, f32[1,129,512]{2,1,0:T(8,128)S(1)}, u32[]{:S(2)}, u32[]{:S(2)}) collective-permute-start(f32[1,129,512]{2,1,0:T(8,128)S(1)} %pad_maximum_fusion.2), channel_id=1, source_target_pairs={{0,16},{8,24},{16,32},{24,40},{32,48},{40,56},{48,64},{56,72},{64,... | collective-permute-start | bytes 792584 | tf_op jit(solution)/shard_map/ppermute | solution.py:97
  27.6 4.4 collective-permute-done.1
  32.1 7.5 %collective-permute-start.2 = (f32[1,129,512]{2,1,0:T(8,128)S(1)}, f32[1,129,512]{2,1,0:T(8,128)S(1)}, u32[]{:S(2)}, u32[]{:S(2)}) collective-permute-start(f32[1,129,512]{2,1,0:T(8,128)S(1)} %pad_maximum_fusion.3), channel_id=1, source_target_pairs={{0,32},{8,40},{16,48},{24,56},{32,64},{40,72},{48,80},{56,88},{64,... | collective-permute-start | bytes 792584 | tf_op jit(solution)/shard_map/ppermute | solution.py:97
  39.7 3.5 collective-permute-done.2
  43.3 5.2 %collective-permute-start.3 = (f32[1,129,512]{2,1,0:T(8,128)S(1)}, f32[1,129,512]{2,1,0:T(8,128)S(1)}, u32[]{:S(2)}, u32[]{:S(2)}) collective-permute-start(f32[1,129,512]{2,1,0:T(8,128)S(1)} %pad_maximum_fusion.4), channel_id=1, source_target_pairs={{0,64},{8,72},{16,80},{24,88},{32,96},{40,104},{48,112},{56,120},{... | collective-permute-start | bytes 792584 | tf_op jit(solution)/shard_map/ppermute | solution.py:97
  48.5 3.5 collective-permute-done.3
  52.1 19.2 %collective-permute-start.4 = (f32[1,129,512]{2,1,0:T(8,128)S(1)}, f32[1,129,512]{2,1,0:T(8,128)S(1)}, u32[]{:S(2)}, u32[]{:S(2)}) collective-permute-start(f32[1,129,512]{2,1,0:T(8,128)S(1)} %pad_maximum_fusion.5), channel_id=1, source_target_pairs={{0,128},{8,136},{16,144},{24,152},{32,160},{40,168},{48,176},{56,1... | collective-permute-start | bytes 792584 | tf_op jit(solution)/shard_map/ppermute | solution.py:97
  71.3 5.1 %collective-permute-done.4 = f32[1,129,512]{2,1,0:T(8,128)S(1)} collective-permute-done((f32[1,129,512]{2,1,0:T(8,128)S(1)}, f32[1,129,512]{2,1,0:T(8,128)S(1)}, u32[]{:S(2)}, u32[]{:S(2)}) %collective-permute-start.4) | collective-permute-done | bytes 264224 | tf_op jit(solution)/shard_map/ppermute | solution.py:97
  76.6 5.7 %collective-permute-start.5 = (f32[1,129,512]{2,1,0:T(8,128)S(1)}, f32[1,129,512]{2,1,0:T(8,128)S(1)}, u32[]{:S(2)}, u32[]{:S(2)}) collective-permute-start(f32[1,129,512]{2,1,0:T(8,128)S(1)} %pad_maximum_fusion.6), channel_id=1, source_target_pairs={{0,256},{8,264},{16,272},{24,280},{32,288},{40,296},{48,304},{56,3... | collective-permute-start | bytes 792584 | tf_op jit(solution)/shard_map/ppermute | solution.py:97
  82.2 4.2 collective-permute-done.5
  89.1 1.3 collective-permute-start.6
  90.4 3.3 collective-permute-done.6
  93.8 2.9 collective-permute-start.7
  96.7 3.3 collective-permute-done.7
  100.1 6.3 %collective-permute-start.8 = (f32[1,128,512]{2,1,0:T(8,128)S(1)}, f32[1,128,512]{2,1,0:T(8,128)S(1)}, u32[]{:S(2)}, u32[]{:S(2)}) collective-permute-start(f32[1,128,512]{2,1,0:T(8,128)S(1)} %multiply_add_fusion.20), channel_id=1, source_target_pairs={{0,32},{8,40},{16,48},{24,56},{32,64},{40,72},{48,80},{56,88},{64,... | collective-permute-start | bytes 786440 | tf_op jit(solution)/shard_map/ppermute | solution.py:109
  106.4 3.3 collective-permute-done.8
  109.9 7.9 %collective-permute-start.9 = (f32[1,128,512]{2,1,0:T(8,128)S(1)}, f32[1,128,512]{2,1,0:T(8,128)S(1)}, u32[]{:S(2)}, u32[]{:S(2)}) collective-permute-start(f32[1,128,512]{2,1,0:T(8,128)S(1)} %get-tuple-element.29), channel_id=1, source_target_pairs={{0,64},{8,72},{16,80},{24,88},{32,96},{40,104},{48,112},{56,120},{... | collective-permute-start | bytes 786440 | tf_op jit(solution)/shard_map/ppermute | solution.py:109
  117.7 3.3 collective-permute-done.9
  121.2 17.5 %collective-permute-start.10 = (f32[1,128,512]{2,1,0:T(8,128)S(1)}, f32[1,128,512]{2,1,0:T(8,128)S(1)}, u32[]{:S(2)}, u32[]{:S(2)}) collective-permute-start(f32[1,128,512]{2,1,0:T(8,128)S(1)} %multiply_add_fusion.16), channel_id=1, source_target_pairs={{0,128},{8,136},{16,144},{24,152},{32,160},{40,168},{48,176},{56,1... | collective-permute-start | bytes 786440 | tf_op jit(solution)/shard_map/ppermute | solution.py:109
  139.2 5.6 %collective-permute-done.10 = f32[1,128,512]{2,1,0:T(8,128)S(1)} collective-permute-done((f32[1,128,512]{2,1,0:T(8,128)S(1)}, f32[1,128,512]{2,1,0:T(8,128)S(1)}, u32[]{:S(2)}, u32[]{:S(2)}) %collective-permute-start.10) | collective-permute-done | bytes 262176 | tf_op jit(solution)/shard_map/ppermute | solution.py:109
  144.9 6.3 %collective-permute-start.11 = (f32[1,128,512]{2,1,0:T(8,128)S(1)}, f32[1,128,512]{2,1,0:T(8,128)S(1)}, u32[]{:S(2)}, u32[]{:S(2)}) collective-permute-start(f32[1,128,512]{2,1,0:T(8,128)S(1)} %get-tuple-element.27), channel_id=1, source_target_pairs={{0,256},{8,264},{16,272},{24,280},{32,288},{40,296},{48,304},{56,3... | collective-permute-start | bytes 786440 | tf_op jit(solution)/shard_map/ppermute | solution.py:109
  151.7 2.8 collective-permute-done.11
  158.1 0.4 fusion.185
  159.4 0.4 broadcast_add_fusion.1
  159.9 1.3 collective-permute-start.12
  161.2 6.0 %collective-permute-done.12 = f32[1,129,512]{2,1,0:T(8,128)S(1)} collective-permute-done((f32[1,129,512]{2,1,0:T(8,128)S(1)}, f32[1,129,512]{2,1,0:T(8,128)S(1)}, u32[]{:S(2)}, u32[]{:S(2)}) %collective-permute-start.12) | collective-permute-done | bytes 264224 | tf_op jit(solution)/shard_map/ppermute | solution.py:97
  167.3 1.3 collective-permute-start.13
  168.6 7.5 %collective-permute-done.13 = f32[1,129,512]{2,1,0:T(8,128)S(1)} collective-permute-done((f32[1,129,512]{2,1,0:T(8,128)S(1)}, f32[1,129,512]{2,1,0:T(8,128)S(1)}, u32[]{:S(2)}, u32[]{:S(2)}) %collective-permute-start.13) | collective-permute-done | bytes 264224 | tf_op jit(solution)/shard_map/ppermute | solution.py:97
  176.3 1.3 collective-permute-start.14
  177.6 8.3 %collective-permute-done.14 = f32[1,129,512]{2,1,0:T(8,128)S(1)} collective-permute-done((f32[1,129,512]{2,1,0:T(8,128)S(1)}, f32[1,129,512]{2,1,0:T(8,128)S(1)}, u32[]{:S(2)}, u32[]{:S(2)}) %collective-permute-start.14) | collective-permute-done | bytes 264224 | tf_op jit(solution)/shard_map/ppermute | solution.py:97
  186.1 1.3 collective-permute-start.15
  187.4 11.8 %collective-permute-done.15 = f32[1,129,512]{2,1,0:T(8,128)S(1)} collective-permute-done((f32[1,129,512]{2,1,0:T(8,128)S(1)}, f32[1,129,512]{2,1,0:T(8,128)S(1)}, u32[]{:S(2)}, u32[]{:S(2)}) %collective-permute-start.15) | collective-permute-done | bytes 264224 | tf_op jit(solution)/shard_map/ppermute | solution.py:97
  199.3 1.3 collective-permute-start.16
  200.6 6.0 %collective-permute-done.16 = f32[1,129,512]{2,1,0:T(8,128)S(1)} collective-permute-done((f32[1,129,512]{2,1,0:T(8,128)S(1)}, f32[1,129,512]{2,1,0:T(8,128)S(1)}, u32[]{:S(2)}, u32[]{:S(2)}) %collective-permute-start.16) | collective-permute-done | bytes 264224 | tf_op jit(solution)/shard_map/ppermute | solution.py:97
  206.8 1.5 collective-permute-start.17
  208.3 7.3 %collective-permute-done.17 = f32[1,129,512]{2,1,0:T(8,128)S(1)} collective-permute-done((f32[1,129,512]{2,1,0:T(8,128)S(1)}, f32[1,129,512]{2,1,0:T(8,128)S(1)}, u32[]{:S(2)}, u32[]{:S(2)}) %collective-permute-start.17) | collective-permute-done | bytes 264224 | tf_op jit(solution)/shard_map/ppermute | solution.py:97
  216.7 0.4 fusion.186
  218.0 0.4 broadcast_add_fusion
  218.4 1.3 collective-permute-start.18
  219.7 7.1 %collective-permute-done.18 = f32[1,128,512]{2,1,0:T(8,128)S(1)} collective-permute-done((f32[1,128,512]{2,1,0:T(8,128)S(1)}, f32[1,128,512]{2,1,0:T(8,128)S(1)}, u32[]{:S(2)}, u32[]{:S(2)}) %collective-permute-start.18) | collective-permute-done | bytes 262176 | tf_op jit(solution)/shard_map/ppermute | solution.py:109
  226.9 1.3 collective-permute-start.19
  228.2 9.1 %collective-permute-done.19 = f32[1,128,512]{2,1,0:T(8,128)S(1)} collective-permute-done((f32[1,128,512]{2,1,0:T(8,128)S(1)}, f32[1,128,512]{2,1,0:T(8,128)S(1)}, u32[]{:S(2)}, u32[]{:S(2)}) %collective-permute-start.19) | collective-permute-done | bytes 262176 | tf_op jit(solution)/shard_map/ppermute | solution.py:109
  237.4 1.3 collective-permute-start.20
  238.7 8.1 %collective-permute-done.20 = f32[1,128,512]{2,1,0:T(8,128)S(1)} collective-permute-done((f32[1,128,512]{2,1,0:T(8,128)S(1)}, f32[1,128,512]{2,1,0:T(8,128)S(1)}, u32[]{:S(2)}, u32[]{:S(2)}) %collective-permute-start.20) | collective-permute-done | bytes 262176 | tf_op jit(solution)/shard_map/ppermute | solution.py:109
  247.0 1.3 collective-permute-start.21
  248.3 12.6 %collective-permute-done.21 = f32[1,128,512]{2,1,0:T(8,128)S(1)} collective-permute-done((f32[1,128,512]{2,1,0:T(8,128)S(1)}, f32[1,128,512]{2,1,0:T(8,128)S(1)}, u32[]{:S(2)}, u32[]{:S(2)}) %collective-permute-start.21) | collective-permute-done | bytes 262176 | tf_op jit(solution)/shard_map/ppermute | solution.py:109
  261.0 1.3 collective-permute-start.22
  262.3 5.8 %collective-permute-done.22 = f32[1,128,512]{2,1,0:T(8,128)S(1)} collective-permute-done((f32[1,128,512]{2,1,0:T(8,128)S(1)}, f32[1,128,512]{2,1,0:T(8,128)S(1)}, u32[]{:S(2)}, u32[]{:S(2)}) %collective-permute-start.22) | collective-permute-done | bytes 262176 | tf_op jit(solution)/shard_map/ppermute | solution.py:109
  268.3 1.3 collective-permute-start.23
  269.6 9.7 %collective-permute-done.23 = f32[1,128,512]{2,1,0:T(8,128)S(1)} collective-permute-done((f32[1,128,512]{2,1,0:T(8,128)S(1)}, f32[1,128,512]{2,1,0:T(8,128)S(1)}, u32[]{:S(2)}, u32[]{:S(2)}) %collective-permute-start.23) | collective-permute-done | bytes 262176 | tf_op jit(solution)/shard_map/ppermute | solution.py:109
  279.5 0.5 fusion.12
  280.9 0.4 fusion.70
  281.3 0.8 fusion.291
  282.1 0.5 fusion.16
  282.9 1.1 pad_maximum_fusion
  284.9 1.1 fusion.67
  285.9 140.7 %all-reduce.28.cloned.1.call-done = f32[2,129,1152]{2,1,0:T(8,128)} async-done(((f32[2,129,1152]{2,1,0:T(8,128)}), f32[2,129,1152]{2,1,0:T(8,128)}) %all-reduce.28.cloned.1.call-update) | async-done | bytes 1188880 | tf_op jit(solution)/shard_map/psum | solution.py:164
  426.7 1.3 slice.541
  427.9 2.4 slice.540
  (203 shorter events, 17.1 us)
Async XLA Ops:
  7.2 2.9 copy-start.1
  7.2 419.5 %all-reduce.28.cloned.1.call-start = ((), (), s32[]{:S(2)}) async-start(), calls=%async_computation | async-start | bytes 2506752 | tf_op jit(solution)/shard_map/psum | solution.py:164
  9.8 1.1 copy-start
  11.2 0.9 copy-start.3
  12.6 7.4 %collective-permute-start = (f32[1,129,512]{2,1,0:T(8,128)S(1)}, f32[1,129,512]{2,1,0:T(8,128)S(1)}, u32[]{:S(2)}, u32[]{:S(2)}) collective-permute-start(f32[1,129,512]{2,1,0:T(8,128)S(1)} %pad_maximum_fusion.1), channel_id=1, source_target_pairs={{0,8},{8,16},{16,24},{24,32},{32,40},{40,48},{48,56},{56,64},{64,7... | collective-permute-start | bytes 792584 | tf_op jit(solution)/shard_map/ppermute | solution.py:97
  20.1 11.9 %collective-permute-start.1 = (f32[1,129,512]{2,1,0:T(8,128)S(1)}, f32[1,129,512]{2,1,0:T(8,128)S(1)}, u32[]{:S(2)}, u32[]{:S(2)}) collective-permute-start(f32[1,129,512]{2,1,0:T(8,128)S(1)} %pad_maximum_fusion.2), channel_id=1, source_target_pairs={{0,16},{8,24},{16,32},{24,40},{32,48},{40,56},{48,64},{56,72},{64,... | collective-permute-start | bytes 792584 | tf_op jit(solution)/shard_map/ppermute | solution.py:97
  32.1 11.0 %collective-permute-start.2 = (f32[1,129,512]{2,1,0:T(8,128)S(1)}, f32[1,129,512]{2,1,0:T(8,128)S(1)}, u32[]{:S(2)}, u32[]{:S(2)}) collective-permute-start(f32[1,129,512]{2,1,0:T(8,128)S(1)} %pad_maximum_fusion.3), channel_id=1, source_target_pairs={{0,32},{8,40},{16,48},{24,56},{32,64},{40,72},{48,80},{56,88},{64,... | collective-permute-start | bytes 792584 | tf_op jit(solution)/shard_map/ppermute | solution.py:97
  43.3 8.7 %collective-permute-start.3 = (f32[1,129,512]{2,1,0:T(8,128)S(1)}, f32[1,129,512]{2,1,0:T(8,128)S(1)}, u32[]{:S(2)}, u32[]{:S(2)}) collective-permute-start(f32[1,129,512]{2,1,0:T(8,128)S(1)} %pad_maximum_fusion.4), channel_id=1, source_target_pairs={{0,64},{8,72},{16,80},{24,88},{32,96},{40,104},{48,112},{56,120},{... | collective-permute-start | bytes 792584 | tf_op jit(solution)/shard_map/ppermute | solution.py:97
  52.1 24.3 %collective-permute-start.4 = (f32[1,129,512]{2,1,0:T(8,128)S(1)}, f32[1,129,512]{2,1,0:T(8,128)S(1)}, u32[]{:S(2)}, u32[]{:S(2)}) collective-permute-start(f32[1,129,512]{2,1,0:T(8,128)S(1)} %pad_maximum_fusion.5), channel_id=1, source_target_pairs={{0,128},{8,136},{16,144},{24,152},{32,160},{40,168},{48,176},{56,1... | collective-permute-start | bytes 792584 | tf_op jit(solution)/shard_map/ppermute | solution.py:97
  76.6 9.8 %collective-permute-start.5 = (f32[1,129,512]{2,1,0:T(8,128)S(1)}, f32[1,129,512]{2,1,0:T(8,128)S(1)}, u32[]{:S(2)}, u32[]{:S(2)}) collective-permute-start(f32[1,129,512]{2,1,0:T(8,128)S(1)} %pad_maximum_fusion.6), channel_id=1, source_target_pairs={{0,256},{8,264},{16,272},{24,280},{32,288},{40,296},{48,304},{56,3... | collective-permute-start | bytes 792584 | tf_op jit(solution)/shard_map/ppermute | solution.py:97
  89.1 4.6 %collective-permute-start.6 = (f32[1,128,512]{2,1,0:T(8,128)S(1)}, f32[1,128,512]{2,1,0:T(8,128)S(1)}, u32[]{:S(2)}, u32[]{:S(2)}) collective-permute-start(f32[1,128,512]{2,1,0:T(8,128)S(1)} %get-tuple-element.59), channel_id=1, source_target_pairs={{0,8},{8,16},{16,24},{24,32},{32,40},{40,48},{48,56},{56,64},{64,7... | collective-permute-start | bytes 786440 | tf_op jit(solution)/shard_map/ppermute | solution.py:109
  93.8 6.2 %collective-permute-start.7 = (f32[1,128,512]{2,1,0:T(8,128)S(1)}, f32[1,128,512]{2,1,0:T(8,128)S(1)}, u32[]{:S(2)}, u32[]{:S(2)}) collective-permute-start(f32[1,128,512]{2,1,0:T(8,128)S(1)} %multiply_add_fusion.22), channel_id=1, source_target_pairs={{0,16},{8,24},{16,32},{24,40},{32,48},{40,56},{48,64},{56,72},{64,... | collective-permute-start | bytes 786440 | tf_op jit(solution)/shard_map/ppermute | solution.py:109
  100.1 9.6 %collective-permute-start.8 = (f32[1,128,512]{2,1,0:T(8,128)S(1)}, f32[1,128,512]{2,1,0:T(8,128)S(1)}, u32[]{:S(2)}, u32[]{:S(2)}) collective-permute-start(f32[1,128,512]{2,1,0:T(8,128)S(1)} %multiply_add_fusion.20), channel_id=1, source_target_pairs={{0,32},{8,40},{16,48},{24,56},{32,64},{40,72},{48,80},{56,88},{64,... | collective-permute-start | bytes 786440 | tf_op jit(solution)/shard_map/ppermute | solution.py:109
  109.9 11.2 %collective-permute-start.9 = (f32[1,128,512]{2,1,0:T(8,128)S(1)}, f32[1,128,512]{2,1,0:T(8,128)S(1)}, u32[]{:S(2)}, u32[]{:S(2)}) collective-permute-start(f32[1,128,512]{2,1,0:T(8,128)S(1)} %get-tuple-element.29), channel_id=1, source_target_pairs={{0,64},{8,72},{16,80},{24,88},{32,96},{40,104},{48,112},{56,120},{... | collective-permute-start | bytes 786440 | tf_op jit(solution)/shard_map/ppermute | solution.py:109
  121.2 23.6 %collective-permute-start.10 = (f32[1,128,512]{2,1,0:T(8,128)S(1)}, f32[1,128,512]{2,1,0:T(8,128)S(1)}, u32[]{:S(2)}, u32[]{:S(2)}) collective-permute-start(f32[1,128,512]{2,1,0:T(8,128)S(1)} %multiply_add_fusion.16), channel_id=1, source_target_pairs={{0,128},{8,136},{16,144},{24,152},{32,160},{40,168},{48,176},{56,1... | collective-permute-start | bytes 786440 | tf_op jit(solution)/shard_map/ppermute | solution.py:109
  139.2 12.0 %copy-start.4 = (f32[1,128]{1,0:T(1,128)S(1)}, f32[1,128]{1,0:T(1,128)}, u32[]{:S(2)}) copy-start(f32[1,128]{1,0:T(1,128)} %param.11) | copy-start | bytes 1540
  144.9 9.5 %collective-permute-start.11 = (f32[1,128,512]{2,1,0:T(8,128)S(1)}, f32[1,128,512]{2,1,0:T(8,128)S(1)}, u32[]{:S(2)}, u32[]{:S(2)}) collective-permute-start(f32[1,128,512]{2,1,0:T(8,128)S(1)} %get-tuple-element.27), channel_id=1, source_target_pairs={{0,256},{8,264},{16,272},{24,280},{32,288},{40,296},{48,304},{56,3... | collective-permute-start | bytes 786440 | tf_op jit(solution)/shard_map/ppermute | solution.py:109
  155.9 1.0 copy-start.2
  159.9 7.3 %collective-permute-start.12 = (f32[1,129,512]{2,1,0:T(8,128)S(1)}, f32[1,129,512]{2,1,0:T(8,128)S(1)}, u32[]{:S(2)}, u32[]{:S(2)}) collective-permute-start(f32[1,129,512]{2,1,0:T(8,128)S(1)} %pad_maximum_fusion.7), channel_id=1, source_target_pairs={{8,0},{16,8},{24,16},{32,24},{40,32},{48,40},{56,48},{64,56},{72,6... | collective-permute-start | bytes 792584 | tf_op jit(solution)/shard_map/ppermute | solution.py:97
  167.3 8.8 %collective-permute-start.13 = (f32[1,129,512]{2,1,0:T(8,128)S(1)}, f32[1,129,512]{2,1,0:T(8,128)S(1)}, u32[]{:S(2)}, u32[]{:S(2)}) collective-permute-start(f32[1,129,512]{2,1,0:T(8,128)S(1)} %pad_maximum_fusion.8), channel_id=1, source_target_pairs={{16,0},{24,8},{32,16},{40,24},{48,32},{56,40},{64,48},{72,56},{80,... | collective-permute-start | bytes 792584 | tf_op jit(solution)/shard_map/ppermute | solution.py:97
  176.3 9.6 %collective-permute-start.14 = (f32[1,129,512]{2,1,0:T(8,128)S(1)}, f32[1,129,512]{2,1,0:T(8,128)S(1)}, u32[]{:S(2)}, u32[]{:S(2)}) collective-permute-start(f32[1,129,512]{2,1,0:T(8,128)S(1)} %pad_maximum_fusion.9), channel_id=1, source_target_pairs={{32,0},{40,8},{48,16},{56,24},{64,32},{72,40},{80,48},{88,56},{96,... | collective-permute-start | bytes 792584 | tf_op jit(solution)/shard_map/ppermute | solution.py:97
  186.1 13.1 %collective-permute-start.15 = (f32[1,129,512]{2,1,0:T(8,128)S(1)}, f32[1,129,512]{2,1,0:T(8,128)S(1)}, u32[]{:S(2)}, u32[]{:S(2)}) collective-permute-start(f32[1,129,512]{2,1,0:T(8,128)S(1)} %pad_maximum_fusion.10), channel_id=1, source_target_pairs={{64,0},{72,8},{80,16},{88,24},{96,32},{104,40},{112,48},{120,56},{... | collective-permute-start | bytes 792584 | tf_op jit(solution)/shard_map/ppermute | solution.py:97
  199.3 7.3 %collective-permute-start.16 = (f32[1,129,512]{2,1,0:T(8,128)S(1)}, f32[1,129,512]{2,1,0:T(8,128)S(1)}, u32[]{:S(2)}, u32[]{:S(2)}) collective-permute-start(f32[1,129,512]{2,1,0:T(8,128)S(1)} %pad_maximum_fusion.11), channel_id=1, source_target_pairs={{128,0},{136,8},{144,16},{152,24},{160,32},{168,40},{176,48},{184,... | collective-permute-start | bytes 792584 | tf_op jit(solution)/shard_map/ppermute | solution.py:97
  206.8 8.8 %collective-permute-start.17 = (f32[1,129,512]{2,1,0:T(8,128)S(1)}, f32[1,129,512]{2,1,0:T(8,128)S(1)}, u32[]{:S(2)}, u32[]{:S(2)}) collective-permute-start(f32[1,129,512]{2,1,0:T(8,128)S(1)} %pad_maximum_fusion.12), channel_id=1, source_target_pairs={{256,0},{264,8},{272,16},{280,24},{288,32},{296,40},{304,48},{312,... | collective-permute-start | bytes 792584 | tf_op jit(solution)/shard_map/ppermute | solution.py:97
  218.4 8.4 %collective-permute-start.18 = (f32[1,128,512]{2,1,0:T(8,128)S(1)}, f32[1,128,512]{2,1,0:T(8,128)S(1)}, u32[]{:S(2)}, u32[]{:S(2)}) collective-permute-start(f32[1,128,512]{2,1,0:T(8,128)S(1)} %get-tuple-element.71), channel_id=1, source_target_pairs={{8,0},{16,8},{24,16},{32,24},{40,32},{48,40},{56,48},{64,56},{72,6... | collective-permute-start | bytes 786440 | tf_op jit(solution)/shard_map/ppermute | solution.py:109
  226.9 10.4 %collective-permute-start.19 = (f32[1,128,512]{2,1,0:T(8,128)S(1)}, f32[1,128,512]{2,1,0:T(8,128)S(1)}, u32[]{:S(2)}, u32[]{:S(2)}) collective-permute-start(f32[1,128,512]{2,1,0:T(8,128)S(1)} %multiply_add_fusion.8), channel_id=1, source_target_pairs={{16,0},{24,8},{32,16},{40,24},{48,32},{56,40},{64,48},{72,56},{80,... | collective-permute-start | bytes 786440 | tf_op jit(solution)/shard_map/ppermute | solution.py:109
  237.4 9.4 %collective-permute-start.20 = (f32[1,128,512]{2,1,0:T(8,128)S(1)}, f32[1,128,512]{2,1,0:T(8,128)S(1)}, u32[]{:S(2)}, u32[]{:S(2)}) collective-permute-start(f32[1,128,512]{2,1,0:T(8,128)S(1)} %multiply_add_fusion.6), channel_id=1, source_target_pairs={{32,0},{40,8},{48,16},{56,24},{64,32},{72,40},{80,48},{88,56},{96,... | collective-permute-start | bytes 786440 | tf_op jit(solution)/shard_map/ppermute | solution.py:109
  247.0 13.9 %collective-permute-start.21 = (f32[1,128,512]{2,1,0:T(8,128)S(1)}, f32[1,128,512]{2,1,0:T(8,128)S(1)}, u32[]{:S(2)}, u32[]{:S(2)}) collective-permute-start(f32[1,128,512]{2,1,0:T(8,128)S(1)} %get-tuple-element.8), channel_id=1, source_target_pairs={{64,0},{72,8},{80,16},{88,24},{96,32},{104,40},{112,48},{120,56},{... | collective-permute-start | bytes 786440 | tf_op jit(solution)/shard_map/ppermute | solution.py:109
  261.0 7.1 %collective-permute-start.22 = (f32[1,128,512]{2,1,0:T(8,128)S(1)}, f32[1,128,512]{2,1,0:T(8,128)S(1)}, u32[]{:S(2)}, u32[]{:S(2)}) collective-permute-start(f32[1,128,512]{2,1,0:T(8,128)S(1)} %multiply_add_fusion.2), channel_id=1, source_target_pairs={{128,0},{136,8},{144,16},{152,24},{160,32},{168,40},{176,48},{184,... | collective-permute-start | bytes 786440 | tf_op jit(solution)/shard_map/ppermute | solution.py:109
  268.3 11.0 %collective-permute-start.23 = (f32[1,128,512]{2,1,0:T(8,128)S(1)}, f32[1,128,512]{2,1,0:T(8,128)S(1)}, u32[]{:S(2)}, u32[]{:S(2)}) collective-permute-start(f32[1,128,512]{2,1,0:T(8,128)S(1)} %get-tuple-element.6), channel_id=1, source_target_pairs={{256,0},{264,8},{272,16},{280,24},{288,32},{296,40},{304,48},{312,... | collective-permute-start | bytes 786440 | tf_op jit(solution)/shard_map/ppermute | solution.py:109
Sparse Core Ops, SparseCore 0:
  284.2 142.4 all-reduce.27

commit v3 on v2

--- a/solution.py
+++ b/solution.py
@@ -109,6 +109,38 @@
         received = lax.ppermute(sending, axis, scan_pairs(count, d, reverse))
         total = total + factor[None, :, None] * received
     return total
+
+
+def batch_sum(value, axis):
+    count = lax.axis_size(axis)
+    me = lax.axis_index(axis)
+    shape = value.shape
+    flat = value.reshape(-1)
+    lanes = 128
+    quantum = lanes * 8 * count
+    padded_size = -(-flat.shape[0] // quantum) * quantum
+    current = jnp.pad(flat, (0, padded_size - flat.shape[0])).reshape(-1, lanes)
+    steps = []
+    step = 1
+    while step < count:
+        steps.append(step)
+        step *= 2
+    for step in steps:
+        rows = current.shape[0] // 2
+        mine = (me // step) % 2
+        keep = lax.dynamic_slice_in_dim(current, mine * rows, rows, 0)
+        give = lax.dynamic_slice_in_dim(current, (1 - mine) * rows, rows, 0)
+        pairs = [(k, k ^ step) for k in range(count)]
+        current = keep + lax.ppermute(give, axis, pairs)
+    for step in steps[::-1]:
+        rows = current.shape[0]
+        mine = (me // step) % 2
+        pairs = [(k, k ^ step) for k in range(count)]
+        other = lax.ppermute(current, axis, pairs)
+        whole = jnp.zeros((2 * rows, lanes), current.dtype)
+        whole = lax.dynamic_update_slice_in_dim(whole, current, mine * rows, 0)
+        current = lax.dynamic_update_slice_in_dim(whole, other, (1 - mine) * rows, 0)
+    return current.reshape(-1)[: flat.shape[0]].reshape(shape)
 
 
 def per_device(initial_state, cotangent, conv_weight, conv_bias, block_gain, adjoint_gain):
@@ -161,7 +193,7 @@
             for w, b in zip(weight_parts, bias_parts)
         ]
     )
-    packed = lax.psum(packed, "batch")
+    packed = batch_sum(packed, "batch")
     weight_grad = packed[:, :channels, :]
     bias_grad = packed[:, channels, :channels]
     return (ending[None], adjoint[None], weight_grad, bias_grad)

time: 438 us -> 422 us (0.963); the launches traced: 437 us -> 414 us
  waiting for transfers between devices: 286 us -> 218 us
  starting transfers between devices: 107 us -> 163 us
  between operations: 15.6 us -> 2.52 us
    psum x1 -> x0, waiting for transfers between devices: 141 us -> none  [per_device(): packed = lax.psum(packed, 'batch')]
    ppermute x0 -> x6, waiting for transfers between devices: none -> 73.9 us  [the longest x3 37.4 us: batch_sum(): other = lax.ppermute(current, axis, pairs)]
    ppermute x0 -> x6, starting transfers between devices: none -> 56.3 us  [the longest x3 45.6 us: batch_sum(): current = keep + lax.ppermute(give, axis, pairs)]
  transfers between devices with their start and end apart: 25 -> 30, of which waited for: 25 -> 30; matrix products, arithmetic and copies ran while one was open for 1% -> 1% of each run, Pallas kernels for 0% -> 0%
where the time goes in v3:
time: 422 us; the launch traced here: 414 us
  waiting for transfers between devices  218 us (52%)
  starting transfers between devices  163 us (39%)
  other arithmetic  17.9 us (4%)
  matrix products  6.24 us (1%)
  local copies, waits for them, and re-layouts  5.96 us (1%)
    ppermute x12, waiting for transfers between devices, exclusive_scan_again(): received = lax.ppermute(sending, axis, scan_pairs(count, d, reverse))  73.5 us
    ppermute x12, waiting for transfers between devices, exclusive_scan_first(): received = lax.ppermute(packed, axis, scan_pairs(count, d, reverse))  70.8 us
    ppermute x12, starting transfers between devices, exclusive_scan_first(): received = lax.ppermute(packed, axis, scan_pairs(count, d, reverse))  57 us
    ppermute x12, starting transfers between devices, exclusive_scan_again(): received = lax.ppermute(sending, axis, scan_pairs(count, d, reverse))  49.8 us
    ppermute x3, starting transfers between devices, batch_sum(): current = keep + lax.ppermute(give, axis, pairs)  45.6 us
    ppermute x3, waiting for transfers between devices, batch_sum(): other = lax.ppermute(current, axis, pairs)  37.4 us
    ppermute x3, waiting for transfers between devices, batch_sum(): current = keep + lax.ppermute(give, axis, pairs)  36.4 us
    ppermute x3, starting transfers between devices, batch_sum(): other = lax.ppermute(current, axis, pairs)  10.7 us
  transfers between devices with their start and end apart: 30, of which 30 were waited for; matrix products, arithmetic and copies ran while one was open for 1% of the time, Pallas kernels for 0%

profile of v3, /device:TPU:1, one launch (start us, length us, event | category | flops | bytes accessed | tf_op | source)
XLA Modules:
  0.0 413.9 jit_solution(13291644465001188903)
XLA Ops:
  2.1 1.0 convert_element_type.67
  6.0 4.0 collective-permute-start
  10.0 3.5 collective-permute-done
  13.5 7.5 %collective-permute-start.1 = (f32[1,129,512]{2,1,0:T(8,128)S(1)}, f32[1,129,512]{2,1,0:T(8,128)S(1)}, u32[]{:S(2)}, u32[]{:S(2)}) collective-permute-start(f32[1,129,512]{2,1,0:T(8,128)S(1)} %pad_maximum_fusion.2), channel_id=1, source_target_pairs={{0,16},{8,24},{16,32},{24,40},{32,48},{40,56},{48,64},{56,72},{64,... | collective-permute-start | bytes 792584 | tf_op jit(solution)/shard_map/ppermute | solution.py:97
  21.0 4.4 %collective-permute-done.1 = f32[1,129,512]{2,1,0:T(8,128)S(1)} collective-permute-done((f32[1,129,512]{2,1,0:T(8,128)S(1)}, f32[1,129,512]{2,1,0:T(8,128)S(1)}, u32[]{:S(2)}, u32[]{:S(2)}) %collective-permute-start.1) | collective-permute-done | bytes 264224 | tf_op jit(solution)/shard_map/ppermute | solution.py:97
  25.6 7.5 %collective-permute-start.2 = (f32[1,129,512]{2,1,0:T(8,128)S(1)}, f32[1,129,512]{2,1,0:T(8,128)S(1)}, u32[]{:S(2)}, u32[]{:S(2)}) collective-permute-start(f32[1,129,512]{2,1,0:T(8,128)S(1)} %pad_maximum_fusion.3), channel_id=1, source_target_pairs={{0,32},{8,40},{16,48},{24,56},{32,64},{40,72},{48,80},{56,88},{64,... | collective-permute-start | bytes 792584 | tf_op jit(solution)/shard_map/ppermute | solution.py:97
  33.1 3.5 collective-permute-done.2
  36.7 5.2 %collective-permute-start.3 = (f32[1,129,512]{2,1,0:T(8,128)S(1)}, f32[1,129,512]{2,1,0:T(8,128)S(1)}, u32[]{:S(2)}, u32[]{:S(2)}) collective-permute-start(f32[1,129,512]{2,1,0:T(8,128)S(1)} %pad_maximum_fusion.4), channel_id=1, source_target_pairs={{0,64},{8,72},{16,80},{24,88},{32,96},{40,104},{48,112},{56,120},{... | collective-permute-start | bytes 792584 | tf_op jit(solution)/shard_map/ppermute | solution.py:97
  41.9 3.5 collective-permute-done.3
  45.5 19.1 %collective-permute-start.4 = (f32[1,129,512]{2,1,0:T(8,128)S(1)}, f32[1,129,512]{2,1,0:T(8,128)S(1)}, u32[]{:S(2)}, u32[]{:S(2)}) collective-permute-start(f32[1,129,512]{2,1,0:T(8,128)S(1)} %pad_maximum_fusion.5), channel_id=1, source_target_pairs={{0,128},{8,136},{16,144},{24,152},{32,160},{40,168},{48,176},{56,1... | collective-permute-start | bytes 792584 | tf_op jit(solution)/shard_map/ppermute | solution.py:97
  64.7 5.1 %collective-permute-done.4 = f32[1,129,512]{2,1,0:T(8,128)S(1)} collective-permute-done((f32[1,129,512]{2,1,0:T(8,128)S(1)}, f32[1,129,512]{2,1,0:T(8,128)S(1)}, u32[]{:S(2)}, u32[]{:S(2)}) %collective-permute-start.4) | collective-permute-done | bytes 264224 | tf_op jit(solution)/shard_map/ppermute | solution.py:97
  69.9 5.7 %collective-permute-start.5 = (f32[1,129,512]{2,1,0:T(8,128)S(1)}, f32[1,129,512]{2,1,0:T(8,128)S(1)}, u32[]{:S(2)}, u32[]{:S(2)}) collective-permute-start(f32[1,129,512]{2,1,0:T(8,128)S(1)} %pad_maximum_fusion.6), channel_id=1, source_target_pairs={{0,256},{8,264},{16,272},{24,280},{32,288},{40,296},{48,304},{56,3... | collective-permute-start | bytes 792584 | tf_op jit(solution)/shard_map/ppermute | solution.py:97
  75.6 4.2 %collective-permute-done.5 = f32[1,129,512]{2,1,0:T(8,128)S(1)} collective-permute-done((f32[1,129,512]{2,1,0:T(8,128)S(1)}, f32[1,129,512]{2,1,0:T(8,128)S(1)}, u32[]{:S(2)}, u32[]{:S(2)}) %collective-permute-start.5) | collective-permute-done | bytes 264224 | tf_op jit(solution)/shard_map/ppermute | solution.py:97
  82.5 1.3 collective-permute-start.6
  83.9 3.3 collective-permute-done.6
  87.2 2.9 collective-permute-start.7
  90.1 3.3 collective-permute-done.7
  93.5 6.3 %collective-permute-start.8 = (f32[1,128,512]{2,1,0:T(8,128)S(1)}, f32[1,128,512]{2,1,0:T(8,128)S(1)}, u32[]{:S(2)}, u32[]{:S(2)}) collective-permute-start(f32[1,128,512]{2,1,0:T(8,128)S(1)} %multiply_add_fusion.20), channel_id=1, source_target_pairs={{0,32},{8,40},{16,48},{24,56},{32,64},{40,72},{48,80},{56,88},{64,... | collective-permute-start | bytes 786440 | tf_op jit(solution)/shard_map/ppermute | solution.py:109
  99.8 3.3 collective-permute-done.8
  103.2 7.9 %collective-permute-start.9 = (f32[1,128,512]{2,1,0:T(8,128)S(1)}, f32[1,128,512]{2,1,0:T(8,128)S(1)}, u32[]{:S(2)}, u32[]{:S(2)}) collective-permute-start(f32[1,128,512]{2,1,0:T(8,128)S(1)} %get-tuple-element.35), channel_id=1, source_target_pairs={{0,64},{8,72},{16,80},{24,88},{32,96},{40,104},{48,112},{56,120},{... | collective-permute-start | bytes 786440 | tf_op jit(solution)/shard_map/ppermute | solution.py:109
  111.1 3.3 collective-permute-done.9
  114.5 17.5 %collective-permute-start.10 = (f32[1,128,512]{2,1,0:T(8,128)S(1)}, f32[1,128,512]{2,1,0:T(8,128)S(1)}, u32[]{:S(2)}, u32[]{:S(2)}) collective-permute-start(f32[1,128,512]{2,1,0:T(8,128)S(1)} %multiply_add_fusion.16), channel_id=1, source_target_pairs={{0,128},{8,136},{16,144},{24,152},{32,160},{40,168},{48,176},{56,1... | collective-permute-start | bytes 786440 | tf_op jit(solution)/shard_map/ppermute | solution.py:109
  132.6 5.6 %collective-permute-done.10 = f32[1,128,512]{2,1,0:T(8,128)S(1)} collective-permute-done((f32[1,128,512]{2,1,0:T(8,128)S(1)}, f32[1,128,512]{2,1,0:T(8,128)S(1)}, u32[]{:S(2)}, u32[]{:S(2)}) %collective-permute-start.10) | collective-permute-done | bytes 262176 | tf_op jit(solution)/shard_map/ppermute | solution.py:109
  138.3 6.2 %collective-permute-start.11 = (f32[1,128,512]{2,1,0:T(8,128)S(1)}, f32[1,128,512]{2,1,0:T(8,128)S(1)}, u32[]{:S(2)}, u32[]{:S(2)}) collective-permute-start(f32[1,128,512]{2,1,0:T(8,128)S(1)} %get-tuple-element.33), channel_id=1, source_target_pairs={{0,256},{8,264},{16,272},{24,280},{32,288},{40,296},{48,304},{56,3... | collective-permute-start | bytes 786440 | tf_op jit(solution)/shard_map/ppermute | solution.py:109
  145.7 2.1 collective-permute-done.11
  153.4 1.3 collective-permute-start.12
  154.7 6.0 %collective-permute-done.12 = f32[1,129,512]{2,1,0:T(8,128)S(1)} collective-permute-done((f32[1,129,512]{2,1,0:T(8,128)S(1)}, f32[1,129,512]{2,1,0:T(8,128)S(1)}, u32[]{:S(2)}, u32[]{:S(2)}) %collective-permute-start.12) | collective-permute-done | bytes 264224 | tf_op jit(solution)/shard_map/ppermute | solution.py:97
  160.8 1.3 collective-permute-start.13
  162.1 7.5 %collective-permute-done.13 = f32[1,129,512]{2,1,0:T(8,128)S(1)} collective-permute-done((f32[1,129,512]{2,1,0:T(8,128)S(1)}, f32[1,129,512]{2,1,0:T(8,128)S(1)}, u32[]{:S(2)}, u32[]{:S(2)}) %collective-permute-start.13) | collective-permute-done | bytes 264224 | tf_op jit(solution)/shard_map/ppermute | solution.py:97
  169.8 1.3 collective-permute-start.14
  171.1 8.3 %collective-permute-done.14 = f32[1,129,512]{2,1,0:T(8,128)S(1)} collective-permute-done((f32[1,129,512]{2,1,0:T(8,128)S(1)}, f32[1,129,512]{2,1,0:T(8,128)S(1)}, u32[]{:S(2)}, u32[]{:S(2)}) %collective-permute-start.14) | collective-permute-done | bytes 264224 | tf_op jit(solution)/shard_map/ppermute | solution.py:97
  179.5 1.3 collective-permute-start.15
  180.8 11.7 %collective-permute-done.15 = f32[1,129,512]{2,1,0:T(8,128)S(1)} collective-permute-done((f32[1,129,512]{2,1,0:T(8,128)S(1)}, f32[1,129,512]{2,1,0:T(8,128)S(1)}, u32[]{:S(2)}, u32[]{:S(2)}) %collective-permute-start.15) | collective-permute-done | bytes 264224 | tf_op jit(solution)/shard_map/ppermute | solution.py:97
  192.7 1.3 collective-permute-start.16
  194.0 6.1 %collective-permute-done.16 = f32[1,129,512]{2,1,0:T(8,128)S(1)} collective-permute-done((f32[1,129,512]{2,1,0:T(8,128)S(1)}, f32[1,129,512]{2,1,0:T(8,128)S(1)}, u32[]{:S(2)}, u32[]{:S(2)}) %collective-permute-start.16) | collective-permute-done | bytes 264224 | tf_op jit(solution)/shard_map/ppermute | solution.py:97
  200.2 1.5 collective-permute-start.17
  201.7 7.3 %collective-permute-done.17 = f32[1,129,512]{2,1,0:T(8,128)S(1)} collective-permute-done((f32[1,129,512]{2,1,0:T(8,128)S(1)}, f32[1,129,512]{2,1,0:T(8,128)S(1)}, u32[]{:S(2)}, u32[]{:S(2)}) %collective-permute-start.17) | collective-permute-done | bytes 264224 | tf_op jit(solution)/shard_map/ppermute | solution.py:97
  211.9 1.3 collective-permute-start.18
  213.2 7.2 %collective-permute-done.18 = f32[1,128,512]{2,1,0:T(8,128)S(1)} collective-permute-done((f32[1,128,512]{2,1,0:T(8,128)S(1)}, f32[1,128,512]{2,1,0:T(8,128)S(1)}, u32[]{:S(2)}, u32[]{:S(2)}) %collective-permute-start.18) | collective-permute-done | bytes 262176 | tf_op jit(solution)/shard_map/ppermute | solution.py:109
  220.4 1.3 collective-permute-start.19
  221.7 9.1 %collective-permute-done.19 = f32[1,128,512]{2,1,0:T(8,128)S(1)} collective-permute-done((f32[1,128,512]{2,1,0:T(8,128)S(1)}, f32[1,128,512]{2,1,0:T(8,128)S(1)}, u32[]{:S(2)}, u32[]{:S(2)}) %collective-permute-start.19) | collective-permute-done | bytes 262176 | tf_op jit(solution)/shard_map/ppermute | solution.py:109
  230.9 1.3 collective-permute-start.20
  232.2 8.1 %collective-permute-done.20 = f32[1,128,512]{2,1,0:T(8,128)S(1)} collective-permute-done((f32[1,128,512]{2,1,0:T(8,128)S(1)}, f32[1,128,512]{2,1,0:T(8,128)S(1)}, u32[]{:S(2)}, u32[]{:S(2)}) %collective-permute-start.20) | collective-permute-done | bytes 262176 | tf_op jit(solution)/shard_map/ppermute | solution.py:109
  240.5 1.3 collective-permute-start.21
  241.8 12.6 %collective-permute-done.21 = f32[1,128,512]{2,1,0:T(8,128)S(1)} collective-permute-done((f32[1,128,512]{2,1,0:T(8,128)S(1)}, f32[1,128,512]{2,1,0:T(8,128)S(1)}, u32[]{:S(2)}, u32[]{:S(2)}) %collective-permute-start.21) | collective-permute-done | bytes 262176 | tf_op jit(solution)/shard_map/ppermute | solution.py:109
  254.5 1.3 collective-permute-start.22
  255.8 5.8 %collective-permute-done.22 = f32[1,128,512]{2,1,0:T(8,128)S(1)} collective-permute-done((f32[1,128,512]{2,1,0:T(8,128)S(1)}, f32[1,128,512]{2,1,0:T(8,128)S(1)}, u32[]{:S(2)}, u32[]{:S(2)}) %collective-permute-start.22) | collective-permute-done | bytes 262176 | tf_op jit(solution)/shard_map/ppermute | solution.py:109
  261.6 0.9 multiply_add_fusion
  262.5 1.3 collective-permute-start.23
  263.9 9.8 %collective-permute-done.23 = f32[1,128,512]{2,1,0:T(8,128)S(1)} collective-permute-done((f32[1,128,512]{2,1,0:T(8,128)}, f32[1,128,512]{2,1,0:T(8,128)S(1)}, u32[]{:S(2)}, u32[]{:S(2)}) %collective-permute-start.23) | collective-permute-done | bytes 262176 | tf_op jit(solution)/shard_map/ppermute | solution.py:109
  273.7 1.1 fusion.289
  279.1 21.9 %collective-permute-start.24 = (f32[1184,128]{1,0:T(8,128)S(1)}, f32[1184,128]{1,0:T(8,128)S(1)}, u32[]{:S(2)}, u32[]{:S(2)}) collective-permute-start(f32[1184,128]{1,0:T(8,128)S(1)} %constant_dynamic-slice_fusion.2), channel_id=1, source_target_pairs={{0,1},{1,0},{2,3},{3,2},{4,5},{5,4},{6,7},{7,6},{8,9},{9,8},{10,11... | collective-permute-start | bytes 1818632 | tf_op jit(solution)/shard_map/ppermute | solution.py:134
  301.4 1.3 collective-permute-done.24
  302.8 8.8 %collective-permute-start.25 = (f32[592,128]{1,0:T(8,128)S(1)}, f32[592,128]{1,0:T(8,128)S(1)}, u32[]{:S(2)}, u32[]{:S(2)}) collective-permute-start(f32[592,128]{1,0:T(8,128)S(1)} %constant_dynamic-slice_fusion.1), channel_id=1, source_target_pairs={{0,2},{1,3},{2,0},{3,1},{4,6},{5,7},{6,4},{7,5},{8,10},{9,11},{10,... | collective-permute-start | bytes 909320 | tf_op jit(solution)/shard_map/ppermute | solution.py:134
  311.7 26.0 %collective-permute-done.25 = f32[592,128]{1,0:T(8,128)S(1)} collective-permute-done((f32[592,128]{1,0:T(8,128)S(1)}, f32[592,128]{1,0:T(8,128)S(1)}, u32[]{:S(2)}, u32[]{:S(2)}) %collective-permute-start.25) | collective-permute-done | bytes 303136 | tf_op jit(solution)/shard_map/ppermute | solution.py:134
  337.8 14.9 %collective-permute-start.26 = (f32[296,128]{1,0:T(8,128)S(1)}, f32[296,128]{1,0:T(8,128)S(1)}, u32[]{:S(2)}, u32[]{:S(2)}) collective-permute-start(f32[296,128]{1,0:T(8,128)S(1)} %constant_dynamic-slice_fusion), channel_id=1, source_target_pairs={{0,4},{1,5},{2,6},{3,7},{4,0},{5,1},{6,2},{7,3},{8,12},{9,13},{10,... | collective-permute-start | bytes 454664 | tf_op jit(solution)/shard_map/ppermute | solution.py:134
  352.8 9.2 %collective-permute-done.26 = f32[296,128]{1,0:T(8,128)S(1)} collective-permute-done((f32[296,128]{1,0:T(8,128)S(1)}, f32[296,128]{1,0:T(8,128)S(1)}, u32[]{:S(2)}, u32[]{:S(2)}) %collective-permute-start.26) | collective-permute-done | bytes 151584 | tf_op jit(solution)/shard_map/ppermute | solution.py:134
  362.0 6.2 %collective-permute-start.27 = (f32[296,128]{1,0:T(8,128)S(1)}, f32[296,128]{1,0:T(8,128)S(1)}, u32[]{:S(2)}, u32[]{:S(2)}) collective-permute-start(f32[296,128]{1,0:T(8,128)S(1)} %get-tuple-element.9), channel_id=1, source_target_pairs={{0,4},{1,5},{2,6},{3,7},{4,0},{5,1},{6,2},{7,3},{8,12},{9,13},{10,... | collective-permute-start | bytes 454664 | tf_op jit(solution)/shard_map/ppermute | solution.py:139
  368.4 10.5 %collective-permute-done.27 = f32[296,128]{1,0:T(8,128)S(1)} collective-permute-done((f32[296,128]{1,0:T(8,128)S(1)}, f32[296,128]{1,0:T(8,128)S(1)}, u32[]{:S(2)}, u32[]{:S(2)}) %collective-permute-start.27) | collective-permute-done | bytes 151584 | tf_op jit(solution)/shard_map/ppermute | solution.py:139
  378.9 2.1 collective-permute-start.28
  381.1 26.7 %collective-permute-done.28 = f32[592,128]{1,0:T(8,128)S(1)} collective-permute-done((f32[592,128]{1,0:T(8,128)S(1)}, f32[592,128]{1,0:T(8,128)S(1)}, u32[]{:S(2)}, u32[]{:S(2)}) %collective-permute-start.28) | collective-permute-done | bytes 303136 | tf_op jit(solution)/shard_map/ppermute | solution.py:139
  407.9 2.4 collective-permute-start.29
  410.4 1.1 fusion.67
  412.3 1.1 slice.546
  (242 shorter events, 25.2 us)
Async XLA Ops:
  0.6 2.9 copy-start.1
  3.2 1.1 copy-start
  4.6 0.9 copy-start.9
  6.0 7.4 %collective-permute-start = (f32[1,129,512]{2,1,0:T(8,128)S(1)}, f32[1,129,512]{2,1,0:T(8,128)S(1)}, u32[]{:S(2)}, u32[]{:S(2)}) collective-permute-start(f32[1,129,512]{2,1,0:T(8,128)S(1)} %pad_maximum_fusion.1), channel_id=1, source_target_pairs={{0,8},{8,16},{16,24},{24,32},{32,40},{40,48},{48,56},{56,64},{64,7... | collective-permute-start | bytes 792584 | tf_op jit(solution)/shard_map/ppermute | solution.py:97
  13.5 11.9 %collective-permute-start.1 = (f32[1,129,512]{2,1,0:T(8,128)S(1)}, f32[1,129,512]{2,1,0:T(8,128)S(1)}, u32[]{:S(2)}, u32[]{:S(2)}) collective-permute-start(f32[1,129,512]{2,1,0:T(8,128)S(1)} %pad_maximum_fusion.2), channel_id=1, source_target_pairs={{0,16},{8,24},{16,32},{24,40},{32,48},{40,56},{48,64},{56,72},{64,... | collective-permute-start | bytes 792584 | tf_op jit(solution)/shard_map/ppermute | solution.py:97
  25.6 11.0 %collective-permute-start.2 = (f32[1,129,512]{2,1,0:T(8,128)S(1)}, f32[1,129,512]{2,1,0:T(8,128)S(1)}, u32[]{:S(2)}, u32[]{:S(2)}) collective-permute-start(f32[1,129,512]{2,1,0:T(8,128)S(1)} %pad_maximum_fusion.3), channel_id=1, source_target_pairs={{0,32},{8,40},{16,48},{24,56},{32,64},{40,72},{48,80},{56,88},{64,... | collective-permute-start | bytes 792584 | tf_op jit(solution)/shard_map/ppermute | solution.py:97
  36.7 8.6 %collective-permute-start.3 = (f32[1,129,512]{2,1,0:T(8,128)S(1)}, f32[1,129,512]{2,1,0:T(8,128)S(1)}, u32[]{:S(2)}, u32[]{:S(2)}) collective-permute-start(f32[1,129,512]{2,1,0:T(8,128)S(1)} %pad_maximum_fusion.4), channel_id=1, source_target_pairs={{0,64},{8,72},{16,80},{24,88},{32,96},{40,104},{48,112},{56,120},{... | collective-permute-start | bytes 792584 | tf_op jit(solution)/shard_map/ppermute | solution.py:97
  45.5 24.2 %collective-permute-start.4 = (f32[1,129,512]{2,1,0:T(8,128)S(1)}, f32[1,129,512]{2,1,0:T(8,128)S(1)}, u32[]{:S(2)}, u32[]{:S(2)}) collective-permute-start(f32[1,129,512]{2,1,0:T(8,128)S(1)} %pad_maximum_fusion.5), channel_id=1, source_target_pairs={{0,128},{8,136},{16,144},{24,152},{32,160},{40,168},{48,176},{56,1... | collective-permute-start | bytes 792584 | tf_op jit(solution)/shard_map/ppermute | solution.py:97
  69.9 9.9 %collective-permute-start.5 = (f32[1,129,512]{2,1,0:T(8,128)S(1)}, f32[1,129,512]{2,1,0:T(8,128)S(1)}, u32[]{:S(2)}, u32[]{:S(2)}) collective-permute-start(f32[1,129,512]{2,1,0:T(8,128)S(1)} %pad_maximum_fusion.6), channel_id=1, source_target_pairs={{0,256},{8,264},{16,272},{24,280},{32,288},{40,296},{48,304},{56,3... | collective-permute-start | bytes 792584 | tf_op jit(solution)/shard_map/ppermute | solution.py:97
  82.5 4.6 %collective-permute-start.6 = (f32[1,128,512]{2,1,0:T(8,128)S(1)}, f32[1,128,512]{2,1,0:T(8,128)S(1)}, u32[]{:S(2)}, u32[]{:S(2)}) collective-permute-start(f32[1,128,512]{2,1,0:T(8,128)S(1)} %get-tuple-element.65), channel_id=1, source_target_pairs={{0,8},{8,16},{16,24},{24,32},{32,40},{40,48},{48,56},{56,64},{64,7... | collective-permute-start | bytes 786440 | tf_op jit(solution)/shard_map/ppermute | solution.py:109
  87.2 6.2 %collective-permute-start.7 = (f32[1,128,512]{2,1,0:T(8,128)S(1)}, f32[1,128,512]{2,1,0:T(8,128)S(1)}, u32[]{:S(2)}, u32[]{:S(2)}) collective-permute-start(f32[1,128,512]{2,1,0:T(8,128)S(1)} %multiply_add_fusion.22), channel_id=1, source_target_pairs={{0,16},{8,24},{16,32},{24,40},{32,48},{40,56},{48,64},{56,72},{64,... | collective-permute-start | bytes 786440 | tf_op jit(solution)/shard_map/ppermute | solution.py:109
  93.5 9.5 %collective-permute-start.8 = (f32[1,128,512]{2,1,0:T(8,128)S(1)}, f32[1,128,512]{2,1,0:T(8,128)S(1)}, u32[]{:S(2)}, u32[]{:S(2)}) collective-permute-start(f32[1,128,512]{2,1,0:T(8,128)S(1)} %multiply_add_fusion.20), channel_id=1, source_target_pairs={{0,32},{8,40},{16,48},{24,56},{32,64},{40,72},{48,80},{56,88},{64,... | collective-permute-start | bytes 786440 | tf_op jit(solution)/shard_map/ppermute | solution.py:109
  103.2 11.2 %collective-permute-start.9 = (f32[1,128,512]{2,1,0:T(8,128)S(1)}, f32[1,128,512]{2,1,0:T(8,128)S(1)}, u32[]{:S(2)}, u32[]{:S(2)}) collective-permute-start(f32[1,128,512]{2,1,0:T(8,128)S(1)} %get-tuple-element.35), channel_id=1, source_target_pairs={{0,64},{8,72},{16,80},{24,88},{32,96},{40,104},{48,112},{56,120},{... | collective-permute-start | bytes 786440 | tf_op jit(solution)/shard_map/ppermute | solution.py:109
  114.5 23.6 %collective-permute-start.10 = (f32[1,128,512]{2,1,0:T(8,128)S(1)}, f32[1,128,512]{2,1,0:T(8,128)S(1)}, u32[]{:S(2)}, u32[]{:S(2)}) collective-permute-start(f32[1,128,512]{2,1,0:T(8,128)S(1)} %multiply_add_fusion.16), channel_id=1, source_target_pairs={{0,128},{8,136},{16,144},{24,152},{32,160},{40,168},{48,176},{56,1... | collective-permute-start | bytes 786440 | tf_op jit(solution)/shard_map/ppermute | solution.py:109
  132.6 12.0 %copy-start.10 = (f32[1,128]{1,0:T(1,128)S(1)}, f32[1,128]{1,0:T(1,128)}, u32[]{:S(2)}) copy-start(f32[1,128]{1,0:T(1,128)} %param.11) | copy-start | bytes 1540
  138.3 9.5 %collective-permute-start.11 = (f32[1,128,512]{2,1,0:T(8,128)S(1)}, f32[1,128,512]{2,1,0:T(8,128)S(1)}, u32[]{:S(2)}, u32[]{:S(2)}) collective-permute-start(f32[1,128,512]{2,1,0:T(8,128)S(1)} %get-tuple-element.33), channel_id=1, source_target_pairs={{0,256},{8,264},{16,272},{24,280},{32,288},{40,296},{48,304},{56,3... | collective-permute-start | bytes 786440 | tf_op jit(solution)/shard_map/ppermute | solution.py:109
  147.9 0.9 copy-start.7
  149.2 60.9 %copy-start.5 = (f32[1,512,128]{1,2,0:T(8,128)}, f32[1,512,128]{1,2,0:T(8,128)S(1)}, u32[]{:S(2)}) copy-start(f32[1,512,128]{1,2,0:T(8,128)S(1)} %get-tuple-element.68) | copy-start | bytes 786436
  149.2 1.0 copy-start.2
  152.0 1.0 copy-start.3
  153.4 7.3 %collective-permute-start.12 = (f32[1,129,512]{2,1,0:T(8,128)S(1)}, f32[1,129,512]{2,1,0:T(8,128)S(1)}, u32[]{:S(2)}, u32[]{:S(2)}) collective-permute-start(f32[1,129,512]{2,1,0:T(8,128)S(1)} %pad_maximum_fusion.7), channel_id=1, source_target_pairs={{8,0},{16,8},{24,16},{32,24},{40,32},{48,40},{56,48},{64,56},{72,6... | collective-permute-start | bytes 792584 | tf_op jit(solution)/shard_map/ppermute | solution.py:97
  160.8 8.8 %collective-permute-start.13 = (f32[1,129,512]{2,1,0:T(8,128)S(1)}, f32[1,129,512]{2,1,0:T(8,128)S(1)}, u32[]{:S(2)}, u32[]{:S(2)}) collective-permute-start(f32[1,129,512]{2,1,0:T(8,128)S(1)} %pad_maximum_fusion.8), channel_id=1, source_target_pairs={{16,0},{24,8},{32,16},{40,24},{48,32},{56,40},{64,48},{72,56},{80,... | collective-permute-start | bytes 792584 | tf_op jit(solution)/shard_map/ppermute | solution.py:97
  169.8 9.6 %collective-permute-start.14 = (f32[1,129,512]{2,1,0:T(8,128)S(1)}, f32[1,129,512]{2,1,0:T(8,128)S(1)}, u32[]{:S(2)}, u32[]{:S(2)}) collective-permute-start(f32[1,129,512]{2,1,0:T(8,128)S(1)} %pad_maximum_fusion.9), channel_id=1, source_target_pairs={{32,0},{40,8},{48,16},{56,24},{64,32},{72,40},{80,48},{88,56},{96,... | collective-permute-start | bytes 792584 | tf_op jit(solution)/shard_map/ppermute | solution.py:97
  179.5 13.0 %collective-permute-start.15 = (f32[1,129,512]{2,1,0:T(8,128)S(1)}, f32[1,129,512]{2,1,0:T(8,128)S(1)}, u32[]{:S(2)}, u32[]{:S(2)}) collective-permute-start(f32[1,129,512]{2,1,0:T(8,128)S(1)} %pad_maximum_fusion.10), channel_id=1, source_target_pairs={{64,0},{72,8},{80,16},{88,24},{96,32},{104,40},{112,48},{120,56},{... | collective-permute-start | bytes 792584 | tf_op jit(solution)/shard_map/ppermute | solution.py:97
  192.7 7.4 %collective-permute-start.16 = (f32[1,129,512]{2,1,0:T(8,128)S(1)}, f32[1,129,512]{2,1,0:T(8,128)S(1)}, u32[]{:S(2)}, u32[]{:S(2)}) collective-permute-start(f32[1,129,512]{2,1,0:T(8,128)S(1)} %pad_maximum_fusion.11), channel_id=1, source_target_pairs={{128,0},{136,8},{144,16},{152,24},{160,32},{168,40},{176,48},{184,... | collective-permute-start | bytes 792584 | tf_op jit(solution)/shard_map/ppermute | solution.py:97
  200.2 8.8 %collective-permute-start.17 = (f32[1,129,512]{2,1,0:T(8,128)S(1)}, f32[1,129,512]{2,1,0:T(8,128)S(1)}, u32[]{:S(2)}, u32[]{:S(2)}) collective-permute-start(f32[1,129,512]{2,1,0:T(8,128)S(1)} %pad_maximum_fusion.12), channel_id=1, source_target_pairs={{256,0},{264,8},{272,16},{280,24},{288,32},{296,40},{304,48},{312,... | collective-permute-start | bytes 792584 | tf_op jit(solution)/shard_map/ppermute | solution.py:97
  211.9 8.5 %collective-permute-start.18 = (f32[1,128,512]{2,1,0:T(8,128)S(1)}, f32[1,128,512]{2,1,0:T(8,128)S(1)}, u32[]{:S(2)}, u32[]{:S(2)}) collective-permute-start(f32[1,128,512]{2,1,0:T(8,128)S(1)} %get-tuple-element.77), channel_id=1, source_target_pairs={{8,0},{16,8},{24,16},{32,24},{40,32},{48,40},{56,48},{64,56},{72,6... | collective-permute-start | bytes 786440 | tf_op jit(solution)/shard_map/ppermute | solution.py:109
  220.4 10.4 %collective-permute-start.19 = (f32[1,128,512]{2,1,0:T(8,128)S(1)}, f32[1,128,512]{2,1,0:T(8,128)S(1)}, u32[]{:S(2)}, u32[]{:S(2)}) collective-permute-start(f32[1,128,512]{2,1,0:T(8,128)S(1)} %multiply_add_fusion.8), channel_id=1, source_target_pairs={{16,0},{24,8},{32,16},{40,24},{48,32},{56,40},{64,48},{72,56},{80,... | collective-permute-start | bytes 786440 | tf_op jit(solution)/shard_map/ppermute | solution.py:109
  230.9 9.4 %collective-permute-start.20 = (f32[1,128,512]{2,1,0:T(8,128)S(1)}, f32[1,128,512]{2,1,0:T(8,128)S(1)}, u32[]{:S(2)}, u32[]{:S(2)}) collective-permute-start(f32[1,128,512]{2,1,0:T(8,128)S(1)} %multiply_add_fusion.6), channel_id=1, source_target_pairs={{32,0},{40,8},{48,16},{56,24},{64,32},{72,40},{80,48},{88,56},{96,... | collective-permute-start | bytes 786440 | tf_op jit(solution)/shard_map/ppermute | solution.py:109
  240.5 13.9 %collective-permute-start.21 = (f32[1,128,512]{2,1,0:T(8,128)S(1)}, f32[1,128,512]{2,1,0:T(8,128)S(1)}, u32[]{:S(2)}, u32[]{:S(2)}) collective-permute-start(f32[1,128,512]{2,1,0:T(8,128)S(1)} %get-tuple-element.14), channel_id=1, source_target_pairs={{64,0},{72,8},{80,16},{88,24},{96,32},{104,40},{112,48},{120,56},{... | collective-permute-start | bytes 786440 | tf_op jit(solution)/shard_map/ppermute | solution.py:109
  254.5 7.1 %collective-permute-start.22 = (f32[1,128,512]{2,1,0:T(8,128)S(1)}, f32[1,128,512]{2,1,0:T(8,128)S(1)}, u32[]{:S(2)}, u32[]{:S(2)}) collective-permute-start(f32[1,128,512]{2,1,0:T(8,128)S(1)} %multiply_add_fusion.2), channel_id=1, source_target_pairs={{128,0},{136,8},{144,16},{152,24},{160,32},{168,40},{176,48},{184,... | collective-permute-start | bytes 786440 | tf_op jit(solution)/shard_map/ppermute | solution.py:109
  262.5 11.2 %collective-permute-start.23 = (f32[1,128,512]{2,1,0:T(8,128)}, f32[1,128,512]{2,1,0:T(8,128)S(1)}, u32[]{:S(2)}, u32[]{:S(2)}) collective-permute-start(f32[1,128,512]{2,1,0:T(8,128)} %get-tuple-element.12), channel_id=1, source_target_pairs={{256,0},{264,8},{272,16},{280,24},{288,32},{296,40},{304,48},{312,... | collective-permute-start | bytes 786440 | tf_op jit(solution)/shard_map/ppermute | solution.py:109
  276.2 1.0 copy-start.6
  276.3 1.0 copy-start.8
  279.1 23.6 %collective-permute-start.24 = (f32[1184,128]{1,0:T(8,128)S(1)}, f32[1184,128]{1,0:T(8,128)S(1)}, u32[]{:S(2)}, u32[]{:S(2)}) collective-permute-start(f32[1184,128]{1,0:T(8,128)S(1)} %constant_dynamic-slice_fusion.2), channel_id=1, source_target_pairs={{0,1},{1,0},{2,3},{3,2},{4,5},{5,4},{6,7},{7,6},{8,9},{9,8},{10,11... | collective-permute-start | bytes 1818632 | tf_op jit(solution)/shard_map/ppermute | solution.py:134
  302.8 34.9 %collective-permute-start.25 = (f32[592,128]{1,0:T(8,128)S(1)}, f32[592,128]{1,0:T(8,128)S(1)}, u32[]{:S(2)}, u32[]{:S(2)}) collective-permute-start(f32[592,128]{1,0:T(8,128)S(1)} %constant_dynamic-slice_fusion.1), channel_id=1, source_target_pairs={{0,2},{1,3},{2,0},{3,1},{4,6},{5,7},{6,4},{7,5},{8,10},{9,11},{10,... | collective-permute-start | bytes 909320 | tf_op jit(solution)/shard_map/ppermute | solution.py:134
  337.8 24.2 %collective-permute-start.26 = (f32[296,128]{1,0:T(8,128)S(1)}, f32[296,128]{1,0:T(8,128)S(1)}, u32[]{:S(2)}, u32[]{:S(2)}) collective-permute-start(f32[296,128]{1,0:T(8,128)S(1)} %constant_dynamic-slice_fusion), channel_id=1, source_target_pairs={{0,4},{1,5},{2,6},{3,7},{4,0},{5,1},{6,2},{7,3},{8,12},{9,13},{10,... | collective-permute-start | bytes 454664 | tf_op jit(solution)/shard_map/ppermute | solution.py:134
  362.0 16.8 %collective-permute-start.27 = (f32[296,128]{1,0:T(8,128)S(1)}, f32[296,128]{1,0:T(8,128)S(1)}, u32[]{:S(2)}, u32[]{:S(2)}) collective-permute-start(f32[296,128]{1,0:T(8,128)S(1)} %get-tuple-element.9), channel_id=1, source_target_pairs={{0,4},{1,5},{2,6},{3,7},{4,0},{5,1},{6,2},{7,3},{8,12},{9,13},{10,... | collective-permute-start | bytes 454664 | tf_op jit(solution)/shard_map/ppermute | solution.py:139
  378.9 31.5 %copy-start.4 = (bf16[128,9,128]{0,2,1:T(8,128)(2,1)S(1)}, bf16[128,9,128]{0,2,1:T(8,128)(2,1)}, u32[]{:S(2)}) copy-start(bf16[128,9,128]{0,2,1:T(8,128)(2,1)} %copy.26) | copy-start | bytes 884740
  378.9 29.0 %collective-permute-start.28 = (f32[592,128]{1,0:T(8,128)S(1)}, f32[592,128]{1,0:T(8,128)S(1)}, u32[]{:S(2)}, u32[]{:S(2)}) collective-permute-start(f32[592,128]{1,0:T(8,128)S(1)} %constant_dynamic-update-slice_fusion.112), channel_id=1, source_target_pairs={{0,2},{1,3},{2,0},{3,1},{4,6},{5,7},{6,4},{7,5},{8,10},{9,11},{10,... | collective-permute-start | bytes 909320 | tf_op jit(solution)/shard_map/ppermute | solution.py:139
  407.9 4.0 collective-permute-start.29

commit v4 on v2

--- a/solution.py
+++ b/solution.py
@@ -109,6 +109,49 @@
         received = lax.ppermute(sending, axis, scan_pairs(count, d, reverse))
         total = total + factor[None, :, None] * received
     return total
+
+
+def batch_sum(value, axis):
+    count = lax.axis_size(axis)
+    chips = count // 2
+    me = lax.axis_index(axis)
+    core = me % 2
+    chip = me // 2
+    shape = value.shape
+    flat = value.reshape(-1)
+    lanes = 128
+    quantum = lanes * 8 * count
+    padded_size = -(-flat.shape[0] // quantum) * quantum
+    current = jnp.pad(flat, (0, padded_size - flat.shape[0])).reshape(-1, lanes)
+    half_rows = current.shape[0] // 2
+    partner = [(k, k ^ 1) for k in range(count)]
+    keep = lax.dynamic_slice_in_dim(current, core * half_rows, half_rows, 0)
+    give = lax.dynamic_slice_in_dim(current, (1 - core) * half_rows, half_rows, 0)
+    half = keep + lax.ppermute(give, axis, partner)
+
+    def following(k):
+        step = 1 if k % 2 == 0 else -1
+        return ((k // 2 + step) % chips) * 2 + k % 2
+
+    ring = [(k, following(k)) for k in range(count)]
+    place = jnp.where(core == 0, chip, (chips - chip) % chips)
+    pieces = half.reshape(chips, half_rows // chips, lanes)
+    for t in range(chips - 1):
+        sent = lax.dynamic_index_in_dim(pieces, (place - t) % chips, 0, False)
+        got = lax.ppermute(sent, axis, ring)
+        slot = (place - t - 1 + chips) % chips
+        mine = lax.dynamic_index_in_dim(pieces, slot, 0, False)
+        pieces = lax.dynamic_update_index_in_dim(pieces, mine + got, slot, 0)
+    for t in range(chips - 1):
+        sent = lax.dynamic_index_in_dim(pieces, (place + 1 - t + chips) % chips, 0, False)
+        got = lax.ppermute(sent, axis, ring)
+        pieces = lax.dynamic_update_index_in_dim(pieces, got, (place - t + chips) % chips, 0)
+    half = pieces.reshape(half_rows, lanes)
+    other = lax.ppermute(half, axis, partner)
+    whole = jnp.zeros_like(current)
+    whole = lax.dynamic_update_slice_in_dim(whole, half, core * half_rows, 0)
+    whole = lax.dynamic_update_slice_in_dim(whole, other, (1 - core) * half_rows, 0)
+    return whole.reshape(-1)[: flat.shape[0]].reshape(shape)
 
 
 def per_device(initial_state, cotangent, conv_weight, conv_bias, block_gain, adjoint_gain):
@@ -161,7 +204,7 @@
             for w, b in zip(weight_parts, bias_parts)
         ]
     )
-    packed = lax.psum(packed, "batch")
+    packed = batch_sum(packed, "batch")
     weight_grad = packed[:, :channels, :]
     bias_grad = packed[:, channels, :channels]
     return (ending[None], adjoint[None], weight_grad, bias_grad)

time: 438 us -> 395 us (0.902)
  waiting for transfers between devices: 286 us -> 181 us
  starting transfers between devices: 107 us -> 177 us
  between operations: 15.6 us -> 2.65 us
    psum x1 -> x0, waiting for transfers between devices: 141 us -> none  [per_device(): packed = lax.psum(packed, 'batch')]
    ppermute x0 -> x8, starting transfers between devices: none -> 70.3 us  [the longest x6 46.5 us: batch_sum(): got = lax.ppermute(sent, axis, ring)]
    ppermute x0 -> x8, waiting for transfers between devices: none -> 36.2 us  [the longest x6 34.2 us: batch_sum(): got = lax.ppermute(sent, axis, ring)]
  transfers between devices with their start and end apart: 25 -> 32, of which waited for: 25 -> 32; matrix products, arithmetic and copies ran while one was open for 1% -> 1% of each run, Pallas kernels for 0% -> 0%
where the time goes in v4:
time: 395 us; the launch traced here: 392 us
  waiting for transfers between devices  181 us (46%)
  starting transfers between devices  177 us (45%)
  other arithmetic  19 us (5%)
  matrix products  6.24 us (2%)
  local copies, waits for them, and re-layouts  6.02 us (2%)
    ppermute x12, waiting for transfers between devices, exclusive_scan_again(): received = lax.ppermute(sending, axis, scan_pairs(count, d, reverse))  73.5 us
    ppermute x12, waiting for transfers between devices, exclusive_scan_first(): received = lax.ppermute(packed, axis, scan_pairs(count, d, reverse))  70.8 us
    ppermute x12, starting transfers between devices, exclusive_scan_first(): received = lax.ppermute(packed, axis, scan_pairs(count, d, reverse))  57 us
    ppermute x12, starting transfers between devices, exclusive_scan_again(): received = lax.ppermute(sending, axis, scan_pairs(count, d, reverse))  49.8 us
    ppermute x6, starting transfers between devices, batch_sum(): got = lax.ppermute(sent, axis, ring)  46.5 us
    ppermute x6, waiting for transfers between devices, batch_sum(): got = lax.ppermute(sent, axis, ring)  34.2 us
    ppermute x1, starting transfers between devices, batch_sum(): half = keep + lax.ppermute(give, axis, partner)  21.9 us
    unnamed x96, other arithmetic  9.1 us
  transfers between devices with their start and end apart: 32, of which 32 were waited for; matrix products, arithmetic and copies ran while one was open for 1% of the time, Pallas kernels for 0%

profile of v4, /device:TPU:1, one launch (start us, length us, event | category | flops | bytes accessed | tf_op | source)
XLA Modules:
  0.0 391.6 jit_solution(5557814565889296718)
XLA Ops:
  6.0 4.0 %collective-permute-start = (f32[1,129,512]{2,1,0:T(8,128)S(1)}, f32[1,129,512]{2,1,0:T(8,128)S(1)}, u32[]{:S(2)}, u32[]{:S(2)}) collective-permute-start(f32[1,129,512]{2,1,0:T(8,128)S(1)} %pad_maximum_fusion.1), channel_id=1, source_target_pairs={{0,8},{8,16},{16,24},{24,32},{32,40},{40,48},{48,56},{56,64},{64,7... | collective-permute-start | bytes 792584 | tf_op jit(solution)/shard_map/ppermute | solution.py:97
  10.0 3.5 collective-permute-done
  13.5 7.5 %collective-permute-start.1 = (f32[1,129,512]{2,1,0:T(8,128)S(1)}, f32[1,129,512]{2,1,0:T(8,128)S(1)}, u32[]{:S(2)}, u32[]{:S(2)}) collective-permute-start(f32[1,129,512]{2,1,0:T(8,128)S(1)} %pad_maximum_fusion.2), channel_id=1, source_target_pairs={{0,16},{8,24},{16,32},{24,40},{32,48},{40,56},{48,64},{56,72},{64,... | collective-permute-start | bytes 792584 | tf_op jit(solution)/shard_map/ppermute | solution.py:97
  21.0 4.4 %collective-permute-done.1 = f32[1,129,512]{2,1,0:T(8,128)S(1)} collective-permute-done((f32[1,129,512]{2,1,0:T(8,128)S(1)}, f32[1,129,512]{2,1,0:T(8,128)S(1)}, u32[]{:S(2)}, u32[]{:S(2)}) %collective-permute-start.1) | collective-permute-done | bytes 264224 | tf_op jit(solution)/shard_map/ppermute | solution.py:97
  25.6 7.5 %collective-permute-start.2 = (f32[1,129,512]{2,1,0:T(8,128)S(1)}, f32[1,129,512]{2,1,0:T(8,128)S(1)}, u32[]{:S(2)}, u32[]{:S(2)}) collective-permute-start(f32[1,129,512]{2,1,0:T(8,128)S(1)} %pad_maximum_fusion.3), channel_id=1, source_target_pairs={{0,32},{8,40},{16,48},{24,56},{32,64},{40,72},{48,80},{56,88},{64,... | collective-permute-start | bytes 792584 | tf_op jit(solution)/shard_map/ppermute | solution.py:97
  33.1 3.5 collective-permute-done.2
  36.7 5.2 %collective-permute-start.3 = (f32[1,129,512]{2,1,0:T(8,128)S(1)}, f32[1,129,512]{2,1,0:T(8,128)S(1)}, u32[]{:S(2)}, u32[]{:S(2)}) collective-permute-start(f32[1,129,512]{2,1,0:T(8,128)S(1)} %pad_maximum_fusion.4), channel_id=1, source_target_pairs={{0,64},{8,72},{16,80},{24,88},{32,96},{40,104},{48,112},{56,120},{... | collective-permute-start | bytes 792584 | tf_op jit(solution)/shard_map/ppermute | solution.py:97
  41.9 3.5 collective-permute-done.3
  45.5 19.1 %collective-permute-start.4 = (f32[1,129,512]{2,1,0:T(8,128)S(1)}, f32[1,129,512]{2,1,0:T(8,128)S(1)}, u32[]{:S(2)}, u32[]{:S(2)}) collective-permute-start(f32[1,129,512]{2,1,0:T(8,128)S(1)} %pad_maximum_fusion.5), channel_id=1, source_target_pairs={{0,128},{8,136},{16,144},{24,152},{32,160},{40,168},{48,176},{56,1... | collective-permute-start | bytes 792584 | tf_op jit(solution)/shard_map/ppermute | solution.py:97
  64.7 5.1 %collective-permute-done.4 = f32[1,129,512]{2,1,0:T(8,128)S(1)} collective-permute-done((f32[1,129,512]{2,1,0:T(8,128)S(1)}, f32[1,129,512]{2,1,0:T(8,128)S(1)}, u32[]{:S(2)}, u32[]{:S(2)}) %collective-permute-start.4) | collective-permute-done | bytes 264224 | tf_op jit(solution)/shard_map/ppermute | solution.py:97
  69.9 5.7 %collective-permute-start.5 = (f32[1,129,512]{2,1,0:T(8,128)S(1)}, f32[1,129,512]{2,1,0:T(8,128)S(1)}, u32[]{:S(2)}, u32[]{:S(2)}) collective-permute-start(f32[1,129,512]{2,1,0:T(8,128)S(1)} %pad_maximum_fusion.6), channel_id=1, source_target_pairs={{0,256},{8,264},{16,272},{24,280},{32,288},{40,296},{48,304},{56,3... | collective-permute-start | bytes 792584 | tf_op jit(solution)/shard_map/ppermute | solution.py:97
  75.6 4.2 %collective-permute-done.5 = f32[1,129,512]{2,1,0:T(8,128)S(1)} collective-permute-done((f32[1,129,512]{2,1,0:T(8,128)S(1)}, f32[1,129,512]{2,1,0:T(8,128)S(1)}, u32[]{:S(2)}, u32[]{:S(2)}) %collective-permute-start.5) | collective-permute-done | bytes 264224 | tf_op jit(solution)/shard_map/ppermute | solution.py:97
  82.5 1.3 collective-permute-start.6
  83.9 3.3 collective-permute-done.6
  87.2 2.9 collective-permute-start.7
  90.1 3.3 collective-permute-done.7
  93.5 6.3 %collective-permute-start.8 = (f32[1,128,512]{2,1,0:T(8,128)S(1)}, f32[1,128,512]{2,1,0:T(8,128)S(1)}, u32[]{:S(2)}, u32[]{:S(2)}) collective-permute-start(f32[1,128,512]{2,1,0:T(8,128)S(1)} %multiply_add_fusion.20), channel_id=1, source_target_pairs={{0,32},{8,40},{16,48},{24,56},{32,64},{40,72},{48,80},{56,88},{64,... | collective-permute-start | bytes 786440 | tf_op jit(solution)/shard_map/ppermute | solution.py:109
  99.8 3.3 collective-permute-done.8
  103.2 7.9 %collective-permute-start.9 = (f32[1,128,512]{2,1,0:T(8,128)S(1)}, f32[1,128,512]{2,1,0:T(8,128)S(1)}, u32[]{:S(2)}, u32[]{:S(2)}) collective-permute-start(f32[1,128,512]{2,1,0:T(8,128)S(1)} %get-tuple-element.33), channel_id=1, source_target_pairs={{0,64},{8,72},{16,80},{24,88},{32,96},{40,104},{48,112},{56,120},{... | collective-permute-start | bytes 786440 | tf_op jit(solution)/shard_map/ppermute | solution.py:109
  111.1 3.3 collective-permute-done.9
  114.5 17.5 %collective-permute-start.10 = (f32[1,128,512]{2,1,0:T(8,128)S(1)}, f32[1,128,512]{2,1,0:T(8,128)S(1)}, u32[]{:S(2)}, u32[]{:S(2)}) collective-permute-start(f32[1,128,512]{2,1,0:T(8,128)S(1)} %multiply_add_fusion.16), channel_id=1, source_target_pairs={{0,128},{8,136},{16,144},{24,152},{32,160},{40,168},{48,176},{56,1... | collective-permute-start | bytes 786440 | tf_op jit(solution)/shard_map/ppermute | solution.py:109
  132.6 5.6 %collective-permute-done.10 = f32[1,128,512]{2,1,0:T(8,128)S(1)} collective-permute-done((f32[1,128,512]{2,1,0:T(8,128)S(1)}, f32[1,128,512]{2,1,0:T(8,128)S(1)}, u32[]{:S(2)}, u32[]{:S(2)}) %collective-permute-start.10) | collective-permute-done | bytes 262176 | tf_op jit(solution)/shard_map/ppermute | solution.py:109
  138.3 6.2 %collective-permute-start.11 = (f32[1,128,512]{2,1,0:T(8,128)S(1)}, f32[1,128,512]{2,1,0:T(8,128)S(1)}, u32[]{:S(2)}, u32[]{:S(2)}) collective-permute-start(f32[1,128,512]{2,1,0:T(8,128)S(1)} %get-tuple-element.31), channel_id=1, source_target_pairs={{0,256},{8,264},{16,272},{24,280},{32,288},{40,296},{48,304},{56,3... | collective-permute-start | bytes 786440 | tf_op jit(solution)/shard_map/ppermute | solution.py:109
  145.7 2.1 collective-permute-done.11
  153.4 1.3 collective-permute-start.12
  154.7 6.0 %collective-permute-done.12 = f32[1,129,512]{2,1,0:T(8,128)S(1)} collective-permute-done((f32[1,129,512]{2,1,0:T(8,128)S(1)}, f32[1,129,512]{2,1,0:T(8,128)S(1)}, u32[]{:S(2)}, u32[]{:S(2)}) %collective-permute-start.12) | collective-permute-done | bytes 264224 | tf_op jit(solution)/shard_map/ppermute | solution.py:97
  160.8 1.3 collective-permute-start.13
  162.1 7.5 %collective-permute-done.13 = f32[1,129,512]{2,1,0:T(8,128)S(1)} collective-permute-done((f32[1,129,512]{2,1,0:T(8,128)S(1)}, f32[1,129,512]{2,1,0:T(8,128)S(1)}, u32[]{:S(2)}, u32[]{:S(2)}) %collective-permute-start.13) | collective-permute-done | bytes 264224 | tf_op jit(solution)/shard_map/ppermute | solution.py:97
  169.8 1.3 collective-permute-start.14
  171.1 8.3 %collective-permute-done.14 = f32[1,129,512]{2,1,0:T(8,128)S(1)} collective-permute-done((f32[1,129,512]{2,1,0:T(8,128)S(1)}, f32[1,129,512]{2,1,0:T(8,128)S(1)}, u32[]{:S(2)}, u32[]{:S(2)}) %collective-permute-start.14) | collective-permute-done | bytes 264224 | tf_op jit(solution)/shard_map/ppermute | solution.py:97
  179.5 1.3 collective-permute-start.15
  180.8 11.7 %collective-permute-done.15 = f32[1,129,512]{2,1,0:T(8,128)S(1)} collective-permute-done((f32[1,129,512]{2,1,0:T(8,128)S(1)}, f32[1,129,512]{2,1,0:T(8,128)S(1)}, u32[]{:S(2)}, u32[]{:S(2)}) %collective-permute-start.15) | collective-permute-done | bytes 264224 | tf_op jit(solution)/shard_map/ppermute | solution.py:97
  192.7 1.3 collective-permute-start.16
  194.0 6.1 %collective-permute-done.16 = f32[1,129,512]{2,1,0:T(8,128)S(1)} collective-permute-done((f32[1,129,512]{2,1,0:T(8,128)S(1)}, f32[1,129,512]{2,1,0:T(8,128)S(1)}, u32[]{:S(2)}, u32[]{:S(2)}) %collective-permute-start.16) | collective-permute-done | bytes 264224 | tf_op jit(solution)/shard_map/ppermute | solution.py:97
  200.2 1.5 collective-permute-start.17
  201.7 7.3 %collective-permute-done.17 = f32[1,129,512]{2,1,0:T(8,128)S(1)} collective-permute-done((f32[1,129,512]{2,1,0:T(8,128)S(1)}, f32[1,129,512]{2,1,0:T(8,128)S(1)}, u32[]{:S(2)}, u32[]{:S(2)}) %collective-permute-start.17) | collective-permute-done | bytes 264224 | tf_op jit(solution)/shard_map/ppermute | solution.py:97
  211.9 1.3 collective-permute-start.18
  213.2 7.2 %collective-permute-done.18 = f32[1,128,512]{2,1,0:T(8,128)S(1)} collective-permute-done((f32[1,128,512]{2,1,0:T(8,128)S(1)}, f32[1,128,512]{2,1,0:T(8,128)S(1)}, u32[]{:S(2)}, u32[]{:S(2)}) %collective-permute-start.18) | collective-permute-done | bytes 262176 | tf_op jit(solution)/shard_map/ppermute | solution.py:109
  220.4 1.3 collective-permute-start.19
  221.7 9.1 %collective-permute-done.19 = f32[1,128,512]{2,1,0:T(8,128)S(1)} collective-permute-done((f32[1,128,512]{2,1,0:T(8,128)S(1)}, f32[1,128,512]{2,1,0:T(8,128)S(1)}, u32[]{:S(2)}, u32[]{:S(2)}) %collective-permute-start.19) | collective-permute-done | bytes 262176 | tf_op jit(solution)/shard_map/ppermute | solution.py:109
  230.9 1.3 collective-permute-start.20
  232.2 8.1 %collective-permute-done.20 = f32[1,128,512]{2,1,0:T(8,128)S(1)} collective-permute-done((f32[1,128,512]{2,1,0:T(8,128)S(1)}, f32[1,128,512]{2,1,0:T(8,128)S(1)}, u32[]{:S(2)}, u32[]{:S(2)}) %collective-permute-start.20) | collective-permute-done | bytes 262176 | tf_op jit(solution)/shard_map/ppermute | solution.py:109
  240.5 1.3 collective-permute-start.21
  241.8 12.6 %collective-permute-done.21 = f32[1,128,512]{2,1,0:T(8,128)S(1)} collective-permute-done((f32[1,128,512]{2,1,0:T(8,128)S(1)}, f32[1,128,512]{2,1,0:T(8,128)S(1)}, u32[]{:S(2)}, u32[]{:S(2)}) %collective-permute-start.21) | collective-permute-done | bytes 262176 | tf_op jit(solution)/shard_map/ppermute | solution.py:109
  254.5 1.3 collective-permute-start.22
  255.8 5.8 %collective-permute-done.22 = f32[1,128,512]{2,1,0:T(8,128)S(1)} collective-permute-done((f32[1,128,512]{2,1,0:T(8,128)S(1)}, f32[1,128,512]{2,1,0:T(8,128)S(1)}, u32[]{:S(2)}, u32[]{:S(2)}) %collective-permute-start.22) | collective-permute-done | bytes 262176 | tf_op jit(solution)/shard_map/ppermute | solution.py:109
  262.5 1.3 collective-permute-start.23
  263.8 9.9 %collective-permute-done.23 = f32[1,128,512]{2,1,0:T(8,128)S(1)} collective-permute-done((f32[1,128,512]{2,1,0:T(8,128)}, f32[1,128,512]{2,1,0:T(8,128)S(1)}, u32[]{:S(2)}, u32[]{:S(2)}) %collective-permute-start.23) | collective-permute-done | bytes 262176 | tf_op jit(solution)/shard_map/ppermute | solution.py:109
  273.7 1.1 fusion.289
  279.1 21.9 %collective-permute-start.24 = (f32[1184,128]{1,0:T(8,128)S(1)}, f32[1184,128]{1,0:T(8,128)}, u32[]{:S(2)}, u32[]{:S(2)}) collective-permute-start(f32[1184,128]{1,0:T(8,128)S(1)} %constant_dynamic-slice_fusion.3), channel_id=1, source_target_pairs={{0,1},{1,0},{2,3},{3,2},{4,5},{5,4},{6,7},{7,6},{8,9},{9,8},{10,11... | collective-permute-start | bytes 1818632 | tf_op jit(solution)/shard_map/ppermute | solution.py:130
  301.5 1.3 collective-permute-done.24
  304.0 10.2 %collective-permute-start.25 = (f32[296,128]{1,0:T(8,128)S(1)}, f32[296,128]{1,0:T(8,128)S(1)}, u32[]{:S(2)}, u32[]{:S(2)}) collective-permute-start(f32[296,128]{1,0:T(8,128)S(1)} %get-tuple-element.55), channel_id=1, source_target_pairs={{0,2},{1,7},{2,4},{3,1},{4,6},{5,3},{6,0},{7,5},{8,10},{9,15},{10,... | collective-permute-start | bytes 454664 | tf_op jit(solution)/shard_map/ppermute | solution.py:141
  314.3 5.0 %collective-permute-done.25 = f32[296,128]{1,0:T(8,128)S(1)} collective-permute-done((f32[296,128]{1,0:T(8,128)S(1)}, f32[296,128]{1,0:T(8,128)S(1)}, u32[]{:S(2)}, u32[]{:S(2)}) %collective-permute-start.25) | collective-permute-done | bytes 151584 | tf_op jit(solution)/shard_map/ppermute | solution.py:141
  319.4 8.0 %collective-permute-start.26 = (f32[296,128]{1,0:T(8,128)S(1)}, f32[296,128]{1,0:T(8,128)S(1)}, u32[]{:S(2)}, u32[]{:S(2)}) collective-permute-start(f32[296,128]{1,0:T(8,128)S(1)} %get-tuple-element.53), channel_id=1, source_target_pairs={{0,2},{1,7},{2,4},{3,1},{4,6},{5,3},{6,0},{7,5},{8,10},{9,15},{10,... | collective-permute-start | bytes 454664 | tf_op jit(solution)/shard_map/ppermute | solution.py:141
  327.6 3.6 collective-permute-done.26
  331.3 9.8 %collective-permute-start.27 = (f32[296,128]{1,0:T(8,128)S(1)}, f32[296,128]{1,0:T(8,128)S(1)}, u32[]{:S(2)}, u32[]{:S(2)}) collective-permute-start(f32[296,128]{1,0:T(8,128)S(1)} %get-tuple-element.51), channel_id=1, source_target_pairs={{0,2},{1,7},{2,4},{3,1},{4,6},{5,3},{6,0},{7,5},{8,10},{9,15},{10,... | collective-permute-start | bytes 454664 | tf_op jit(solution)/shard_map/ppermute | solution.py:141
  341.1 4.9 %collective-permute-done.27 = f32[296,128]{1,0:T(8,128)S(1)} collective-permute-done((f32[296,128]{1,0:T(8,128)S(1)}, f32[296,128]{1,0:T(8,128)S(1)}, u32[]{:S(2)}, u32[]{:S(2)}) %collective-permute-start.27) | collective-permute-done | bytes 151584 | tf_op jit(solution)/shard_map/ppermute | solution.py:141
  346.0 8.0 %collective-permute-start.28 = (f32[296,128]{1,0:T(8,128)S(1)}, f32[296,128]{1,0:T(8,128)S(1)}, u32[]{:S(2)}, u32[]{:S(2)}) collective-permute-start(f32[296,128]{1,0:T(8,128)S(1)} %dynamic-slice_bitcast_fusion.2), channel_id=1, source_target_pairs={{0,2},{1,7},{2,4},{3,1},{4,6},{5,3},{6,0},{7,5},{8,10},{9,15},{10,... | collective-permute-start | bytes 454664 | tf_op jit(solution)/shard_map/ppermute | solution.py:147
  354.2 6.6 %collective-permute-done.28 = f32[296,128]{1,0:T(8,128)S(1)} collective-permute-done((f32[296,128]{1,0:T(8,128)S(1)}, f32[296,128]{1,0:T(8,128)S(1)}, u32[]{:S(2)}, u32[]{:S(2)}) %collective-permute-start.28) | collective-permute-done | bytes 151584 | tf_op jit(solution)/shard_map/ppermute | solution.py:147
  360.8 6.3 %collective-permute-start.29 = (f32[296,128]{1,0:T(8,128)S(1)}, f32[296,128]{1,0:T(8,128)S(1)}, u32[]{:S(2)}, u32[]{:S(2)}) collective-permute-start(f32[296,128]{1,0:T(8,128)S(1)} %dynamic-slice_bitcast_fusion.1), channel_id=1, source_target_pairs={{0,2},{1,7},{2,4},{3,1},{4,6},{5,3},{6,0},{7,5},{8,10},{9,15},{10,... | collective-permute-start | bytes 454664 | tf_op jit(solution)/shard_map/ppermute | solution.py:147
  367.2 6.5 %collective-permute-done.29 = f32[296,128]{1,0:T(8,128)S(1)} collective-permute-done((f32[296,128]{1,0:T(8,128)S(1)}, f32[296,128]{1,0:T(8,128)S(1)}, u32[]{:S(2)}, u32[]{:S(2)}) %collective-permute-start.29) | collective-permute-done | bytes 151584 | tf_op jit(solution)/shard_map/ppermute | solution.py:147
  373.7 4.2 %collective-permute-start.30 = (f32[296,128]{1,0:T(8,128)S(1)}, f32[296,128]{1,0:T(8,128)S(1)}, u32[]{:S(2)}, u32[]{:S(2)}) collective-permute-start(f32[296,128]{1,0:T(8,128)S(1)} %dynamic-slice_bitcast_fusion), channel_id=1, source_target_pairs={{0,2},{1,7},{2,4},{3,1},{4,6},{5,3},{6,0},{7,5},{8,10},{9,15},{10,... | collective-permute-start | bytes 454664 | tf_op jit(solution)/shard_map/ppermute | solution.py:147
  378.0 7.7 %collective-permute-done.30 = f32[296,128]{1,0:T(8,128)S(1)} collective-permute-done((f32[296,128]{1,0:T(8,128)S(1)}, f32[296,128]{1,0:T(8,128)S(1)}, u32[]{:S(2)}, u32[]{:S(2)}) %collective-permute-start.30) | collective-permute-done | bytes 151584 | tf_op jit(solution)/shard_map/ppermute | solution.py:147
  385.7 1.9 collective-permute-start.31
  (249 shorter events, 30.8 us)
Async XLA Ops:
  0.6 2.9 copy-start.1
  3.2 1.1 copy-start
  4.6 0.9 copy-start.9
  6.0 7.4 %collective-permute-start = (f32[1,129,512]{2,1,0:T(8,128)S(1)}, f32[1,129,512]{2,1,0:T(8,128)S(1)}, u32[]{:S(2)}, u32[]{:S(2)}) collective-permute-start(f32[1,129,512]{2,1,0:T(8,128)S(1)} %pad_maximum_fusion.1), channel_id=1, source_target_pairs={{0,8},{8,16},{16,24},{24,32},{32,40},{40,48},{48,56},{56,64},{64,7... | collective-permute-start | bytes 792584 | tf_op jit(solution)/shard_map/ppermute | solution.py:97
  13.5 11.9 %collective-permute-start.1 = (f32[1,129,512]{2,1,0:T(8,128)S(1)}, f32[1,129,512]{2,1,0:T(8,128)S(1)}, u32[]{:S(2)}, u32[]{:S(2)}) collective-permute-start(f32[1,129,512]{2,1,0:T(8,128)S(1)} %pad_maximum_fusion.2), channel_id=1, source_target_pairs={{0,16},{8,24},{16,32},{24,40},{32,48},{40,56},{48,64},{56,72},{64,... | collective-permute-start | bytes 792584 | tf_op jit(solution)/shard_map/ppermute | solution.py:97
  25.6 11.0 %collective-permute-start.2 = (f32[1,129,512]{2,1,0:T(8,128)S(1)}, f32[1,129,512]{2,1,0:T(8,128)S(1)}, u32[]{:S(2)}, u32[]{:S(2)}) collective-permute-start(f32[1,129,512]{2,1,0:T(8,128)S(1)} %pad_maximum_fusion.3), channel_id=1, source_target_pairs={{0,32},{8,40},{16,48},{24,56},{32,64},{40,72},{48,80},{56,88},{64,... | collective-permute-start | bytes 792584 | tf_op jit(solution)/shard_map/ppermute | solution.py:97
  36.7 8.6 %collective-permute-start.3 = (f32[1,129,512]{2,1,0:T(8,128)S(1)}, f32[1,129,512]{2,1,0:T(8,128)S(1)}, u32[]{:S(2)}, u32[]{:S(2)}) collective-permute-start(f32[1,129,512]{2,1,0:T(8,128)S(1)} %pad_maximum_fusion.4), channel_id=1, source_target_pairs={{0,64},{8,72},{16,80},{24,88},{32,96},{40,104},{48,112},{56,120},{... | collective-permute-start | bytes 792584 | tf_op jit(solution)/shard_map/ppermute | solution.py:97
  45.5 24.2 %collective-permute-start.4 = (f32[1,129,512]{2,1,0:T(8,128)S(1)}, f32[1,129,512]{2,1,0:T(8,128)S(1)}, u32[]{:S(2)}, u32[]{:S(2)}) collective-permute-start(f32[1,129,512]{2,1,0:T(8,128)S(1)} %pad_maximum_fusion.5), channel_id=1, source_target_pairs={{0,128},{8,136},{16,144},{24,152},{32,160},{40,168},{48,176},{56,1... | collective-permute-start | bytes 792584 | tf_op jit(solution)/shard_map/ppermute | solution.py:97
  69.9 9.9 %collective-permute-start.5 = (f32[1,129,512]{2,1,0:T(8,128)S(1)}, f32[1,129,512]{2,1,0:T(8,128)S(1)}, u32[]{:S(2)}, u32[]{:S(2)}) collective-permute-start(f32[1,129,512]{2,1,0:T(8,128)S(1)} %pad_maximum_fusion.6), channel_id=1, source_target_pairs={{0,256},{8,264},{16,272},{24,280},{32,288},{40,296},{48,304},{56,3... | collective-permute-start | bytes 792584 | tf_op jit(solution)/shard_map/ppermute | solution.py:97
  82.5 4.6 %collective-permute-start.6 = (f32[1,128,512]{2,1,0:T(8,128)S(1)}, f32[1,128,512]{2,1,0:T(8,128)S(1)}, u32[]{:S(2)}, u32[]{:S(2)}) collective-permute-start(f32[1,128,512]{2,1,0:T(8,128)S(1)} %get-tuple-element.69), channel_id=1, source_target_pairs={{0,8},{8,16},{16,24},{24,32},{32,40},{40,48},{48,56},{56,64},{64,7... | collective-permute-start | bytes 786440 | tf_op jit(solution)/shard_map/ppermute | solution.py:109
  87.2 6.2 %collective-permute-start.7 = (f32[1,128,512]{2,1,0:T(8,128)S(1)}, f32[1,128,512]{2,1,0:T(8,128)S(1)}, u32[]{:S(2)}, u32[]{:S(2)}) collective-permute-start(f32[1,128,512]{2,1,0:T(8,128)S(1)} %multiply_add_fusion.22), channel_id=1, source_target_pairs={{0,16},{8,24},{16,32},{24,40},{32,48},{40,56},{48,64},{56,72},{64,... | collective-permute-start | bytes 786440 | tf_op jit(solution)/shard_map/ppermute | solution.py:109
  93.5 9.5 %collective-permute-start.8 = (f32[1,128,512]{2,1,0:T(8,128)S(1)}, f32[1,128,512]{2,1,0:T(8,128)S(1)}, u32[]{:S(2)}, u32[]{:S(2)}) collective-permute-start(f32[1,128,512]{2,1,0:T(8,128)S(1)} %multiply_add_fusion.20), channel_id=1, source_target_pairs={{0,32},{8,40},{16,48},{24,56},{32,64},{40,72},{48,80},{56,88},{64,... | collective-permute-start | bytes 786440 | tf_op jit(solution)/shard_map/ppermute | solution.py:109
  103.2 11.2 %collective-permute-start.9 = (f32[1,128,512]{2,1,0:T(8,128)S(1)}, f32[1,128,512]{2,1,0:T(8,128)S(1)}, u32[]{:S(2)}, u32[]{:S(2)}) collective-permute-start(f32[1,128,512]{2,1,0:T(8,128)S(1)} %get-tuple-element.33), channel_id=1, source_target_pairs={{0,64},{8,72},{16,80},{24,88},{32,96},{40,104},{48,112},{56,120},{... | collective-permute-start | bytes 786440 | tf_op jit(solution)/shard_map/ppermute | solution.py:109
  114.5 23.6 %collective-permute-start.10 = (f32[1,128,512]{2,1,0:T(8,128)S(1)}, f32[1,128,512]{2,1,0:T(8,128)S(1)}, u32[]{:S(2)}, u32[]{:S(2)}) collective-permute-start(f32[1,128,512]{2,1,0:T(8,128)S(1)} %multiply_add_fusion.16), channel_id=1, source_target_pairs={{0,128},{8,136},{16,144},{24,152},{32,160},{40,168},{48,176},{56,1... | collective-permute-start | bytes 786440 | tf_op jit(solution)/shard_map/ppermute | solution.py:109
  132.6 12.0 %copy-start.10 = (f32[1,128]{1,0:T(1,128)S(1)}, f32[1,128]{1,0:T(1,128)}, u32[]{:S(2)}) copy-start(f32[1,128]{1,0:T(1,128)} %param.11) | copy-start | bytes 1540
  138.3 9.5 %collective-permute-start.11 = (f32[1,128,512]{2,1,0:T(8,128)S(1)}, f32[1,128,512]{2,1,0:T(8,128)S(1)}, u32[]{:S(2)}, u32[]{:S(2)}) collective-permute-start(f32[1,128,512]{2,1,0:T(8,128)S(1)} %get-tuple-element.31), channel_id=1, source_target_pairs={{0,256},{8,264},{16,272},{24,280},{32,288},{40,296},{48,304},{56,3... | collective-permute-start | bytes 786440 | tf_op jit(solution)/shard_map/ppermute | solution.py:109
  147.9 0.9 copy-start.7
  149.2 60.9 %copy-start.5 = (f32[1,512,128]{1,2,0:T(8,128)}, f32[1,512,128]{1,2,0:T(8,128)S(1)}, u32[]{:S(2)}) copy-start(f32[1,512,128]{1,2,0:T(8,128)S(1)} %get-tuple-element.72) | copy-start | bytes 786436
  149.2 1.0 copy-start.2
  152.0 1.0 copy-start.3
  153.4 7.3 %collective-permute-start.12 = (f32[1,129,512]{2,1,0:T(8,128)S(1)}, f32[1,129,512]{2,1,0:T(8,128)S(1)}, u32[]{:S(2)}, u32[]{:S(2)}) collective-permute-start(f32[1,129,512]{2,1,0:T(8,128)S(1)} %pad_maximum_fusion.7), channel_id=1, source_target_pairs={{8,0},{16,8},{24,16},{32,24},{40,32},{48,40},{56,48},{64,56},{72,6... | collective-permute-start | bytes 792584 | tf_op jit(solution)/shard_map/ppermute | solution.py:97
  160.8 8.8 %collective-permute-start.13 = (f32[1,129,512]{2,1,0:T(8,128)S(1)}, f32[1,129,512]{2,1,0:T(8,128)S(1)}, u32[]{:S(2)}, u32[]{:S(2)}) collective-permute-start(f32[1,129,512]{2,1,0:T(8,128)S(1)} %pad_maximum_fusion.8), channel_id=1, source_target_pairs={{16,0},{24,8},{32,16},{40,24},{48,32},{56,40},{64,48},{72,56},{80,... | collective-permute-start | bytes 792584 | tf_op jit(solution)/shard_map/ppermute | solution.py:97
  169.8 9.6 %collective-permute-start.14 = (f32[1,129,512]{2,1,0:T(8,128)S(1)}, f32[1,129,512]{2,1,0:T(8,128)S(1)}, u32[]{:S(2)}, u32[]{:S(2)}) collective-permute-start(f32[1,129,512]{2,1,0:T(8,128)S(1)} %pad_maximum_fusion.9), channel_id=1, source_target_pairs={{32,0},{40,8},{48,16},{56,24},{64,32},{72,40},{80,48},{88,56},{96,... | collective-permute-start | bytes 792584 | tf_op jit(solution)/shard_map/ppermute | solution.py:97
  179.5 13.0 %collective-permute-start.15 = (f32[1,129,512]{2,1,0:T(8,128)S(1)}, f32[1,129,512]{2,1,0:T(8,128)S(1)}, u32[]{:S(2)}, u32[]{:S(2)}) collective-permute-start(f32[1,129,512]{2,1,0:T(8,128)S(1)} %pad_maximum_fusion.10), channel_id=1, source_target_pairs={{64,0},{72,8},{80,16},{88,24},{96,32},{104,40},{112,48},{120,56},{... | collective-permute-start | bytes 792584 | tf_op jit(solution)/shard_map/ppermute | solution.py:97
  192.7 7.4 %collective-permute-start.16 = (f32[1,129,512]{2,1,0:T(8,128)S(1)}, f32[1,129,512]{2,1,0:T(8,128)S(1)}, u32[]{:S(2)}, u32[]{:S(2)}) collective-permute-start(f32[1,129,512]{2,1,0:T(8,128)S(1)} %pad_maximum_fusion.11), channel_id=1, source_target_pairs={{128,0},{136,8},{144,16},{152,24},{160,32},{168,40},{176,48},{184,... | collective-permute-start | bytes 792584 | tf_op jit(solution)/shard_map/ppermute | solution.py:97
  200.2 8.8 %collective-permute-start.17 = (f32[1,129,512]{2,1,0:T(8,128)S(1)}, f32[1,129,512]{2,1,0:T(8,128)S(1)}, u32[]{:S(2)}, u32[]{:S(2)}) collective-permute-start(f32[1,129,512]{2,1,0:T(8,128)S(1)} %pad_maximum_fusion.12), channel_id=1, source_target_pairs={{256,0},{264,8},{272,16},{280,24},{288,32},{296,40},{304,48},{312,... | collective-permute-start | bytes 792584 | tf_op jit(solution)/shard_map/ppermute | solution.py:97
  211.9 8.5 %collective-permute-start.18 = (f32[1,128,512]{2,1,0:T(8,128)S(1)}, f32[1,128,512]{2,1,0:T(8,128)S(1)}, u32[]{:S(2)}, u32[]{:S(2)}) collective-permute-start(f32[1,128,512]{2,1,0:T(8,128)S(1)} %get-tuple-element.81), channel_id=1, source_target_pairs={{8,0},{16,8},{24,16},{32,24},{40,32},{48,40},{56,48},{64,56},{72,6... | collective-permute-start | bytes 786440 | tf_op jit(solution)/shard_map/ppermute | solution.py:109
  220.4 10.4 %collective-permute-start.19 = (f32[1,128,512]{2,1,0:T(8,128)S(1)}, f32[1,128,512]{2,1,0:T(8,128)S(1)}, u32[]{:S(2)}, u32[]{:S(2)}) collective-permute-start(f32[1,128,512]{2,1,0:T(8,128)S(1)} %multiply_add_fusion.8), channel_id=1, source_target_pairs={{16,0},{24,8},{32,16},{40,24},{48,32},{56,40},{64,48},{72,56},{80,... | collective-permute-start | bytes 786440 | tf_op jit(solution)/shard_map/ppermute | solution.py:109
  230.9 9.4 %collective-permute-start.20 = (f32[1,128,512]{2,1,0:T(8,128)S(1)}, f32[1,128,512]{2,1,0:T(8,128)S(1)}, u32[]{:S(2)}, u32[]{:S(2)}) collective-permute-start(f32[1,128,512]{2,1,0:T(8,128)S(1)} %multiply_add_fusion.6), channel_id=1, source_target_pairs={{32,0},{40,8},{48,16},{56,24},{64,32},{72,40},{80,48},{88,56},{96,... | collective-permute-start | bytes 786440 | tf_op jit(solution)/shard_map/ppermute | solution.py:109
  240.5 13.9 %collective-permute-start.21 = (f32[1,128,512]{2,1,0:T(8,128)S(1)}, f32[1,128,512]{2,1,0:T(8,128)S(1)}, u32[]{:S(2)}, u32[]{:S(2)}) collective-permute-start(f32[1,128,512]{2,1,0:T(8,128)S(1)} %get-tuple-element.12), channel_id=1, source_target_pairs={{64,0},{72,8},{80,16},{88,24},{96,32},{104,40},{112,48},{120,56},{... | collective-permute-start | bytes 786440 | tf_op jit(solution)/shard_map/ppermute | solution.py:109
  254.5 7.1 %collective-permute-start.22 = (f32[1,128,512]{2,1,0:T(8,128)S(1)}, f32[1,128,512]{2,1,0:T(8,128)S(1)}, u32[]{:S(2)}, u32[]{:S(2)}) collective-permute-start(f32[1,128,512]{2,1,0:T(8,128)S(1)} %multiply_add_fusion.2), channel_id=1, source_target_pairs={{128,0},{136,8},{144,16},{152,24},{160,32},{168,40},{176,48},{184,... | collective-permute-start | bytes 786440 | tf_op jit(solution)/shard_map/ppermute | solution.py:109
  262.5 11.2 %collective-permute-start.23 = (f32[1,128,512]{2,1,0:T(8,128)}, f32[1,128,512]{2,1,0:T(8,128)S(1)}, u32[]{:S(2)}, u32[]{:S(2)}) collective-permute-start(f32[1,128,512]{2,1,0:T(8,128)} %get-tuple-element.10), channel_id=1, source_target_pairs={{256,0},{264,8},{272,16},{280,24},{288,32},{296,40},{304,48},{312,... | collective-permute-start | bytes 786440 | tf_op jit(solution)/shard_map/ppermute | solution.py:109
  276.2 1.0 copy-start.6
  276.3 1.0 copy-start.8
  279.1 23.7 %collective-permute-start.24 = (f32[1184,128]{1,0:T(8,128)S(1)}, f32[1184,128]{1,0:T(8,128)}, u32[]{:S(2)}, u32[]{:S(2)}) collective-permute-start(f32[1184,128]{1,0:T(8,128)S(1)} %constant_dynamic-slice_fusion.3), channel_id=1, source_target_pairs={{0,1},{1,0},{2,3},{3,2},{4,5},{5,4},{6,7},{7,6},{8,9},{9,8},{10,11... | collective-permute-start | bytes 1818632 | tf_op jit(solution)/shard_map/ppermute | solution.py:130
  304.0 15.4 %collective-permute-start.25 = (f32[296,128]{1,0:T(8,128)S(1)}, f32[296,128]{1,0:T(8,128)S(1)}, u32[]{:S(2)}, u32[]{:S(2)}) collective-permute-start(f32[296,128]{1,0:T(8,128)S(1)} %get-tuple-element.55), channel_id=1, source_target_pairs={{0,2},{1,7},{2,4},{3,1},{4,6},{5,3},{6,0},{7,5},{8,10},{9,15},{10,... | collective-permute-start | bytes 454664 | tf_op jit(solution)/shard_map/ppermute | solution.py:141
  319.4 11.7 %collective-permute-start.26 = (f32[296,128]{1,0:T(8,128)S(1)}, f32[296,128]{1,0:T(8,128)S(1)}, u32[]{:S(2)}, u32[]{:S(2)}) collective-permute-start(f32[296,128]{1,0:T(8,128)S(1)} %get-tuple-element.53), channel_id=1, source_target_pairs={{0,2},{1,7},{2,4},{3,1},{4,6},{5,3},{6,0},{7,5},{8,10},{9,15},{10,... | collective-permute-start | bytes 454664 | tf_op jit(solution)/shard_map/ppermute | solution.py:141
  331.3 14.7 %collective-permute-start.27 = (f32[296,128]{1,0:T(8,128)S(1)}, f32[296,128]{1,0:T(8,128)S(1)}, u32[]{:S(2)}, u32[]{:S(2)}) collective-permute-start(f32[296,128]{1,0:T(8,128)S(1)} %get-tuple-element.51), channel_id=1, source_target_pairs={{0,2},{1,7},{2,4},{3,1},{4,6},{5,3},{6,0},{7,5},{8,10},{9,15},{10,... | collective-permute-start | bytes 454664 | tf_op jit(solution)/shard_map/ppermute | solution.py:141
  346.0 14.7 %collective-permute-start.28 = (f32[296,128]{1,0:T(8,128)S(1)}, f32[296,128]{1,0:T(8,128)S(1)}, u32[]{:S(2)}, u32[]{:S(2)}) collective-permute-start(f32[296,128]{1,0:T(8,128)S(1)} %dynamic-slice_bitcast_fusion.2), channel_id=1, source_target_pairs={{0,2},{1,7},{2,4},{3,1},{4,6},{5,3},{6,0},{7,5},{8,10},{9,15},{10,... | collective-permute-start | bytes 454664 | tf_op jit(solution)/shard_map/ppermute | solution.py:147
  354.1 33.6 %copy-start.4 = (bf16[128,9,128]{0,2,1:T(8,128)(2,1)S(1)}, bf16[128,9,128]{0,2,1:T(8,128)(2,1)}, u32[]{:S(2)}) copy-start(bf16[128,9,128]{0,2,1:T(8,128)(2,1)} %copy.26) | copy-start | bytes 884740
  360.8 12.9 %collective-permute-start.29 = (f32[296,128]{1,0:T(8,128)S(1)}, f32[296,128]{1,0:T(8,128)S(1)}, u32[]{:S(2)}, u32[]{:S(2)}) collective-permute-start(f32[296,128]{1,0:T(8,128)S(1)} %dynamic-slice_bitcast_fusion.1), channel_id=1, source_target_pairs={{0,2},{1,7},{2,4},{3,1},{4,6},{5,3},{6,0},{7,5},{8,10},{9,15},{10,... | collective-permute-start | bytes 454664 | tf_op jit(solution)/shard_map/ppermute | solution.py:147
  373.7 12.0 %collective-permute-start.30 = (f32[296,128]{1,0:T(8,128)S(1)}, f32[296,128]{1,0:T(8,128)S(1)}, u32[]{:S(2)}, u32[]{:S(2)}) collective-permute-start(f32[296,128]{1,0:T(8,128)S(1)} %dynamic-slice_bitcast_fusion), channel_id=1, source_target_pairs={{0,2},{1,7},{2,4},{3,1},{4,6},{5,3},{6,0},{7,5},{8,10},{9,15},{10,... | collective-permute-start | bytes 454664 | tf_op jit(solution)/shard_map/ppermute | solution.py:147
  385.7 3.9 %collective-permute-start.31 = (f32[1184,128]{1,0:T(8,128)S(1)}, f32[1184,128]{1,0:T(8,128)S(1)}, u32[]{:S(2)}, u32[]{:S(2)}) collective-permute-start(f32[1184,128]{1,0:T(8,128)S(1)} %bitcast.501), channel_id=1, source_target_pairs={{0,1},{1,0},{2,3},{3,2},{4,5},{5,4},{6,7},{7,6},{8,9},{9,8},{10,11... | collective-permute-start | bytes 1818632 | tf_op jit(solution)/shard_map/ppermute | solution.py:150

commit v5 on v4

--- a/solution.py
+++ b/solution.py
@@ -69,13 +69,14 @@
     return adjoint
 
 
-def scan_distances(count):
-    distances = []
+def scan_rounds(count):
+    rounds = []
     d = 1
     while d < count:
-        distances.append(d)
-        d *= 2
-    return distances
+        m = 3 if count % (4 * d) == 0 and d in (1, count // 4) else 1
+        rounds.append((d, m))
+        d *= m + 1
+    return rounds
 
 
 def scan_pairs(count, d, reverse):
@@ -90,24 +91,32 @@
     total = jnp.zeros_like(local)
     product = jnp.ones_like(gain)
     factors = []
-    for d in scan_distances(count):
+    for d, m in scan_rounds(count):
         sending = gain[None, :, None] * total + local
         gain_row = jnp.pad(gain * product, (0, pixels - channels))
         packed = jnp.concatenate([sending, gain_row[None, None, :]], axis=1)
-        received = lax.ppermute(packed, axis, scan_pairs(count, d, reverse))
-        factors.append(product)
-        total = total + product[None, :, None] * received[:, :channels, :]
-        product = product * received[0, channels, :channels]
+        received = [
+            lax.ppermute(packed, axis, scan_pairs(count, j * d, reverse)) for j in range(1, m + 1)
+        ]
+        for part in received:
+            factors.append(product)
+            total = total + product[None, :, None] * part[:, :channels, :]
+            product = product * part[0, channels, :channels]
     return total, factors
 
 
 def exclusive_scan_again(gain, local, factors, axis, reverse):
     count = lax.axis_size(axis)
     total = jnp.zeros_like(local)
-    for d, factor in zip(scan_distances(count), factors):
+    used = 0
+    for d, m in scan_rounds(count):
         sending = gain[None, :, None] * total + local
-        received = lax.ppermute(sending, axis, scan_pairs(count, d, reverse))
-        total = total + factor[None, :, None] * received
+        received = [
+            lax.ppermute(sending, axis, scan_pairs(count, j * d, reverse)) for j in range(1, m + 1)
+        ]
+        for part in received:
+            total = total + factors[used][None, :, None] * part
+            used += 1
     return total
 
 

time: 395 us -> 398 us (level)
  the two profiles are of different devices: /device:TPU:1 before, /device:TPU:23 now
where the time goes in v5:
time: 398 us; the launch traced here: 397 us
  waiting for transfers between devices  220 us (55%)
  starting transfers between devices  142 us (36%)
  other arithmetic  19.4 us (5%)
  matrix products  6.27 us (2%)
  local copies, waits for them, and re-layouts  6 us (2%)
    ppermute x16, waiting for transfers between devices, exclusive_scan_first(): lax.ppermute(packed, axis, scan_pairs(count, j * d, reverse))  91.7 us
    ppermute x16, waiting for transfers between devices, exclusive_scan_again(): lax.ppermute(sending, axis, scan_pairs(count, j * d, reverse))  80.6 us
    ppermute x16, starting transfers between devices, exclusive_scan_again(): lax.ppermute(sending, axis, scan_pairs(count, j * d, reverse))  56.8 us
    ppermute x6, waiting for transfers between devices, batch_sum(): got = lax.ppermute(sent, axis, ring)  46.3 us
    ppermute x16, starting transfers between devices, exclusive_scan_first(): lax.ppermute(packed, axis, scan_pairs(count, j * d, reverse))  41.2 us
    ppermute x1, starting transfers between devices, batch_sum(): other = lax.ppermute(half, axis, partner)  21 us
    ppermute x6, starting transfers between devices, batch_sum(): got = lax.ppermute(sent, axis, ring)  19.8 us
    unnamed x96, other arithmetic  9.1 us
  transfers between devices with their start and end apart: 40, of which 32 were waited for; matrix products, arithmetic and copies ran while one was open for 1% of the time, Pallas kernels for 0%

profile of v5, /device:TPU:23, one launch (start us, length us, event | category | flops | bytes accessed | tf_op | source)
XLA Modules:
  0.0 396.7 jit_solution(3112081226965270686)
XLA Ops:
  6.0 3.8 collective-permute-start.2
  9.8 4.1 %collective-permute-start.1 = (f32[1,129,512]{2,1,0:T(8,128)S(1)}, f32[1,129,512]{2,1,0:T(8,128)S(1)}, u32[]{:S(2)}, u32[]{:S(2)}) collective-permute-start(f32[1,129,512]{2,1,0:T(8,128)S(1)} %pad_maximum_fusion.1), channel_id=1, source_target_pairs={{0,16},{8,24},{16,32},{24,40},{32,48},{40,56},{48,64},{56,72},{64,... | collective-permute-start | bytes 792584 | tf_op jit(solution)/shard_map/ppermute | solution.py:99
  13.9 3.7 collective-permute-start
  17.6 8.5 %collective-permute-done.1 = f32[1,129,512]{2,1,0:T(8,128)S(1)} collective-permute-done((f32[1,129,512]{2,1,0:T(8,128)S(1)}, f32[1,129,512]{2,1,0:T(8,128)S(1)}, u32[]{:S(2)}, u32[]{:S(2)}) %collective-permute-start.1) | collective-permute-done | bytes 264224 | tf_op jit(solution)/shard_map/ppermute | solution.py:99
  26.1 3.2 collective-permute-done
  29.5 2.8 collective-permute-start.3
  32.4 8.4 %collective-permute-done.3 = f32[1,129,512]{2,1,0:T(8,128)S(1)} collective-permute-done((f32[1,129,512]{2,1,0:T(8,128)S(1)}, f32[1,129,512]{2,1,0:T(8,128)S(1)}, u32[]{:S(2)}, u32[]{:S(2)}) %collective-permute-start.3) | collective-permute-done | bytes 264224 | tf_op jit(solution)/shard_map/ppermute | solution.py:99
  40.9 2.0 collective-permute-start.4
  42.9 15.3 %collective-permute-done.4 = f32[1,129,512]{2,1,0:T(8,128)S(1)} collective-permute-done((f32[1,129,512]{2,1,0:T(8,128)S(1)}, f32[1,129,512]{2,1,0:T(8,128)S(1)}, u32[]{:S(2)}, u32[]{:S(2)}) %collective-permute-start.4) | collective-permute-done | bytes 264224 | tf_op jit(solution)/shard_map/ppermute | solution.py:99
  59.7 1.9 collective-permute-start.5
  62.3 7.3 %collective-permute-done.6 = f32[1,129,512]{2,1,0:T(8,128)S(1)} collective-permute-done((f32[1,129,512]{2,1,0:T(8,128)S(1)}, f32[1,129,512]{2,1,0:T(8,128)S(1)}, u32[]{:S(2)}, u32[]{:S(2)}) %collective-permute-start.6) | collective-permute-done | bytes 264224 | tf_op jit(solution)/shard_map/ppermute | solution.py:99
  69.5 6.8 %collective-permute-done.5 = f32[1,129,512]{2,1,0:T(8,128)S(1)} collective-permute-done((f32[1,129,512]{2,1,0:T(8,128)S(1)}, f32[1,129,512]{2,1,0:T(8,128)S(1)}, u32[]{:S(2)}, u32[]{:S(2)}) %collective-permute-start.5) | collective-permute-done | bytes 264224 | tf_op jit(solution)/shard_map/ppermute | solution.py:99
  79.1 1.9 collective-permute-start.10
  81.0 1.9 collective-permute-start.8
  82.9 3.4 collective-permute-start.9
  86.4 3.3 collective-permute-done.10
  89.6 6.7 %collective-permute-done.8 = f32[1,128,512]{2,1,0:T(8,128)S(1)} collective-permute-done((f32[1,128,512]{2,1,0:T(8,128)S(1)}, f32[1,128,512]{2,1,0:T(8,128)S(1)}, u32[]{:S(2)}, u32[]{:S(2)}) %collective-permute-start.8) | collective-permute-done | bytes 262176 | tf_op jit(solution)/shard_map/ppermute | solution.py:115
  96.3 5.8 %collective-permute-done.9 = f32[1,128,512]{2,1,0:T(8,128)S(1)} collective-permute-done((f32[1,128,512]{2,1,0:T(8,128)S(1)}, f32[1,128,512]{2,1,0:T(8,128)S(1)}, u32[]{:S(2)}, u32[]{:S(2)}) %collective-permute-start.9) | collective-permute-done | bytes 262176 | tf_op jit(solution)/shard_map/ppermute | solution.py:115
  102.2 1.9 collective-permute-start.11
  104.2 9.5 %collective-permute-done.11 = f32[1,128,512]{2,1,0:T(8,128)S(1)} collective-permute-done((f32[1,128,512]{2,1,0:T(8,128)S(1)}, f32[1,128,512]{2,1,0:T(8,128)S(1)}, u32[]{:S(2)}, u32[]{:S(2)}) %collective-permute-start.11) | collective-permute-done | bytes 262176 | tf_op jit(solution)/shard_map/ppermute | solution.py:115
  113.7 1.9 collective-permute-start.12
  116.2 12.4 %collective-permute-done.12 = f32[1,128,512]{2,1,0:T(8,128)S(1)} collective-permute-done((f32[1,128,512]{2,1,0:T(8,128)S(1)}, f32[1,128,512]{2,1,0:T(8,128)S(1)}, u32[]{:S(2)}, u32[]{:S(2)}) %collective-permute-start.12) | collective-permute-done | bytes 262176 | tf_op jit(solution)/shard_map/ppermute | solution.py:115
  130.8 2.4 collective-permute-start.13
  134.3 5.9 %collective-permute-done.14 = f32[1,128,512]{2,1,0:T(8,128)S(1)} collective-permute-done((f32[1,128,512]{2,1,0:T(8,128)S(1)}, f32[1,128,512]{2,1,0:T(8,128)S(1)}, u32[]{:S(2)}, u32[]{:S(2)}) %collective-permute-start.14) | collective-permute-done | bytes 262176 | tf_op jit(solution)/shard_map/ppermute | solution.py:115
  140.3 6.5 %collective-permute-done.13 = f32[1,128,512]{2,1,0:T(8,128)} collective-permute-done((f32[1,128,512]{2,1,0:T(8,128)S(1)}, f32[1,128,512]{2,1,0:T(8,128)}, u32[]{:S(2)}, u32[]{:S(2)}) %collective-permute-start.13) | collective-permute-done | bytes 262176 | tf_op jit(solution)/shard_map/ppermute | solution.py:115
  153.4 2.6 collective-permute-start.18
  155.9 7.1 %collective-permute-start.17 = (f32[1,129,512]{2,1,0:T(8,128)S(1)}, f32[1,129,512]{2,1,0:T(8,128)S(1)}, u32[]{:S(2)}, u32[]{:S(2)}) collective-permute-start(f32[1,129,512]{2,1,0:T(8,128)S(1)} %pad_maximum_fusion.5), channel_id=1, source_target_pairs={{16,0},{24,8},{32,16},{40,24},{48,32},{56,40},{64,48},{72,56},{80,... | collective-permute-start | bytes 792584 | tf_op jit(solution)/shard_map/ppermute | solution.py:99
  163.1 1.9 collective-permute-start.16
  165.0 4.5 %collective-permute-done.17 = f32[1,129,512]{2,1,0:T(8,128)S(1)} collective-permute-done((f32[1,129,512]{2,1,0:T(8,128)S(1)}, f32[1,129,512]{2,1,0:T(8,128)S(1)}, u32[]{:S(2)}, u32[]{:S(2)}) %collective-permute-start.17) | collective-permute-done | bytes 264224 | tf_op jit(solution)/shard_map/ppermute | solution.py:99
  169.6 11.0 %collective-permute-done.16 = f32[1,129,512]{2,1,0:T(8,128)S(1)} collective-permute-done((f32[1,129,512]{2,1,0:T(8,128)S(1)}, f32[1,129,512]{2,1,0:T(8,128)S(1)}, u32[]{:S(2)}, u32[]{:S(2)}) %collective-permute-start.16) | collective-permute-done | bytes 264224 | tf_op jit(solution)/shard_map/ppermute | solution.py:99
  180.7 3.2 collective-permute-start.19
  184.0 5.5 %collective-permute-done.19 = f32[1,129,512]{2,1,0:T(8,128)S(1)} collective-permute-done((f32[1,129,512]{2,1,0:T(8,128)S(1)}, f32[1,129,512]{2,1,0:T(8,128)S(1)}, u32[]{:S(2)}, u32[]{:S(2)}) %collective-permute-start.19) | collective-permute-done | bytes 264224 | tf_op jit(solution)/shard_map/ppermute | solution.py:99
  189.6 1.9 collective-permute-start.20
  191.5 13.6 %collective-permute-done.20 = f32[1,129,512]{2,1,0:T(8,128)S(1)} collective-permute-done((f32[1,129,512]{2,1,0:T(8,128)S(1)}, f32[1,129,512]{2,1,0:T(8,128)S(1)}, u32[]{:S(2)}, u32[]{:S(2)}) %collective-permute-start.20) | collective-permute-done | bytes 264224 | tf_op jit(solution)/shard_map/ppermute | solution.py:99
  206.6 1.9 collective-permute-start.21
  210.6 6.6 %collective-permute-done.21 = f32[1,129,512]{2,1,0:T(8,128)S(1)} collective-permute-done((f32[1,129,512]{2,1,0:T(8,128)S(1)}, f32[1,129,512]{2,1,0:T(8,128)S(1)}, u32[]{:S(2)}, u32[]{:S(2)}) %collective-permute-start.21) | collective-permute-done | bytes 264224 | tf_op jit(solution)/shard_map/ppermute | solution.py:99
  220.0 2.5 collective-permute-start.26
  222.5 11.1 %collective-permute-start.24 = (f32[1,128,512]{2,1,0:T(8,128)S(1)}, f32[1,128,512]{2,1,0:T(8,128)S(1)}, u32[]{:S(2)}, u32[]{:S(2)}) collective-permute-start(f32[1,128,512]{2,1,0:T(8,128)S(1)} %get-tuple-element.83), channel_id=1, source_target_pairs={{8,0},{16,8},{24,16},{32,24},{40,32},{48,40},{56,48},{64,56},{72,6... | collective-permute-start | bytes 786440 | tf_op jit(solution)/shard_map/ppermute | solution.py:115
  233.6 2.1 collective-permute-start.25
  235.7 2.8 collective-permute-done.24
  238.5 6.2 %collective-permute-done.25 = f32[1,128,512]{2,1,0:T(8,128)S(1)} collective-permute-done((f32[1,128,512]{2,1,0:T(8,128)S(1)}, f32[1,128,512]{2,1,0:T(8,128)S(1)}, u32[]{:S(2)}, u32[]{:S(2)}) %collective-permute-start.25) | collective-permute-done | bytes 262176 | tf_op jit(solution)/shard_map/ppermute | solution.py:115
  244.8 8.9 %collective-permute-start.27 = (f32[1,128,512]{2,1,0:T(8,128)S(1)}, f32[1,128,512]{2,1,0:T(8,128)S(1)}, u32[]{:S(2)}, u32[]{:S(2)}) collective-permute-start(f32[1,128,512]{2,1,0:T(8,128)S(1)} %get-tuple-element.12), channel_id=1, source_target_pairs={{32,0},{40,8},{48,16},{56,24},{64,32},{72,40},{80,48},{88,56},{96,... | collective-permute-start | bytes 786440 | tf_op jit(solution)/shard_map/ppermute | solution.py:115
  253.8 3.3 collective-permute-done.27
  257.2 3.0 collective-permute-start.28
  260.2 6.0 %collective-permute-done.28 = f32[1,128,512]{2,1,0:T(8,128)S(1)} collective-permute-done((f32[1,128,512]{2,1,0:T(8,128)S(1)}, f32[1,128,512]{2,1,0:T(8,128)S(1)}, u32[]{:S(2)}, u32[]{:S(2)}) %collective-permute-start.28) | collective-permute-done | bytes 262176 | tf_op jit(solution)/shard_map/ppermute | solution.py:115
  267.8 4.1 %collective-permute-start.30 = (f32[1,128,512]{2,1,0:T(8,128)}, f32[1,128,512]{2,1,0:T(8,128)}, u32[]{:S(2)}, u32[]{:S(2)}) collective-permute-start(f32[1,128,512]{2,1,0:T(8,128)} %get-tuple-element.10), channel_id=1, source_target_pairs={{256,0},{264,8},{272,16},{280,24},{288,32},{296,40},{304,48},{312,... | collective-permute-start | bytes 786440 | tf_op jit(solution)/shard_map/ppermute | solution.py:115
  271.9 8.9 %collective-permute-start.29 = (f32[1,128,512]{2,1,0:T(8,128)}, f32[1,128,512]{2,1,0:T(8,128)}, u32[]{:S(2)}, u32[]{:S(2)}) collective-permute-start(f32[1,128,512]{2,1,0:T(8,128)} %get-tuple-element.10), channel_id=1, source_target_pairs={{128,0},{136,8},{144,16},{152,24},{160,32},{168,40},{176,48},{184,... | collective-permute-start | bytes 786440 | tf_op jit(solution)/shard_map/ppermute | solution.py:115
  280.8 12.2 %collective-permute-done.29 = f32[1,128,512]{2,1,0:T(8,128)} collective-permute-done((f32[1,128,512]{2,1,0:T(8,128)}, f32[1,128,512]{2,1,0:T(8,128)}, u32[]{:S(2)}, u32[]{:S(2)}) %collective-permute-start.29) | collective-permute-done | bytes 262176 | tf_op jit(solution)/shard_map/ppermute | solution.py:115
  293.0 1.3 fusion.293
  298.6 3.4 collective-permute-start.32
  302.4 1.3 collective-permute-done.32
  305.0 6.2 %collective-permute-start.33 = (f32[296,128]{1,0:T(8,128)S(1)}, f32[296,128]{1,0:T(8,128)S(1)}, u32[]{:S(2)}, u32[]{:S(2)}) collective-permute-start(f32[296,128]{1,0:T(8,128)S(1)} %get-tuple-element.57), channel_id=1, source_target_pairs={{0,2},{1,7},{2,4},{3,1},{4,6},{5,3},{6,0},{7,5},{8,10},{9,15},{10,... | collective-permute-start | bytes 454664 | tf_op jit(solution)/shard_map/ppermute | solution.py:150
  311.3 8.7 %collective-permute-done.33 = f32[296,128]{1,0:T(8,128)S(1)} collective-permute-done((f32[296,128]{1,0:T(8,128)S(1)}, f32[296,128]{1,0:T(8,128)S(1)}, u32[]{:S(2)}, u32[]{:S(2)}) %collective-permute-start.33) | collective-permute-done | bytes 151584 | tf_op jit(solution)/shard_map/ppermute | solution.py:150
  320.1 3.1 collective-permute-start.34
  323.2 8.4 %collective-permute-done.34 = f32[296,128]{1,0:T(8,128)S(1)} collective-permute-done((f32[296,128]{1,0:T(8,128)S(1)}, f32[296,128]{1,0:T(8,128)S(1)}, u32[]{:S(2)}, u32[]{:S(2)}) %collective-permute-start.34) | collective-permute-done | bytes 151584 | tf_op jit(solution)/shard_map/ppermute | solution.py:150
  331.7 2.1 collective-permute-start.35
  333.8 7.8 %collective-permute-done.35 = f32[296,128]{1,0:T(8,128)S(1)} collective-permute-done((f32[296,128]{1,0:T(8,128)S(1)}, f32[296,128]{1,0:T(8,128)S(1)}, u32[]{:S(2)}, u32[]{:S(2)}) %collective-permute-start.35) | collective-permute-done | bytes 151584 | tf_op jit(solution)/shard_map/ppermute | solution.py:150
  341.7 2.3 collective-permute-start.36
  344.1 7.4 %collective-permute-done.36 = f32[296,128]{1,0:T(8,128)S(1)} collective-permute-done((f32[296,128]{1,0:T(8,128)S(1)}, f32[296,128]{1,0:T(8,128)S(1)}, u32[]{:S(2)}, u32[]{:S(2)}) %collective-permute-start.36) | collective-permute-done | bytes 151584 | tf_op jit(solution)/shard_map/ppermute | solution.py:156
  351.6 2.3 collective-permute-start.37
  354.0 7.4 %collective-permute-done.37 = f32[296,128]{1,0:T(8,128)S(1)} collective-permute-done((f32[296,128]{1,0:T(8,128)S(1)}, f32[296,128]{1,0:T(8,128)S(1)}, u32[]{:S(2)}, u32[]{:S(2)}) %collective-permute-start.37) | collective-permute-done | bytes 151584 | tf_op jit(solution)/shard_map/ppermute | solution.py:156
  361.4 3.8 collective-permute-start.38
  365.4 6.6 %collective-permute-done.38 = f32[296,128]{1,0:T(8,128)S(1)} collective-permute-done((f32[296,128]{1,0:T(8,128)S(1)}, f32[296,128]{1,0:T(8,128)S(1)}, u32[]{:S(2)}, u32[]{:S(2)}) %collective-permute-start.38) | collective-permute-done | bytes 151584 | tf_op jit(solution)/shard_map/ppermute | solution.py:156
  372.0 21.0 %collective-permute-start.39 = (f32[1184,128]{1,0:T(8,128)S(1)}, f32[1184,128]{1,0:T(8,128)S(1)}, u32[]{:S(2)}, u32[]{:S(2)}) collective-permute-start(f32[1184,128]{1,0:T(8,128)S(1)} %bitcast.507), channel_id=1, source_target_pairs={{0,1},{1,0},{2,3},{3,2},{4,5},{5,4},{6,7},{7,6},{8,9},{9,8},{10,11... | collective-permute-start | bytes 1818632 | tf_op jit(solution)/shard_map/ppermute | solution.py:159
  (247 shorter events, 38.5 us)
Async XLA Ops:
  0.6 2.9 copy-start.1
  3.2 1.1 copy-start
  4.6 0.9 copy-start.9
  6.0 11.6 %collective-permute-start.2 = (f32[1,129,512]{2,1,0:T(8,128)S(1)}, f32[1,129,512]{2,1,0:T(8,128)S(1)}, u32[]{:S(2)}, u32[]{:S(2)}) collective-permute-start(f32[1,129,512]{2,1,0:T(8,128)S(1)} %pad_maximum_fusion.1), channel_id=1, source_target_pairs={{0,24},{8,32},{16,40},{24,48},{32,56},{40,64},{48,72},{56,80},{64,... | collective-permute-start | bytes 792584 | tf_op jit(solution)/shard_map/ppermute | solution.py:99
  9.8 16.3 %collective-permute-start.1 = (f32[1,129,512]{2,1,0:T(8,128)S(1)}, f32[1,129,512]{2,1,0:T(8,128)S(1)}, u32[]{:S(2)}, u32[]{:S(2)}) collective-permute-start(f32[1,129,512]{2,1,0:T(8,128)S(1)} %pad_maximum_fusion.1), channel_id=1, source_target_pairs={{0,16},{8,24},{16,32},{24,40},{32,48},{40,56},{48,64},{56,72},{64,... | collective-permute-start | bytes 792584 | tf_op jit(solution)/shard_map/ppermute | solution.py:99
  13.9 15.4 %collective-permute-start = (f32[1,129,512]{2,1,0:T(8,128)S(1)}, f32[1,129,512]{2,1,0:T(8,128)S(1)}, u32[]{:S(2)}, u32[]{:S(2)}) collective-permute-start(f32[1,129,512]{2,1,0:T(8,128)S(1)} %pad_maximum_fusion.1), channel_id=1, source_target_pairs={{0,8},{8,16},{16,24},{24,32},{32,40},{40,48},{48,56},{56,64},{64,7... | collective-permute-start | bytes 792584 | tf_op jit(solution)/shard_map/ppermute | solution.py:99
  29.5 11.2 %collective-permute-start.3 = (f32[1,129,512]{2,1,0:T(8,128)S(1)}, f32[1,129,512]{2,1,0:T(8,128)S(1)}, u32[]{:S(2)}, u32[]{:S(2)}) collective-permute-start(f32[1,129,512]{2,1,0:T(8,128)S(1)} %pad_maximum_fusion.2), channel_id=1, source_target_pairs={{0,32},{8,40},{16,48},{24,56},{32,64},{40,72},{48,80},{56,88},{64,... | collective-permute-start | bytes 792584 | tf_op jit(solution)/shard_map/ppermute | solution.py:99
  40.9 17.3 %collective-permute-start.4 = (f32[1,129,512]{2,1,0:T(8,128)S(1)}, f32[1,129,512]{2,1,0:T(8,128)S(1)}, u32[]{:S(2)}, u32[]{:S(2)}) collective-permute-start(f32[1,129,512]{2,1,0:T(8,128)S(1)} %pad_maximum_fusion.3), channel_id=1, source_target_pairs={{0,64},{8,72},{16,80},{24,88},{32,96},{40,104},{48,112},{56,120},{... | collective-permute-start | bytes 792584 | tf_op jit(solution)/shard_map/ppermute | solution.py:99
  58.4 11.2 %collective-permute-start.6 = (f32[1,129,512]{2,1,0:T(8,128)S(1)}, f32[1,129,512]{2,1,0:T(8,128)S(1)}, u32[]{:S(2)}, u32[]{:S(2)}) collective-permute-start(f32[1,129,512]{2,1,0:T(8,128)S(1)} %pad_maximum_fusion.4), channel_id=1, source_target_pairs={{0,256},{8,264},{16,272},{24,280},{32,288},{40,296},{48,304},{56,3... | collective-permute-start | bytes 792584 | tf_op jit(solution)/shard_map/ppermute | solution.py:99
  59.7 16.6 %collective-permute-start.5 = (f32[1,129,512]{2,1,0:T(8,128)S(1)}, f32[1,129,512]{2,1,0:T(8,128)S(1)}, u32[]{:S(2)}, u32[]{:S(2)}) collective-permute-start(f32[1,129,512]{2,1,0:T(8,128)S(1)} %pad_maximum_fusion.4), channel_id=1, source_target_pairs={{0,128},{8,136},{16,144},{24,152},{32,160},{40,168},{48,176},{56,1... | collective-permute-start | bytes 792584 | tf_op jit(solution)/shard_map/ppermute | solution.py:99
  61.6 14.7 %collective-permute-start.7 = (f32[1,129,512]{2,1,0:T(8,128)S(1)}, f32[1,129,512]{2,1,0:T(8,128)S(1)}, u32[]{:S(2)}, u32[]{:S(2)}) collective-permute-start(f32[1,129,512]{2,1,0:T(8,128)S(1)} %pad_maximum_fusion.4), channel_id=1, source_target_pairs={{0,384},{8,392},{16,400},{24,408},{32,416},{40,424},{48,432},{56,4... | collective-permute-start | bytes 792584 | tf_op jit(solution)/shard_map/ppermute | solution.py:99
  79.1 10.5 %collective-permute-start.10 = (f32[1,128,512]{2,1,0:T(8,128)S(1)}, f32[1,128,512]{2,1,0:T(8,128)S(1)}, u32[]{:S(2)}, u32[]{:S(2)}) collective-permute-start(f32[1,128,512]{2,1,0:T(8,128)S(1)} %get-tuple-element.71), channel_id=1, source_target_pairs={{0,24},{8,32},{16,40},{24,48},{32,56},{40,64},{48,72},{56,80},{64,... | collective-permute-start | bytes 786440 | tf_op jit(solution)/shard_map/ppermute | solution.py:115
  81.0 15.3 %collective-permute-start.8 = (f32[1,128,512]{2,1,0:T(8,128)S(1)}, f32[1,128,512]{2,1,0:T(8,128)S(1)}, u32[]{:S(2)}, u32[]{:S(2)}) collective-permute-start(f32[1,128,512]{2,1,0:T(8,128)S(1)} %get-tuple-element.71), channel_id=1, source_target_pairs={{0,8},{8,16},{16,24},{24,32},{32,40},{40,48},{48,56},{56,64},{64,7... | collective-permute-start | bytes 786440 | tf_op jit(solution)/shard_map/ppermute | solution.py:115
  82.9 19.2 %collective-permute-start.9 = (f32[1,128,512]{2,1,0:T(8,128)S(1)}, f32[1,128,512]{2,1,0:T(8,128)S(1)}, u32[]{:S(2)}, u32[]{:S(2)}) collective-permute-start(f32[1,128,512]{2,1,0:T(8,128)S(1)} %get-tuple-element.71), channel_id=1, source_target_pairs={{0,16},{8,24},{16,32},{24,40},{32,48},{40,56},{48,64},{56,72},{64,... | collective-permute-start | bytes 786440 | tf_op jit(solution)/shard_map/ppermute | solution.py:115
  102.2 11.4 %collective-permute-start.11 = (f32[1,128,512]{2,1,0:T(8,128)S(1)}, f32[1,128,512]{2,1,0:T(8,128)S(1)}, u32[]{:S(2)}, u32[]{:S(2)}) collective-permute-start(f32[1,128,512]{2,1,0:T(8,128)S(1)} %get-tuple-element.34), channel_id=1, source_target_pairs={{0,32},{8,40},{16,48},{24,56},{32,64},{40,72},{48,80},{56,88},{64,... | collective-permute-start | bytes 786440 | tf_op jit(solution)/shard_map/ppermute | solution.py:115
  113.7 14.9 %collective-permute-start.12 = (f32[1,128,512]{2,1,0:T(8,128)S(1)}, f32[1,128,512]{2,1,0:T(8,128)S(1)}, u32[]{:S(2)}, u32[]{:S(2)}) collective-permute-start(f32[1,128,512]{2,1,0:T(8,128)S(1)} %multiply_add_fusion.11), channel_id=1, source_target_pairs={{0,64},{8,72},{16,80},{24,88},{32,96},{40,104},{48,112},{56,120},{... | collective-permute-start | bytes 786440 | tf_op jit(solution)/shard_map/ppermute | solution.py:115
  116.2 17.0 %copy-start.10 = (f32[1,128]{1,0:T(1,128)S(1)}, f32[1,128]{1,0:T(1,128)}, u32[]{:S(2)}) copy-start(f32[1,128]{1,0:T(1,128)} %param.11) | copy-start | bytes 1540
  128.8 5.6 %collective-permute-start.15 = (f32[1,128,512]{2,1,0:T(8,128)S(1)}, f32[1,128,512]{2,1,0:T(8,128)S(1)}, u32[]{:S(2)}, u32[]{:S(2)}) collective-permute-start(f32[1,128,512]{2,1,0:T(8,128)S(1)} %get-tuple-element.32), channel_id=1, source_target_pairs={{0,384},{8,392},{16,400},{24,408},{32,416},{40,424},{48,432},{56,4... | collective-permute-start | bytes 786440 | tf_op jit(solution)/shard_map/ppermute | solution.py:115
  129.5 10.8 %collective-permute-start.14 = (f32[1,128,512]{2,1,0:T(8,128)S(1)}, f32[1,128,512]{2,1,0:T(8,128)S(1)}, u32[]{:S(2)}, u32[]{:S(2)}) collective-permute-start(f32[1,128,512]{2,1,0:T(8,128)S(1)} %get-tuple-element.32), channel_id=1, source_target_pairs={{0,256},{8,264},{16,272},{24,280},{32,288},{40,296},{48,304},{56,3... | collective-permute-start | bytes 786440 | tf_op jit(solution)/shard_map/ppermute | solution.py:115
  130.8 16.1 %collective-permute-start.13 = (f32[1,128,512]{2,1,0:T(8,128)S(1)}, f32[1,128,512]{2,1,0:T(8,128)}, u32[]{:S(2)}, u32[]{:S(2)}) collective-permute-start(f32[1,128,512]{2,1,0:T(8,128)S(1)} %get-tuple-element.32), channel_id=1, source_target_pairs={{0,128},{8,136},{16,144},{24,152},{32,160},{40,168},{48,176},{56,1... | collective-permute-start | bytes 786440 | tf_op jit(solution)/shard_map/ppermute | solution.py:115
  147.9 0.9 copy-start.7
  149.2 69.0 %copy-start.5 = (f32[1,512,128]{1,2,0:T(8,128)}, f32[1,512,128]{1,2,0:T(8,128)S(1)}, u32[]{:S(2)}) copy-start(f32[1,512,128]{1,2,0:T(8,128)S(1)} %get-tuple-element.74) | copy-start | bytes 786436
  149.2 1.0 copy-start.2
  152.0 1.0 copy-start.3
  153.4 11.7 %collective-permute-start.18 = (f32[1,129,512]{2,1,0:T(8,128)S(1)}, f32[1,129,512]{2,1,0:T(8,128)S(1)}, u32[]{:S(2)}, u32[]{:S(2)}) collective-permute-start(f32[1,129,512]{2,1,0:T(8,128)S(1)} %pad_maximum_fusion.5), channel_id=1, source_target_pairs={{24,0},{32,8},{40,16},{48,24},{56,32},{64,40},{72,48},{80,56},{88,... | collective-permute-start | bytes 792584 | tf_op jit(solution)/shard_map/ppermute | solution.py:99
  155.9 13.6 %collective-permute-start.17 = (f32[1,129,512]{2,1,0:T(8,128)S(1)}, f32[1,129,512]{2,1,0:T(8,128)S(1)}, u32[]{:S(2)}, u32[]{:S(2)}) collective-permute-start(f32[1,129,512]{2,1,0:T(8,128)S(1)} %pad_maximum_fusion.5), channel_id=1, source_target_pairs={{16,0},{24,8},{32,16},{40,24},{48,32},{56,40},{64,48},{72,56},{80,... | collective-permute-start | bytes 792584 | tf_op jit(solution)/shard_map/ppermute | solution.py:99
  163.1 17.4 %collective-permute-start.16 = (f32[1,129,512]{2,1,0:T(8,128)S(1)}, f32[1,129,512]{2,1,0:T(8,128)S(1)}, u32[]{:S(2)}, u32[]{:S(2)}) collective-permute-start(f32[1,129,512]{2,1,0:T(8,128)S(1)} %pad_maximum_fusion.5), channel_id=1, source_target_pairs={{8,0},{16,8},{24,16},{32,24},{40,32},{48,40},{56,48},{64,56},{72,6... | collective-permute-start | bytes 792584 | tf_op jit(solution)/shard_map/ppermute | solution.py:99
  180.7 8.7 %collective-permute-start.19 = (f32[1,129,512]{2,1,0:T(8,128)S(1)}, f32[1,129,512]{2,1,0:T(8,128)S(1)}, u32[]{:S(2)}, u32[]{:S(2)}) collective-permute-start(f32[1,129,512]{2,1,0:T(8,128)S(1)} %pad_maximum_fusion.6), channel_id=1, source_target_pairs={{32,0},{40,8},{48,16},{56,24},{64,32},{72,40},{80,48},{88,56},{96,... | collective-permute-start | bytes 792584 | tf_op jit(solution)/shard_map/ppermute | solution.py:99
  189.6 15.6 %collective-permute-start.20 = (f32[1,129,512]{2,1,0:T(8,128)S(1)}, f32[1,129,512]{2,1,0:T(8,128)S(1)}, u32[]{:S(2)}, u32[]{:S(2)}) collective-permute-start(f32[1,129,512]{2,1,0:T(8,128)S(1)} %pad_maximum_fusion.7), channel_id=1, source_target_pairs={{64,0},{72,8},{80,16},{88,24},{96,32},{104,40},{112,48},{120,56},{... | collective-permute-start | bytes 792584 | tf_op jit(solution)/shard_map/ppermute | solution.py:99
  205.3 5.2 %collective-permute-start.22 = (f32[1,129,512]{2,1,0:T(8,128)S(1)}, f32[1,129,512]{2,1,0:T(8,128)S(1)}, u32[]{:S(2)}, u32[]{:S(2)}) collective-permute-start(f32[1,129,512]{2,1,0:T(8,128)S(1)} %pad_maximum_fusion.8), channel_id=1, source_target_pairs={{256,0},{264,8},{272,16},{280,24},{288,32},{296,40},{304,48},{312,... | collective-permute-start | bytes 792584 | tf_op jit(solution)/shard_map/ppermute | solution.py:99
  206.6 10.5 %collective-permute-start.21 = (f32[1,129,512]{2,1,0:T(8,128)S(1)}, f32[1,129,512]{2,1,0:T(8,128)S(1)}, u32[]{:S(2)}, u32[]{:S(2)}) collective-permute-start(f32[1,129,512]{2,1,0:T(8,128)S(1)} %pad_maximum_fusion.8), channel_id=1, source_target_pairs={{128,0},{136,8},{144,16},{152,24},{160,32},{168,40},{176,48},{184,... | collective-permute-start | bytes 792584 | tf_op jit(solution)/shard_map/ppermute | solution.py:99
  208.6 8.6 %collective-permute-start.23 = (f32[1,129,512]{2,1,0:T(8,128)S(1)}, f32[1,129,512]{2,1,0:T(8,128)S(1)}, u32[]{:S(2)}, u32[]{:S(2)}) collective-permute-start(f32[1,129,512]{2,1,0:T(8,128)S(1)} %pad_maximum_fusion.8), channel_id=1, source_target_pairs={{384,0},{392,8},{400,16},{408,24},{416,32},{424,40},{432,48},{440,... | collective-permute-start | bytes 792584 | tf_op jit(solution)/shard_map/ppermute | solution.py:99
  220.0 15.7 %collective-permute-start.26 = (f32[1,128,512]{2,1,0:T(8,128)S(1)}, f32[1,128,512]{2,1,0:T(8,128)S(1)}, u32[]{:S(2)}, u32[]{:S(2)}) collective-permute-start(f32[1,128,512]{2,1,0:T(8,128)S(1)} %get-tuple-element.83), channel_id=1, source_target_pairs={{24,0},{32,8},{40,16},{48,24},{56,32},{64,40},{72,48},{80,56},{88,... | collective-permute-start | bytes 786440 | tf_op jit(solution)/shard_map/ppermute | solution.py:115
  222.5 16.0 %collective-permute-start.24 = (f32[1,128,512]{2,1,0:T(8,128)S(1)}, f32[1,128,512]{2,1,0:T(8,128)S(1)}, u32[]{:S(2)}, u32[]{:S(2)}) collective-permute-start(f32[1,128,512]{2,1,0:T(8,128)S(1)} %get-tuple-element.83), channel_id=1, source_target_pairs={{8,0},{16,8},{24,16},{32,24},{40,32},{48,40},{56,48},{64,56},{72,6... | collective-permute-start | bytes 786440 | tf_op jit(solution)/shard_map/ppermute | solution.py:115
  233.6 11.1 %collective-permute-start.25 = (f32[1,128,512]{2,1,0:T(8,128)S(1)}, f32[1,128,512]{2,1,0:T(8,128)S(1)}, u32[]{:S(2)}, u32[]{:S(2)}) collective-permute-start(f32[1,128,512]{2,1,0:T(8,128)S(1)} %get-tuple-element.83), channel_id=1, source_target_pairs={{16,0},{24,8},{32,16},{40,24},{48,32},{56,40},{64,48},{72,56},{80,... | collective-permute-start | bytes 786440 | tf_op jit(solution)/shard_map/ppermute | solution.py:115
  244.8 12.2 %collective-permute-start.27 = (f32[1,128,512]{2,1,0:T(8,128)S(1)}, f32[1,128,512]{2,1,0:T(8,128)S(1)}, u32[]{:S(2)}, u32[]{:S(2)}) collective-permute-start(f32[1,128,512]{2,1,0:T(8,128)S(1)} %get-tuple-element.12), channel_id=1, source_target_pairs={{32,0},{40,8},{48,16},{56,24},{64,32},{72,40},{80,48},{88,56},{96,... | collective-permute-start | bytes 786440 | tf_op jit(solution)/shard_map/ppermute | solution.py:115
  257.2 9.0 %collective-permute-start.28 = (f32[1,128,512]{2,1,0:T(8,128)S(1)}, f32[1,128,512]{2,1,0:T(8,128)S(1)}, u32[]{:S(2)}, u32[]{:S(2)}) collective-permute-start(f32[1,128,512]{2,1,0:T(8,128)S(1)} %multiply_add_fusion.2), channel_id=1, source_target_pairs={{64,0},{72,8},{80,16},{88,24},{96,32},{104,40},{112,48},{120,56},{... | collective-permute-start | bytes 786440 | tf_op jit(solution)/shard_map/ppermute | solution.py:115
  267.1 13.7 %collective-permute-start.31 = (f32[1,128,512]{2,1,0:T(8,128)}, f32[1,128,512]{2,1,0:T(8,128)S(1)}, u32[]{:S(2)}, u32[]{:S(2)}) collective-permute-start(f32[1,128,512]{2,1,0:T(8,128)} %get-tuple-element.10), channel_id=1, source_target_pairs={{384,0},{392,8},{400,16},{408,24},{416,32},{424,40},{432,48},{440,... | collective-permute-start | bytes 786440 | tf_op jit(solution)/shard_map/ppermute | solution.py:115
  267.8 13.1 %collective-permute-start.30 = (f32[1,128,512]{2,1,0:T(8,128)}, f32[1,128,512]{2,1,0:T(8,128)}, u32[]{:S(2)}, u32[]{:S(2)}) collective-permute-start(f32[1,128,512]{2,1,0:T(8,128)} %get-tuple-element.10), channel_id=1, source_target_pairs={{256,0},{264,8},{272,16},{280,24},{288,32},{296,40},{304,48},{312,... | collective-permute-start | bytes 786440 | tf_op jit(solution)/shard_map/ppermute | solution.py:115
  271.9 21.1 %collective-permute-start.29 = (f32[1,128,512]{2,1,0:T(8,128)}, f32[1,128,512]{2,1,0:T(8,128)}, u32[]{:S(2)}, u32[]{:S(2)}) collective-permute-start(f32[1,128,512]{2,1,0:T(8,128)} %get-tuple-element.10), channel_id=1, source_target_pairs={{128,0},{136,8},{144,16},{152,24},{160,32},{168,40},{176,48},{184,... | collective-permute-start | bytes 786440 | tf_op jit(solution)/shard_map/ppermute | solution.py:115
  295.7 1.0 copy-start.6
  295.8 1.0 copy-start.8
  298.6 5.2 %collective-permute-start.32 = (f32[1184,128]{1,0:T(8,128)S(1)}, f32[1184,128]{1,0:T(8,128)}, u32[]{:S(2)}, u32[]{:S(2)}) collective-permute-start(f32[1184,128]{1,0:T(8,128)S(1)} %constant_dynamic-slice_fusion.3), channel_id=1, source_target_pairs={{0,1},{1,0},{2,3},{3,2},{4,5},{5,4},{6,7},{7,6},{8,9},{9,8},{10,11... | collective-permute-start | bytes 1818632 | tf_op jit(solution)/shard_map/ppermute | solution.py:139
  305.0 15.0 %collective-permute-start.33 = (f32[296,128]{1,0:T(8,128)S(1)}, f32[296,128]{1,0:T(8,128)S(1)}, u32[]{:S(2)}, u32[]{:S(2)}) collective-permute-start(f32[296,128]{1,0:T(8,128)S(1)} %get-tuple-element.57), channel_id=1, source_target_pairs={{0,2},{1,7},{2,4},{3,1},{4,6},{5,3},{6,0},{7,5},{8,10},{9,15},{10,... | collective-permute-start | bytes 454664 | tf_op jit(solution)/shard_map/ppermute | solution.py:150
  320.1 11.6 %collective-permute-start.34 = (f32[296,128]{1,0:T(8,128)S(1)}, f32[296,128]{1,0:T(8,128)S(1)}, u32[]{:S(2)}, u32[]{:S(2)}) collective-permute-start(f32[296,128]{1,0:T(8,128)S(1)} %get-tuple-element.55), channel_id=1, source_target_pairs={{0,2},{1,7},{2,4},{3,1},{4,6},{5,3},{6,0},{7,5},{8,10},{9,15},{10,... | collective-permute-start | bytes 454664 | tf_op jit(solution)/shard_map/ppermute | solution.py:150
  331.7 9.9 %collective-permute-start.35 = (f32[296,128]{1,0:T(8,128)S(1)}, f32[296,128]{1,0:T(8,128)S(1)}, u32[]{:S(2)}, u32[]{:S(2)}) collective-permute-start(f32[296,128]{1,0:T(8,128)S(1)} %get-tuple-element.53), channel_id=1, source_target_pairs={{0,2},{1,7},{2,4},{3,1},{4,6},{5,3},{6,0},{7,5},{8,10},{9,15},{10,... | collective-permute-start | bytes 454664 | tf_op jit(solution)/shard_map/ppermute | solution.py:150
  341.7 9.8 %collective-permute-start.36 = (f32[296,128]{1,0:T(8,128)S(1)}, f32[296,128]{1,0:T(8,128)S(1)}, u32[]{:S(2)}, u32[]{:S(2)}) collective-permute-start(f32[296,128]{1,0:T(8,128)S(1)} %dynamic-slice_bitcast_fusion.2), channel_id=1, source_target_pairs={{0,2},{1,7},{2,4},{3,1},{4,6},{5,3},{6,0},{7,5},{8,10},{9,15},{10,... | collective-permute-start | bytes 454664 | tf_op jit(solution)/shard_map/ppermute | solution.py:156
  344.1 49.0 %copy-start.4 = (bf16[128,9,128]{0,2,1:T(8,128)(2,1)S(1)}, bf16[128,9,128]{0,2,1:T(8,128)(2,1)}, u32[]{:S(2)}) copy-start(bf16[128,9,128]{0,2,1:T(8,128)(2,1)} %copy.26) | copy-start | bytes 884740
  351.6 9.8 %collective-permute-start.37 = (f32[296,128]{1,0:T(8,128)S(1)}, f32[296,128]{1,0:T(8,128)S(1)}, u32[]{:S(2)}, u32[]{:S(2)}) collective-permute-start(f32[296,128]{1,0:T(8,128)S(1)} %dynamic-slice_bitcast_fusion.1), channel_id=1, source_target_pairs={{0,2},{1,7},{2,4},{3,1},{4,6},{5,3},{6,0},{7,5},{8,10},{9,15},{10,... | collective-permute-start | bytes 454664 | tf_op jit(solution)/shard_map/ppermute | solution.py:156
  361.4 10.6 %collective-permute-start.38 = (f32[296,128]{1,0:T(8,128)S(1)}, f32[296,128]{1,0:T(8,128)S(1)}, u32[]{:S(2)}, u32[]{:S(2)}) collective-permute-start(f32[296,128]{1,0:T(8,128)S(1)} %dynamic-slice_bitcast_fusion), channel_id=1, source_target_pairs={{0,2},{1,7},{2,4},{3,1},{4,6},{5,3},{6,0},{7,5},{8,10},{9,15},{10,... | collective-permute-start | bytes 454664 | tf_op jit(solution)/shard_map/ppermute | solution.py:156
  372.0 22.6 %collective-permute-start.39 = (f32[1184,128]{1,0:T(8,128)S(1)}, f32[1184,128]{1,0:T(8,128)S(1)}, u32[]{:S(2)}, u32[]{:S(2)}) collective-permute-start(f32[1184,128]{1,0:T(8,128)S(1)} %bitcast.507), channel_id=1, source_target_pairs={{0,1},{1,0},{2,3},{3,2},{4,5},{5,4},{6,7},{7,6},{8,9},{9,8},{10,11... | collective-permute-start | bytes 1818632 | tf_op jit(solution)/shard_map/ppermute | solution.py:159

commit v6 on v5

--- a/solution.py
+++ b/solution.py
@@ -138,23 +138,17 @@
     give = lax.dynamic_slice_in_dim(current, (1 - core) * half_rows, half_rows, 0)
     half = keep + lax.ppermute(give, axis, partner)
 
-    def following(k):
-        step = 1 if k % 2 == 0 else -1
-        return ((k // 2 + step) % chips) * 2 + k % 2
-
-    ring = [(k, following(k)) for k in range(count)]
-    place = jnp.where(core == 0, chip, (chips - chip) % chips)
     pieces = half.reshape(chips, half_rows // chips, lanes)
-    for t in range(chips - 1):
-        sent = lax.dynamic_index_in_dim(pieces, (place - t) % chips, 0, False)
-        got = lax.ppermute(sent, axis, ring)
-        slot = (place - t - 1 + chips) % chips
-        mine = lax.dynamic_index_in_dim(pieces, slot, 0, False)
-        pieces = lax.dynamic_update_index_in_dim(pieces, mine + got, slot, 0)
-    for t in range(chips - 1):
-        sent = lax.dynamic_index_in_dim(pieces, (place + 1 - t + chips) % chips, 0, False)
-        got = lax.ppermute(sent, axis, ring)
-        pieces = lax.dynamic_update_index_in_dim(pieces, got, (place - t + chips) % chips, 0)
+    mine = lax.dynamic_index_in_dim(pieces, chip, 0, False)
+    for shift in range(1, chips):
+        target = [(k, ((k // 2 + shift) % chips) * 2 + k % 2) for k in range(count)]
+        sent = lax.dynamic_index_in_dim(pieces, (chip + shift) % chips, 0, False)
+        mine = mine + lax.ppermute(sent, axis, target)
+    pieces = lax.dynamic_update_index_in_dim(pieces, mine, chip, 0)
+    for shift in range(1, chips):
+        target = [(k, ((k // 2 + shift) % chips) * 2 + k % 2) for k in range(count)]
+        got = lax.ppermute(mine, axis, target)
+        pieces = lax.dynamic_update_index_in_dim(pieces, got, (chip - shift + chips) % chips, 0)
     half = pieces.reshape(half_rows, lanes)
     other = lax.ppermute(half, axis, partner)
     whole = jnp.zeros_like(current)

time: 398 us -> 396 us (level)
  the two profiles are of different devices: /device:TPU:23 before, /device:TPU:1 now
where the time goes in v6:
time: 396 us; the launch traced here: 391 us
  waiting for transfers between devices  196 us (49%)
  starting transfers between devices  161 us (41%)
  other arithmetic  18.2 us (5%)
  local copies, waits for them, and re-layouts  6.86 us (2%)
  matrix products  6.27 us (2%)
    ppermute x16, waiting for transfers between devices, exclusive_scan_first(): lax.ppermute(packed, axis, scan_pairs(count, j * d, reverse))  82.9 us
    ppermute x16, waiting for transfers between devices, exclusive_scan_again(): lax.ppermute(sending, axis, scan_pairs(count, j * d, reverse))  73 us
    ppermute x16, starting transfers between devices, exclusive_scan_first(): lax.ppermute(packed, axis, scan_pairs(count, j * d, reverse))  57.1 us
    ppermute x16, starting transfers between devices, exclusive_scan_again(): lax.ppermute(sending, axis, scan_pairs(count, j * d, reverse))  55 us
    ppermute x3, starting transfers between devices, batch_sum(): mine = mine + lax.ppermute(sent, axis, target)  23.7 us
    ppermute x3, waiting for transfers between devices, batch_sum(): got = lax.ppermute(mine, axis, target)  23.1 us
    ppermute x3, starting transfers between devices, batch_sum(): got = lax.ppermute(mine, axis, target)  19.7 us
    ppermute x3, waiting for transfers between devices, batch_sum(): mine = mine + lax.ppermute(sent, axis, target)  15.4 us
  transfers between devices with their start and end apart: 40, of which 34 were waited for; matrix products, arithmetic and copies ran while one was open for 1% of the time, Pallas kernels for 0%

profile of v6, /device:TPU:1, one launch (start us, length us, event | category | flops | bytes accessed | tf_op | source)
XLA Modules:
  0.0 390.8 jit_solution(1133422791859502593)
XLA Ops:
  6.0 5.2 %collective-permute-start.2 = (f32[1,129,512]{2,1,0:T(8,128)S(1)}, f32[1,129,512]{2,1,0:T(8,128)S(1)}, u32[]{:S(2)}, u32[]{:S(2)}) collective-permute-start(f32[1,129,512]{2,1,0:T(8,128)S(1)} %pad_maximum_fusion.1), channel_id=1, source_target_pairs={{0,24},{8,32},{16,40},{24,48},{32,56},{40,64},{48,72},{56,80},{64,... | collective-permute-start | bytes 792584 | tf_op jit(solution)/shard_map/ppermute | solution.py:99
  11.2 3.8 collective-permute-start.1
  15.0 2.5 collective-permute-start
  17.5 2.5 collective-permute-done.1
  20.0 6.0 %collective-permute-done = f32[1,129,512]{2,1,0:T(8,128)S(1)} collective-permute-done((f32[1,129,512]{2,1,0:T(8,128)S(1)}, f32[1,129,512]{2,1,0:T(8,128)S(1)}, u32[]{:S(2)}, u32[]{:S(2)}) %collective-permute-start) | collective-permute-done | bytes 264224 | tf_op jit(solution)/shard_map/ppermute | solution.py:99
  26.2 8.2 %collective-permute-start.3 = (f32[1,129,512]{2,1,0:T(8,128)S(1)}, f32[1,129,512]{2,1,0:T(8,128)S(1)}, u32[]{:S(2)}, u32[]{:S(2)}) collective-permute-start(f32[1,129,512]{2,1,0:T(8,128)S(1)} %pad_maximum_fusion.2), channel_id=1, source_target_pairs={{0,32},{8,40},{16,48},{24,56},{32,64},{40,72},{48,80},{56,88},{64,... | collective-permute-start | bytes 792584 | tf_op jit(solution)/shard_map/ppermute | solution.py:99
  34.4 4.3 %collective-permute-done.3 = f32[1,129,512]{2,1,0:T(8,128)S(1)} collective-permute-done((f32[1,129,512]{2,1,0:T(8,128)S(1)}, f32[1,129,512]{2,1,0:T(8,128)S(1)}, u32[]{:S(2)}, u32[]{:S(2)}) %collective-permute-start.3) | collective-permute-done | bytes 264224 | tf_op jit(solution)/shard_map/ppermute | solution.py:99
  38.9 5.4 %collective-permute-start.4 = (f32[1,129,512]{2,1,0:T(8,128)S(1)}, f32[1,129,512]{2,1,0:T(8,128)S(1)}, u32[]{:S(2)}, u32[]{:S(2)}) collective-permute-start(f32[1,129,512]{2,1,0:T(8,128)S(1)} %pad_maximum_fusion.3), channel_id=1, source_target_pairs={{0,64},{8,72},{16,80},{24,88},{32,96},{40,104},{48,112},{56,120},{... | collective-permute-start | bytes 792584 | tf_op jit(solution)/shard_map/ppermute | solution.py:99
  44.3 3.5 collective-permute-done.4
  48.0 17.2 %collective-permute-start.6 = (f32[1,129,512]{2,1,0:T(8,128)S(1)}, f32[1,129,512]{2,1,0:T(8,128)S(1)}, u32[]{:S(2)}, u32[]{:S(2)}) collective-permute-start(f32[1,129,512]{2,1,0:T(8,128)S(1)} %pad_maximum_fusion.4), channel_id=1, source_target_pairs={{0,256},{8,264},{16,272},{24,280},{32,288},{40,296},{48,304},{56,3... | collective-permute-start | bytes 792584 | tf_op jit(solution)/shard_map/ppermute | solution.py:99
  65.3 2.8 collective-permute-start.5
  68.1 1.3 collective-permute-start.7
  69.4 1.4 collective-permute-done.6
  70.8 6.0 %collective-permute-done.5 = f32[1,129,512]{2,1,0:T(8,128)S(1)} collective-permute-done((f32[1,129,512]{2,1,0:T(8,128)S(1)}, f32[1,129,512]{2,1,0:T(8,128)S(1)}, u32[]{:S(2)}, u32[]{:S(2)}) %collective-permute-start.5) | collective-permute-done | bytes 264224 | tf_op jit(solution)/shard_map/ppermute | solution.py:99
  76.8 1.4 collective-permute-done.7
  81.0 1.8 collective-permute-start.10
  82.7 1.3 collective-permute-start.8
  84.0 3.7 collective-permute-start.9
  88.3 5.6 %collective-permute-done.9 = f32[1,128,512]{2,1,0:T(8,128)S(1)} collective-permute-done((f32[1,128,512]{2,1,0:T(8,128)S(1)}, f32[1,128,512]{2,1,0:T(8,128)S(1)}, u32[]{:S(2)}, u32[]{:S(2)}) %collective-permute-start.9) | collective-permute-done | bytes 262176 | tf_op jit(solution)/shard_map/ppermute | solution.py:115
  94.0 5.8 %collective-permute-start.11 = (f32[1,128,512]{2,1,0:T(8,128)S(1)}, f32[1,128,512]{2,1,0:T(8,128)S(1)}, u32[]{:S(2)}, u32[]{:S(2)}) collective-permute-start(f32[1,128,512]{2,1,0:T(8,128)S(1)} %get-tuple-element.34), channel_id=1, source_target_pairs={{0,32},{8,40},{16,48},{24,56},{32,64},{40,72},{48,80},{56,88},{64,... | collective-permute-start | bytes 786440 | tf_op jit(solution)/shard_map/ppermute | solution.py:115
  99.8 3.3 collective-permute-done.11
  103.2 4.5 %collective-permute-start.12 = (f32[1,128,512]{2,1,0:T(8,128)S(1)}, f32[1,128,512]{2,1,0:T(8,128)S(1)}, u32[]{:S(2)}, u32[]{:S(2)}) collective-permute-start(f32[1,128,512]{2,1,0:T(8,128)S(1)} %multiply_add_fusion.11), channel_id=1, source_target_pairs={{0,64},{8,72},{16,80},{24,88},{32,96},{40,104},{48,112},{56,120},{... | collective-permute-start | bytes 786440 | tf_op jit(solution)/shard_map/ppermute | solution.py:115
  108.2 2.8 collective-permute-done.12
  111.1 23.1 %collective-permute-start.15 = (f32[1,128,512]{2,1,0:T(8,128)S(1)}, f32[1,128,512]{2,1,0:T(8,128)S(1)}, u32[]{:S(2)}, u32[]{:S(2)}) collective-permute-start(f32[1,128,512]{2,1,0:T(8,128)S(1)} %get-tuple-element.32), channel_id=1, source_target_pairs={{0,384},{8,392},{16,400},{24,408},{32,416},{40,424},{48,432},{56,4... | collective-permute-start | bytes 786440 | tf_op jit(solution)/shard_map/ppermute | solution.py:115
  134.3 1.3 collective-permute-start.14
  135.6 3.2 collective-permute-start.13
  139.9 4.3 %collective-permute-done.15 = f32[1,128,512]{2,1,0:T(8,128)S(1)} collective-permute-done((f32[1,128,512]{2,1,0:T(8,128)S(1)}, f32[1,128,512]{2,1,0:T(8,128)S(1)}, u32[]{:S(2)}, u32[]{:S(2)}) %collective-permute-start.15) | collective-permute-done | bytes 262176 | tf_op jit(solution)/shard_map/ppermute | solution.py:115
  144.3 1.3 collective-permute-done.13
  152.2 1.3 collective-permute-start.18
  153.5 1.3 collective-permute-start.17
  154.8 1.3 collective-permute-start.16
  156.1 7.0 %collective-permute-done.18 = f32[1,129,512]{2,1,0:T(8,128)S(1)} collective-permute-done((f32[1,129,512]{2,1,0:T(8,128)S(1)}, f32[1,129,512]{2,1,0:T(8,128)S(1)}, u32[]{:S(2)}, u32[]{:S(2)}) %collective-permute-start.18) | collective-permute-done | bytes 264224 | tf_op jit(solution)/shard_map/ppermute | solution.py:99
  163.0 7.7 %collective-permute-done.17 = f32[1,129,512]{2,1,0:T(8,128)S(1)} collective-permute-done((f32[1,129,512]{2,1,0:T(8,128)S(1)}, f32[1,129,512]{2,1,0:T(8,128)S(1)}, u32[]{:S(2)}, u32[]{:S(2)}) %collective-permute-start.17) | collective-permute-done | bytes 264224 | tf_op jit(solution)/shard_map/ppermute | solution.py:99
  170.8 3.6 collective-permute-done.16
  175.9 9.1 %collective-permute-done.19 = f32[1,129,512]{2,1,0:T(8,128)S(1)} collective-permute-done((f32[1,129,512]{2,1,0:T(8,128)S(1)}, f32[1,129,512]{2,1,0:T(8,128)S(1)}, u32[]{:S(2)}, u32[]{:S(2)}) %collective-permute-start.19) | collective-permute-done | bytes 264224 | tf_op jit(solution)/shard_map/ppermute | solution.py:99
  185.1 1.3 collective-permute-start.20
  186.4 15.1 %collective-permute-done.20 = f32[1,129,512]{2,1,0:T(8,128)S(1)} collective-permute-done((f32[1,129,512]{2,1,0:T(8,128)S(1)}, f32[1,129,512]{2,1,0:T(8,128)S(1)}, u32[]{:S(2)}, u32[]{:S(2)}) %collective-permute-start.20) | collective-permute-done | bytes 264224 | tf_op jit(solution)/shard_map/ppermute | solution.py:99
  201.6 1.3 collective-permute-start.22
  202.9 1.3 collective-permute-start.21
  204.2 1.5 collective-permute-start.23
  205.7 7.2 %collective-permute-done.22 = f32[1,129,512]{2,1,0:T(8,128)S(1)} collective-permute-done((f32[1,129,512]{2,1,0:T(8,128)S(1)}, f32[1,129,512]{2,1,0:T(8,128)S(1)}, u32[]{:S(2)}, u32[]{:S(2)}) %collective-permute-start.22) | collective-permute-done | bytes 264224 | tf_op jit(solution)/shard_map/ppermute | solution.py:99
  212.9 8.2 %collective-permute-done.23 = f32[1,129,512]{2,1,0:T(8,128)S(1)} collective-permute-done((f32[1,129,512]{2,1,0:T(8,128)S(1)}, f32[1,129,512]{2,1,0:T(8,128)S(1)}, u32[]{:S(2)}, u32[]{:S(2)}) %collective-permute-start.23) | collective-permute-done | bytes 264224 | tf_op jit(solution)/shard_map/ppermute | solution.py:99
  227.9 8.7 %collective-permute-done.26 = f32[1,128,512]{2,1,0:T(8,128)S(1)} collective-permute-done((f32[1,128,512]{2,1,0:T(8,128)S(1)}, f32[1,128,512]{2,1,0:T(8,128)S(1)}, u32[]{:S(2)}, u32[]{:S(2)}) %collective-permute-start.26) | collective-permute-done | bytes 262176 | tf_op jit(solution)/shard_map/ppermute | solution.py:115
  236.6 8.3 %collective-permute-done.25 = f32[1,128,512]{2,1,0:T(8,128)S(1)} collective-permute-done((f32[1,128,512]{2,1,0:T(8,128)S(1)}, f32[1,128,512]{2,1,0:T(8,128)S(1)}, u32[]{:S(2)}, u32[]{:S(2)}) %collective-permute-start.25) | collective-permute-done | bytes 262176 | tf_op jit(solution)/shard_map/ppermute | solution.py:115
  246.4 11.6 %collective-permute-done.27 = f32[1,128,512]{2,1,0:T(8,128)S(1)} collective-permute-done((f32[1,128,512]{2,1,0:T(8,128)S(1)}, f32[1,128,512]{2,1,0:T(8,128)S(1)}, u32[]{:S(2)}, u32[]{:S(2)}) %collective-permute-start.27) | collective-permute-done | bytes 262176 | tf_op jit(solution)/shard_map/ppermute | solution.py:115
  259.4 7.3 %collective-permute-done.28 = f32[1,128,512]{2,1,0:T(8,128)S(1)} collective-permute-done((f32[1,128,512]{2,1,0:T(8,128)S(1)}, f32[1,128,512]{2,1,0:T(8,128)S(1)}, u32[]{:S(2)}, u32[]{:S(2)}) %collective-permute-start.28) | collective-permute-done | bytes 262176 | tf_op jit(solution)/shard_map/ppermute | solution.py:115
  268.8 1.3 collective-permute-start.30
  270.1 1.3 collective-permute-start.29
  271.5 9.1 %collective-permute-done.31 = f32[1,128,512]{2,1,0:T(8,128)} collective-permute-done((f32[1,128,512]{2,1,0:T(8,128)}, f32[1,128,512]{2,1,0:T(8,128)}, u32[]{:S(2)}, u32[]{:S(2)}) %collective-permute-start.31) | collective-permute-done | bytes 262176 | tf_op jit(solution)/shard_map/ppermute | solution.py:115
  280.7 7.9 %collective-permute-done.30 = f32[1,128,512]{2,1,0:T(8,128)} collective-permute-done((f32[1,128,512]{2,1,0:T(8,128)}, f32[1,128,512]{2,1,0:T(8,128)}, u32[]{:S(2)}, u32[]{:S(2)}) %collective-permute-start.30) | collective-permute-done | bytes 262176 | tf_op jit(solution)/shard_map/ppermute | solution.py:115
  288.6 2.1 collective-permute-done.29
  290.7 1.3 fusion.295
  297.7 3.1 collective-permute-start.32
  301.1 1.4 collective-permute-done.32
  302.5 11.1 %collective-permute-start.35 = (f32[296,128]{1,0:T(8,128)S(1)}, f32[296,128]{1,0:T(8,128)S(1)}, u32[]{:S(2)}, u32[]{:S(2)}) collective-permute-start(f32[296,128]{1,0:T(8,128)S(1)} %get-tuple-element.53), channel_id=1, source_target_pairs={{0,6},{1,7},{2,0},{3,1},{4,2},{5,3},{6,4},{7,5},{8,14},{9,15},{10,... | collective-permute-start | bytes 454664 | tf_op jit(solution)/shard_map/ppermute | solution.py:146
  313.6 5.3 %collective-permute-start.34 = (f32[296,128]{1,0:T(8,128)S(1)}, f32[296,128]{1,0:T(8,128)S(1)}, u32[]{:S(2)}, u32[]{:S(2)}) collective-permute-start(f32[296,128]{1,0:T(8,128)S(1)} %get-tuple-element.54), channel_id=1, source_target_pairs={{0,4},{1,5},{2,6},{3,7},{4,0},{5,1},{6,2},{7,3},{8,12},{9,13},{10,... | collective-permute-start | bytes 454664 | tf_op jit(solution)/shard_map/ppermute | solution.py:146
  319.0 7.3 %collective-permute-start.33 = (f32[296,128]{1,0:T(8,128)S(1)}, f32[296,128]{1,0:T(8,128)S(1)}, u32[]{:S(2)}, u32[]{:S(2)}) collective-permute-start(f32[296,128]{1,0:T(8,128)S(1)} %get-tuple-element.52), channel_id=1, source_target_pairs={{0,2},{1,3},{2,4},{3,5},{4,6},{5,7},{6,0},{7,1},{8,10},{9,11},{10,... | collective-permute-start | bytes 454664 | tf_op jit(solution)/shard_map/ppermute | solution.py:146
  326.4 15.4 %collective-permute-done.34 = f32[296,128]{1,0:T(8,128)S(1)} collective-permute-done((f32[296,128]{1,0:T(8,128)S(1)}, f32[296,128]{1,0:T(8,128)S(1)}, u32[]{:S(2)}, u32[]{:S(2)}) %collective-permute-start.34) | collective-permute-done | bytes 151584 | tf_op jit(solution)/shard_map/ppermute | solution.py:146
  341.9 5.7 %collective-permute-start.36 = (f32[296,128]{1,0:T(8,128)S(1)}, f32[296,128]{1,0:T(8,128)S(1)}, u32[]{:S(2)}, u32[]{:S(2)}) collective-permute-start(f32[296,128]{1,0:T(8,128)S(1)} %fusion.195), channel_id=1, source_target_pairs={{0,2},{1,3},{2,4},{3,5},{4,6},{5,7},{6,0},{7,1},{8,10},{9,11},{10,... | collective-permute-start | bytes 454664 | tf_op jit(solution)/shard_map/ppermute | solution.py:150
  347.5 10.5 %collective-permute-start.37 = (f32[296,128]{1,0:T(8,128)S(1)}, f32[296,128]{1,0:T(8,128)S(1)}, u32[]{:S(2)}, u32[]{:S(2)}) collective-permute-start(f32[296,128]{1,0:T(8,128)S(1)} %fusion.195), channel_id=1, source_target_pairs={{0,4},{1,5},{2,6},{3,7},{4,0},{5,1},{6,2},{7,3},{8,12},{9,13},{10,... | collective-permute-start | bytes 454664 | tf_op jit(solution)/shard_map/ppermute | solution.py:150
  358.1 3.5 collective-permute-start.38
  362.5 9.0 %collective-permute-done.37 = f32[296,128]{1,0:T(8,128)S(1)} collective-permute-done((f32[296,128]{1,0:T(8,128)S(1)}, f32[296,128]{1,0:T(8,128)S(1)}, u32[]{:S(2)}, u32[]{:S(2)}) %collective-permute-start.37) | collective-permute-done | bytes 151584 | tf_op jit(solution)/shard_map/ppermute | solution.py:150
  371.6 13.1 %collective-permute-done.38 = f32[296,128]{1,0:T(8,128)S(1)} collective-permute-done((f32[296,128]{1,0:T(8,128)S(1)}, f32[296,128]{1,0:T(8,128)S(1)}, u32[]{:S(2)}, u32[]{:S(2)}) %collective-permute-start.38) | collective-permute-done | bytes 151584 | tf_op jit(solution)/shard_map/ppermute | solution.py:150
  384.7 2.4 collective-permute-start.39
  (245 shorter events, 40.8 us)
Async XLA Ops:
  0.6 2.9 copy-start.1
  3.2 1.1 copy-start
  4.6 0.9 copy-start.11
  6.0 11.6 %collective-permute-start.2 = (f32[1,129,512]{2,1,0:T(8,128)S(1)}, f32[1,129,512]{2,1,0:T(8,128)S(1)}, u32[]{:S(2)}, u32[]{:S(2)}) collective-permute-start(f32[1,129,512]{2,1,0:T(8,128)S(1)} %pad_maximum_fusion.1), channel_id=1, source_target_pairs={{0,24},{8,32},{16,40},{24,48},{32,56},{40,64},{48,72},{56,80},{64,... | collective-permute-start | bytes 792584 | tf_op jit(solution)/shard_map/ppermute | solution.py:99
  11.2 8.8 %collective-permute-start.1 = (f32[1,129,512]{2,1,0:T(8,128)S(1)}, f32[1,129,512]{2,1,0:T(8,128)S(1)}, u32[]{:S(2)}, u32[]{:S(2)}) collective-permute-start(f32[1,129,512]{2,1,0:T(8,128)S(1)} %pad_maximum_fusion.1), channel_id=1, source_target_pairs={{0,16},{8,24},{16,32},{24,40},{32,48},{40,56},{48,64},{56,72},{64,... | collective-permute-start | bytes 792584 | tf_op jit(solution)/shard_map/ppermute | solution.py:99
  15.0 11.0 %collective-permute-start = (f32[1,129,512]{2,1,0:T(8,128)S(1)}, f32[1,129,512]{2,1,0:T(8,128)S(1)}, u32[]{:S(2)}, u32[]{:S(2)}) collective-permute-start(f32[1,129,512]{2,1,0:T(8,128)S(1)} %pad_maximum_fusion.1), channel_id=1, source_target_pairs={{0,8},{8,16},{16,24},{24,32},{32,40},{40,48},{48,56},{56,64},{64,7... | collective-permute-start | bytes 792584 | tf_op jit(solution)/shard_map/ppermute | solution.py:99
  26.2 12.5 %collective-permute-start.3 = (f32[1,129,512]{2,1,0:T(8,128)S(1)}, f32[1,129,512]{2,1,0:T(8,128)S(1)}, u32[]{:S(2)}, u32[]{:S(2)}) collective-permute-start(f32[1,129,512]{2,1,0:T(8,128)S(1)} %pad_maximum_fusion.2), channel_id=1, source_target_pairs={{0,32},{8,40},{16,48},{24,56},{32,64},{40,72},{48,80},{56,88},{64,... | collective-permute-start | bytes 792584 | tf_op jit(solution)/shard_map/ppermute | solution.py:99
  38.9 8.9 %collective-permute-start.4 = (f32[1,129,512]{2,1,0:T(8,128)S(1)}, f32[1,129,512]{2,1,0:T(8,128)S(1)}, u32[]{:S(2)}, u32[]{:S(2)}) collective-permute-start(f32[1,129,512]{2,1,0:T(8,128)S(1)} %pad_maximum_fusion.3), channel_id=1, source_target_pairs={{0,64},{8,72},{16,80},{24,88},{32,96},{40,104},{48,112},{56,120},{... | collective-permute-start | bytes 792584 | tf_op jit(solution)/shard_map/ppermute | solution.py:99
  48.0 22.8 %collective-permute-start.6 = (f32[1,129,512]{2,1,0:T(8,128)S(1)}, f32[1,129,512]{2,1,0:T(8,128)S(1)}, u32[]{:S(2)}, u32[]{:S(2)}) collective-permute-start(f32[1,129,512]{2,1,0:T(8,128)S(1)} %pad_maximum_fusion.4), channel_id=1, source_target_pairs={{0,256},{8,264},{16,272},{24,280},{32,288},{40,296},{48,304},{56,3... | collective-permute-start | bytes 792584 | tf_op jit(solution)/shard_map/ppermute | solution.py:99
  65.3 11.5 %collective-permute-start.5 = (f32[1,129,512]{2,1,0:T(8,128)S(1)}, f32[1,129,512]{2,1,0:T(8,128)S(1)}, u32[]{:S(2)}, u32[]{:S(2)}) collective-permute-start(f32[1,129,512]{2,1,0:T(8,128)S(1)} %pad_maximum_fusion.4), channel_id=1, source_target_pairs={{0,128},{8,136},{16,144},{24,152},{32,160},{40,168},{48,176},{56,1... | collective-permute-start | bytes 792584 | tf_op jit(solution)/shard_map/ppermute | solution.py:99
  68.1 10.1 %collective-permute-start.7 = (f32[1,129,512]{2,1,0:T(8,128)S(1)}, f32[1,129,512]{2,1,0:T(8,128)S(1)}, u32[]{:S(2)}, u32[]{:S(2)}) collective-permute-start(f32[1,129,512]{2,1,0:T(8,128)S(1)} %pad_maximum_fusion.4), channel_id=1, source_target_pairs={{0,384},{8,392},{16,400},{24,408},{32,416},{40,424},{48,432},{56,4... | collective-permute-start | bytes 792584 | tf_op jit(solution)/shard_map/ppermute | solution.py:99
  81.0 6.8 %collective-permute-start.10 = (f32[1,128,512]{2,1,0:T(8,128)S(1)}, f32[1,128,512]{2,1,0:T(8,128)S(1)}, u32[]{:S(2)}, u32[]{:S(2)}) collective-permute-start(f32[1,128,512]{2,1,0:T(8,128)S(1)} %get-tuple-element.68), channel_id=1, source_target_pairs={{0,24},{8,32},{16,40},{24,48},{32,56},{40,64},{48,72},{56,80},{64,... | collective-permute-start | bytes 786440 | tf_op jit(solution)/shard_map/ppermute | solution.py:115
  82.7 5.5 %collective-permute-start.8 = (f32[1,128,512]{2,1,0:T(8,128)S(1)}, f32[1,128,512]{2,1,0:T(8,128)S(1)}, u32[]{:S(2)}, u32[]{:S(2)}) collective-permute-start(f32[1,128,512]{2,1,0:T(8,128)S(1)} %get-tuple-element.68), channel_id=1, source_target_pairs={{0,8},{8,16},{16,24},{24,32},{32,40},{40,48},{48,56},{56,64},{64,7... | collective-permute-start | bytes 786440 | tf_op jit(solution)/shard_map/ppermute | solution.py:115
  84.0 9.8 %collective-permute-start.9 = (f32[1,128,512]{2,1,0:T(8,128)S(1)}, f32[1,128,512]{2,1,0:T(8,128)S(1)}, u32[]{:S(2)}, u32[]{:S(2)}) collective-permute-start(f32[1,128,512]{2,1,0:T(8,128)S(1)} %get-tuple-element.68), channel_id=1, source_target_pairs={{0,16},{8,24},{16,32},{24,40},{32,48},{40,56},{48,64},{56,72},{64,... | collective-permute-start | bytes 786440 | tf_op jit(solution)/shard_map/ppermute | solution.py:115
  94.0 9.1 %collective-permute-start.11 = (f32[1,128,512]{2,1,0:T(8,128)S(1)}, f32[1,128,512]{2,1,0:T(8,128)S(1)}, u32[]{:S(2)}, u32[]{:S(2)}) collective-permute-start(f32[1,128,512]{2,1,0:T(8,128)S(1)} %get-tuple-element.34), channel_id=1, source_target_pairs={{0,32},{8,40},{16,48},{24,56},{32,64},{40,72},{48,80},{56,88},{64,... | collective-permute-start | bytes 786440 | tf_op jit(solution)/shard_map/ppermute | solution.py:115
  103.2 7.8 %collective-permute-start.12 = (f32[1,128,512]{2,1,0:T(8,128)S(1)}, f32[1,128,512]{2,1,0:T(8,128)S(1)}, u32[]{:S(2)}, u32[]{:S(2)}) collective-permute-start(f32[1,128,512]{2,1,0:T(8,128)S(1)} %multiply_add_fusion.11), channel_id=1, source_target_pairs={{0,64},{8,72},{16,80},{24,88},{32,96},{40,104},{48,112},{56,120},{... | collective-permute-start | bytes 786440 | tf_op jit(solution)/shard_map/ppermute | solution.py:115
  108.2 30.6 %copy-start.12 = (f32[1,128]{1,0:T(1,128)S(1)}, f32[1,128]{1,0:T(1,128)}, u32[]{:S(2)}) copy-start(f32[1,128]{1,0:T(1,128)} %param.11) | copy-start | bytes 1540
  111.1 33.2 %collective-permute-start.15 = (f32[1,128,512]{2,1,0:T(8,128)S(1)}, f32[1,128,512]{2,1,0:T(8,128)S(1)}, u32[]{:S(2)}, u32[]{:S(2)}) collective-permute-start(f32[1,128,512]{2,1,0:T(8,128)S(1)} %get-tuple-element.32), channel_id=1, source_target_pairs={{0,384},{8,392},{16,400},{24,408},{32,416},{40,424},{48,432},{56,4... | collective-permute-start | bytes 786440 | tf_op jit(solution)/shard_map/ppermute | solution.py:115
  134.3 10.0 %collective-permute-start.14 = (f32[1,128,512]{2,1,0:T(8,128)S(1)}, f32[1,128,512]{2,1,0:T(8,128)S(1)}, u32[]{:S(2)}, u32[]{:S(2)}) collective-permute-start(f32[1,128,512]{2,1,0:T(8,128)S(1)} %get-tuple-element.32), channel_id=1, source_target_pairs={{0,256},{8,264},{16,272},{24,280},{32,288},{40,296},{48,304},{56,3... | collective-permute-start | bytes 786440 | tf_op jit(solution)/shard_map/ppermute | solution.py:115
  135.6 10.0 %collective-permute-start.13 = (f32[1,128,512]{2,1,0:T(8,128)S(1)}, f32[1,128,512]{2,1,0:T(8,128)}, u32[]{:S(2)}, u32[]{:S(2)}) collective-permute-start(f32[1,128,512]{2,1,0:T(8,128)S(1)} %get-tuple-element.32), channel_id=1, source_target_pairs={{0,128},{8,136},{16,144},{24,152},{32,160},{40,168},{48,176},{56,1... | collective-permute-start | bytes 786440 | tf_op jit(solution)/shard_map/ppermute | solution.py:115
  146.7 0.9 copy-start.7
  148.0 74.2 %copy-start.5 = (f32[1,512,128]{1,2,0:T(8,128)}, f32[1,512,128]{1,2,0:T(8,128)S(1)}, u32[]{:S(2)}) copy-start(f32[1,512,128]{1,2,0:T(8,128)S(1)} %get-tuple-element.71) | copy-start | bytes 786436
  148.0 1.0 copy-start.2
  150.8 1.0 copy-start.3
  152.2 10.9 %collective-permute-start.18 = (f32[1,129,512]{2,1,0:T(8,128)S(1)}, f32[1,129,512]{2,1,0:T(8,128)S(1)}, u32[]{:S(2)}, u32[]{:S(2)}) collective-permute-start(f32[1,129,512]{2,1,0:T(8,128)S(1)} %pad_maximum_fusion.5), channel_id=1, source_target_pairs={{24,0},{32,8},{40,16},{48,24},{56,32},{64,40},{72,48},{80,56},{88,... | collective-permute-start | bytes 792584 | tf_op jit(solution)/shard_map/ppermute | solution.py:99
  153.5 17.3 %collective-permute-start.17 = (f32[1,129,512]{2,1,0:T(8,128)S(1)}, f32[1,129,512]{2,1,0:T(8,128)S(1)}, u32[]{:S(2)}, u32[]{:S(2)}) collective-permute-start(f32[1,129,512]{2,1,0:T(8,128)S(1)} %pad_maximum_fusion.5), channel_id=1, source_target_pairs={{16,0},{24,8},{32,16},{40,24},{48,32},{56,40},{64,48},{72,56},{80,... | collective-permute-start | bytes 792584 | tf_op jit(solution)/shard_map/ppermute | solution.py:99
  154.8 19.6 %collective-permute-start.16 = (f32[1,129,512]{2,1,0:T(8,128)S(1)}, f32[1,129,512]{2,1,0:T(8,128)S(1)}, u32[]{:S(2)}, u32[]{:S(2)}) collective-permute-start(f32[1,129,512]{2,1,0:T(8,128)S(1)} %pad_maximum_fusion.5), channel_id=1, source_target_pairs={{8,0},{16,8},{24,16},{32,24},{40,32},{48,40},{56,48},{64,56},{72,6... | collective-permute-start | bytes 792584 | tf_op jit(solution)/shard_map/ppermute | solution.py:99
  174.6 10.4 %collective-permute-start.19 = (f32[1,129,512]{2,1,0:T(8,128)S(1)}, f32[1,129,512]{2,1,0:T(8,128)S(1)}, u32[]{:S(2)}, u32[]{:S(2)}) collective-permute-start(f32[1,129,512]{2,1,0:T(8,128)S(1)} %pad_maximum_fusion.6), channel_id=1, source_target_pairs={{32,0},{40,8},{48,16},{56,24},{64,32},{72,40},{80,48},{88,56},{96,... | collective-permute-start | bytes 792584 | tf_op jit(solution)/shard_map/ppermute | solution.py:99
  185.1 16.4 %collective-permute-start.20 = (f32[1,129,512]{2,1,0:T(8,128)S(1)}, f32[1,129,512]{2,1,0:T(8,128)S(1)}, u32[]{:S(2)}, u32[]{:S(2)}) collective-permute-start(f32[1,129,512]{2,1,0:T(8,128)S(1)} %pad_maximum_fusion.7), channel_id=1, source_target_pairs={{64,0},{72,8},{80,16},{88,24},{96,32},{104,40},{112,48},{120,56},{... | collective-permute-start | bytes 792584 | tf_op jit(solution)/shard_map/ppermute | solution.py:99
  201.6 11.3 %collective-permute-start.22 = (f32[1,129,512]{2,1,0:T(8,128)S(1)}, f32[1,129,512]{2,1,0:T(8,128)S(1)}, u32[]{:S(2)}, u32[]{:S(2)}) collective-permute-start(f32[1,129,512]{2,1,0:T(8,128)S(1)} %pad_maximum_fusion.8), channel_id=1, source_target_pairs={{256,0},{264,8},{272,16},{280,24},{288,32},{296,40},{304,48},{312,... | collective-permute-start | bytes 792584 | tf_op jit(solution)/shard_map/ppermute | solution.py:99
  202.9 10.0 %collective-permute-start.21 = (f32[1,129,512]{2,1,0:T(8,128)S(1)}, f32[1,129,512]{2,1,0:T(8,128)S(1)}, u32[]{:S(2)}, u32[]{:S(2)}) collective-permute-start(f32[1,129,512]{2,1,0:T(8,128)S(1)} %pad_maximum_fusion.8), channel_id=1, source_target_pairs={{128,0},{136,8},{144,16},{152,24},{160,32},{168,40},{176,48},{184,... | collective-permute-start | bytes 792584 | tf_op jit(solution)/shard_map/ppermute | solution.py:99
  204.2 16.9 %collective-permute-start.23 = (f32[1,129,512]{2,1,0:T(8,128)S(1)}, f32[1,129,512]{2,1,0:T(8,128)S(1)}, u32[]{:S(2)}, u32[]{:S(2)}) collective-permute-start(f32[1,129,512]{2,1,0:T(8,128)S(1)} %pad_maximum_fusion.8), channel_id=1, source_target_pairs={{384,0},{392,8},{400,16},{408,24},{416,32},{424,40},{432,48},{440,... | collective-permute-start | bytes 792584 | tf_op jit(solution)/shard_map/ppermute | solution.py:99
  224.0 12.6 %collective-permute-start.26 = (f32[1,128,512]{2,1,0:T(8,128)S(1)}, f32[1,128,512]{2,1,0:T(8,128)S(1)}, u32[]{:S(2)}, u32[]{:S(2)}) collective-permute-start(f32[1,128,512]{2,1,0:T(8,128)S(1)} %get-tuple-element.80), channel_id=1, source_target_pairs={{24,0},{32,8},{40,16},{48,24},{56,32},{64,40},{72,48},{80,56},{88,... | collective-permute-start | bytes 786440 | tf_op jit(solution)/shard_map/ppermute | solution.py:115
  225.3 11.4 %collective-permute-start.24 = (f32[1,128,512]{2,1,0:T(8,128)S(1)}, f32[1,128,512]{2,1,0:T(8,128)S(1)}, u32[]{:S(2)}, u32[]{:S(2)}) collective-permute-start(f32[1,128,512]{2,1,0:T(8,128)S(1)} %get-tuple-element.80), channel_id=1, source_target_pairs={{8,0},{16,8},{24,16},{32,24},{40,32},{48,40},{56,48},{64,56},{72,6... | collective-permute-start | bytes 786440 | tf_op jit(solution)/shard_map/ppermute | solution.py:115
  226.6 18.4 %collective-permute-start.25 = (f32[1,128,512]{2,1,0:T(8,128)S(1)}, f32[1,128,512]{2,1,0:T(8,128)S(1)}, u32[]{:S(2)}, u32[]{:S(2)}) collective-permute-start(f32[1,128,512]{2,1,0:T(8,128)S(1)} %get-tuple-element.80), channel_id=1, source_target_pairs={{16,0},{24,8},{32,16},{40,24},{48,32},{56,40},{64,48},{72,56},{80,... | collective-permute-start | bytes 786440 | tf_op jit(solution)/shard_map/ppermute | solution.py:115
  245.1 12.9 %collective-permute-start.27 = (f32[1,128,512]{2,1,0:T(8,128)S(1)}, f32[1,128,512]{2,1,0:T(8,128)S(1)}, u32[]{:S(2)}, u32[]{:S(2)}) collective-permute-start(f32[1,128,512]{2,1,0:T(8,128)S(1)} %get-tuple-element.12), channel_id=1, source_target_pairs={{32,0},{40,8},{48,16},{56,24},{64,32},{72,40},{80,48},{88,56},{96,... | collective-permute-start | bytes 786440 | tf_op jit(solution)/shard_map/ppermute | solution.py:115
  258.1 8.6 %collective-permute-start.28 = (f32[1,128,512]{2,1,0:T(8,128)S(1)}, f32[1,128,512]{2,1,0:T(8,128)S(1)}, u32[]{:S(2)}, u32[]{:S(2)}) collective-permute-start(f32[1,128,512]{2,1,0:T(8,128)S(1)} %multiply_add_fusion.2), channel_id=1, source_target_pairs={{64,0},{72,8},{80,16},{88,24},{96,32},{104,40},{112,48},{120,56},{... | collective-permute-start | bytes 786440 | tf_op jit(solution)/shard_map/ppermute | solution.py:115
  267.6 13.1 %collective-permute-start.31 = (f32[1,128,512]{2,1,0:T(8,128)}, f32[1,128,512]{2,1,0:T(8,128)}, u32[]{:S(2)}, u32[]{:S(2)}) collective-permute-start(f32[1,128,512]{2,1,0:T(8,128)} %get-tuple-element.10), channel_id=1, source_target_pairs={{384,0},{392,8},{400,16},{408,24},{416,32},{424,40},{432,48},{440,... | collective-permute-start | bytes 786440 | tf_op jit(solution)/shard_map/ppermute | solution.py:115
  268.8 19.7 %collective-permute-start.30 = (f32[1,128,512]{2,1,0:T(8,128)}, f32[1,128,512]{2,1,0:T(8,128)}, u32[]{:S(2)}, u32[]{:S(2)}) collective-permute-start(f32[1,128,512]{2,1,0:T(8,128)} %get-tuple-element.10), channel_id=1, source_target_pairs={{256,0},{264,8},{272,16},{280,24},{288,32},{296,40},{304,48},{312,... | collective-permute-start | bytes 786440 | tf_op jit(solution)/shard_map/ppermute | solution.py:115
  270.1 20.5 %collective-permute-start.29 = (f32[1,128,512]{2,1,0:T(8,128)}, f32[1,128,512]{2,1,0:T(8,128)}, u32[]{:S(2)}, u32[]{:S(2)}) collective-permute-start(f32[1,128,512]{2,1,0:T(8,128)} %get-tuple-element.10), channel_id=1, source_target_pairs={{128,0},{136,8},{144,16},{152,24},{160,32},{168,40},{176,48},{184,... | collective-permute-start | bytes 786440 | tf_op jit(solution)/shard_map/ppermute | solution.py:115
  293.4 1.0 copy-start.6
  293.4 1.0 copy-start.8
  296.2 1.0 copy-start.9
  297.7 3.1 copy-start.10
  297.7 4.7 %collective-permute-start.32 = (f32[1184,128]{1,0:T(8,128)S(1)}, f32[1184,128]{1,0:T(8,128)S(1)}, u32[]{:S(2)}, u32[]{:S(2)}) collective-permute-start(f32[1184,128]{1,0:T(8,128)S(1)} %constant_dynamic-slice_fusion), channel_id=1, source_target_pairs={{0,1},{1,0},{2,3},{3,2},{4,5},{5,4},{6,7},{7,6},{8,9},{9,8},{10,11... | collective-permute-start | bytes 1818632 | tf_op jit(solution)/shard_map/ppermute | solution.py:139
  302.5 23.8 %collective-permute-start.35 = (f32[296,128]{1,0:T(8,128)S(1)}, f32[296,128]{1,0:T(8,128)S(1)}, u32[]{:S(2)}, u32[]{:S(2)}) collective-permute-start(f32[296,128]{1,0:T(8,128)S(1)} %get-tuple-element.53), channel_id=1, source_target_pairs={{0,6},{1,7},{2,0},{3,1},{4,2},{5,3},{6,4},{7,5},{8,14},{9,15},{10,... | collective-permute-start | bytes 454664 | tf_op jit(solution)/shard_map/ppermute | solution.py:146
  313.6 28.2 %collective-permute-start.34 = (f32[296,128]{1,0:T(8,128)S(1)}, f32[296,128]{1,0:T(8,128)S(1)}, u32[]{:S(2)}, u32[]{:S(2)}) collective-permute-start(f32[296,128]{1,0:T(8,128)S(1)} %get-tuple-element.54), channel_id=1, source_target_pairs={{0,4},{1,5},{2,6},{3,7},{4,0},{5,1},{6,2},{7,3},{8,12},{9,13},{10,... | collective-permute-start | bytes 454664 | tf_op jit(solution)/shard_map/ppermute | solution.py:146
  319.0 22.8 %collective-permute-start.33 = (f32[296,128]{1,0:T(8,128)S(1)}, f32[296,128]{1,0:T(8,128)S(1)}, u32[]{:S(2)}, u32[]{:S(2)}) collective-permute-start(f32[296,128]{1,0:T(8,128)S(1)} %get-tuple-element.52), channel_id=1, source_target_pairs={{0,2},{1,3},{2,4},{3,5},{4,6},{5,7},{6,0},{7,1},{8,10},{9,11},{10,... | collective-permute-start | bytes 454664 | tf_op jit(solution)/shard_map/ppermute | solution.py:146
  326.4 60.9 %copy-start.4 = (bf16[128,9,128]{0,2,1:T(8,128)(2,1)S(1)}, bf16[128,9,128]{0,2,1:T(8,128)(2,1)}, u32[]{:S(2)}) copy-start(bf16[128,9,128]{0,2,1:T(8,128)(2,1)} %copy.26) | copy-start | bytes 884740
  341.9 20.7 %collective-permute-start.36 = (f32[296,128]{1,0:T(8,128)S(1)}, f32[296,128]{1,0:T(8,128)S(1)}, u32[]{:S(2)}, u32[]{:S(2)}) collective-permute-start(f32[296,128]{1,0:T(8,128)S(1)} %fusion.195), channel_id=1, source_target_pairs={{0,2},{1,3},{2,4},{3,5},{4,6},{5,7},{6,0},{7,1},{8,10},{9,11},{10,... | collective-permute-start | bytes 454664 | tf_op jit(solution)/shard_map/ppermute | solution.py:150
  347.5 24.0 %collective-permute-start.37 = (f32[296,128]{1,0:T(8,128)S(1)}, f32[296,128]{1,0:T(8,128)S(1)}, u32[]{:S(2)}, u32[]{:S(2)}) collective-permute-start(f32[296,128]{1,0:T(8,128)S(1)} %fusion.195), channel_id=1, source_target_pairs={{0,4},{1,5},{2,6},{3,7},{4,0},{5,1},{6,2},{7,3},{8,12},{9,13},{10,... | collective-permute-start | bytes 454664 | tf_op jit(solution)/shard_map/ppermute | solution.py:150
  358.1 26.7 %collective-permute-start.38 = (f32[296,128]{1,0:T(8,128)S(1)}, f32[296,128]{1,0:T(8,128)S(1)}, u32[]{:S(2)}, u32[]{:S(2)}) collective-permute-start(f32[296,128]{1,0:T(8,128)S(1)} %fusion.195), channel_id=1, source_target_pairs={{0,6},{1,7},{2,0},{3,1},{4,2},{5,3},{6,4},{7,5},{8,14},{9,15},{10,... | collective-permute-start | bytes 454664 | tf_op jit(solution)/shard_map/ppermute | solution.py:150
  384.7 4.1 %collective-permute-start.39 = (f32[1184,128]{1,0:T(8,128)S(1)}, f32[1184,128]{1,0:T(8,128)S(1)}, u32[]{:S(2)}, u32[]{:S(2)}) collective-permute-start(f32[1184,128]{1,0:T(8,128)S(1)} %bitcast.492), channel_id=1, source_target_pairs={{0,1},{1,0},{2,3},{3,2},{4,5},{5,4},{6,7},{7,6},{8,9},{9,8},{10,11... | collective-permute-start | bytes 1818632 | tf_op jit(solution)/shard_map/ppermute | solution.py:153

commit v7 on v6

--- a/solution.py
+++ b/solution.py
@@ -33,21 +33,32 @@
     return jnp.transpose(taps, (2, 1, 0)).reshape(channels, 9 * channels)
 
 
+def conv_same(current, kernel):
+    batch, channels, pixels = current.shape
+    image = current.astype(jnp.bfloat16).reshape(batch, channels, HEIGHT, WIDTH)
+    out = lax.conv_general_dilated(
+        image,
+        jnp.transpose(kernel, (0, 3, 1, 2)),
+        (1, 1),
+        ((1, 1), (1, 1)),
+        dimension_numbers=("NCHW", "OIHW", "NCHW"),
+        preferred_element_type=jnp.float32,
+    )
+    return out.reshape(batch, kernel.shape[0], pixels)
+
+
 def forward_layer(current, weight, bias_row):
-    stacked = columns(current)
-    pre_act = (
-        jnp.einsum("ok,bkp->bop", weight, stacked, preferred_element_type=jnp.float32)
-        + bias_row[None, :, None]
-    )
+    channels = weight.shape[0]
+    pre_act = conv_same(current, weight.reshape(channels, 3, 3, channels)) + bias_row[None, :, None]
     activity = jnp.tanh(pre_act)
-    return (current + step_size * activity, activity, stacked)
+    return (current + step_size * activity, activity, current)
 
 
 def backward_layer(adjoint, activity, flipped):
     scaled = step_size * (1.0 - activity * activity) * adjoint
     rounded = scaled.astype(jnp.bfloat16)
-    gathered = columns(rounded)
-    back = jnp.einsum("ck,bkp->bcp", flipped, gathered, preferred_element_type=jnp.float32)
+    channels = flipped.shape[0]
+    back = conv_same(rounded, flipped.reshape(channels, 3, 3, channels))
     return (adjoint + back, rounded, scaled)
 
 
@@ -194,7 +205,7 @@
             adjoint, stored[layer_index][1], flipped_list[layer_index]
         )
         weight_part = jnp.einsum(
-            "bop,bkp->ok", rounded, stored[layer_index][0], preferred_element_type=jnp.float32
+            "bop,bkp->ok", rounded, columns(stored[layer_index][0]), preferred_element_type=jnp.float32
         )
         bias_part = jnp.sum(scaled, axis=(0, 2))
         weight_parts.insert(0, weight_part)

time: 396 us -> 482 us (1.22)
  waiting for transfers between devices: 196 us -> 265 us
  local copies, waits for them, and re-layouts: 6.86 us -> 21.4 us
  starting transfers between devices: 161 us -> 166 us
    ppermute x16, waiting for transfers between devices: 82.9 us -> 147 us  [exclusive_scan_first(): lax.ppermute(packed, axis, scan_pairs(count, j * d, reverse))]
    ppermute x16, starting transfers between devices: 57.1 us -> 67.8 us  [exclusive_scan_first(): lax.ppermute(packed, axis, scan_pairs(count, j * d, reverse))]
    conv_general_dilated x0 -> x12, matrix products: none -> 6.63 us  [conv_same(): lax.conv_general_dilated(image, jnp.transpose(kernel, (0, 3, 1, 2)), (1,...]
    unnamed x96 -> x13, other arithmetic: 9.1 us -> 2.76 us
    unnamed x28 -> x66, local copies, waits for them, and re-layouts: 2.32 us -> 8.31 us
    ppermute x3, starting transfers between devices: 19.7 us -> 13.9 us  [batch_sum(): got = lax.ppermute(mine, axis, target)]
    slice x0 -> x15, local copies, waits for them, and re-layouts: none -> 5.57 us  [the longest x14 4.81 us: exclusive_scan_first(): product = product * part[0, channels, :channels]]
    dot_general x14 -> x2, matrix products: 6.27 us -> 0.74 us  [per_device(): jnp.einsum('bop,bkp->ok', rounded, columns(stored[layer_index][0]), prefe...]
  transfers between devices with their start and end apart: 40 -> 40, of which waited for: 34 -> 28; matrix products, arithmetic and copies ran while one was open for 1% -> 2% of each run, Pallas kernels for 0% -> 0%
where the time goes in v7:
time: 482 us; the launch traced here: 478 us
  waiting for transfers between devices  265 us (55%)
  starting transfers between devices  166 us (34%)
  local copies, waits for them, and re-layouts  21.4 us (4%)
  other arithmetic  14.6 us (3%)
  matrix products  7.37 us (2%)
    ppermute x16, waiting for transfers between devices, exclusive_scan_first(): lax.ppermute(packed, axis, scan_pairs(count, j * d, reverse))  147 us
    ppermute x16, waiting for transfers between devices, exclusive_scan_again(): lax.ppermute(sending, axis, scan_pairs(count, j * d, reverse))  73.2 us
    ppermute x16, starting transfers between devices, exclusive_scan_first(): lax.ppermute(packed, axis, scan_pairs(count, j * d, reverse))  67.8 us
    ppermute x16, starting transfers between devices, exclusive_scan_again(): lax.ppermute(sending, axis, scan_pairs(count, j * d, reverse))  53.8 us
    ppermute x3, starting transfers between devices, batch_sum(): mine = mine + lax.ppermute(sent, axis, target)  24.4 us
    ppermute x3, waiting for transfers between devices, batch_sum(): got = lax.ppermute(mine, axis, target)  23.7 us
    ppermute x3, waiting for transfers between devices, batch_sum(): mine = mine + lax.ppermute(sent, axis, target)  19.2 us
    ppermute x3, starting transfers between devices, batch_sum(): got = lax.ppermute(mine, axis, target)  13.9 us
  transfers between devices with their start and end apart: 40, of which 28 were waited for; matrix products, arithmetic and copies ran while one was open for 2% of the time, Pallas kernels for 0%

profile of v7, /device:TPU:1, one launch (start us, length us, event | category | flops | bytes accessed | tf_op | source)
XLA Modules:
  0.0 477.5 jit_solution(3383595568901416788)
XLA Ops:
  6.9 5.2 %collective-permute-start.2 = (f32[1,129,512]{1,2,0:T(8,128)S(1)}, f32[1,129,512]{1,2,0:T(8,128)S(1)}, u32[]{:S(2)}, u32[]{:S(2)}) collective-permute-start(f32[1,129,512]{1,2,0:T(8,128)S(1)} %pad_maximum_fusion.1), channel_id=1, source_target_pairs={{0,24},{8,32},{16,40},{24,48},{32,56},{40,64},{48,72},{56,80},{64,... | collective-permute-start | bytes 792584 | tf_op jit(solution)/shard_map/ppermute | solution.py:110
  12.2 3.8 collective-permute-start.1
  16.0 2.5 collective-permute-start
  18.5 2.2 collective-permute-done.2
  20.9 5.4 %collective-permute-done.1 = f32[1,129,512]{1,2,0:T(8,128)S(1)} collective-permute-done((f32[1,129,512]{1,2,0:T(8,128)S(1)}, f32[1,129,512]{1,2,0:T(8,128)S(1)}, u32[]{:S(2)}, u32[]{:S(2)}) %collective-permute-start.1) | collective-permute-done | bytes 264224 | tf_op jit(solution)/shard_map/ppermute | solution.py:110
  26.4 11.1 %collective-permute-done = f32[1,129,512]{1,2,0:T(8,128)S(1)} collective-permute-done((f32[1,129,512]{1,2,0:T(8,128)S(1)}, f32[1,129,512]{1,2,0:T(8,128)S(1)}, u32[]{:S(2)}, u32[]{:S(2)}) %collective-permute-start) | collective-permute-done | bytes 264224 | tf_op jit(solution)/shard_map/ppermute | solution.py:110
  39.5 13.5 %collective-permute-start.3 = (f32[1,129,512]{1,2,0:T(8,128)S(1)}, f32[1,129,512]{1,2,0:T(8,128)S(1)}, u32[]{:S(2)}, u32[]{:S(2)}) collective-permute-start(f32[1,129,512]{1,2,0:T(8,128)S(1)} %pad_maximum_fusion.2), channel_id=1, source_target_pairs={{0,32},{8,40},{16,48},{24,56},{32,64},{40,72},{48,80},{56,88},{64,... | collective-permute-start | bytes 792584 | tf_op jit(solution)/shard_map/ppermute | solution.py:110
  53.0 9.6 %collective-permute-done.3 = f32[1,129,512]{1,2,0:T(8,128)S(1)} collective-permute-done((f32[1,129,512]{1,2,0:T(8,128)S(1)}, f32[1,129,512]{1,2,0:T(8,128)S(1)}, u32[]{:S(2)}, u32[]{:S(2)}) %collective-permute-start.3) | collective-permute-done | bytes 264224 | tf_op jit(solution)/shard_map/ppermute | solution.py:110
  62.9 5.5 %collective-permute-start.4 = (f32[1,129,512]{1,2,0:T(8,128)S(1)}, f32[1,129,512]{1,2,0:T(8,128)S(1)}, u32[]{:S(2)}, u32[]{:S(2)}) collective-permute-start(f32[1,129,512]{1,2,0:T(8,128)S(1)} %pad_maximum_fusion.3), channel_id=1, source_target_pairs={{0,64},{8,72},{16,80},{24,88},{32,96},{40,104},{48,112},{56,120},{... | collective-permute-start | bytes 792584 | tf_op jit(solution)/shard_map/ppermute | solution.py:110
  68.4 8.7 %collective-permute-done.4 = f32[1,129,512]{1,2,0:T(8,128)S(1)} collective-permute-done((f32[1,129,512]{1,2,0:T(8,128)S(1)}, f32[1,129,512]{1,2,0:T(8,128)S(1)}, u32[]{:S(2)}, u32[]{:S(2)}) %collective-permute-start.4) | collective-permute-done | bytes 264224 | tf_op jit(solution)/shard_map/ppermute | solution.py:110
  77.6 22.6 %collective-permute-start.6 = (f32[1,129,512]{1,2,0:T(8,128)S(1)}, f32[1,129,512]{1,2,0:T(8,128)S(1)}, u32[]{:S(2)}, u32[]{:S(2)}) collective-permute-start(f32[1,129,512]{1,2,0:T(8,128)S(1)} %pad_maximum_fusion.4), channel_id=1, source_target_pairs={{0,256},{8,264},{16,272},{24,280},{32,288},{40,296},{48,304},{56,3... | collective-permute-start | bytes 792584 | tf_op jit(solution)/shard_map/ppermute | solution.py:110
  100.1 2.9 collective-permute-start.5
  103.0 1.3 collective-permute-start.7
  104.3 6.6 %collective-permute-done.6 = f32[1,129,512]{1,2,0:T(8,128)S(1)} collective-permute-done((f32[1,129,512]{1,2,0:T(8,128)S(1)}, f32[1,129,512]{1,2,0:T(8,128)S(1)}, u32[]{:S(2)}, u32[]{:S(2)}) %collective-permute-start.6) | collective-permute-done | bytes 264224 | tf_op jit(solution)/shard_map/ppermute | solution.py:110
  111.0 11.1 %collective-permute-done.5 = f32[1,129,512]{1,2,0:T(8,128)S(1)} collective-permute-done((f32[1,129,512]{1,2,0:T(8,128)S(1)}, f32[1,129,512]{1,2,0:T(8,128)S(1)}, u32[]{:S(2)}, u32[]{:S(2)}) %collective-permute-start.5) | collective-permute-done | bytes 264224 | tf_op jit(solution)/shard_map/ppermute | solution.py:110
  122.3 1.3 collective-permute-done.7
  125.7 1.3 collective-permute-start.10
  127.0 1.3 collective-permute-start.9
  128.3 1.7 collective-permute-start.8
  130.1 6.7 %collective-permute-done.10 = f32[1,128,512]{1,2,0:T(8,128)S(1)} collective-permute-done((f32[1,128,512]{1,2,0:T(8,128)S(1)}, f32[1,128,512]{1,2,0:T(8,128)S(1)}, u32[]{:S(2)}, u32[]{:S(2)}) %collective-permute-start.10) | collective-permute-done | bytes 262176 | tf_op jit(solution)/shard_map/ppermute | solution.py:126
  136.8 2.7 collective-permute-done.8
  139.5 5.4 %collective-permute-start.11 = (f32[1,128,512]{1,2,0:T(8,128)S(1)}, f32[1,128,512]{1,2,0:T(8,128)S(1)}, u32[]{:S(2)}, u32[]{:S(2)}) collective-permute-start(f32[1,128,512]{1,2,0:T(8,128)S(1)} %get-tuple-element.48), channel_id=1, source_target_pairs={{0,32},{8,40},{16,48},{24,56},{32,64},{40,72},{48,80},{56,88},{64,... | collective-permute-start | bytes 786440 | tf_op jit(solution)/shard_map/ppermute | solution.py:126
  144.9 3.3 collective-permute-done.11
  148.3 7.6 %collective-permute-start.12 = (f32[1,128,512]{1,2,0:T(8,128)S(1)}, f32[1,128,512]{1,2,0:T(8,128)S(1)}, u32[]{:S(2)}, u32[]{:S(2)}) collective-permute-start(f32[1,128,512]{1,2,0:T(8,128)S(1)} %multiply_add_fusion.12), channel_id=1, source_target_pairs={{0,64},{8,72},{16,80},{24,88},{32,96},{40,104},{48,112},{56,120},{... | collective-permute-start | bytes 786440 | tf_op jit(solution)/shard_map/ppermute | solution.py:126
  155.9 3.3 collective-permute-done.12
  159.3 21.7 %collective-permute-start.15 = (f32[1,128,512]{1,2,0:T(8,128)S(1)}, f32[1,128,512]{1,2,0:T(8,128)S(1)}, u32[]{:S(2)}, u32[]{:S(2)}) collective-permute-start(f32[1,128,512]{1,2,0:T(8,128)S(1)} %get-tuple-element.46), channel_id=1, source_target_pairs={{0,384},{8,392},{16,400},{24,408},{32,416},{40,424},{48,432},{56,4... | collective-permute-start | bytes 786440 | tf_op jit(solution)/shard_map/ppermute | solution.py:126
  180.9 1.3 collective-permute-start.14
  182.2 3.2 collective-permute-start.13
  186.4 5.3 %collective-permute-done.15 = f32[1,128,512]{1,2,0:T(8,128)S(1)} collective-permute-done((f32[1,128,512]{1,2,0:T(8,128)S(1)}, f32[1,128,512]{1,2,0:T(8,128)S(1)}, u32[]{:S(2)}, u32[]{:S(2)}) %collective-permute-start.15) | collective-permute-done | bytes 262176 | tf_op jit(solution)/shard_map/ppermute | solution.py:126
  191.7 1.4 collective-permute-done.13
  198.2 1.3 collective-permute-start.18
  201.3 1.5 collective-permute-start.16
  203.5 21.1 %collective-permute-done.18 = f32[1,129,512]{1,2,0:T(8,128)} collective-permute-done((f32[1,129,512]{1,2,0:T(8,128)S(1)}, f32[1,129,512]{1,2,0:T(8,128)}, u32[]{:S(2)}, u32[]{:S(2)}) %collective-permute-start.18) | collective-permute-done | bytes 264224 | tf_op jit(solution)/shard_map/ppermute | solution.py:110
  229.0 1.3 collective-permute-start.19
  230.6 11.3 %collective-permute-done.19 = f32[1,129,512]{1,2,0:T(8,128)} collective-permute-done((f32[1,129,512]{1,2,0:T(8,128)S(1)}, f32[1,129,512]{1,2,0:T(8,128)}, u32[]{:S(2)}, u32[]{:S(2)}) %collective-permute-start.19) | collective-permute-done | bytes 264224 | tf_op jit(solution)/shard_map/ppermute | solution.py:110
  244.1 1.3 collective-permute-start.20
  245.8 26.0 %collective-permute-done.20 = f32[1,129,512]{1,2,0:T(8,128)S(1)} collective-permute-done((f32[1,129,512]{1,2,0:T(8,128)S(1)}, f32[1,129,512]{1,2,0:T(8,128)S(1)}, u32[]{:S(2)}, u32[]{:S(2)}) %collective-permute-start.20) | collective-permute-done | bytes 264224 | tf_op jit(solution)/shard_map/ppermute | solution.py:110
  273.9 1.3 collective-permute-start.22
  275.4 1.3 collective-permute-start.21
  276.8 1.3 collective-permute-start.23
  278.1 21.4 %collective-permute-done.22 = f32[1,129,512]{1,2,0:T(8,128)S(1)} collective-permute-done((f32[1,129,512]{1,2,0:T(8,128)S(1)}, f32[1,129,512]{1,2,0:T(8,128)S(1)}, u32[]{:S(2)}, u32[]{:S(2)}) %collective-permute-start.22) | collective-permute-done | bytes 264224 | tf_op jit(solution)/shard_map/ppermute | solution.py:110
  299.7 11.5 %collective-permute-done.23 = f32[1,129,512]{1,2,0:T(8,128)S(1)} collective-permute-done((f32[1,129,512]{1,2,0:T(8,128)S(1)}, f32[1,129,512]{1,2,0:T(8,128)S(1)}, u32[]{:S(2)}, u32[]{:S(2)}) %collective-permute-start.23) | collective-permute-done | bytes 264224 | tf_op jit(solution)/shard_map/ppermute | solution.py:110
  315.1 1.3 collective-permute-start.26
  316.4 1.3 collective-permute-start.25
  317.7 1.3 collective-permute-start.24
  319.4 10.3 %collective-permute-done.26 = f32[1,128,512]{1,2,0:T(8,128)S(1)} collective-permute-done((f32[1,128,512]{1,2,0:T(8,128)S(1)}, f32[1,128,512]{1,2,0:T(8,128)S(1)}, u32[]{:S(2)}, u32[]{:S(2)}) %collective-permute-start.26) | collective-permute-done | bytes 262176 | tf_op jit(solution)/shard_map/ppermute | solution.py:126
  329.7 3.1 collective-permute-done.25
  332.9 1.3 collective-permute-start.27
  334.6 11.9 %collective-permute-done.27 = f32[1,128,512]{1,2,0:T(8,128)S(1)} collective-permute-done((f32[1,128,512]{1,2,0:T(8,128)S(1)}, f32[1,128,512]{1,2,0:T(8,128)S(1)}, u32[]{:S(2)}, u32[]{:S(2)}) %collective-permute-start.27) | collective-permute-done | bytes 262176 | tf_op jit(solution)/shard_map/ppermute | solution.py:126
  346.6 1.3 collective-permute-start.28
  348.2 14.1 %collective-permute-done.28 = f32[1,128,512]{1,2,0:T(8,128)S(1)} collective-permute-done((f32[1,128,512]{1,2,0:T(8,128)S(1)}, f32[1,128,512]{1,2,0:T(8,128)S(1)}, u32[]{:S(2)}, u32[]{:S(2)}) %collective-permute-start.28) | collective-permute-done | bytes 262176 | tf_op jit(solution)/shard_map/ppermute | solution.py:126
  366.6 11.1 %collective-permute-done.31 = f32[1,128,512]{1,2,0:T(8,128)S(1)} collective-permute-done((f32[1,128,512]{1,2,0:T(8,128)S(1)}, f32[1,128,512]{1,2,0:T(8,128)S(1)}, u32[]{:S(2)}, u32[]{:S(2)}) %collective-permute-start.31) | collective-permute-done | bytes 262176 | tf_op jit(solution)/shard_map/ppermute | solution.py:126
  381.9 4.1 collective-permute-start.32
  386.3 1.5 collective-permute-done.32
  388.9 8.8 %collective-permute-start.33 = (f32[296,128]{1,0:T(8,128)S(1)}, f32[296,128]{1,0:T(8,128)S(1)}, u32[]{:S(2)}, u32[]{:S(2)}) collective-permute-start(f32[296,128]{1,0:T(8,128)S(1)} %get-tuple-element.70), channel_id=1, source_target_pairs={{0,2},{1,3},{2,4},{3,5},{4,6},{5,7},{6,0},{7,1},{8,10},{9,11},{10,... | collective-permute-start | bytes 454664 | tf_op jit(solution)/shard_map/ppermute | solution.py:157
  397.8 5.4 %collective-permute-start.35 = (f32[296,128]{1,0:T(8,128)S(1)}, f32[296,128]{1,0:T(8,128)S(1)}, u32[]{:S(2)}, u32[]{:S(2)}) collective-permute-start(f32[296,128]{1,0:T(8,128)S(1)} %get-tuple-element.71), channel_id=1, source_target_pairs={{0,6},{1,7},{2,0},{3,1},{4,2},{5,3},{6,4},{7,5},{8,14},{9,15},{10,... | collective-permute-start | bytes 454664 | tf_op jit(solution)/shard_map/ppermute | solution.py:157
  403.1 10.2 %collective-permute-start.34 = (f32[296,128]{1,0:T(8,128)S(1)}, f32[296,128]{1,0:T(8,128)S(1)}, u32[]{:S(2)}, u32[]{:S(2)}) collective-permute-start(f32[296,128]{1,0:T(8,128)S(1)} %get-tuple-element.72), channel_id=1, source_target_pairs={{0,4},{1,5},{2,6},{3,7},{4,0},{5,1},{6,2},{7,3},{8,12},{9,13},{10,... | collective-permute-start | bytes 454664 | tf_op jit(solution)/shard_map/ppermute | solution.py:157
  414.1 8.0 %collective-permute-done.35 = f32[296,128]{1,0:T(8,128)S(1)} collective-permute-done((f32[296,128]{1,0:T(8,128)S(1)}, f32[296,128]{1,0:T(8,128)S(1)}, u32[]{:S(2)}, u32[]{:S(2)}) %collective-permute-start.35) | collective-permute-done | bytes 151584 | tf_op jit(solution)/shard_map/ppermute | solution.py:157
  422.1 11.2 %collective-permute-done.34 = f32[296,128]{1,0:T(8,128)S(1)} collective-permute-done((f32[296,128]{1,0:T(8,128)S(1)}, f32[296,128]{1,0:T(8,128)S(1)}, u32[]{:S(2)}, u32[]{:S(2)}) %collective-permute-start.34) | collective-permute-done | bytes 151584 | tf_op jit(solution)/shard_map/ppermute | solution.py:157
  433.3 1.9 collective-permute-start.38
  435.2 4.8 collective-permute-start.37
  440.0 7.3 %collective-permute-start.36 = (f32[296,128]{1,0:T(8,128)S(1)}, f32[296,128]{1,0:T(8,128)S(1)}, u32[]{:S(2)}, u32[]{:S(2)}) collective-permute-start(f32[296,128]{1,0:T(8,128)S(1)} %fusion.122), channel_id=1, source_target_pairs={{0,2},{1,3},{2,4},{3,5},{4,6},{5,7},{6,0},{7,1},{8,10},{9,11},{10,... | collective-permute-start | bytes 454664 | tf_op jit(solution)/shard_map/ppermute | solution.py:161
  447.3 23.7 %collective-permute-done.36 = f32[296,128]{1,0:T(8,128)S(1)} collective-permute-done((f32[296,128]{1,0:T(8,128)S(1)}, f32[296,128]{1,0:T(8,128)S(1)}, u32[]{:S(2)}, u32[]{:S(2)}) %collective-permute-start.36) | collective-permute-done | bytes 151584 | tf_op jit(solution)/shard_map/ppermute | solution.py:161
  471.1 2.4 collective-permute-start.39
  (291 shorter events, 48.5 us)
Async XLA Ops:
  0.6 3.6 copy-start.5
  4.1 0.7 copy-start.20
  6.8 30.9 %copy-start.14 = (f32[1,128]{1,0:T(1,128)S(1)}, f32[1,128]{1,0:T(1,128)}, u32[]{:S(2)}) copy-start(f32[1,128]{1,0:T(1,128)} %param.10) | copy-start | bytes 1540
  6.9 13.8 %collective-permute-start.2 = (f32[1,129,512]{1,2,0:T(8,128)S(1)}, f32[1,129,512]{1,2,0:T(8,128)S(1)}, u32[]{:S(2)}, u32[]{:S(2)}) collective-permute-start(f32[1,129,512]{1,2,0:T(8,128)S(1)} %pad_maximum_fusion.1), channel_id=1, source_target_pairs={{0,24},{8,32},{16,40},{24,48},{32,56},{40,64},{48,72},{56,80},{64,... | collective-permute-start | bytes 792584 | tf_op jit(solution)/shard_map/ppermute | solution.py:110
  12.2 14.1 %collective-permute-start.1 = (f32[1,129,512]{1,2,0:T(8,128)S(1)}, f32[1,129,512]{1,2,0:T(8,128)S(1)}, u32[]{:S(2)}, u32[]{:S(2)}) collective-permute-start(f32[1,129,512]{1,2,0:T(8,128)S(1)} %pad_maximum_fusion.1), channel_id=1, source_target_pairs={{0,16},{8,24},{16,32},{24,40},{32,48},{40,56},{48,64},{56,72},{64,... | collective-permute-start | bytes 792584 | tf_op jit(solution)/shard_map/ppermute | solution.py:110
  16.0 21.5 %collective-permute-start = (f32[1,129,512]{1,2,0:T(8,128)S(1)}, f32[1,129,512]{1,2,0:T(8,128)S(1)}, u32[]{:S(2)}, u32[]{:S(2)}) collective-permute-start(f32[1,129,512]{1,2,0:T(8,128)S(1)} %pad_maximum_fusion.1), channel_id=1, source_target_pairs={{0,8},{8,16},{16,24},{24,32},{32,40},{40,48},{48,56},{56,64},{64,7... | collective-permute-start | bytes 792584 | tf_op jit(solution)/shard_map/ppermute | solution.py:110
  37.5 0.8 copy-start.12
  39.5 23.0 %collective-permute-start.3 = (f32[1,129,512]{1,2,0:T(8,128)S(1)}, f32[1,129,512]{1,2,0:T(8,128)S(1)}, u32[]{:S(2)}, u32[]{:S(2)}) collective-permute-start(f32[1,129,512]{1,2,0:T(8,128)S(1)} %pad_maximum_fusion.2), channel_id=1, source_target_pairs={{0,32},{8,40},{16,48},{24,56},{32,64},{40,72},{48,80},{56,88},{64,... | collective-permute-start | bytes 792584 | tf_op jit(solution)/shard_map/ppermute | solution.py:110
  62.9 14.2 %collective-permute-start.4 = (f32[1,129,512]{1,2,0:T(8,128)S(1)}, f32[1,129,512]{1,2,0:T(8,128)S(1)}, u32[]{:S(2)}, u32[]{:S(2)}) collective-permute-start(f32[1,129,512]{1,2,0:T(8,128)S(1)} %pad_maximum_fusion.3), channel_id=1, source_target_pairs={{0,64},{8,72},{16,80},{24,88},{32,96},{40,104},{48,112},{56,120},{... | collective-permute-start | bytes 792584 | tf_op jit(solution)/shard_map/ppermute | solution.py:110
  77.6 33.4 %collective-permute-start.6 = (f32[1,129,512]{1,2,0:T(8,128)S(1)}, f32[1,129,512]{1,2,0:T(8,128)S(1)}, u32[]{:S(2)}, u32[]{:S(2)}) collective-permute-start(f32[1,129,512]{1,2,0:T(8,128)S(1)} %pad_maximum_fusion.4), channel_id=1, source_target_pairs={{0,256},{8,264},{16,272},{24,280},{32,288},{40,296},{48,304},{56,3... | collective-permute-start | bytes 792584 | tf_op jit(solution)/shard_map/ppermute | solution.py:110
  100.1 22.0 %collective-permute-start.5 = (f32[1,129,512]{1,2,0:T(8,128)S(1)}, f32[1,129,512]{1,2,0:T(8,128)S(1)}, u32[]{:S(2)}, u32[]{:S(2)}) collective-permute-start(f32[1,129,512]{1,2,0:T(8,128)S(1)} %pad_maximum_fusion.4), channel_id=1, source_target_pairs={{0,128},{8,136},{16,144},{24,152},{32,160},{40,168},{48,176},{56,1... | collective-permute-start | bytes 792584 | tf_op jit(solution)/shard_map/ppermute | solution.py:110
  103.0 20.6 %collective-permute-start.7 = (f32[1,129,512]{1,2,0:T(8,128)S(1)}, f32[1,129,512]{1,2,0:T(8,128)S(1)}, u32[]{:S(2)}, u32[]{:S(2)}) collective-permute-start(f32[1,129,512]{1,2,0:T(8,128)S(1)} %pad_maximum_fusion.4), channel_id=1, source_target_pairs={{0,384},{8,392},{16,400},{24,408},{32,416},{40,424},{48,432},{56,4... | collective-permute-start | bytes 792584 | tf_op jit(solution)/shard_map/ppermute | solution.py:110
  125.7 11.1 %collective-permute-start.10 = (f32[1,128,512]{1,2,0:T(8,128)S(1)}, f32[1,128,512]{1,2,0:T(8,128)S(1)}, u32[]{:S(2)}, u32[]{:S(2)}) collective-permute-start(f32[1,128,512]{1,2,0:T(8,128)S(1)} %get-tuple-element.50), channel_id=1, source_target_pairs={{0,24},{8,32},{16,40},{24,48},{32,56},{40,64},{48,72},{56,80},{64,... | collective-permute-start | bytes 786440 | tf_op jit(solution)/shard_map/ppermute | solution.py:126
  127.0 9.8 %collective-permute-start.9 = (f32[1,128,512]{1,2,0:T(8,128)S(1)}, f32[1,128,512]{1,2,0:T(8,128)S(1)}, u32[]{:S(2)}, u32[]{:S(2)}) collective-permute-start(f32[1,128,512]{1,2,0:T(8,128)S(1)} %get-tuple-element.50), channel_id=1, source_target_pairs={{0,16},{8,24},{16,32},{24,40},{32,48},{40,56},{48,64},{56,72},{64,... | collective-permute-start | bytes 786440 | tf_op jit(solution)/shard_map/ppermute | solution.py:126
  128.3 11.1 %collective-permute-start.8 = (f32[1,128,512]{1,2,0:T(8,128)S(1)}, f32[1,128,512]{1,2,0:T(8,128)S(1)}, u32[]{:S(2)}, u32[]{:S(2)}) collective-permute-start(f32[1,128,512]{1,2,0:T(8,128)S(1)} %get-tuple-element.50), channel_id=1, source_target_pairs={{0,8},{8,16},{16,24},{24,32},{32,40},{40,48},{48,56},{56,64},{64,7... | collective-permute-start | bytes 786440 | tf_op jit(solution)/shard_map/ppermute | solution.py:126
  139.5 8.7 %collective-permute-start.11 = (f32[1,128,512]{1,2,0:T(8,128)S(1)}, f32[1,128,512]{1,2,0:T(8,128)S(1)}, u32[]{:S(2)}, u32[]{:S(2)}) collective-permute-start(f32[1,128,512]{1,2,0:T(8,128)S(1)} %get-tuple-element.48), channel_id=1, source_target_pairs={{0,32},{8,40},{16,48},{24,56},{32,64},{40,72},{48,80},{56,88},{64,... | collective-permute-start | bytes 786440 | tf_op jit(solution)/shard_map/ppermute | solution.py:126
  148.2 37.7 %copy-start.15 = (f32[1,128]{1,0:T(1,128)S(1)}, f32[1,128]{1,0:T(1,128)}, u32[]{:S(2)}) copy-start(f32[1,128]{1,0:T(1,128)} %param.11) | copy-start | bytes 1540
  148.3 37.8 %copy-start.11 = (f32[1,128,512]{2,1,0:T(8,128)S(1)}, f32[1,128,512]{2,1,0:T(8,128)}, u32[]{:S(2)}) copy-start(f32[1,128,512]{2,1,0:T(8,128)} %param.7) | copy-start | bytes 786436
  148.3 10.9 %collective-permute-start.12 = (f32[1,128,512]{1,2,0:T(8,128)S(1)}, f32[1,128,512]{1,2,0:T(8,128)S(1)}, u32[]{:S(2)}, u32[]{:S(2)}) collective-permute-start(f32[1,128,512]{1,2,0:T(8,128)S(1)} %multiply_add_fusion.12), channel_id=1, source_target_pairs={{0,64},{8,72},{16,80},{24,88},{32,96},{40,104},{48,112},{56,120},{... | collective-permute-start | bytes 786440 | tf_op jit(solution)/shard_map/ppermute | solution.py:126
  159.3 32.4 %collective-permute-start.15 = (f32[1,128,512]{1,2,0:T(8,128)S(1)}, f32[1,128,512]{1,2,0:T(8,128)S(1)}, u32[]{:S(2)}, u32[]{:S(2)}) collective-permute-start(f32[1,128,512]{1,2,0:T(8,128)S(1)} %get-tuple-element.46), channel_id=1, source_target_pairs={{0,384},{8,392},{16,400},{24,408},{32,416},{40,424},{48,432},{56,4... | collective-permute-start | bytes 786440 | tf_op jit(solution)/shard_map/ppermute | solution.py:126
  180.9 10.8 %collective-permute-start.14 = (f32[1,128,512]{1,2,0:T(8,128)S(1)}, f32[1,128,512]{1,2,0:T(8,128)S(1)}, u32[]{:S(2)}, u32[]{:S(2)}) collective-permute-start(f32[1,128,512]{1,2,0:T(8,128)S(1)} %get-tuple-element.46), channel_id=1, source_target_pairs={{0,256},{8,264},{16,272},{24,280},{32,288},{40,296},{48,304},{56,3... | collective-permute-start | bytes 786440 | tf_op jit(solution)/shard_map/ppermute | solution.py:126
  182.2 10.8 %collective-permute-start.13 = (f32[1,128,512]{1,2,0:T(8,128)S(1)}, f32[1,128,512]{1,2,0:T(8,128)}, u32[]{:S(2)}, u32[]{:S(2)}) collective-permute-start(f32[1,128,512]{1,2,0:T(8,128)S(1)} %get-tuple-element.46), channel_id=1, source_target_pairs={{0,128},{8,136},{16,144},{24,152},{32,160},{40,168},{48,176},{56,1... | collective-permute-start | bytes 786440 | tf_op jit(solution)/shard_map/ppermute | solution.py:126
  186.3 10.0 %copy-start.9 = (bf16[128,9,128]{0,2,1:T(8,128)(2,1)}, bf16[128,9,128]{0,2,1:T(8,128)(2,1)S(1)}, u32[]{:S(2)}) copy-start(bf16[128,9,128]{0,2,1:T(8,128)(2,1)S(1)} %rev.6) | copy-start | bytes 884740
  186.3 11.0 %copy-start.6 = (bf16[128,9,128]{0,2,1:T(8,128)(2,1)}, bf16[128,9,128]{0,2,1:T(8,128)(2,1)S(1)}, u32[]{:S(2)}) copy-start(bf16[128,9,128]{0,2,1:T(8,128)(2,1)S(1)} %rev.7) | copy-start | bytes 884740
  186.3 11.7 %copy-start.18 = (f32[128]{0:T(128)}, f32[128]{0:T(128)S(1)}, u32[]{:S(2)}) copy-start(f32[128]{0:T(128)S(1)} %broadcast_multiply_fusion) | copy-start | bytes 1540
  193.1 1.2 copy-start.21
  198.2 26.5 %collective-permute-start.18 = (f32[1,129,512]{1,2,0:T(8,128)S(1)}, f32[1,129,512]{1,2,0:T(8,128)}, u32[]{:S(2)}, u32[]{:S(2)}) collective-permute-start(f32[1,129,512]{1,2,0:T(8,128)S(1)} %pad_maximum_fusion.5), channel_id=1, source_target_pairs={{24,0},{32,8},{40,16},{48,24},{56,32},{64,40},{72,48},{80,56},{88,... | collective-permute-start | bytes 792584 | tf_op jit(solution)/shard_map/ppermute | solution.py:110
  200.0 25.7 %collective-permute-start.17 = (f32[1,129,512]{1,2,0:T(8,128)S(1)}, f32[1,129,512]{1,2,0:T(8,128)}, u32[]{:S(2)}, u32[]{:S(2)}) collective-permute-start(f32[1,129,512]{1,2,0:T(8,128)S(1)} %pad_maximum_fusion.5), channel_id=1, source_target_pairs={{16,0},{24,8},{32,16},{40,24},{48,32},{56,40},{64,48},{72,56},{80,... | collective-permute-start | bytes 792584 | tf_op jit(solution)/shard_map/ppermute | solution.py:110
  201.3 25.3 %collective-permute-start.16 = (f32[1,129,512]{1,2,0:T(8,128)S(1)}, f32[1,129,512]{1,2,0:T(8,128)}, u32[]{:S(2)}, u32[]{:S(2)}) collective-permute-start(f32[1,129,512]{1,2,0:T(8,128)S(1)} %pad_maximum_fusion.5), channel_id=1, source_target_pairs={{8,0},{16,8},{24,16},{32,24},{40,32},{48,40},{56,48},{64,56},{72,6... | collective-permute-start | bytes 792584 | tf_op jit(solution)/shard_map/ppermute | solution.py:110
  227.7 2.7 copy-start.17
  229.0 13.0 %collective-permute-start.19 = (f32[1,129,512]{1,2,0:T(8,128)S(1)}, f32[1,129,512]{1,2,0:T(8,128)}, u32[]{:S(2)}, u32[]{:S(2)}) collective-permute-start(f32[1,129,512]{1,2,0:T(8,128)S(1)} %pad_maximum_fusion.6), channel_id=1, source_target_pairs={{32,0},{40,8},{48,16},{56,24},{64,32},{72,40},{80,48},{88,56},{96,... | collective-permute-start | bytes 792584 | tf_op jit(solution)/shard_map/ppermute | solution.py:110
  242.9 2.5 copy-start.16
  244.1 27.7 %collective-permute-start.20 = (f32[1,129,512]{1,2,0:T(8,128)S(1)}, f32[1,129,512]{1,2,0:T(8,128)S(1)}, u32[]{:S(2)}, u32[]{:S(2)}) collective-permute-start(f32[1,129,512]{1,2,0:T(8,128)S(1)} %pad_maximum_fusion.7), channel_id=1, source_target_pairs={{64,0},{72,8},{80,16},{88,24},{96,32},{104,40},{112,48},{120,56},{... | collective-permute-start | bytes 792584 | tf_op jit(solution)/shard_map/ppermute | solution.py:110
  271.8 0.8 copy-start.13
  273.9 25.6 %collective-permute-start.22 = (f32[1,129,512]{1,2,0:T(8,128)S(1)}, f32[1,129,512]{1,2,0:T(8,128)S(1)}, u32[]{:S(2)}, u32[]{:S(2)}) collective-permute-start(f32[1,129,512]{1,2,0:T(8,128)S(1)} %pad_maximum_fusion.8), channel_id=1, source_target_pairs={{256,0},{264,8},{272,16},{280,24},{288,32},{296,40},{304,48},{312,... | collective-permute-start | bytes 792584 | tf_op jit(solution)/shard_map/ppermute | solution.py:110
  275.4 24.2 %collective-permute-start.21 = (f32[1,129,512]{1,2,0:T(8,128)S(1)}, f32[1,129,512]{1,2,0:T(8,128)S(1)}, u32[]{:S(2)}, u32[]{:S(2)}) collective-permute-start(f32[1,129,512]{1,2,0:T(8,128)S(1)} %pad_maximum_fusion.8), channel_id=1, source_target_pairs={{128,0},{136,8},{144,16},{152,24},{160,32},{168,40},{176,48},{184,... | collective-permute-start | bytes 792584 | tf_op jit(solution)/shard_map/ppermute | solution.py:110
  276.8 34.4 %collective-permute-start.23 = (f32[1,129,512]{1,2,0:T(8,128)S(1)}, f32[1,129,512]{1,2,0:T(8,128)S(1)}, u32[]{:S(2)}, u32[]{:S(2)}) collective-permute-start(f32[1,129,512]{1,2,0:T(8,128)S(1)} %pad_maximum_fusion.8), channel_id=1, source_target_pairs={{384,0},{392,8},{400,16},{408,24},{416,32},{424,40},{432,48},{440,... | collective-permute-start | bytes 792584 | tf_op jit(solution)/shard_map/ppermute | solution.py:110
  311.2 1.0 copy-start.10
  311.2 1.0 copy-start.22
  312.8 1.0 copy-start.7
  314.4 0.7 copy-start.19
  315.1 14.6 %collective-permute-start.26 = (f32[1,128,512]{1,2,0:T(8,128)S(1)}, f32[1,128,512]{1,2,0:T(8,128)S(1)}, u32[]{:S(2)}, u32[]{:S(2)}) collective-permute-start(f32[1,128,512]{1,2,0:T(8,128)S(1)} %get-tuple-element.24), channel_id=1, source_target_pairs={{24,0},{32,8},{40,16},{48,24},{56,32},{64,40},{72,48},{80,56},{88,... | collective-permute-start | bytes 786440 | tf_op jit(solution)/shard_map/ppermute | solution.py:126
  316.4 16.5 %collective-permute-start.25 = (f32[1,128,512]{1,2,0:T(8,128)S(1)}, f32[1,128,512]{1,2,0:T(8,128)S(1)}, u32[]{:S(2)}, u32[]{:S(2)}) collective-permute-start(f32[1,128,512]{1,2,0:T(8,128)S(1)} %get-tuple-element.24), channel_id=1, source_target_pairs={{16,0},{24,8},{32,16},{40,24},{48,32},{56,40},{64,48},{72,56},{80,... | collective-permute-start | bytes 786440 | tf_op jit(solution)/shard_map/ppermute | solution.py:126
  317.7 15.2 %collective-permute-start.24 = (f32[1,128,512]{1,2,0:T(8,128)S(1)}, f32[1,128,512]{1,2,0:T(8,128)S(1)}, u32[]{:S(2)}, u32[]{:S(2)}) collective-permute-start(f32[1,128,512]{1,2,0:T(8,128)S(1)} %get-tuple-element.24), channel_id=1, source_target_pairs={{8,0},{16,8},{24,16},{32,24},{40,32},{48,40},{56,48},{64,56},{72,6... | collective-permute-start | bytes 786440 | tf_op jit(solution)/shard_map/ppermute | solution.py:126
  319.4 27.2 %copy-start = (bf16[1,1152,512]{1,2,0:T(8,128)(2,1)}, bf16[1,1152,512]{1,2,0:T(8,128)(2,1)S(1)}, u32[]{:S(2)}) copy-start(bf16[1,1152,512]{1,2,0:T(8,128)(2,1)S(1)} %get-tuple-element.78) | copy-start | bytes 3538948
  332.9 13.6 %collective-permute-start.27 = (f32[1,128,512]{1,2,0:T(8,128)S(1)}, f32[1,128,512]{1,2,0:T(8,128)S(1)}, u32[]{:S(2)}, u32[]{:S(2)}) collective-permute-start(f32[1,128,512]{1,2,0:T(8,128)S(1)} %get-tuple-element.22), channel_id=1, source_target_pairs={{32,0},{40,8},{48,16},{56,24},{64,32},{72,40},{80,48},{88,56},{96,... | collective-permute-start | bytes 786440 | tf_op jit(solution)/shard_map/ppermute | solution.py:126
  346.6 15.7 %collective-permute-start.28 = (f32[1,128,512]{1,2,0:T(8,128)S(1)}, f32[1,128,512]{1,2,0:T(8,128)S(1)}, u32[]{:S(2)}, u32[]{:S(2)}) collective-permute-start(f32[1,128,512]{1,2,0:T(8,128)S(1)} %multiply_add_fusion.2), channel_id=1, source_target_pairs={{64,0},{72,8},{80,16},{88,24},{96,32},{104,40},{112,48},{120,56},{... | collective-permute-start | bytes 786440 | tf_op jit(solution)/shard_map/ppermute | solution.py:126
  362.3 15.3 %collective-permute-start.31 = (f32[1,128,512]{1,2,0:T(8,128)S(1)}, f32[1,128,512]{1,2,0:T(8,128)S(1)}, u32[]{:S(2)}, u32[]{:S(2)}) collective-permute-start(f32[1,128,512]{1,2,0:T(8,128)S(1)} %get-tuple-element.20), channel_id=1, source_target_pairs={{384,0},{392,8},{400,16},{408,24},{416,32},{424,40},{432,48},{440,... | collective-permute-start | bytes 786440 | tf_op jit(solution)/shard_map/ppermute | solution.py:126
  363.6 14.0 %collective-permute-start.30 = (f32[1,128,512]{1,2,0:T(8,128)S(1)}, f32[1,128,512]{1,2,0:T(8,128)S(1)}, u32[]{:S(2)}, u32[]{:S(2)}) collective-permute-start(f32[1,128,512]{1,2,0:T(8,128)S(1)} %get-tuple-element.20), channel_id=1, source_target_pairs={{256,0},{264,8},{272,16},{280,24},{288,32},{296,40},{304,48},{312,... | collective-permute-start | bytes 786440 | tf_op jit(solution)/shard_map/ppermute | solution.py:126
  364.9 12.7 %collective-permute-start.29 = (f32[1,128,512]{1,2,0:T(8,128)S(1)}, f32[1,128,512]{1,2,0:T(8,128)S(1)}, u32[]{:S(2)}, u32[]{:S(2)}) collective-permute-start(f32[1,128,512]{1,2,0:T(8,128)S(1)} %get-tuple-element.20), channel_id=1, source_target_pairs={{128,0},{136,8},{144,16},{152,24},{160,32},{168,40},{176,48},{184,... | collective-permute-start | bytes 786440 | tf_op jit(solution)/shard_map/ppermute | solution.py:126
  379.7 1.7 copy-start.2
  379.7 1.3 copy-start.1
  381.8 4.2 copy-start.3
  381.9 5.8 %collective-permute-start.32 = (f32[1184,128]{1,0:T(8,128)S(1)}, f32[1184,128]{1,0:T(8,128)}, u32[]{:S(2)}, u32[]{:S(2)}) collective-permute-start(f32[1184,128]{1,0:T(8,128)S(1)} %constant_dynamic-slice_fusion), channel_id=1, source_target_pairs={{0,1},{1,0},{2,3},{3,2},{4,5},{5,4},{6,7},{7,6},{8,9},{9,8},{10,11... | collective-permute-start | bytes 1818632 | tf_op jit(solution)/shard_map/ppermute | solution.py:150
  386.2 27.1 %copy-start.8 = (bf16[128,9,128]{0,2,1:T(8,128)(2,1)S(1)}, bf16[128,9,128]{0,2,1:T(8,128)(2,1)}, u32[]{:S(2)}) copy-start(bf16[128,9,128]{0,2,1:T(8,128)(2,1)} %copy-done.6) | copy-start | bytes 884740
  386.2 27.1 %copy-start.23 = (pred[8,5]{0,1:T(8,128)(4,1)S(1)}, pred[8,5]{0,1:T(8,128)(4,1)}, u32[]{:S(2)}) copy-start(pred[8,5]{0,1:T(8,128)(4,1)} %constant.205) | copy-start | bytes 124
  388.9 25.1 %collective-permute-start.33 = (f32[296,128]{1,0:T(8,128)S(1)}, f32[296,128]{1,0:T(8,128)S(1)}, u32[]{:S(2)}, u32[]{:S(2)}) collective-permute-start(f32[296,128]{1,0:T(8,128)S(1)} %get-tuple-element.70), channel_id=1, source_target_pairs={{0,2},{1,3},{2,4},{3,5},{4,6},{5,7},{6,0},{7,1},{8,10},{9,11},{10,... | collective-permute-start | bytes 454664 | tf_op jit(solution)/shard_map/ppermute | solution.py:157
  397.8 24.3 %collective-permute-start.35 = (f32[296,128]{1,0:T(8,128)S(1)}, f32[296,128]{1,0:T(8,128)S(1)}, u32[]{:S(2)}, u32[]{:S(2)}) collective-permute-start(f32[296,128]{1,0:T(8,128)S(1)} %get-tuple-element.71), channel_id=1, source_target_pairs={{0,6},{1,7},{2,0},{3,1},{4,2},{5,3},{6,4},{7,5},{8,14},{9,15},{10,... | collective-permute-start | bytes 454664 | tf_op jit(solution)/shard_map/ppermute | solution.py:157
  403.1 30.1 %collective-permute-start.34 = (f32[296,128]{1,0:T(8,128)S(1)}, f32[296,128]{1,0:T(8,128)S(1)}, u32[]{:S(2)}, u32[]{:S(2)}) collective-permute-start(f32[296,128]{1,0:T(8,128)S(1)} %get-tuple-element.72), channel_id=1, source_target_pairs={{0,4},{1,5},{2,6},{3,7},{4,0},{5,1},{6,2},{7,3},{8,12},{9,13},{10,... | collective-permute-start | bytes 454664 | tf_op jit(solution)/shard_map/ppermute | solution.py:157
  433.3 37.7 %collective-permute-start.38 = (f32[296,128]{1,0:T(8,128)S(1)}, f32[296,128]{1,0:T(8,128)S(1)}, u32[]{:S(2)}, u32[]{:S(2)}) collective-permute-start(f32[296,128]{1,0:T(8,128)S(1)} %fusion.122), channel_id=1, source_target_pairs={{0,6},{1,7},{2,0},{3,1},{4,2},{5,3},{6,4},{7,5},{8,14},{9,15},{10,... | collective-permute-start | bytes 454664 | tf_op jit(solution)/shard_map/ppermute | solution.py:161
  435.2 35.8 %collective-permute-start.37 = (f32[296,128]{1,0:T(8,128)S(1)}, f32[296,128]{1,0:T(8,128)S(1)}, u32[]{:S(2)}, u32[]{:S(2)}) collective-permute-start(f32[296,128]{1,0:T(8,128)S(1)} %fusion.122), channel_id=1, source_target_pairs={{0,4},{1,5},{2,6},{3,7},{4,0},{5,1},{6,2},{7,3},{8,12},{9,13},{10,... | collective-permute-start | bytes 454664 | tf_op jit(solution)/shard_map/ppermute | solution.py:161
  440.0 31.0 %collective-permute-start.36 = (f32[296,128]{1,0:T(8,128)S(1)}, f32[296,128]{1,0:T(8,128)S(1)}, u32[]{:S(2)}, u32[]{:S(2)}) collective-permute-start(f32[296,128]{1,0:T(8,128)S(1)} %fusion.122), channel_id=1, source_target_pairs={{0,2},{1,3},{2,4},{3,5},{4,6},{5,7},{6,0},{7,1},{8,10},{9,11},{10,... | collective-permute-start | bytes 454664 | tf_op jit(solution)/shard_map/ppermute | solution.py:161
  471.1 4.4 collective-permute-start.39
  473.5 1.0 copy-start.4

commit v8 on v4

--- a/solution.py
+++ b/solution.py
@@ -27,27 +27,49 @@
     return jnp.concatenate(pieces, axis=1)
 
 
-def flip_weight(weight):
+def shifted_sum(spread, inverse):
+    pixels = HEIGHT * WIDTH
+    margin = WIDTH + 1
+    across = jnp.arange(pixels) % WIDTH
+    summed = None
+    tap_index = 0
+    for offset_y in (-1, 0, 1):
+        for offset_x in (-1, 0, 1):
+            shift_by = offset_y * WIDTH + offset_x
+            window = spread[:, tap_index]
+            if inverse:
+                inside = (across + offset_x >= 0) & (across + offset_x < WIDTH)
+                masked = jnp.where(inside, window, jnp.zeros_like(window))
+                placed = jnp.pad(masked, ((0, 0), (0, 0), (margin + shift_by, margin - shift_by)))
+                piece = placed[:, :, margin : margin + pixels]
+            else:
+                padded = jnp.pad(window, ((0, 0), (0, 0), (margin, margin)))
+                piece = padded[:, :, margin + shift_by : margin + shift_by + pixels]
+                inside = (across + offset_x >= 0) & (across + offset_x < WIDTH)
+                piece = jnp.where(inside, piece, jnp.zeros_like(piece))
+            summed = piece if summed is None else summed + piece
+            tap_index = tap_index + 1
+    return summed
+
+
+def forward_layer(current, weight, bias_row):
     channels = weight.shape[0]
-    taps = weight.reshape(channels, 9, channels)[:, ::-1, :]
-    return jnp.transpose(taps, (2, 1, 0)).reshape(channels, 9 * channels)
-
-
-def forward_layer(current, weight, bias_row):
-    stacked = columns(current)
-    pre_act = (
-        jnp.einsum("ok,bkp->bop", weight, stacked, preferred_element_type=jnp.float32)
-        + bias_row[None, :, None]
+    per_tap = jnp.transpose(weight.reshape(channels, 9, channels), (1, 0, 2))
+    spread = jnp.einsum(
+        "toc,bcp->btop", per_tap, current.astype(jnp.bfloat16), preferred_element_type=jnp.float32
     )
+    pre_act = shifted_sum(spread, False) + bias_row[None, :, None]
     activity = jnp.tanh(pre_act)
-    return (current + step_size * activity, activity, stacked)
-
-
-def backward_layer(adjoint, activity, flipped):
+    return (current + step_size * activity, activity, current)
+
+
+def backward_layer(adjoint, activity, weight):
     scaled = step_size * (1.0 - activity * activity) * adjoint
     rounded = scaled.astype(jnp.bfloat16)
-    gathered = columns(rounded)
-    back = jnp.einsum("ck,bkp->bcp", flipped, gathered, preferred_element_type=jnp.float32)
+    channels = weight.shape[0]
+    per_tap = weight.reshape(channels, 9, channels)
+    spread = jnp.einsum("otc,bop->btcp", per_tap, rounded, preferred_element_type=jnp.float32)
+    back = shifted_sum(spread, True)
     return (adjoint + back, rounded, scaled)
 
 
@@ -62,10 +84,10 @@
     return (current, stored)
 
 
-def adjoint_block(finish, stored, flipped_list):
+def adjoint_block(finish, stored, weight_list):
     adjoint = finish
     for layer_index in range(len(stored) - 1, -1, -1):
-        adjoint = backward_layer(adjoint, stored[layer_index][1], flipped_list[layer_index])[0]
+        adjoint = backward_layer(adjoint, stored[layer_index][1], weight_list[layer_index])[0]
     return adjoint
 
 
@@ -157,9 +179,7 @@
 def per_device(initial_state, cotangent, conv_weight, conv_bias, block_gain, adjoint_gain):
     gain_row = block_gain[0]
     back_row = adjoint_gain[0]
-    flipped_list = [
-        flip_weight(conv_weight[layer_index]) for layer_index in range(conv_weight.shape[0])
-    ]
+    weight_list = [conv_weight[layer_index] for layer_index in range(conv_weight.shape[0])]
     c_points = initial_state
     following = initial_state
     for sweep_index in range(ITERS):
@@ -175,7 +195,7 @@
     target = cotangent
     previous = cotangent
     for sweep_index in range(ITERS):
-        start_adj = adjoint_block(target, stored, flipped_list)
+        start_adj = adjoint_block(target, stored, weight_list)
         residual = start_adj - previous
         if sweep_index == 0:
             error, factors = exclusive_scan_first(back_row, residual, "layer", True)
@@ -188,10 +208,13 @@
     bias_parts = []
     for layer_index in range(len(stored) - 1, -1, -1):
         adjoint, rounded, scaled = backward_layer(
-            adjoint, stored[layer_index][1], flipped_list[layer_index]
+            adjoint, stored[layer_index][1], weight_list[layer_index]
         )
         weight_part = jnp.einsum(
-            "bop,bkp->ok", rounded, stored[layer_index][0], preferred_element_type=jnp.float32
+            "bop,bkp->ok",
+            rounded,
+            columns(stored[layer_index][0]),
+            preferred_element_type=jnp.float32,
         )
         bias_part = jnp.sum(scaled, axis=(0, 2))
         weight_parts.insert(0, weight_part)

time: 395 us -> 478 us (1.21)
  the two profiles are of different devices: /device:TPU:1 before, /device:TPU:15 now
where the time goes in v8:
time: 478 us; the launch traced here: 476 us
  waiting for transfers between devices  252 us (53%)
  starting transfers between devices  181 us (38%)
  local copies, waits for them, and re-layouts  17.9 us (4%)
  other arithmetic  15.4 us (3%)
  matrix products  7.45 us (2%)
    ppermute x12, waiting for transfers between devices, exclusive_scan_first(): received = lax.ppermute(packed, axis, scan_pairs(count, d, reverse))  140 us
    ppermute x12, waiting for transfers between devices, exclusive_scan_again(): received = lax.ppermute(sending, axis, scan_pairs(count, d, reverse))  85.4 us
    ppermute x12, starting transfers between devices, exclusive_scan_first(): received = lax.ppermute(packed, axis, scan_pairs(count, d, reverse))  54.8 us
    ppermute x6, starting transfers between devices, batch_sum(): got = lax.ppermute(sent, axis, ring)  46.7 us
    ppermute x12, starting transfers between devices, exclusive_scan_again(): received = lax.ppermute(sending, axis, scan_pairs(count, d, reverse))  41.8 us
    ppermute x6, waiting for transfers between devices, batch_sum(): got = lax.ppermute(sent, axis, ring)  24.9 us
    ppermute x1, starting transfers between devices, batch_sum(): half = keep + lax.ppermute(give, axis, partner)  22.2 us
    ppermute x1, starting transfers between devices, batch_sum(): other = lax.ppermute(half, axis, partner)  15.8 us
  transfers between devices with their start and end apart: 32, of which 32 were waited for; matrix products, arithmetic and copies ran while one was open for 1% of the time, Pallas kernels for 0%

profile of v8, /device:TPU:15, one launch (start us, length us, event | category | flops | bytes accessed | tf_op | source)
XLA Modules:
  0.0 476.4 jit_solution(4894762505399037085)
XLA Ops:
  5.5 1.6 convolution_bitcast_fusion.11
  7.1 1.3 slice_bitcast_fusion.99
  8.8 2.0 fusion.22
  12.5 3.5 collective-permute-start
  15.9 11.2 %collective-permute-done = f32[1,129,512]{1,2,0:T(8,128)S(1)} collective-permute-done((f32[1,129,512]{1,2,0:T(8,128)S(1)}, f32[1,129,512]{1,2,0:T(8,128)S(1)}, u32[]{:S(2)}, u32[]{:S(2)}) %collective-permute-start) | collective-permute-done | bytes 264224 | tf_op jit(solution)/shard_map/ppermute | solution.py:119
  27.5 4.4 collective-permute-start.1
  31.9 10.9 %collective-permute-done.1 = f32[1,129,512]{1,2,0:T(8,128)S(1)} collective-permute-done((f32[1,129,512]{1,2,0:T(8,128)S(1)}, f32[1,129,512]{1,2,0:T(8,128)S(1)}, u32[]{:S(2)}, u32[]{:S(2)}) %collective-permute-start.1) | collective-permute-done | bytes 264224 | tf_op jit(solution)/shard_map/ppermute | solution.py:119
  44.8 3.5 collective-permute-start.2
  48.3 12.2 %collective-permute-done.2 = f32[1,129,512]{1,2,0:T(8,128)S(1)} collective-permute-done((f32[1,129,512]{1,2,0:T(8,128)S(1)}, f32[1,129,512]{1,2,0:T(8,128)S(1)}, u32[]{:S(2)}, u32[]{:S(2)}) %collective-permute-start.2) | collective-permute-done | bytes 264224 | tf_op jit(solution)/shard_map/ppermute | solution.py:119
  60.9 2.0 collective-permute-start.3
  62.9 25.2 %collective-permute-done.3 = f32[1,129,512]{1,2,0:T(8,128)S(1)} collective-permute-done((f32[1,129,512]{1,2,0:T(8,128)S(1)}, f32[1,129,512]{1,2,0:T(8,128)S(1)}, u32[]{:S(2)}, u32[]{:S(2)}) %collective-permute-start.3) | collective-permute-done | bytes 264224 | tf_op jit(solution)/shard_map/ppermute | solution.py:119
  90.1 3.2 collective-permute-start.4
  93.4 11.7 %collective-permute-done.4 = f32[1,129,512]{1,2,0:T(8,128)S(1)} collective-permute-done((f32[1,129,512]{1,2,0:T(8,128)S(1)}, f32[1,129,512]{1,2,0:T(8,128)S(1)}, u32[]{:S(2)}, u32[]{:S(2)}) %collective-permute-start.4) | collective-permute-done | bytes 264224 | tf_op jit(solution)/shard_map/ppermute | solution.py:119
  105.4 4.1 collective-permute-start.5
  109.5 9.8 %collective-permute-done.5 = f32[1,129,512]{1,2,0:T(8,128)S(1)} collective-permute-done((f32[1,129,512]{1,2,0:T(8,128)S(1)}, f32[1,129,512]{1,2,0:T(8,128)S(1)}, u32[]{:S(2)}, u32[]{:S(2)}) %collective-permute-start.5) | collective-permute-done | bytes 264224 | tf_op jit(solution)/shard_map/ppermute | solution.py:119
  121.5 4.2 collective-permute-start.6
  125.7 5.4 %collective-permute-done.6 = f32[1,128,512]{1,2,0:T(8,128)S(1)} collective-permute-done((f32[1,128,512]{1,2,0:T(8,128)S(1)}, f32[1,128,512]{1,2,0:T(8,128)S(1)}, u32[]{:S(2)}, u32[]{:S(2)}) %collective-permute-start.6) | collective-permute-done | bytes 262176 | tf_op jit(solution)/shard_map/ppermute | solution.py:131
  131.1 1.9 collective-permute-start.7
  133.0 10.3 %collective-permute-done.7 = f32[1,128,512]{1,2,0:T(8,128)S(1)} collective-permute-done((f32[1,128,512]{1,2,0:T(8,128)S(1)}, f32[1,128,512]{1,2,0:T(8,128)S(1)}, u32[]{:S(2)}, u32[]{:S(2)}) %collective-permute-start.7) | collective-permute-done | bytes 262176 | tf_op jit(solution)/shard_map/ppermute | solution.py:131
  143.4 1.9 collective-permute-start.8
  145.3 8.3 %collective-permute-done.8 = f32[1,128,512]{1,2,0:T(8,128)S(1)} collective-permute-done((f32[1,128,512]{1,2,0:T(8,128)S(1)}, f32[1,128,512]{1,2,0:T(8,128)S(1)}, u32[]{:S(2)}, u32[]{:S(2)}) %collective-permute-start.8) | collective-permute-done | bytes 262176 | tf_op jit(solution)/shard_map/ppermute | solution.py:131
  153.7 2.8 collective-permute-start.9
  156.6 7.2 %collective-permute-done.9 = f32[1,128,512]{1,2,0:T(8,128)S(1)} collective-permute-done((f32[1,128,512]{1,2,0:T(8,128)S(1)}, f32[1,128,512]{1,2,0:T(8,128)S(1)}, u32[]{:S(2)}, u32[]{:S(2)}) %collective-permute-start.9) | collective-permute-done | bytes 262176 | tf_op jit(solution)/shard_map/ppermute | solution.py:131
  163.9 4.3 collective-permute-start.10
  168.2 4.4 collective-permute-done.10
  172.7 5.2 %collective-permute-start.11 = (f32[1,128,512]{1,2,0:T(8,128)S(1)}, f32[1,128,512]{1,2,0:T(8,128)S(1)}, u32[]{:S(2)}, u32[]{:S(2)}) collective-permute-start(f32[1,128,512]{1,2,0:T(8,128)S(1)} %get-tuple-element.44), channel_id=1, source_target_pairs={{0,256},{8,264},{16,272},{24,280},{32,288},{40,296},{48,304},{56,3... | collective-permute-start | bytes 786440 | tf_op jit(solution)/shard_map/ppermute | solution.py:131
  179.0 2.3 collective-permute-done.11
  186.8 9.1 %collective-permute-start.12 = (f32[1,129,512]{1,2,0:T(8,128)S(1)}, f32[1,129,512]{1,2,0:T(8,128)S(1)}, u32[]{:S(2)}, u32[]{:S(2)}) collective-permute-start(f32[1,129,512]{1,2,0:T(8,128)S(1)} %pad_maximum_fusion.7), channel_id=1, source_target_pairs={{8,0},{16,8},{24,16},{32,24},{40,32},{48,40},{56,48},{64,56},{72,6... | collective-permute-start | bytes 792584 | tf_op jit(solution)/shard_map/ppermute | solution.py:119
  195.9 7.7 %collective-permute-done.12 = f32[1,129,512]{1,2,0:T(8,128)S(1)} collective-permute-done((f32[1,129,512]{1,2,0:T(8,128)S(1)}, f32[1,129,512]{1,2,0:T(8,128)S(1)}, u32[]{:S(2)}, u32[]{:S(2)}) %collective-permute-start.12) | collective-permute-done | bytes 264224 | tf_op jit(solution)/shard_map/ppermute | solution.py:119
  203.9 7.6 %collective-permute-start.13 = (f32[1,129,512]{1,2,0:T(8,128)S(1)}, f32[1,129,512]{1,2,0:T(8,128)S(1)}, u32[]{:S(2)}, u32[]{:S(2)}) collective-permute-start(f32[1,129,512]{1,2,0:T(8,128)S(1)} %pad_maximum_fusion.8), channel_id=1, source_target_pairs={{16,0},{24,8},{32,16},{40,24},{48,32},{56,40},{64,48},{72,56},{80,... | collective-permute-start | bytes 792584 | tf_op jit(solution)/shard_map/ppermute | solution.py:119
  211.5 6.1 %collective-permute-done.13 = f32[1,129,512]{1,2,0:T(8,128)S(1)} collective-permute-done((f32[1,129,512]{1,2,0:T(8,128)S(1)}, f32[1,129,512]{1,2,0:T(8,128)S(1)}, u32[]{:S(2)}, u32[]{:S(2)}) %collective-permute-start.13) | collective-permute-done | bytes 264224 | tf_op jit(solution)/shard_map/ppermute | solution.py:119
  218.0 12.2 %collective-permute-start.14 = (f32[1,129,512]{1,2,0:T(8,128)S(1)}, f32[1,129,512]{1,2,0:T(8,128)S(1)}, u32[]{:S(2)}, u32[]{:S(2)}) collective-permute-start(f32[1,129,512]{1,2,0:T(8,128)S(1)} %pad_maximum_fusion.9), channel_id=1, source_target_pairs={{32,0},{40,8},{48,16},{56,24},{64,32},{72,40},{80,48},{88,56},{96,... | collective-permute-start | bytes 792584 | tf_op jit(solution)/shard_map/ppermute | solution.py:119
  230.3 7.3 %collective-permute-done.14 = f32[1,129,512]{1,2,0:T(8,128)S(1)} collective-permute-done((f32[1,129,512]{1,2,0:T(8,128)S(1)}, f32[1,129,512]{1,2,0:T(8,128)S(1)}, u32[]{:S(2)}, u32[]{:S(2)}) %collective-permute-start.14) | collective-permute-done | bytes 264224 | tf_op jit(solution)/shard_map/ppermute | solution.py:119
  238.0 1.9 collective-permute-start.15
  239.9 19.7 %collective-permute-done.15 = f32[1,129,512]{1,2,0:T(8,128)S(1)} collective-permute-done((f32[1,129,512]{1,2,0:T(8,128)S(1)}, f32[1,129,512]{1,2,0:T(8,128)S(1)}, u32[]{:S(2)}, u32[]{:S(2)}) %collective-permute-start.15) | collective-permute-done | bytes 264224 | tf_op jit(solution)/shard_map/ppermute | solution.py:119
  261.7 1.9 collective-permute-start.16
  263.6 8.3 %collective-permute-done.16 = f32[1,129,512]{1,2,0:T(8,128)S(1)} collective-permute-done((f32[1,129,512]{1,2,0:T(8,128)S(1)}, f32[1,129,512]{1,2,0:T(8,128)S(1)}, u32[]{:S(2)}, u32[]{:S(2)}) %collective-permute-start.16) | collective-permute-done | bytes 264224 | tf_op jit(solution)/shard_map/ppermute | solution.py:119
  273.6 10.2 %collective-permute-done.17 = f32[1,129,512]{1,2,0:T(8,128)S(1)} collective-permute-done((f32[1,129,512]{1,2,0:T(8,128)S(1)}, f32[1,129,512]{1,2,0:T(8,128)S(1)}, u32[]{:S(2)}, u32[]{:S(2)}) %collective-permute-start.17) | collective-permute-done | bytes 264224 | tf_op jit(solution)/shard_map/ppermute | solution.py:119
  285.9 1.9 collective-permute-start.18
  287.8 11.2 %collective-permute-done.18 = f32[1,128,512]{1,2,0:T(8,128)S(1)} collective-permute-done((f32[1,128,512]{1,2,0:T(8,128)S(1)}, f32[1,128,512]{1,2,0:T(8,128)S(1)}, u32[]{:S(2)}, u32[]{:S(2)}) %collective-permute-start.18) | collective-permute-done | bytes 262176 | tf_op jit(solution)/shard_map/ppermute | solution.py:131
  299.1 1.9 collective-permute-start.19
  301.2 7.5 %collective-permute-done.19 = f32[1,128,512]{1,2,0:T(8,128)S(1)} collective-permute-done((f32[1,128,512]{1,2,0:T(8,128)S(1)}, f32[1,128,512]{1,2,0:T(8,128)S(1)}, u32[]{:S(2)}, u32[]{:S(2)}) %collective-permute-start.19) | collective-permute-done | bytes 262176 | tf_op jit(solution)/shard_map/ppermute | solution.py:131
  308.7 11.7 %collective-permute-start.20 = (f32[1,128,512]{1,2,0:T(8,128)S(1)}, f32[1,128,512]{1,2,0:T(8,128)S(1)}, u32[]{:S(2)}, u32[]{:S(2)}) collective-permute-start(f32[1,128,512]{1,2,0:T(8,128)S(1)} %multiply_add_fusion.6), channel_id=1, source_target_pairs={{32,0},{40,8},{48,16},{56,24},{64,32},{72,40},{80,48},{88,56},{96,... | collective-permute-start | bytes 786440 | tf_op jit(solution)/shard_map/ppermute | solution.py:131
  320.8 2.9 collective-permute-done.20
  323.8 2.6 collective-permute-start.21
  326.8 13.8 %collective-permute-done.21 = f32[1,128,512]{1,2,0:T(8,128)S(1)} collective-permute-done((f32[1,128,512]{1,2,0:T(8,128)S(1)}, f32[1,128,512]{1,2,0:T(8,128)S(1)}, u32[]{:S(2)}, u32[]{:S(2)}) %collective-permute-start.21) | collective-permute-done | bytes 262176 | tf_op jit(solution)/shard_map/ppermute | solution.py:131
  340.6 1.9 collective-permute-start.22
  343.0 4.8 %collective-permute-done.22 = f32[1,128,512]{1,2,0:T(8,128)S(1)} collective-permute-done((f32[1,128,512]{1,2,0:T(8,128)S(1)}, f32[1,128,512]{1,2,0:T(8,128)S(1)}, u32[]{:S(2)}, u32[]{:S(2)}) %collective-permute-start.22) | collective-permute-done | bytes 262176 | tf_op jit(solution)/shard_map/ppermute | solution.py:131
  349.5 7.2 %collective-permute-done.23 = f32[1,128,512]{1,2,0:T(8,128)S(1)} collective-permute-done((f32[1,128,512]{1,2,0:T(8,128)S(1)}, f32[1,128,512]{1,2,0:T(8,128)S(1)}, u32[]{:S(2)}, u32[]{:S(2)}) %collective-permute-start.23) | collective-permute-done | bytes 262176 | tf_op jit(solution)/shard_map/ppermute | solution.py:131
  359.5 22.2 %collective-permute-start.24 = (f32[1184,128]{1,0:T(8,128)S(1)}, f32[1184,128]{1,0:T(8,128)S(1)}, u32[]{:S(2)}, u32[]{:S(2)}) collective-permute-start(f32[1184,128]{1,0:T(8,128)S(1)} %constant_dynamic-slice_fusion.3), channel_id=1, source_target_pairs={{0,1},{1,0},{2,3},{3,2},{4,5},{5,4},{6,7},{7,6},{8,9},{9,8},{10,11... | collective-permute-start | bytes 1818632 | tf_op jit(solution)/shard_map/ppermute | solution.py:152
  381.9 1.5 collective-permute-done.24
  383.5 11.2 %collective-permute-start.25 = (f32[296,128]{1,0:T(8,128)S(1)}, f32[296,128]{1,0:T(8,128)S(1)}, u32[]{:S(2)}, u32[]{:S(2)}) collective-permute-start(f32[296,128]{1,0:T(8,128)S(1)} %get-tuple-element.197), channel_id=1, source_target_pairs={{0,2},{1,7},{2,4},{3,1},{4,6},{5,3},{6,0},{7,5},{8,10},{9,15},{10,... | collective-permute-start | bytes 454664 | tf_op jit(solution)/shard_map/ppermute | solution.py:163
  394.7 2.1 collective-permute-done.25
  396.9 8.0 %collective-permute-start.26 = (f32[296,128]{1,0:T(8,128)S(1)}, f32[296,128]{1,0:T(8,128)S(1)}, u32[]{:S(2)}, u32[]{:S(2)}) collective-permute-start(f32[296,128]{1,0:T(8,128)S(1)} %get-tuple-element.195), channel_id=1, source_target_pairs={{0,2},{1,7},{2,4},{3,1},{4,6},{5,3},{6,0},{7,5},{8,10},{9,15},{10,... | collective-permute-start | bytes 454664 | tf_op jit(solution)/shard_map/ppermute | solution.py:163
  404.9 2.4 collective-permute-done.26
  407.4 7.9 %collective-permute-start.27 = (f32[296,128]{1,0:T(8,128)S(1)}, f32[296,128]{1,0:T(8,128)S(1)}, u32[]{:S(2)}, u32[]{:S(2)}) collective-permute-start(f32[296,128]{1,0:T(8,128)S(1)} %get-tuple-element.193), channel_id=1, source_target_pairs={{0,2},{1,7},{2,4},{3,1},{4,6},{5,3},{6,0},{7,5},{8,10},{9,15},{10,... | collective-permute-start | bytes 454664 | tf_op jit(solution)/shard_map/ppermute | solution.py:163
  415.3 6.9 %collective-permute-done.27 = f32[296,128]{1,0:T(8,128)S(1)} collective-permute-done((f32[296,128]{1,0:T(8,128)S(1)}, f32[296,128]{1,0:T(8,128)S(1)}, u32[]{:S(2)}, u32[]{:S(2)}) %collective-permute-start.27) | collective-permute-done | bytes 151584 | tf_op jit(solution)/shard_map/ppermute | solution.py:163
  422.2 7.7 %collective-permute-start.28 = (f32[296,128]{1,0:T(8,128)S(1)}, f32[296,128]{1,0:T(8,128)S(1)}, u32[]{:S(2)}, u32[]{:S(2)}) collective-permute-start(f32[296,128]{1,0:T(8,128)S(1)} %dynamic-slice_bitcast_fusion.2), channel_id=1, source_target_pairs={{0,2},{1,7},{2,4},{3,1},{4,6},{5,3},{6,0},{7,5},{8,10},{9,15},{10,... | collective-permute-start | bytes 454664 | tf_op jit(solution)/shard_map/ppermute | solution.py:169
  430.0 5.3 %collective-permute-done.28 = f32[296,128]{1,0:T(8,128)S(1)} collective-permute-done((f32[296,128]{1,0:T(8,128)S(1)}, f32[296,128]{1,0:T(8,128)S(1)}, u32[]{:S(2)}, u32[]{:S(2)}) %collective-permute-start.28) | collective-permute-done | bytes 151584 | tf_op jit(solution)/shard_map/ppermute | solution.py:169
  435.4 6.6 %collective-permute-start.29 = (f32[296,128]{1,0:T(8,128)S(1)}, f32[296,128]{1,0:T(8,128)S(1)}, u32[]{:S(2)}, u32[]{:S(2)}) collective-permute-start(f32[296,128]{1,0:T(8,128)S(1)} %dynamic-slice_bitcast_fusion.1), channel_id=1, source_target_pairs={{0,2},{1,7},{2,4},{3,1},{4,6},{5,3},{6,0},{7,5},{8,10},{9,15},{10,... | collective-permute-start | bytes 454664 | tf_op jit(solution)/shard_map/ppermute | solution.py:169
  441.9 4.5 collective-permute-done.29
  446.5 5.4 %collective-permute-start.30 = (f32[296,128]{1,0:T(8,128)S(1)}, f32[296,128]{1,0:T(8,128)S(1)}, u32[]{:S(2)}, u32[]{:S(2)}) collective-permute-start(f32[296,128]{1,0:T(8,128)S(1)} %dynamic-slice_bitcast_fusion), channel_id=1, source_target_pairs={{0,2},{1,7},{2,4},{3,1},{4,6},{5,3},{6,0},{7,5},{8,10},{9,15},{10,... | collective-permute-start | bytes 454664 | tf_op jit(solution)/shard_map/ppermute | solution.py:169
  453.2 3.7 collective-permute-done.30
  456.9 15.8 %collective-permute-start.31 = (f32[1184,128]{1,0:T(8,128)S(1)}, f32[1184,128]{1,0:T(8,128)S(1)}, u32[]{:S(2)}, u32[]{:S(2)}) collective-permute-start(f32[1184,128]{1,0:T(8,128)S(1)} %bitcast.577), channel_id=1, source_target_pairs={{0,1},{1,0},{2,3},{3,2},{4,5},{5,4},{6,7},{7,6},{8,9},{9,8},{10,11... | collective-permute-start | bytes 1818632 | tf_op jit(solution)/shard_map/ppermute | solution.py:172
  (201 shorter events, 38.6 us)
Async XLA Ops:
  5.5 1.6 copy-start
  7.0 1.3 copy-start.13
  11.5 1.0 copy-start.6
  11.5 15.8 %copy-start.11 = (f32[1,128]{1,0:T(1,128)S(1)}, f32[1,128]{1,0:T(1,128)}, u32[]{:S(2)}) copy-start(f32[1,128]{1,0:T(1,128)} %param.10) | copy-start | bytes 1540
  12.5 14.7 %collective-permute-start = (f32[1,129,512]{1,2,0:T(8,128)S(1)}, f32[1,129,512]{1,2,0:T(8,128)S(1)}, u32[]{:S(2)}, u32[]{:S(2)}) collective-permute-start(f32[1,129,512]{1,2,0:T(8,128)S(1)} %pad_maximum_fusion.1), channel_id=1, source_target_pairs={{0,8},{8,16},{16,24},{24,32},{32,40},{40,48},{48,56},{56,64},{64,7... | collective-permute-start | bytes 792584 | tf_op jit(solution)/shard_map/ppermute | solution.py:119
  27.5 15.3 %collective-permute-start.1 = (f32[1,129,512]{1,2,0:T(8,128)S(1)}, f32[1,129,512]{1,2,0:T(8,128)S(1)}, u32[]{:S(2)}, u32[]{:S(2)}) collective-permute-start(f32[1,129,512]{1,2,0:T(8,128)S(1)} %pad_maximum_fusion.2), channel_id=1, source_target_pairs={{0,16},{8,24},{16,32},{24,40},{32,48},{40,56},{48,64},{56,72},{64,... | collective-permute-start | bytes 792584 | tf_op jit(solution)/shard_map/ppermute | solution.py:119
  42.8 0.8 copy-start.10
  44.8 15.7 %collective-permute-start.2 = (f32[1,129,512]{1,2,0:T(8,128)S(1)}, f32[1,129,512]{1,2,0:T(8,128)S(1)}, u32[]{:S(2)}, u32[]{:S(2)}) collective-permute-start(f32[1,129,512]{1,2,0:T(8,128)S(1)} %pad_maximum_fusion.3), channel_id=1, source_target_pairs={{0,32},{8,40},{16,48},{24,56},{32,64},{40,72},{48,80},{56,88},{64,... | collective-permute-start | bytes 792584 | tf_op jit(solution)/shard_map/ppermute | solution.py:119
  60.9 27.2 %collective-permute-start.3 = (f32[1,129,512]{1,2,0:T(8,128)S(1)}, f32[1,129,512]{1,2,0:T(8,128)S(1)}, u32[]{:S(2)}, u32[]{:S(2)}) collective-permute-start(f32[1,129,512]{1,2,0:T(8,128)S(1)} %pad_maximum_fusion.4), channel_id=1, source_target_pairs={{0,64},{8,72},{16,80},{24,88},{32,96},{40,104},{48,112},{56,120},{... | collective-permute-start | bytes 792584 | tf_op jit(solution)/shard_map/ppermute | solution.py:119
  88.1 0.8 copy-start.8
  90.1 14.9 %collective-permute-start.4 = (f32[1,129,512]{1,2,0:T(8,128)S(1)}, f32[1,129,512]{1,2,0:T(8,128)S(1)}, u32[]{:S(2)}, u32[]{:S(2)}) collective-permute-start(f32[1,129,512]{1,2,0:T(8,128)S(1)} %pad_maximum_fusion.5), channel_id=1, source_target_pairs={{0,128},{8,136},{16,144},{24,152},{32,160},{40,168},{48,176},{56,1... | collective-permute-start | bytes 792584 | tf_op jit(solution)/shard_map/ppermute | solution.py:119
  105.4 14.1 %copy-start.1 = (bf16[128,9,128]{2,0,1:T(8,128)(2,1)S(1)}, bf16[128,9,128]{2,0,1:T(8,128)(2,1)}, u32[]{:S(2)}) copy-start(bf16[128,9,128]{2,0,1:T(8,128)(2,1)} %copy-done) | copy-start | bytes 884740
  105.4 13.9 %collective-permute-start.5 = (f32[1,129,512]{1,2,0:T(8,128)S(1)}, f32[1,129,512]{1,2,0:T(8,128)S(1)}, u32[]{:S(2)}, u32[]{:S(2)}) collective-permute-start(f32[1,129,512]{1,2,0:T(8,128)S(1)} %pad_maximum_fusion.6), channel_id=1, source_target_pairs={{0,256},{8,264},{16,272},{24,280},{32,288},{40,296},{48,304},{56,3... | collective-permute-start | bytes 792584 | tf_op jit(solution)/shard_map/ppermute | solution.py:119
  121.5 9.5 %collective-permute-start.6 = (f32[1,128,512]{1,2,0:T(8,128)S(1)}, f32[1,128,512]{1,2,0:T(8,128)S(1)}, u32[]{:S(2)}, u32[]{:S(2)}) collective-permute-start(f32[1,128,512]{1,2,0:T(8,128)S(1)} %get-tuple-element.48), channel_id=1, source_target_pairs={{0,8},{8,16},{16,24},{24,32},{32,40},{40,48},{48,56},{56,64},{64,7... | collective-permute-start | bytes 786440 | tf_op jit(solution)/shard_map/ppermute | solution.py:131
  131.1 12.3 %collective-permute-start.7 = (f32[1,128,512]{1,2,0:T(8,128)S(1)}, f32[1,128,512]{1,2,0:T(8,128)S(1)}, u32[]{:S(2)}, u32[]{:S(2)}) collective-permute-start(f32[1,128,512]{1,2,0:T(8,128)S(1)} %multiply_add_fusion.23), channel_id=1, source_target_pairs={{0,16},{8,24},{16,32},{24,40},{32,48},{40,56},{48,64},{56,72},{64,... | collective-permute-start | bytes 786440 | tf_op jit(solution)/shard_map/ppermute | solution.py:131
  143.4 10.3 %collective-permute-start.8 = (f32[1,128,512]{1,2,0:T(8,128)S(1)}, f32[1,128,512]{1,2,0:T(8,128)S(1)}, u32[]{:S(2)}, u32[]{:S(2)}) collective-permute-start(f32[1,128,512]{1,2,0:T(8,128)S(1)} %multiply_add_fusion.21), channel_id=1, source_target_pairs={{0,32},{8,40},{16,48},{24,56},{32,64},{40,72},{48,80},{56,88},{64,... | collective-permute-start | bytes 786440 | tf_op jit(solution)/shard_map/ppermute | solution.py:131
  153.7 10.1 %collective-permute-start.9 = (f32[1,128,512]{1,2,0:T(8,128)S(1)}, f32[1,128,512]{1,2,0:T(8,128)S(1)}, u32[]{:S(2)}, u32[]{:S(2)}) collective-permute-start(f32[1,128,512]{1,2,0:T(8,128)S(1)} %get-tuple-element.46), channel_id=1, source_target_pairs={{0,64},{8,72},{16,80},{24,88},{32,96},{40,104},{48,112},{56,120},{... | collective-permute-start | bytes 786440 | tf_op jit(solution)/shard_map/ppermute | solution.py:131
  163.8 14.1 %copy-start.7 = (f32[1,128,512]{2,1,0:T(8,128)S(1)}, f32[1,128,512]{2,1,0:T(8,128)}, u32[]{:S(2)}) copy-start(f32[1,128,512]{2,1,0:T(8,128)} %param.7) | copy-start | bytes 786436
  163.9 14.2 %copy-start.12 = (f32[1,128]{1,0:T(1,128)S(1)}, f32[1,128]{1,0:T(1,128)}, u32[]{:S(2)}) copy-start(f32[1,128]{1,0:T(1,128)} %param.11) | copy-start | bytes 1540
  163.9 8.7 %collective-permute-start.10 = (f32[1,128,512]{1,2,0:T(8,128)S(1)}, f32[1,128,512]{1,2,0:T(8,128)S(1)}, u32[]{:S(2)}, u32[]{:S(2)}) collective-permute-start(f32[1,128,512]{1,2,0:T(8,128)S(1)} %multiply_add_fusion.17), channel_id=1, source_target_pairs={{0,128},{8,136},{16,144},{24,152},{32,160},{40,168},{48,176},{56,1... | collective-permute-start | bytes 786440 | tf_op jit(solution)/shard_map/ppermute | solution.py:131
  172.7 8.5 %collective-permute-start.11 = (f32[1,128,512]{1,2,0:T(8,128)S(1)}, f32[1,128,512]{1,2,0:T(8,128)S(1)}, u32[]{:S(2)}, u32[]{:S(2)}) collective-permute-start(f32[1,128,512]{1,2,0:T(8,128)S(1)} %get-tuple-element.44), channel_id=1, source_target_pairs={{0,256},{8,264},{16,272},{24,280},{32,288},{40,296},{48,304},{56,3... | collective-permute-start | bytes 786440 | tf_op jit(solution)/shard_map/ppermute | solution.py:131
  185.8 1.0 copy-start.5
  186.8 16.7 %collective-permute-start.12 = (f32[1,129,512]{1,2,0:T(8,128)S(1)}, f32[1,129,512]{1,2,0:T(8,128)S(1)}, u32[]{:S(2)}, u32[]{:S(2)}) collective-permute-start(f32[1,129,512]{1,2,0:T(8,128)S(1)} %pad_maximum_fusion.7), channel_id=1, source_target_pairs={{8,0},{16,8},{24,16},{32,24},{40,32},{48,40},{56,48},{64,56},{72,6... | collective-permute-start | bytes 792584 | tf_op jit(solution)/shard_map/ppermute | solution.py:119
  203.9 13.7 %collective-permute-start.13 = (f32[1,129,512]{1,2,0:T(8,128)S(1)}, f32[1,129,512]{1,2,0:T(8,128)S(1)}, u32[]{:S(2)}, u32[]{:S(2)}) collective-permute-start(f32[1,129,512]{1,2,0:T(8,128)S(1)} %pad_maximum_fusion.8), channel_id=1, source_target_pairs={{16,0},{24,8},{32,16},{40,24},{48,32},{56,40},{64,48},{72,56},{80,... | collective-permute-start | bytes 792584 | tf_op jit(solution)/shard_map/ppermute | solution.py:119
  218.0 19.6 %collective-permute-start.14 = (f32[1,129,512]{1,2,0:T(8,128)S(1)}, f32[1,129,512]{1,2,0:T(8,128)S(1)}, u32[]{:S(2)}, u32[]{:S(2)}) collective-permute-start(f32[1,129,512]{1,2,0:T(8,128)S(1)} %pad_maximum_fusion.9), channel_id=1, source_target_pairs={{32,0},{40,8},{48,16},{56,24},{64,32},{72,40},{80,48},{88,56},{96,... | collective-permute-start | bytes 792584 | tf_op jit(solution)/shard_map/ppermute | solution.py:119
  238.0 21.7 %collective-permute-start.15 = (f32[1,129,512]{1,2,0:T(8,128)S(1)}, f32[1,129,512]{1,2,0:T(8,128)S(1)}, u32[]{:S(2)}, u32[]{:S(2)}) collective-permute-start(f32[1,129,512]{1,2,0:T(8,128)S(1)} %pad_maximum_fusion.10), channel_id=1, source_target_pairs={{64,0},{72,8},{80,16},{88,24},{96,32},{104,40},{112,48},{120,56},{... | collective-permute-start | bytes 792584 | tf_op jit(solution)/shard_map/ppermute | solution.py:119
  259.7 0.8 copy-start.9
  261.7 10.2 %collective-permute-start.16 = (f32[1,129,512]{1,2,0:T(8,128)S(1)}, f32[1,129,512]{1,2,0:T(8,128)S(1)}, u32[]{:S(2)}, u32[]{:S(2)}) collective-permute-start(f32[1,129,512]{1,2,0:T(8,128)S(1)} %pad_maximum_fusion.11), channel_id=1, source_target_pairs={{128,0},{136,8},{144,16},{152,24},{160,32},{168,40},{176,48},{184,... | collective-permute-start | bytes 792584 | tf_op jit(solution)/shard_map/ppermute | solution.py:119
  272.3 11.5 %collective-permute-start.17 = (f32[1,129,512]{1,2,0:T(8,128)S(1)}, f32[1,129,512]{1,2,0:T(8,128)S(1)}, u32[]{:S(2)}, u32[]{:S(2)}) collective-permute-start(f32[1,129,512]{1,2,0:T(8,128)S(1)} %pad_maximum_fusion.12), channel_id=1, source_target_pairs={{256,0},{264,8},{272,16},{280,24},{288,32},{296,40},{304,48},{312,... | collective-permute-start | bytes 792584 | tf_op jit(solution)/shard_map/ppermute | solution.py:119
  285.9 13.2 %collective-permute-start.18 = (f32[1,128,512]{1,2,0:T(8,128)S(1)}, f32[1,128,512]{1,2,0:T(8,128)S(1)}, u32[]{:S(2)}, u32[]{:S(2)}) collective-permute-start(f32[1,128,512]{1,2,0:T(8,128)S(1)} %get-tuple-element.20), channel_id=1, source_target_pairs={{8,0},{16,8},{24,16},{32,24},{40,32},{48,40},{56,48},{64,56},{72,6... | collective-permute-start | bytes 786440 | tf_op jit(solution)/shard_map/ppermute | solution.py:131
  299.1 9.6 %collective-permute-start.19 = (f32[1,128,512]{1,2,0:T(8,128)S(1)}, f32[1,128,512]{1,2,0:T(8,128)S(1)}, u32[]{:S(2)}, u32[]{:S(2)}) collective-permute-start(f32[1,128,512]{1,2,0:T(8,128)S(1)} %multiply_add_fusion.8), channel_id=1, source_target_pairs={{16,0},{24,8},{32,16},{40,24},{48,32},{56,40},{64,48},{72,56},{80,... | collective-permute-start | bytes 786440 | tf_op jit(solution)/shard_map/ppermute | solution.py:131
  308.7 15.0 %collective-permute-start.20 = (f32[1,128,512]{1,2,0:T(8,128)S(1)}, f32[1,128,512]{1,2,0:T(8,128)S(1)}, u32[]{:S(2)}, u32[]{:S(2)}) collective-permute-start(f32[1,128,512]{1,2,0:T(8,128)S(1)} %multiply_add_fusion.6), channel_id=1, source_target_pairs={{32,0},{40,8},{48,16},{56,24},{64,32},{72,40},{80,48},{88,56},{96,... | collective-permute-start | bytes 786440 | tf_op jit(solution)/shard_map/ppermute | solution.py:131
  323.8 16.8 %collective-permute-start.21 = (f32[1,128,512]{1,2,0:T(8,128)S(1)}, f32[1,128,512]{1,2,0:T(8,128)S(1)}, u32[]{:S(2)}, u32[]{:S(2)}) collective-permute-start(f32[1,128,512]{1,2,0:T(8,128)S(1)} %get-tuple-element.18), channel_id=1, source_target_pairs={{64,0},{72,8},{80,16},{88,24},{96,32},{104,40},{112,48},{120,56},{... | collective-permute-start | bytes 786440 | tf_op jit(solution)/shard_map/ppermute | solution.py:131
  340.6 7.1 %collective-permute-start.22 = (f32[1,128,512]{1,2,0:T(8,128)S(1)}, f32[1,128,512]{1,2,0:T(8,128)S(1)}, u32[]{:S(2)}, u32[]{:S(2)}) collective-permute-start(f32[1,128,512]{1,2,0:T(8,128)S(1)} %multiply_add_fusion.2), channel_id=1, source_target_pairs={{128,0},{136,8},{144,16},{152,24},{160,32},{168,40},{176,48},{184,... | collective-permute-start | bytes 786440 | tf_op jit(solution)/shard_map/ppermute | solution.py:131
  347.8 8.9 %collective-permute-start.23 = (f32[1,128,512]{1,2,0:T(8,128)S(1)}, f32[1,128,512]{1,2,0:T(8,128)S(1)}, u32[]{:S(2)}, u32[]{:S(2)}) collective-permute-start(f32[1,128,512]{1,2,0:T(8,128)S(1)} %get-tuple-element.16), channel_id=1, source_target_pairs={{256,0},{264,8},{272,16},{280,24},{288,32},{296,40},{304,48},{312,... | collective-permute-start | bytes 786440 | tf_op jit(solution)/shard_map/ppermute | solution.py:131
  358.0 0.7 copy-start.2
  359.5 23.9 %collective-permute-start.24 = (f32[1184,128]{1,0:T(8,128)S(1)}, f32[1184,128]{1,0:T(8,128)S(1)}, u32[]{:S(2)}, u32[]{:S(2)}) collective-permute-start(f32[1184,128]{1,0:T(8,128)S(1)} %constant_dynamic-slice_fusion.3), channel_id=1, source_target_pairs={{0,1},{1,0},{2,3},{3,2},{4,5},{5,4},{6,7},{7,6},{8,9},{9,8},{10,11... | collective-permute-start | bytes 1818632 | tf_op jit(solution)/shard_map/ppermute | solution.py:152
  383.5 13.3 %collective-permute-start.25 = (f32[296,128]{1,0:T(8,128)S(1)}, f32[296,128]{1,0:T(8,128)S(1)}, u32[]{:S(2)}, u32[]{:S(2)}) collective-permute-start(f32[296,128]{1,0:T(8,128)S(1)} %get-tuple-element.197), channel_id=1, source_target_pairs={{0,2},{1,7},{2,4},{3,1},{4,6},{5,3},{6,0},{7,5},{8,10},{9,15},{10,... | collective-permute-start | bytes 454664 | tf_op jit(solution)/shard_map/ppermute | solution.py:163
  396.9 10.4 %collective-permute-start.26 = (f32[296,128]{1,0:T(8,128)S(1)}, f32[296,128]{1,0:T(8,128)S(1)}, u32[]{:S(2)}, u32[]{:S(2)}) collective-permute-start(f32[296,128]{1,0:T(8,128)S(1)} %get-tuple-element.195), channel_id=1, source_target_pairs={{0,2},{1,7},{2,4},{3,1},{4,6},{5,3},{6,0},{7,5},{8,10},{9,15},{10,... | collective-permute-start | bytes 454664 | tf_op jit(solution)/shard_map/ppermute | solution.py:163
  407.3 44.6 %copy-start.4 = (f32[1,1,128,512]{2,3,1,0:T(8,128)S(1)}, f32[1,1,128,512]{2,3,1,0:T(8,128)}, u32[]{:S(2)}) copy-start(f32[1,1,128,512]{2,3,1,0:T(8,128)} %get-tuple-element.38) | copy-start | bytes 786436
  407.4 14.8 %collective-permute-start.27 = (f32[296,128]{1,0:T(8,128)S(1)}, f32[296,128]{1,0:T(8,128)S(1)}, u32[]{:S(2)}, u32[]{:S(2)}) collective-permute-start(f32[296,128]{1,0:T(8,128)S(1)} %get-tuple-element.193), channel_id=1, source_target_pairs={{0,2},{1,7},{2,4},{3,1},{4,6},{5,3},{6,0},{7,5},{8,10},{9,15},{10,... | collective-permute-start | bytes 454664 | tf_op jit(solution)/shard_map/ppermute | solution.py:163
  422.2 13.1 %collective-permute-start.28 = (f32[296,128]{1,0:T(8,128)S(1)}, f32[296,128]{1,0:T(8,128)S(1)}, u32[]{:S(2)}, u32[]{:S(2)}) collective-permute-start(f32[296,128]{1,0:T(8,128)S(1)} %dynamic-slice_bitcast_fusion.2), channel_id=1, source_target_pairs={{0,2},{1,7},{2,4},{3,1},{4,6},{5,3},{6,0},{7,5},{8,10},{9,15},{10,... | collective-permute-start | bytes 454664 | tf_op jit(solution)/shard_map/ppermute | solution.py:169
  435.4 11.1 %collective-permute-start.29 = (f32[296,128]{1,0:T(8,128)S(1)}, f32[296,128]{1,0:T(8,128)S(1)}, u32[]{:S(2)}, u32[]{:S(2)}) collective-permute-start(f32[296,128]{1,0:T(8,128)S(1)} %dynamic-slice_bitcast_fusion.1), channel_id=1, source_target_pairs={{0,2},{1,7},{2,4},{3,1},{4,6},{5,3},{6,0},{7,5},{8,10},{9,15},{10,... | collective-permute-start | bytes 454664 | tf_op jit(solution)/shard_map/ppermute | solution.py:169
  446.5 10.4 %collective-permute-start.30 = (f32[296,128]{1,0:T(8,128)S(1)}, f32[296,128]{1,0:T(8,128)S(1)}, u32[]{:S(2)}, u32[]{:S(2)}) collective-permute-start(f32[296,128]{1,0:T(8,128)S(1)} %dynamic-slice_bitcast_fusion), channel_id=1, source_target_pairs={{0,2},{1,7},{2,4},{3,1},{4,6},{5,3},{6,0},{7,5},{8,10},{9,15},{10,... | collective-permute-start | bytes 454664 | tf_op jit(solution)/shard_map/ppermute | solution.py:169
  456.9 16.1 %copy-start.3 = (f32[1,128,512]{1,2,0:T(8,128)S(1)}, f32[1,128,512]{1,2,0:T(8,128)}, u32[]{:S(2)}) copy-start(f32[1,128,512]{1,2,0:T(8,128)} %copy-done.2) | copy-start | bytes 786436
  456.9 17.4 %collective-permute-start.31 = (f32[1184,128]{1,0:T(8,128)S(1)}, f32[1184,128]{1,0:T(8,128)S(1)}, u32[]{:S(2)}, u32[]{:S(2)}) collective-permute-start(f32[1184,128]{1,0:T(8,128)S(1)} %bitcast.577), channel_id=1, source_target_pairs={{0,1},{1,0},{2,3},{3,2},{4,5},{5,4},{6,7},{7,6},{8,9},{9,8},{10,11... | collective-permute-start | bytes 1818632 | tf_op jit(solution)/shard_map/ppermute | solution.py:172

commit v9 on v4

--- a/solution.py
+++ b/solution.py
@@ -69,45 +69,51 @@
     return adjoint
 
 
-def scan_distances(count):
-    distances = []
-    d = 1
-    while d < count:
-        distances.append(d)
-        d *= 2
-    return distances
-
-
-def scan_pairs(count, d, reverse):
-    if reverse:
-        return [(k, k - d) for k in range(d, count)]
-    return [(k, k + d) for k in range(count - d)]
-
-
-def exclusive_scan_first(gain, local, axis, reverse):
+def butterfly_first(gain, local, axis, reverse):
     count = lax.axis_size(axis)
+    me = lax.axis_index(axis)
+    place = count - 1 - me if reverse else me
     channels, pixels = local.shape[1], local.shape[2]
     total = jnp.zeros_like(local)
     product = jnp.ones_like(gain)
+    block_sum = local
+    block_gain = gain
     factors = []
-    for d in scan_distances(count):
-        sending = gain[None, :, None] * total + local
-        gain_row = jnp.pad(gain * product, (0, pixels - channels))
-        packed = jnp.concatenate([sending, gain_row[None, None, :]], axis=1)
-        received = lax.ppermute(packed, axis, scan_pairs(count, d, reverse))
-        factors.append(product)
-        total = total + product[None, :, None] * received[:, :channels, :]
-        product = product * received[0, channels, :channels]
+    step = 1
+    while step < count:
+        upper = (place // step) % 2 == 1
+        gain_row = jnp.pad(block_gain, (0, pixels - channels))
+        packed = jnp.concatenate([block_sum, gain_row[None, None, :]], axis=1)
+        got = lax.ppermute(packed, axis, [(k, k ^ step) for k in range(count)])
+        other_sum = got[:, :channels, :]
+        other_gain = got[0, channels, :channels]
+        upper_gain = jnp.where(upper, block_gain, other_gain)
+        factors.append((product, upper_gain))
+        total = jnp.where(upper, total + product[None, :, None] * other_sum, total)
+        product = jnp.where(upper, product * other_gain, product)
+        lower_sum = jnp.where(upper, other_sum, block_sum)
+        upper_sum = jnp.where(upper, block_sum, other_sum)
+        block_sum = upper_gain[None, :, None] * lower_sum + upper_sum
+        block_gain = block_gain * other_gain
+        step *= 2
     return total, factors
 
 
-def exclusive_scan_again(gain, local, factors, axis, reverse):
+def butterfly_again(local, factors, axis, reverse):
     count = lax.axis_size(axis)
+    me = lax.axis_index(axis)
+    place = count - 1 - me if reverse else me
     total = jnp.zeros_like(local)
-    for d, factor in zip(scan_distances(count), factors):
-        sending = gain[None, :, None] * total + local
-        received = lax.ppermute(sending, axis, scan_pairs(count, d, reverse))
-        total = total + factor[None, :, None] * received
+    block_sum = local
+    step = 1
+    for product, upper_gain in factors:
+        upper = (place // step) % 2 == 1
+        got = lax.ppermute(block_sum, axis, [(k, k ^ step) for k in range(count)])
+        total = jnp.where(upper, total + product[None, :, None] * got, total)
+        lower_sum = jnp.where(upper, got, block_sum)
+        upper_sum = jnp.where(upper, block_sum, got)
+        block_sum = upper_gain[None, :, None] * lower_sum + upper_sum
+        step *= 2
     return total
 
 
@@ -166,9 +172,9 @@
         ending = relax_block(c_points, conv_weight, conv_bias)[0]
         residual = ending - following
         if sweep_index == 0:
-            error, factors = exclusive_scan_first(gain_row, residual, "layer", False)
+            error, factors = butterfly_first(gain_row, residual, "layer", False)
         else:
-            error = exclusive_scan_again(gain_row, residual, factors, "layer", False)
+            error = butterfly_again(residual, factors, "layer", False)
         c_points = c_points + error
         following = following + gain_row[None, :, None] * error + residual
     ending, stored = relax_block(c_points, conv_weight, conv_bias)
@@ -178,9 +184,9 @@
         start_adj = adjoint_block(target, stored, flipped_list)
         residual = start_adj - previous
         if sweep_index == 0:
-            error, factors = exclusive_scan_first(back_row, residual, "layer", True)
+            error, factors = butterfly_first(back_row, residual, "layer", True)
         else:
-            error = exclusive_scan_again(back_row, residual, factors, "layer", True)
+            error = butterfly_again(residual, factors, "layer", True)
         target = target + error
         previous = previous + back_row[None, :, None] * error + residual
     adjoint = target

time: 395 us -> 394 us (level)
  the two profiles are of different devices: /device:TPU:1 before, /device:TPU:75 now
where the time goes in v9:
time: 394 us; the launch traced here: 392 us
  starting transfers between devices  169 us (43%)
  waiting for transfers between devices  163 us (41%)
  other arithmetic  41.4 us (11%)
  local copies, waits for them, and re-layouts  8.25 us (2%)
  matrix products  7.88 us (2%)
    ppermute x12, waiting for transfers between devices, butterfly_first(): got = lax.ppermute(packed, axis, [(k, k ^ step) for k in range(count)])  73 us
    ppermute x12, waiting for transfers between devices, butterfly_again(): got = lax.ppermute(block_sum, axis, [(k, k ^ step) for k in range(count)])  58.6 us
    ppermute x6, starting transfers between devices, batch_sum(): got = lax.ppermute(sent, axis, ring)  48.3 us
    ppermute x12, starting transfers between devices, butterfly_again(): got = lax.ppermute(block_sum, axis, [(k, k ^ step) for k in range(count)])  40.3 us
    ppermute x12, starting transfers between devices, butterfly_first(): got = lax.ppermute(packed, axis, [(k, k ^ step) for k in range(count)])  40 us
    ppermute x6, waiting for transfers between devices, batch_sum(): got = lax.ppermute(sent, axis, ring)  30.1 us
    ppermute x1, starting transfers between devices, batch_sum(): half = keep + lax.ppermute(give, axis, partner)  27.2 us
    ppermute x1, starting transfers between devices, batch_sum(): other = lax.ppermute(half, axis, partner)  12.8 us
  transfers between devices with their start and end apart: 32, of which 32 were waited for; matrix products, arithmetic and copies ran while one was open for 1% of the time, Pallas kernels for 0%

profile of v9, /device:TPU:75, one launch (start us, length us, event | category | flops | bytes accessed | tf_op | source)
XLA Modules:
  0.0 392.2 jit_solution(18398540139421941583)
XLA Ops:
  5.3 2.2 collective-permute-start
  7.5 7.2 %collective-permute-done = f32[1,129,512]{2,1,0:T(8,128)S(1)} collective-permute-done((f32[1,129,512]{2,1,0:T(8,128)S(1)}, f32[1,129,512]{2,1,0:T(8,128)S(1)}, u32[]{:S(2)}, u32[]{:S(2)}) %collective-permute-start) | collective-permute-done | bytes 264224 | tf_op jit(solution)/shard_map/ppermute | solution.py:87
  14.9 3.8 collective-permute-start.1
  18.7 6.2 %collective-permute-done.1 = f32[1,129,512]{2,1,0:T(8,128)S(1)} collective-permute-done((f32[1,129,512]{2,1,0:T(8,128)S(1)}, f32[1,129,512]{2,1,0:T(8,128)S(1)}, u32[]{:S(2)}, u32[]{:S(2)}) %collective-permute-start.1) | collective-permute-done | bytes 264224 | tf_op jit(solution)/shard_map/ppermute | solution.py:87
  25.0 3.5 collective-permute-start.2
  28.6 4.3 %collective-permute-done.2 = f32[1,129,512]{2,1,0:T(8,128)S(1)} collective-permute-done((f32[1,129,512]{2,1,0:T(8,128)S(1)}, f32[1,129,512]{2,1,0:T(8,128)S(1)}, u32[]{:S(2)}, u32[]{:S(2)}) %collective-permute-start.2) | collective-permute-done | bytes 264224 | tf_op jit(solution)/shard_map/ppermute | solution.py:87
  33.0 1.9 collective-permute-start.3
  35.0 11.5 %collective-permute-done.3 = f32[1,129,512]{2,1,0:T(8,128)S(1)} collective-permute-done((f32[1,129,512]{2,1,0:T(8,128)S(1)}, f32[1,129,512]{2,1,0:T(8,128)S(1)}, u32[]{:S(2)}, u32[]{:S(2)}) %collective-permute-start.3) | collective-permute-done | bytes 264224 | tf_op jit(solution)/shard_map/ppermute | solution.py:87
  46.6 2.2 collective-permute-start.4
  48.8 6.5 %collective-permute-done.4 = f32[1,129,512]{2,1,0:T(8,128)S(1)} collective-permute-done((f32[1,129,512]{2,1,0:T(8,128)S(1)}, f32[1,129,512]{2,1,0:T(8,128)S(1)}, u32[]{:S(2)}, u32[]{:S(2)}) %collective-permute-start.4) | collective-permute-done | bytes 264224 | tf_op jit(solution)/shard_map/ppermute | solution.py:87
  55.5 4.1 %collective-permute-start.5 = (f32[1,129,512]{2,1,0:T(8,128)S(1)}, f32[1,129,512]{2,1,0:T(8,128)S(1)}, u32[]{:S(2)}, u32[]{:S(2)}) collective-permute-start(f32[1,129,512]{2,1,0:T(8,128)S(1)} %pad_maximum_fusion.6), channel_id=1, source_target_pairs={{0,256},{8,264},{16,272},{24,280},{32,288},{40,296},{48,304},{56,3... | collective-permute-start | bytes 792584 | tf_op jit(solution)/shard_map/ppermute | solution.py:87
  59.6 5.2 %collective-permute-done.5 = f32[1,129,512]{2,1,0:T(8,128)S(1)} collective-permute-done((f32[1,129,512]{2,1,0:T(8,128)S(1)}, f32[1,129,512]{2,1,0:T(8,128)S(1)}, u32[]{:S(2)}, u32[]{:S(2)}) %collective-permute-start.5) | collective-permute-done | bytes 264224 | tf_op jit(solution)/shard_map/ppermute | solution.py:87
  69.3 2.2 collective-permute-start.6
  71.5 4.9 %collective-permute-done.6 = f32[1,128,512]{2,1,0:T(8,128)S(1)} collective-permute-done((f32[1,128,512]{2,1,0:T(8,128)S(1)}, f32[1,128,512]{2,1,0:T(8,128)S(1)}, u32[]{:S(2)}, u32[]{:S(2)}) %collective-permute-start.6) | collective-permute-done | bytes 262176 | tf_op jit(solution)/shard_map/ppermute | solution.py:111
  76.5 4.0 %collective-permute-start.7 = (f32[1,128,512]{2,1,0:T(8,128)S(1)}, f32[1,128,512]{2,1,0:T(8,128)S(1)}, u32[]{:S(2)}, u32[]{:S(2)}) collective-permute-start(f32[1,128,512]{2,1,0:T(8,128)S(1)} %select_add_fusion.14), channel_id=1, source_target_pairs={{0,16},{8,24},{16,0},{24,8},{32,48},{40,56},{48,32},{56,40},{64,80... | collective-permute-start | bytes 786440 | tf_op jit(solution)/shard_map/ppermute | solution.py:111
  80.5 4.7 %collective-permute-done.7 = f32[1,128,512]{2,1,0:T(8,128)S(1)} collective-permute-done((f32[1,128,512]{2,1,0:T(8,128)S(1)}, f32[1,128,512]{2,1,0:T(8,128)S(1)}, u32[]{:S(2)}, u32[]{:S(2)}) %collective-permute-start.7) | collective-permute-done | bytes 262176 | tf_op jit(solution)/shard_map/ppermute | solution.py:111
  85.2 5.6 %collective-permute-start.8 = (f32[1,128,512]{2,1,0:T(8,128)S(1)}, f32[1,128,512]{2,1,0:T(8,128)S(1)}, u32[]{:S(2)}, u32[]{:S(2)}) collective-permute-start(f32[1,128,512]{2,1,0:T(8,128)S(1)} %select_add_fusion.13), channel_id=1, source_target_pairs={{0,32},{8,40},{16,48},{24,56},{32,0},{40,8},{48,16},{56,24},{64,96... | collective-permute-start | bytes 786440 | tf_op jit(solution)/shard_map/ppermute | solution.py:111
  90.9 3.7 collective-permute-done.8
  94.7 2.7 collective-permute-start.9
  97.5 6.1 %collective-permute-done.9 = f32[1,128,512]{2,1,0:T(8,128)S(1)} collective-permute-done((f32[1,128,512]{2,1,0:T(8,128)S(1)}, f32[1,128,512]{2,1,0:T(8,128)S(1)}, u32[]{:S(2)}, u32[]{:S(2)}) %collective-permute-start.9) | collective-permute-done | bytes 262176 | tf_op jit(solution)/shard_map/ppermute | solution.py:111
  103.7 2.2 collective-permute-start.10
  105.8 5.2 %collective-permute-done.10 = f32[1,128,512]{2,1,0:T(8,128)S(1)} collective-permute-done((f32[1,128,512]{2,1,0:T(8,128)S(1)}, f32[1,128,512]{2,1,0:T(8,128)S(1)}, u32[]{:S(2)}, u32[]{:S(2)}) %collective-permute-start.10) | collective-permute-done | bytes 262176 | tf_op jit(solution)/shard_map/ppermute | solution.py:111
  111.9 4.1 %collective-permute-start.11 = (f32[1,128,512]{2,1,0:T(8,128)}, f32[1,128,512]{2,1,0:T(8,128)}, u32[]{:S(2)}, u32[]{:S(2)}) collective-permute-start(f32[1,128,512]{2,1,0:T(8,128)} %select_add_fusion.10), channel_id=1, source_target_pairs={{0,256},{8,264},{16,272},{24,280},{32,288},{40,296},{48,304},{56,3... | collective-permute-start | bytes 786440 | tf_op jit(solution)/shard_map/ppermute | solution.py:111
  118.4 5.0 %collective-permute-done.11 = f32[1,128,512]{2,1,0:T(8,128)} collective-permute-done((f32[1,128,512]{2,1,0:T(8,128)}, f32[1,128,512]{2,1,0:T(8,128)}, u32[]{:S(2)}, u32[]{:S(2)}) %collective-permute-start.11) | collective-permute-done | bytes 262176 | tf_op jit(solution)/shard_map/ppermute | solution.py:111
  132.4 2.1 collective-permute-start.12
  134.5 5.5 %collective-permute-done.12 = f32[1,129,512]{2,1,0:T(8,128)} collective-permute-done((f32[1,129,512]{2,1,0:T(8,128)}, f32[1,129,512]{2,1,0:T(8,128)}, u32[]{:S(2)}, u32[]{:S(2)}) %collective-permute-start.12) | collective-permute-done | bytes 264224 | tf_op jit(solution)/shard_map/ppermute | solution.py:87
  143.2 3.8 collective-permute-start.13
  147.0 6.1 %collective-permute-done.13 = f32[1,129,512]{2,1,0:T(8,128)} collective-permute-done((f32[1,129,512]{2,1,0:T(8,128)}, f32[1,129,512]{2,1,0:T(8,128)}, u32[]{:S(2)}, u32[]{:S(2)}) %collective-permute-start.13) | collective-permute-done | bytes 264224 | tf_op jit(solution)/shard_map/ppermute | solution.py:87
  153.8 1.8 select_add_fusion.8
  157.3 5.4 %collective-permute-start.14 = (f32[1,129,512]{2,1,0:T(8,128)}, f32[1,129,512]{2,1,0:T(8,128)}, u32[]{:S(2)}, u32[]{:S(2)}) collective-permute-start(f32[1,129,512]{2,1,0:T(8,128)} %pad_maximum_fusion.9), channel_id=1, source_target_pairs={{0,32},{8,40},{16,48},{24,56},{32,0},{40,8},{48,16},{56,24},{64,96... | collective-permute-start | bytes 792584 | tf_op jit(solution)/shard_map/ppermute | solution.py:87
  162.8 4.2 %collective-permute-done.14 = f32[1,129,512]{2,1,0:T(8,128)} collective-permute-done((f32[1,129,512]{2,1,0:T(8,128)}, f32[1,129,512]{2,1,0:T(8,128)}, u32[]{:S(2)}, u32[]{:S(2)}) %collective-permute-start.14) | collective-permute-done | bytes 264224 | tf_op jit(solution)/shard_map/ppermute | solution.py:87
  167.7 1.8 select_add_fusion.7
  171.2 2.5 collective-permute-start.15
  173.6 7.3 %collective-permute-done.15 = f32[1,129,512]{2,1,0:T(8,128)} collective-permute-done((f32[1,129,512]{2,1,0:T(8,128)}, f32[1,129,512]{2,1,0:T(8,128)}, u32[]{:S(2)}, u32[]{:S(2)}) %collective-permute-start.15) | collective-permute-done | bytes 264224 | tf_op jit(solution)/shard_map/ppermute | solution.py:87
  185.2 4.0 %collective-permute-start.16 = (f32[1,129,512]{2,1,0:T(8,128)}, f32[1,129,512]{2,1,0:T(8,128)}, u32[]{:S(2)}, u32[]{:S(2)}) collective-permute-start(f32[1,129,512]{2,1,0:T(8,128)} %pad_maximum_fusion.11), channel_id=1, source_target_pairs={{0,128},{8,136},{16,144},{24,152},{32,160},{40,168},{48,176},{56,1... | collective-permute-start | bytes 792584 | tf_op jit(solution)/shard_map/ppermute | solution.py:87
  189.3 4.5 %collective-permute-done.16 = f32[1,129,512]{2,1,0:T(8,128)} collective-permute-done((f32[1,129,512]{2,1,0:T(8,128)}, f32[1,129,512]{2,1,0:T(8,128)}, u32[]{:S(2)}, u32[]{:S(2)}) %collective-permute-start.16) | collective-permute-done | bytes 264224 | tf_op jit(solution)/shard_map/ppermute | solution.py:87
  196.4 4.7 %collective-permute-start.17 = (f32[1,129,512]{2,1,0:T(8,128)}, f32[1,129,512]{2,1,0:T(8,128)}, u32[]{:S(2)}, u32[]{:S(2)}) collective-permute-start(f32[1,129,512]{2,1,0:T(8,128)} %pad_maximum_fusion.12), channel_id=1, source_target_pairs={{0,256},{8,264},{16,272},{24,280},{32,288},{40,296},{48,304},{56,3... | collective-permute-start | bytes 792584 | tf_op jit(solution)/shard_map/ppermute | solution.py:87
  201.1 4.4 %collective-permute-done.17 = f32[1,129,512]{2,1,0:T(8,128)} collective-permute-done((f32[1,129,512]{2,1,0:T(8,128)}, f32[1,129,512]{2,1,0:T(8,128)}, u32[]{:S(2)}, u32[]{:S(2)}) %collective-permute-start.17) | collective-permute-done | bytes 264224 | tf_op jit(solution)/shard_map/ppermute | solution.py:87
  210.8 1.9 collective-permute-start.18
  212.7 5.2 %collective-permute-done.18 = f32[1,128,512]{2,1,0:T(8,128)S(1)} collective-permute-done((f32[1,128,512]{2,1,0:T(8,128)S(1)}, f32[1,128,512]{2,1,0:T(8,128)S(1)}, u32[]{:S(2)}, u32[]{:S(2)}) %collective-permute-start.18) | collective-permute-done | bytes 262176 | tf_op jit(solution)/shard_map/ppermute | solution.py:111
  218.0 3.0 collective-permute-start.19
  221.0 5.6 %collective-permute-done.19 = f32[1,128,512]{2,1,0:T(8,128)S(1)} collective-permute-done((f32[1,128,512]{2,1,0:T(8,128)S(1)}, f32[1,128,512]{2,1,0:T(8,128)S(1)}, u32[]{:S(2)}, u32[]{:S(2)}) %collective-permute-start.19) | collective-permute-done | bytes 262176 | tf_op jit(solution)/shard_map/ppermute | solution.py:111
  226.7 4.4 %collective-permute-start.20 = (f32[1,128,512]{2,1,0:T(8,128)S(1)}, f32[1,128,512]{2,1,0:T(8,128)S(1)}, u32[]{:S(2)}, u32[]{:S(2)}) collective-permute-start(f32[1,128,512]{2,1,0:T(8,128)S(1)} %select_add_fusion.3), channel_id=1, source_target_pairs={{0,32},{8,40},{16,48},{24,56},{32,0},{40,8},{48,16},{56,24},{64,96... | collective-permute-start | bytes 786440 | tf_op jit(solution)/shard_map/ppermute | solution.py:111
  231.1 4.0 %collective-permute-done.20 = f32[1,128,512]{2,1,0:T(8,128)S(1)} collective-permute-done((f32[1,128,512]{2,1,0:T(8,128)S(1)}, f32[1,128,512]{2,1,0:T(8,128)S(1)}, u32[]{:S(2)}, u32[]{:S(2)}) %collective-permute-start.20) | collective-permute-done | bytes 262176 | tf_op jit(solution)/shard_map/ppermute | solution.py:111
  235.2 2.1 collective-permute-start.21
  237.3 6.2 %collective-permute-done.21 = f32[1,128,512]{2,1,0:T(8,128)S(1)} collective-permute-done((f32[1,128,512]{2,1,0:T(8,128)S(1)}, f32[1,128,512]{2,1,0:T(8,128)S(1)}, u32[]{:S(2)}, u32[]{:S(2)}) %collective-permute-start.21) | collective-permute-done | bytes 262176 | tf_op jit(solution)/shard_map/ppermute | solution.py:111
  243.7 3.3 collective-permute-start.22
  247.0 3.8 collective-permute-done.22
  251.6 4.7 %collective-permute-start.23 = (f32[1,128,512]{2,1,0:T(8,128)}, f32[1,128,512]{2,1,0:T(8,128)}, u32[]{:S(2)}, u32[]{:S(2)}) collective-permute-start(f32[1,128,512]{2,1,0:T(8,128)} %select_add_fusion), channel_id=1, source_target_pairs={{0,256},{8,264},{16,272},{24,280},{32,288},{40,296},{48,304},{56,3... | collective-permute-start | bytes 786440 | tf_op jit(solution)/shard_map/ppermute | solution.py:111
  256.3 4.2 %collective-permute-done.23 = f32[1,128,512]{2,1,0:T(8,128)} collective-permute-done((f32[1,128,512]{2,1,0:T(8,128)}, f32[1,128,512]{2,1,0:T(8,128)}, u32[]{:S(2)}, u32[]{:S(2)}) %collective-permute-start.23) | collective-permute-done | bytes 262176 | tf_op jit(solution)/shard_map/ppermute | solution.py:111
  266.4 27.2 %collective-permute-start.24 = (f32[1184,128]{1,0:T(8,128)S(1)}, f32[1184,128]{1,0:T(8,128)}, u32[]{:S(2)}, u32[]{:S(2)}) collective-permute-start(f32[1184,128]{1,0:T(8,128)S(1)} %constant_dynamic-slice_fusion.3), channel_id=1, source_target_pairs={{0,1},{1,0},{2,3},{3,2},{4,5},{5,4},{6,7},{7,6},{8,9},{9,8},{10,11... | collective-permute-start | bytes 1818632 | tf_op jit(solution)/shard_map/ppermute | solution.py:136
  296.5 12.0 %collective-permute-start.25 = (f32[296,128]{1,0:T(8,128)S(1)}, f32[296,128]{1,0:T(8,128)S(1)}, u32[]{:S(2)}, u32[]{:S(2)}) collective-permute-start(f32[296,128]{1,0:T(8,128)S(1)} %get-tuple-element.33), channel_id=1, source_target_pairs={{0,2},{1,7},{2,4},{3,1},{4,6},{5,3},{6,0},{7,5},{8,10},{9,15},{10,... | collective-permute-start | bytes 454664 | tf_op jit(solution)/shard_map/ppermute | solution.py:147
  308.6 5.5 %collective-permute-done.25 = f32[296,128]{1,0:T(8,128)S(1)} collective-permute-done((f32[296,128]{1,0:T(8,128)S(1)}, f32[296,128]{1,0:T(8,128)S(1)}, u32[]{:S(2)}, u32[]{:S(2)}) %collective-permute-start.25) | collective-permute-done | bytes 151584 | tf_op jit(solution)/shard_map/ppermute | solution.py:147
  314.2 7.8 %collective-permute-start.26 = (f32[296,128]{1,0:T(8,128)S(1)}, f32[296,128]{1,0:T(8,128)S(1)}, u32[]{:S(2)}, u32[]{:S(2)}) collective-permute-start(f32[296,128]{1,0:T(8,128)S(1)} %get-tuple-element.31), channel_id=1, source_target_pairs={{0,2},{1,7},{2,4},{3,1},{4,6},{5,3},{6,0},{7,5},{8,10},{9,15},{10,... | collective-permute-start | bytes 454664 | tf_op jit(solution)/shard_map/ppermute | solution.py:147
  322.2 3.0 collective-permute-done.26
  325.2 7.2 %collective-permute-start.27 = (f32[296,128]{1,0:T(8,128)S(1)}, f32[296,128]{1,0:T(8,128)S(1)}, u32[]{:S(2)}, u32[]{:S(2)}) collective-permute-start(f32[296,128]{1,0:T(8,128)S(1)} %get-tuple-element.29), channel_id=1, source_target_pairs={{0,2},{1,7},{2,4},{3,1},{4,6},{5,3},{6,0},{7,5},{8,10},{9,15},{10,... | collective-permute-start | bytes 454664 | tf_op jit(solution)/shard_map/ppermute | solution.py:147
  332.5 2.6 collective-permute-done.27
  335.1 9.0 %collective-permute-start.28 = (f32[296,128]{1,0:T(8,128)S(1)}, f32[296,128]{1,0:T(8,128)S(1)}, u32[]{:S(2)}, u32[]{:S(2)}) collective-permute-start(f32[296,128]{1,0:T(8,128)S(1)} %dynamic-slice_bitcast_fusion.2), channel_id=1, source_target_pairs={{0,2},{1,7},{2,4},{3,1},{4,6},{5,3},{6,0},{7,5},{8,10},{9,15},{10,... | collective-permute-start | bytes 454664 | tf_op jit(solution)/shard_map/ppermute | solution.py:153
  344.3 6.9 %collective-permute-done.28 = f32[296,128]{1,0:T(8,128)S(1)} collective-permute-done((f32[296,128]{1,0:T(8,128)S(1)}, f32[296,128]{1,0:T(8,128)S(1)}, u32[]{:S(2)}, u32[]{:S(2)}) %collective-permute-start.28) | collective-permute-done | bytes 151584 | tf_op jit(solution)/shard_map/ppermute | solution.py:153
  351.2 7.7 %collective-permute-start.29 = (f32[296,128]{1,0:T(8,128)S(1)}, f32[296,128]{1,0:T(8,128)S(1)}, u32[]{:S(2)}, u32[]{:S(2)}) collective-permute-start(f32[296,128]{1,0:T(8,128)S(1)} %dynamic-slice_bitcast_fusion.1), channel_id=1, source_target_pairs={{0,2},{1,7},{2,4},{3,1},{4,6},{5,3},{6,0},{7,5},{8,10},{9,15},{10,... | collective-permute-start | bytes 454664 | tf_op jit(solution)/shard_map/ppermute | solution.py:153
  359.1 6.5 %collective-permute-done.29 = f32[296,128]{1,0:T(8,128)S(1)} collective-permute-done((f32[296,128]{1,0:T(8,128)S(1)}, f32[296,128]{1,0:T(8,128)S(1)}, u32[]{:S(2)}, u32[]{:S(2)}) %collective-permute-start.29) | collective-permute-done | bytes 151584 | tf_op jit(solution)/shard_map/ppermute | solution.py:153
  365.6 4.4 %collective-permute-start.30 = (f32[296,128]{1,0:T(8,128)S(1)}, f32[296,128]{1,0:T(8,128)S(1)}, u32[]{:S(2)}, u32[]{:S(2)}) collective-permute-start(f32[296,128]{1,0:T(8,128)S(1)} %dynamic-slice_bitcast_fusion), channel_id=1, source_target_pairs={{0,2},{1,7},{2,4},{3,1},{4,6},{5,3},{6,0},{7,5},{8,10},{9,15},{10,... | collective-permute-start | bytes 454664 | tf_op jit(solution)/shard_map/ppermute | solution.py:153
  370.2 5.6 %collective-permute-done.30 = f32[296,128]{1,0:T(8,128)S(1)} collective-permute-done((f32[296,128]{1,0:T(8,128)S(1)}, f32[296,128]{1,0:T(8,128)S(1)}, u32[]{:S(2)}, u32[]{:S(2)}) %collective-permute-start.30) | collective-permute-done | bytes 151584 | tf_op jit(solution)/shard_map/ppermute | solution.py:153
  375.8 12.8 %collective-permute-start.31 = (f32[1184,128]{1,0:T(8,128)S(1)}, f32[1184,128]{1,0:T(8,128)S(1)}, u32[]{:S(2)}, u32[]{:S(2)}) collective-permute-start(f32[1184,128]{1,0:T(8,128)S(1)} %bitcast.515), channel_id=1, source_target_pairs={{0,1},{1,0},{2,3},{3,2},{4,5},{5,4},{6,7},{7,6},{8,9},{9,8},{10,11... | collective-permute-start | bytes 1818632 | tf_op jit(solution)/shard_map/ppermute | solution.py:156
  (265 shorter events, 55.5 us)
Async XLA Ops:
  0.6 2.2 copy-start.1
  2.5 1.1 copy-start
  3.9 0.9 copy-start.19
  5.3 9.4 %collective-permute-start = (f32[1,129,512]{2,1,0:T(8,128)S(1)}, f32[1,129,512]{2,1,0:T(8,128)S(1)}, u32[]{:S(2)}, u32[]{:S(2)}) collective-permute-start(f32[1,129,512]{2,1,0:T(8,128)S(1)} %pad_maximum_fusion.1), channel_id=1, source_target_pairs={{0,8},{8,0},{16,24},{24,16},{32,40},{40,32},{48,56},{56,48},{64,72... | collective-permute-start | bytes 792584 | tf_op jit(solution)/shard_map/ppermute | solution.py:87
  14.9 10.0 %collective-permute-start.1 = (f32[1,129,512]{2,1,0:T(8,128)S(1)}, f32[1,129,512]{2,1,0:T(8,128)S(1)}, u32[]{:S(2)}, u32[]{:S(2)}) collective-permute-start(f32[1,129,512]{2,1,0:T(8,128)S(1)} %pad_maximum_fusion.2), channel_id=1, source_target_pairs={{0,16},{8,24},{16,0},{24,8},{32,48},{40,56},{48,32},{56,40},{64,80... | collective-permute-start | bytes 792584 | tf_op jit(solution)/shard_map/ppermute | solution.py:87
  25.0 7.9 %collective-permute-start.2 = (f32[1,129,512]{2,1,0:T(8,128)S(1)}, f32[1,129,512]{2,1,0:T(8,128)S(1)}, u32[]{:S(2)}, u32[]{:S(2)}) collective-permute-start(f32[1,129,512]{2,1,0:T(8,128)S(1)} %pad_maximum_fusion.3), channel_id=1, source_target_pairs={{0,32},{8,40},{16,48},{24,56},{32,0},{40,8},{48,16},{56,24},{64,96... | collective-permute-start | bytes 792584 | tf_op jit(solution)/shard_map/ppermute | solution.py:87
  33.0 13.4 %collective-permute-start.3 = (f32[1,129,512]{2,1,0:T(8,128)S(1)}, f32[1,129,512]{2,1,0:T(8,128)S(1)}, u32[]{:S(2)}, u32[]{:S(2)}) collective-permute-start(f32[1,129,512]{2,1,0:T(8,128)S(1)} %pad_maximum_fusion.4), channel_id=1, source_target_pairs={{0,64},{8,72},{16,80},{24,88},{32,96},{40,104},{48,112},{56,120},{... | collective-permute-start | bytes 792584 | tf_op jit(solution)/shard_map/ppermute | solution.py:87
  46.6 8.7 %collective-permute-start.4 = (f32[1,129,512]{2,1,0:T(8,128)S(1)}, f32[1,129,512]{2,1,0:T(8,128)S(1)}, u32[]{:S(2)}, u32[]{:S(2)}) collective-permute-start(f32[1,129,512]{2,1,0:T(8,128)S(1)} %pad_maximum_fusion.5), channel_id=1, source_target_pairs={{0,128},{8,136},{16,144},{24,152},{32,160},{40,168},{48,176},{56,1... | collective-permute-start | bytes 792584 | tf_op jit(solution)/shard_map/ppermute | solution.py:87
  55.5 9.3 %collective-permute-start.5 = (f32[1,129,512]{2,1,0:T(8,128)S(1)}, f32[1,129,512]{2,1,0:T(8,128)S(1)}, u32[]{:S(2)}, u32[]{:S(2)}) collective-permute-start(f32[1,129,512]{2,1,0:T(8,128)S(1)} %pad_maximum_fusion.6), channel_id=1, source_target_pairs={{0,256},{8,264},{16,272},{24,280},{32,288},{40,296},{48,304},{56,3... | collective-permute-start | bytes 792584 | tf_op jit(solution)/shard_map/ppermute | solution.py:87
  64.8 0.7 copy-start.18
  69.3 7.1 %collective-permute-start.6 = (f32[1,128,512]{2,1,0:T(8,128)S(1)}, f32[1,128,512]{2,1,0:T(8,128)S(1)}, u32[]{:S(2)}, u32[]{:S(2)}) collective-permute-start(f32[1,128,512]{2,1,0:T(8,128)S(1)} %fusion.118), channel_id=1, source_target_pairs={{0,8},{8,0},{16,24},{24,16},{32,40},{40,32},{48,56},{56,48},{64,72... | collective-permute-start | bytes 786440 | tf_op jit(solution)/shard_map/ppermute | solution.py:111
  76.5 8.6 %collective-permute-start.7 = (f32[1,128,512]{2,1,0:T(8,128)S(1)}, f32[1,128,512]{2,1,0:T(8,128)S(1)}, u32[]{:S(2)}, u32[]{:S(2)}) collective-permute-start(f32[1,128,512]{2,1,0:T(8,128)S(1)} %select_add_fusion.14), channel_id=1, source_target_pairs={{0,16},{8,24},{16,0},{24,8},{32,48},{40,56},{48,32},{56,40},{64,80... | collective-permute-start | bytes 786440 | tf_op jit(solution)/shard_map/ppermute | solution.py:111
  85.2 9.4 %collective-permute-start.8 = (f32[1,128,512]{2,1,0:T(8,128)S(1)}, f32[1,128,512]{2,1,0:T(8,128)S(1)}, u32[]{:S(2)}, u32[]{:S(2)}) collective-permute-start(f32[1,128,512]{2,1,0:T(8,128)S(1)} %select_add_fusion.13), channel_id=1, source_target_pairs={{0,32},{8,40},{16,48},{24,56},{32,0},{40,8},{48,16},{56,24},{64,96... | collective-permute-start | bytes 786440 | tf_op jit(solution)/shard_map/ppermute | solution.py:111
  94.7 8.9 %collective-permute-start.9 = (f32[1,128,512]{2,1,0:T(8,128)S(1)}, f32[1,128,512]{2,1,0:T(8,128)S(1)}, u32[]{:S(2)}, u32[]{:S(2)}) collective-permute-start(f32[1,128,512]{2,1,0:T(8,128)S(1)} %select_add_fusion.12), channel_id=1, source_target_pairs={{0,64},{8,72},{16,80},{24,88},{32,96},{40,104},{48,112},{56,120},{... | collective-permute-start | bytes 786440 | tf_op jit(solution)/shard_map/ppermute | solution.py:111
  103.7 12.4 %copy-start.20 = (f32[1,128]{1,0:T(1,128)S(1)}, f32[1,128]{1,0:T(1,128)}, u32[]{:S(2)}) copy-start(f32[1,128]{1,0:T(1,128)} %param.11) | copy-start | bytes 1540
  103.7 7.4 %collective-permute-start.10 = (f32[1,128,512]{2,1,0:T(8,128)S(1)}, f32[1,128,512]{2,1,0:T(8,128)S(1)}, u32[]{:S(2)}, u32[]{:S(2)}) collective-permute-start(f32[1,128,512]{2,1,0:T(8,128)S(1)} %select_add_fusion.11), channel_id=1, source_target_pairs={{0,128},{8,136},{16,144},{24,152},{32,160},{40,168},{48,176},{56,1... | collective-permute-start | bytes 786440 | tf_op jit(solution)/shard_map/ppermute | solution.py:111
  111.9 11.5 %collective-permute-start.11 = (f32[1,128,512]{2,1,0:T(8,128)}, f32[1,128,512]{2,1,0:T(8,128)}, u32[]{:S(2)}, u32[]{:S(2)}) collective-permute-start(f32[1,128,512]{2,1,0:T(8,128)} %select_add_fusion.10), channel_id=1, source_target_pairs={{0,256},{8,264},{16,272},{24,280},{32,288},{40,296},{48,304},{56,3... | collective-permute-start | bytes 786440 | tf_op jit(solution)/shard_map/ppermute | solution.py:111
  124.5 0.9 copy-start.9
  125.8 2.4 copy-start.6
  125.8 1.0 copy-start.2
  127.3 1.0 copy-start.5
  128.6 1.0 copy-start.3
  132.4 7.6 %collective-permute-start.12 = (f32[1,129,512]{2,1,0:T(8,128)}, f32[1,129,512]{2,1,0:T(8,128)}, u32[]{:S(2)}, u32[]{:S(2)}) collective-permute-start(f32[1,129,512]{2,1,0:T(8,128)} %pad_maximum_fusion.7), channel_id=1, source_target_pairs={{0,8},{8,0},{16,24},{24,16},{32,40},{40,32},{48,56},{56,48},{64,72... | collective-permute-start | bytes 792584 | tf_op jit(solution)/shard_map/ppermute | solution.py:87
  141.8 0.7 copy-start.11
  143.2 9.9 %collective-permute-start.13 = (f32[1,129,512]{2,1,0:T(8,128)}, f32[1,129,512]{2,1,0:T(8,128)}, u32[]{:S(2)}, u32[]{:S(2)}) collective-permute-start(f32[1,129,512]{2,1,0:T(8,128)} %pad_maximum_fusion.8), channel_id=1, source_target_pairs={{0,16},{8,24},{16,0},{24,8},{32,48},{40,56},{48,32},{56,40},{64,80... | collective-permute-start | bytes 792584 | tf_op jit(solution)/shard_map/ppermute | solution.py:87
  157.3 9.6 %collective-permute-start.14 = (f32[1,129,512]{2,1,0:T(8,128)}, f32[1,129,512]{2,1,0:T(8,128)}, u32[]{:S(2)}, u32[]{:S(2)}) collective-permute-start(f32[1,129,512]{2,1,0:T(8,128)} %pad_maximum_fusion.9), channel_id=1, source_target_pairs={{0,32},{8,40},{16,48},{24,56},{32,0},{40,8},{48,16},{56,24},{64,96... | collective-permute-start | bytes 792584 | tf_op jit(solution)/shard_map/ppermute | solution.py:87
  171.2 9.8 %collective-permute-start.15 = (f32[1,129,512]{2,1,0:T(8,128)}, f32[1,129,512]{2,1,0:T(8,128)}, u32[]{:S(2)}, u32[]{:S(2)}) collective-permute-start(f32[1,129,512]{2,1,0:T(8,128)} %pad_maximum_fusion.10), channel_id=1, source_target_pairs={{0,64},{8,72},{16,80},{24,88},{32,96},{40,104},{48,112},{56,120},{... | collective-permute-start | bytes 792584 | tf_op jit(solution)/shard_map/ppermute | solution.py:87
  185.2 8.6 %collective-permute-start.16 = (f32[1,129,512]{2,1,0:T(8,128)}, f32[1,129,512]{2,1,0:T(8,128)}, u32[]{:S(2)}, u32[]{:S(2)}) collective-permute-start(f32[1,129,512]{2,1,0:T(8,128)} %pad_maximum_fusion.11), channel_id=1, source_target_pairs={{0,128},{8,136},{16,144},{24,152},{32,160},{40,168},{48,176},{56,1... | collective-permute-start | bytes 792584 | tf_op jit(solution)/shard_map/ppermute | solution.py:87
  196.4 9.1 %collective-permute-start.17 = (f32[1,129,512]{2,1,0:T(8,128)}, f32[1,129,512]{2,1,0:T(8,128)}, u32[]{:S(2)}, u32[]{:S(2)}) collective-permute-start(f32[1,129,512]{2,1,0:T(8,128)} %pad_maximum_fusion.12), channel_id=1, source_target_pairs={{0,256},{8,264},{16,272},{24,280},{32,288},{40,296},{48,304},{56,3... | collective-permute-start | bytes 792584 | tf_op jit(solution)/shard_map/ppermute | solution.py:87
  207.0 1.0 copy-start.12
  207.1 1.0 copy-start.7
  210.8 7.1 %collective-permute-start.18 = (f32[1,128,512]{2,1,0:T(8,128)S(1)}, f32[1,128,512]{2,1,0:T(8,128)S(1)}, u32[]{:S(2)}, u32[]{:S(2)}) collective-permute-start(f32[1,128,512]{2,1,0:T(8,128)S(1)} %fusion.76), channel_id=1, source_target_pairs={{0,8},{8,0},{16,24},{24,16},{32,40},{40,32},{48,56},{56,48},{64,72... | collective-permute-start | bytes 786440 | tf_op jit(solution)/shard_map/ppermute | solution.py:111
  218.0 8.6 %collective-permute-start.19 = (f32[1,128,512]{2,1,0:T(8,128)S(1)}, f32[1,128,512]{2,1,0:T(8,128)S(1)}, u32[]{:S(2)}, u32[]{:S(2)}) collective-permute-start(f32[1,128,512]{2,1,0:T(8,128)S(1)} %select_add_fusion.4), channel_id=1, source_target_pairs={{0,16},{8,24},{16,0},{24,8},{32,48},{40,56},{48,32},{56,40},{64,80... | collective-permute-start | bytes 786440 | tf_op jit(solution)/shard_map/ppermute | solution.py:111
  226.6 4.5 %copy-start.14 = (f32[1,128,512]{2,1,0:T(8,128)}, f32[1,128,512]{2,1,0:T(8,128)S(1)}, u32[]{:S(2)}) copy-start(f32[1,128,512]{2,1,0:T(8,128)S(1)} %collective-permute-done.19) | copy-start | bytes 786436
  226.7 33.8 %copy-start.13 = (f32[1,128,512]{2,1,0:T(8,128)S(1)}, f32[1,128,512]{2,1,0:T(8,128)}, u32[]{:S(2)}) copy-start(f32[1,128,512]{2,1,0:T(8,128)} %copy-done.12) | copy-start | bytes 786436
  226.7 8.4 %collective-permute-start.20 = (f32[1,128,512]{2,1,0:T(8,128)S(1)}, f32[1,128,512]{2,1,0:T(8,128)S(1)}, u32[]{:S(2)}, u32[]{:S(2)}) collective-permute-start(f32[1,128,512]{2,1,0:T(8,128)S(1)} %select_add_fusion.3), channel_id=1, source_target_pairs={{0,32},{8,40},{16,48},{24,56},{32,0},{40,8},{48,16},{56,24},{64,96... | collective-permute-start | bytes 786440 | tf_op jit(solution)/shard_map/ppermute | solution.py:111
  235.1 16.5 %copy-start.15 = (f32[1,128,512]{2,1,0:T(8,128)}, f32[1,128,512]{2,1,0:T(8,128)S(1)}, u32[]{:S(2)}) copy-start(f32[1,128,512]{2,1,0:T(8,128)S(1)} %collective-permute-done.20) | copy-start | bytes 786436
  235.2 8.4 %collective-permute-start.21 = (f32[1,128,512]{2,1,0:T(8,128)S(1)}, f32[1,128,512]{2,1,0:T(8,128)S(1)}, u32[]{:S(2)}, u32[]{:S(2)}) collective-permute-start(f32[1,128,512]{2,1,0:T(8,128)S(1)} %select_add_fusion.2), channel_id=1, source_target_pairs={{0,64},{8,72},{16,80},{24,88},{32,96},{40,104},{48,112},{56,120},{... | collective-permute-start | bytes 786440 | tf_op jit(solution)/shard_map/ppermute | solution.py:111
  243.6 8.0 %copy-start.16 = (f32[1,128,512]{2,1,0:T(8,128)}, f32[1,128,512]{2,1,0:T(8,128)S(1)}, u32[]{:S(2)}) copy-start(f32[1,128,512]{2,1,0:T(8,128)S(1)} %collective-permute-done.21) | copy-start | bytes 786436
  243.7 7.1 %collective-permute-start.22 = (f32[1,128,512]{2,1,0:T(8,128)S(1)}, f32[1,128,512]{2,1,0:T(8,128)S(1)}, u32[]{:S(2)}, u32[]{:S(2)}) collective-permute-start(f32[1,128,512]{2,1,0:T(8,128)S(1)} %select_add_fusion.1), channel_id=1, source_target_pairs={{0,128},{8,136},{16,144},{24,152},{32,160},{40,168},{48,176},{56,1... | collective-permute-start | bytes 786440 | tf_op jit(solution)/shard_map/ppermute | solution.py:111
  250.8 0.8 copy-start.17
  251.6 8.9 %collective-permute-start.23 = (f32[1,128,512]{2,1,0:T(8,128)}, f32[1,128,512]{2,1,0:T(8,128)}, u32[]{:S(2)}, u32[]{:S(2)}) collective-permute-start(f32[1,128,512]{2,1,0:T(8,128)} %select_add_fusion), channel_id=1, source_target_pairs={{0,256},{8,264},{16,272},{24,280},{32,288},{40,296},{48,304},{56,3... | collective-permute-start | bytes 786440 | tf_op jit(solution)/shard_map/ppermute | solution.py:111
  263.5 1.0 copy-start.8
  263.5 1.0 copy-start.10
  266.4 28.9 %collective-permute-start.24 = (f32[1184,128]{1,0:T(8,128)S(1)}, f32[1184,128]{1,0:T(8,128)}, u32[]{:S(2)}, u32[]{:S(2)}) collective-permute-start(f32[1184,128]{1,0:T(8,128)S(1)} %constant_dynamic-slice_fusion.3), channel_id=1, source_target_pairs={{0,1},{1,0},{2,3},{3,2},{4,5},{5,4},{6,7},{7,6},{8,9},{9,8},{10,11... | collective-permute-start | bytes 1818632 | tf_op jit(solution)/shard_map/ppermute | solution.py:136
  296.5 17.7 %collective-permute-start.25 = (f32[296,128]{1,0:T(8,128)S(1)}, f32[296,128]{1,0:T(8,128)S(1)}, u32[]{:S(2)}, u32[]{:S(2)}) collective-permute-start(f32[296,128]{1,0:T(8,128)S(1)} %get-tuple-element.33), channel_id=1, source_target_pairs={{0,2},{1,7},{2,4},{3,1},{4,6},{5,3},{6,0},{7,5},{8,10},{9,15},{10,... | collective-permute-start | bytes 454664 | tf_op jit(solution)/shard_map/ppermute | solution.py:147
  314.2 11.0 %collective-permute-start.26 = (f32[296,128]{1,0:T(8,128)S(1)}, f32[296,128]{1,0:T(8,128)S(1)}, u32[]{:S(2)}, u32[]{:S(2)}) collective-permute-start(f32[296,128]{1,0:T(8,128)S(1)} %get-tuple-element.31), channel_id=1, source_target_pairs={{0,2},{1,7},{2,4},{3,1},{4,6},{5,3},{6,0},{7,5},{8,10},{9,15},{10,... | collective-permute-start | bytes 454664 | tf_op jit(solution)/shard_map/ppermute | solution.py:147
  325.2 9.8 %collective-permute-start.27 = (f32[296,128]{1,0:T(8,128)S(1)}, f32[296,128]{1,0:T(8,128)S(1)}, u32[]{:S(2)}, u32[]{:S(2)}) collective-permute-start(f32[296,128]{1,0:T(8,128)S(1)} %get-tuple-element.29), channel_id=1, source_target_pairs={{0,2},{1,7},{2,4},{3,1},{4,6},{5,3},{6,0},{7,5},{8,10},{9,15},{10,... | collective-permute-start | bytes 454664 | tf_op jit(solution)/shard_map/ppermute | solution.py:147
  335.1 16.0 %collective-permute-start.28 = (f32[296,128]{1,0:T(8,128)S(1)}, f32[296,128]{1,0:T(8,128)S(1)}, u32[]{:S(2)}, u32[]{:S(2)}) collective-permute-start(f32[296,128]{1,0:T(8,128)S(1)} %dynamic-slice_bitcast_fusion.2), channel_id=1, source_target_pairs={{0,2},{1,7},{2,4},{3,1},{4,6},{5,3},{6,0},{7,5},{8,10},{9,15},{10,... | collective-permute-start | bytes 454664 | tf_op jit(solution)/shard_map/ppermute | solution.py:153
  344.3 44.4 %copy-start.4 = (bf16[128,9,128]{0,2,1:T(8,128)(2,1)S(1)}, bf16[128,9,128]{0,2,1:T(8,128)(2,1)}, u32[]{:S(2)}) copy-start(bf16[128,9,128]{0,2,1:T(8,128)(2,1)} %copy.26) | copy-start | bytes 884740
  351.2 14.4 %collective-permute-start.29 = (f32[296,128]{1,0:T(8,128)S(1)}, f32[296,128]{1,0:T(8,128)S(1)}, u32[]{:S(2)}, u32[]{:S(2)}) collective-permute-start(f32[296,128]{1,0:T(8,128)S(1)} %dynamic-slice_bitcast_fusion.1), channel_id=1, source_target_pairs={{0,2},{1,7},{2,4},{3,1},{4,6},{5,3},{6,0},{7,5},{8,10},{9,15},{10,... | collective-permute-start | bytes 454664 | tf_op jit(solution)/shard_map/ppermute | solution.py:153
  365.6 10.1 %collective-permute-start.30 = (f32[296,128]{1,0:T(8,128)S(1)}, f32[296,128]{1,0:T(8,128)S(1)}, u32[]{:S(2)}, u32[]{:S(2)}) collective-permute-start(f32[296,128]{1,0:T(8,128)S(1)} %dynamic-slice_bitcast_fusion), channel_id=1, source_target_pairs={{0,2},{1,7},{2,4},{3,1},{4,6},{5,3},{6,0},{7,5},{8,10},{9,15},{10,... | collective-permute-start | bytes 454664 | tf_op jit(solution)/shard_map/ppermute | solution.py:153
  375.8 14.4 %collective-permute-start.31 = (f32[1184,128]{1,0:T(8,128)S(1)}, f32[1184,128]{1,0:T(8,128)S(1)}, u32[]{:S(2)}, u32[]{:S(2)}) collective-permute-start(f32[1184,128]{1,0:T(8,128)S(1)} %bitcast.515), channel_id=1, source_target_pairs={{0,1},{1,0},{2,3},{3,2},{4,5},{5,4},{6,7},{7,6},{8,9},{9,8},{10,11... | collective-permute-start | bytes 1818632 | tf_op jit(solution)/shard_map/ppermute | solution.py:156

commit v10 on v9

--- a/solution.py
+++ b/solution.py
@@ -119,44 +119,15 @@
 
 def batch_sum(value, axis):
     count = lax.axis_size(axis)
-    chips = count // 2
-    me = lax.axis_index(axis)
-    core = me % 2
-    chip = me // 2
     shape = value.shape
     flat = value.reshape(-1)
     lanes = 128
     quantum = lanes * 8 * count
     padded_size = -(-flat.shape[0] // quantum) * quantum
-    current = jnp.pad(flat, (0, padded_size - flat.shape[0])).reshape(-1, lanes)
-    half_rows = current.shape[0] // 2
-    partner = [(k, k ^ 1) for k in range(count)]
-    keep = lax.dynamic_slice_in_dim(current, core * half_rows, half_rows, 0)
-    give = lax.dynamic_slice_in_dim(current, (1 - core) * half_rows, half_rows, 0)
-    half = keep + lax.ppermute(give, axis, partner)
-
-    def following(k):
-        step = 1 if k % 2 == 0 else -1
-        return ((k // 2 + step) % chips) * 2 + k % 2
-
-    ring = [(k, following(k)) for k in range(count)]
-    place = jnp.where(core == 0, chip, (chips - chip) % chips)
-    pieces = half.reshape(chips, half_rows // chips, lanes)
-    for t in range(chips - 1):
-        sent = lax.dynamic_index_in_dim(pieces, (place - t) % chips, 0, False)
-        got = lax.ppermute(sent, axis, ring)
-        slot = (place - t - 1 + chips) % chips
-        mine = lax.dynamic_index_in_dim(pieces, slot, 0, False)
-        pieces = lax.dynamic_update_index_in_dim(pieces, mine + got, slot, 0)
-    for t in range(chips - 1):
-        sent = lax.dynamic_index_in_dim(pieces, (place + 1 - t + chips) % chips, 0, False)
-        got = lax.ppermute(sent, axis, ring)
-        pieces = lax.dynamic_update_index_in_dim(pieces, got, (place - t + chips) % chips, 0)
-    half = pieces.reshape(half_rows, lanes)
-    other = lax.ppermute(half, axis, partner)
-    whole = jnp.zeros_like(current)
-    whole = lax.dynamic_update_slice_in_dim(whole, half, core * half_rows, 0)
-    whole = lax.dynamic_update_slice_in_dim(whole, other, (1 - core) * half_rows, 0)
+    slices = jnp.pad(flat, (0, padded_size - flat.shape[0])).reshape(count, -1, lanes)
+    mine = jnp.sum(lax.all_to_all(slices, axis, 0, 0), axis=0)
+    spread = jnp.broadcast_to(mine[None], slices.shape)
+    whole = lax.all_to_all(spread, axis, 0, 0)
     return whole.reshape(-1)[: flat.shape[0]].reshape(shape)
 
 

time: 394 us -> 439 us (1.11)
  the two profiles are of different devices: /device:TPU:75 before, /device:TPU:12 now
where the time goes in v10:
time: 439 us; the launch traced here: 437 us
  waiting for transfers between devices  219 us (50%)
  starting transfers between devices  84.6 us (19%)
  blocking collectives  75.5 us (17%)
  other arithmetic  38.3 us (9%)
  local copies, waits for them, and re-layouts  8.72 us (2%)
  matrix products  7.91 us (2%)
    ppermute x12, waiting for transfers between devices, butterfly_first(): got = lax.ppermute(packed, axis, [(k, k ^ step) for k in range(count)])  84.9 us
    all_to_all x1, blocking collectives, batch_sum(): mine = jnp.sum(lax.all_to_all(slices, axis, 0, 0), axis=0)  75.5 us
    ppermute x12, waiting for transfers between devices, butterfly_again(): got = lax.ppermute(block_sum, axis, [(k, k ^ step) for k in range(count)])  74 us
    all_to_all x1, waiting for transfers between devices, batch_sum(): whole = lax.all_to_all(spread, axis, 0, 0)  60.5 us
    ppermute x12, starting transfers between devices, butterfly_first(): got = lax.ppermute(packed, axis, [(k, k ^ step) for k in range(count)])  43.9 us
    ppermute x12, starting transfers between devices, butterfly_again(): got = lax.ppermute(block_sum, axis, [(k, k ^ step) for k in range(count)])  37.1 us
    unnamed x96, other arithmetic  9.1 us
  transfers between devices with their start and end apart: 25, of which 25 were waited for; matrix products, arithmetic and copies ran while one was open for 1% of the time, Pallas kernels for 0%

profile of v10, /device:TPU:12, one launch (start us, length us, event | category | flops | bytes accessed | tf_op | source)
XLA Modules:
  0.0 437.0 jit_solution(18106455261353713210)
XLA Ops:
  5.3 3.1 collective-permute-start
  8.5 7.2 %collective-permute-done = f32[1,129,512]{2,1,0:T(8,128)S(1)} collective-permute-done((f32[1,129,512]{2,1,0:T(8,128)S(1)}, f32[1,129,512]{2,1,0:T(8,128)S(1)}, u32[]{:S(2)}, u32[]{:S(2)}) %collective-permute-start) | collective-permute-done | bytes 264224 | tf_op jit(solution)/shard_map/ppermute | solution.py:87
  15.8 2.4 collective-permute-start.1
  18.2 8.5 %collective-permute-done.1 = f32[1,129,512]{2,1,0:T(8,128)S(1)} collective-permute-done((f32[1,129,512]{2,1,0:T(8,128)S(1)}, f32[1,129,512]{2,1,0:T(8,128)S(1)}, u32[]{:S(2)}, u32[]{:S(2)}) %collective-permute-start.1) | collective-permute-done | bytes 264224 | tf_op jit(solution)/shard_map/ppermute | solution.py:87
  26.8 3.8 collective-permute-start.2
  30.7 4.8 %collective-permute-done.2 = f32[1,129,512]{2,1,0:T(8,128)S(1)} collective-permute-done((f32[1,129,512]{2,1,0:T(8,128)S(1)}, f32[1,129,512]{2,1,0:T(8,128)S(1)}, u32[]{:S(2)}, u32[]{:S(2)}) %collective-permute-start.2) | collective-permute-done | bytes 264224 | tf_op jit(solution)/shard_map/ppermute | solution.py:87
  35.6 5.2 %collective-permute-start.3 = (f32[1,129,512]{2,1,0:T(8,128)S(1)}, f32[1,129,512]{2,1,0:T(8,128)S(1)}, u32[]{:S(2)}, u32[]{:S(2)}) collective-permute-start(f32[1,129,512]{2,1,0:T(8,128)S(1)} %pad_maximum_fusion.4), channel_id=1, source_target_pairs={{0,64},{8,72},{16,80},{24,88},{32,96},{40,104},{48,112},{56,120},{... | collective-permute-start | bytes 792584 | tf_op jit(solution)/shard_map/ppermute | solution.py:87
  40.8 10.1 %collective-permute-done.3 = f32[1,129,512]{2,1,0:T(8,128)S(1)} collective-permute-done((f32[1,129,512]{2,1,0:T(8,128)S(1)}, f32[1,129,512]{2,1,0:T(8,128)S(1)}, u32[]{:S(2)}, u32[]{:S(2)}) %collective-permute-start.3) | collective-permute-done | bytes 264224 | tf_op jit(solution)/shard_map/ppermute | solution.py:87
  51.0 2.4 collective-permute-start.4
  53.5 7.3 %collective-permute-done.4 = f32[1,129,512]{2,1,0:T(8,128)S(1)} collective-permute-done((f32[1,129,512]{2,1,0:T(8,128)S(1)}, f32[1,129,512]{2,1,0:T(8,128)S(1)}, u32[]{:S(2)}, u32[]{:S(2)}) %collective-permute-start.4) | collective-permute-done | bytes 264224 | tf_op jit(solution)/shard_map/ppermute | solution.py:87
  60.9 4.2 collective-permute-start.5
  65.1 6.0 %collective-permute-done.5 = f32[1,129,512]{2,1,0:T(8,128)S(1)} collective-permute-done((f32[1,129,512]{2,1,0:T(8,128)S(1)}, f32[1,129,512]{2,1,0:T(8,128)S(1)}, u32[]{:S(2)}, u32[]{:S(2)}) %collective-permute-start.5) | collective-permute-done | bytes 264224 | tf_op jit(solution)/shard_map/ppermute | solution.py:87
  71.9 1.2 fusion.312
  75.7 3.0 collective-permute-start.6
  78.7 5.3 %collective-permute-done.6 = f32[1,128,512]{2,1,0:T(8,128)S(1)} collective-permute-done((f32[1,128,512]{2,1,0:T(8,128)S(1)}, f32[1,128,512]{2,1,0:T(8,128)S(1)}, u32[]{:S(2)}, u32[]{:S(2)}) %collective-permute-start.6) | collective-permute-done | bytes 262176 | tf_op jit(solution)/shard_map/ppermute | solution.py:111
  84.1 2.4 collective-permute-start.7
  86.4 7.4 %collective-permute-done.7 = f32[1,128,512]{2,1,0:T(8,128)S(1)} collective-permute-done((f32[1,128,512]{2,1,0:T(8,128)S(1)}, f32[1,128,512]{2,1,0:T(8,128)S(1)}, u32[]{:S(2)}, u32[]{:S(2)}) %collective-permute-start.7) | collective-permute-done | bytes 262176 | tf_op jit(solution)/shard_map/ppermute | solution.py:111
  93.9 2.0 collective-permute-start.8
  96.0 7.0 %collective-permute-done.8 = f32[1,128,512]{2,1,0:T(8,128)S(1)} collective-permute-done((f32[1,128,512]{2,1,0:T(8,128)S(1)}, f32[1,128,512]{2,1,0:T(8,128)S(1)}, u32[]{:S(2)}, u32[]{:S(2)}) %collective-permute-start.8) | collective-permute-done | bytes 262176 | tf_op jit(solution)/shard_map/ppermute | solution.py:111
  103.0 4.0 collective-permute-start.9
  107.0 7.4 %collective-permute-done.9 = f32[1,128,512]{2,1,0:T(8,128)S(1)} collective-permute-done((f32[1,128,512]{2,1,0:T(8,128)S(1)}, f32[1,128,512]{2,1,0:T(8,128)S(1)}, u32[]{:S(2)}, u32[]{:S(2)}) %collective-permute-start.9) | collective-permute-done | bytes 262176 | tf_op jit(solution)/shard_map/ppermute | solution.py:111
  114.5 2.4 collective-permute-start.10
  116.9 7.0 %collective-permute-done.10 = f32[1,128,512]{2,1,0:T(8,128)S(1)} collective-permute-done((f32[1,128,512]{2,1,0:T(8,128)S(1)}, f32[1,128,512]{2,1,0:T(8,128)S(1)}, u32[]{:S(2)}, u32[]{:S(2)}) %collective-permute-start.10) | collective-permute-done | bytes 262176 | tf_op jit(solution)/shard_map/ppermute | solution.py:111
  124.6 5.0 %collective-permute-start.11 = (f32[1,128,512]{2,1,0:T(8,128)}, f32[1,128,512]{2,1,0:T(8,128)}, u32[]{:S(2)}, u32[]{:S(2)}) collective-permute-start(f32[1,128,512]{2,1,0:T(8,128)} %select_add_fusion.10), channel_id=1, source_target_pairs={{0,256},{8,264},{16,272},{24,280},{32,288},{40,296},{48,304},{56,3... | collective-permute-start | bytes 786440 | tf_op jit(solution)/shard_map/ppermute | solution.py:111
  132.0 2.7 collective-permute-done.11
  134.7 1.2 fusion.310
  142.0 1.7 pad_maximum_fusion.7
  143.7 3.1 collective-permute-start.12
  146.8 6.4 %collective-permute-done.12 = f32[1,129,512]{2,1,0:T(8,128)} collective-permute-done((f32[1,129,512]{2,1,0:T(8,128)}, f32[1,129,512]{2,1,0:T(8,128)}, u32[]{:S(2)}, u32[]{:S(2)}) %collective-permute-start.12) | collective-permute-done | bytes 264224 | tf_op jit(solution)/shard_map/ppermute | solution.py:87
  156.4 1.9 collective-permute-start.13
  158.3 8.3 %collective-permute-done.13 = f32[1,129,512]{2,1,0:T(8,128)} collective-permute-done((f32[1,129,512]{2,1,0:T(8,128)}, f32[1,129,512]{2,1,0:T(8,128)}, u32[]{:S(2)}, u32[]{:S(2)}) %collective-permute-start.13) | collective-permute-done | bytes 264224 | tf_op jit(solution)/shard_map/ppermute | solution.py:87
  167.3 1.8 select_add_fusion.8
  169.2 1.7 pad_maximum_fusion.9
  170.8 2.7 collective-permute-start.14
  173.6 8.4 %collective-permute-done.14 = f32[1,129,512]{2,1,0:T(8,128)} collective-permute-done((f32[1,129,512]{2,1,0:T(8,128)}, f32[1,129,512]{2,1,0:T(8,128)}, u32[]{:S(2)}, u32[]{:S(2)}) %collective-permute-start.14) | collective-permute-done | bytes 264224 | tf_op jit(solution)/shard_map/ppermute | solution.py:87
  182.7 1.8 select_add_fusion.7
  184.5 1.7 pad_maximum_fusion.10
  186.2 4.0 collective-permute-start.15
  190.3 8.6 %collective-permute-done.15 = f32[1,129,512]{2,1,0:T(8,128)} collective-permute-done((f32[1,129,512]{2,1,0:T(8,128)}, f32[1,129,512]{2,1,0:T(8,128)}, u32[]{:S(2)}, u32[]{:S(2)}) %collective-permute-start.15) | collective-permute-done | bytes 264224 | tf_op jit(solution)/shard_map/ppermute | solution.py:87
  199.5 1.8 select_add_fusion.6
  201.3 1.7 pad_maximum_fusion.11
  203.0 4.6 %collective-permute-start.16 = (f32[1,129,512]{2,1,0:T(8,128)}, f32[1,129,512]{2,1,0:T(8,128)}, u32[]{:S(2)}, u32[]{:S(2)}) collective-permute-start(f32[1,129,512]{2,1,0:T(8,128)} %pad_maximum_fusion.11), channel_id=1, source_target_pairs={{0,128},{8,136},{16,144},{24,152},{32,160},{40,168},{48,176},{56,1... | collective-permute-start | bytes 792584 | tf_op jit(solution)/shard_map/ppermute | solution.py:87
  207.7 4.8 %collective-permute-done.16 = f32[1,129,512]{2,1,0:T(8,128)} collective-permute-done((f32[1,129,512]{2,1,0:T(8,128)}, f32[1,129,512]{2,1,0:T(8,128)}, u32[]{:S(2)}, u32[]{:S(2)}) %collective-permute-start.16) | collective-permute-done | bytes 264224 | tf_op jit(solution)/shard_map/ppermute | solution.py:87
  213.2 1.1 select_add_fusion.5
  215.1 6.5 %collective-permute-start.17 = (f32[1,129,512]{2,1,0:T(8,128)}, f32[1,129,512]{2,1,0:T(8,128)}, u32[]{:S(2)}, u32[]{:S(2)}) collective-permute-start(f32[1,129,512]{2,1,0:T(8,128)} %pad_maximum_fusion.12), channel_id=1, source_target_pairs={{0,256},{8,264},{16,272},{24,280},{32,288},{40,296},{48,304},{56,3... | collective-permute-start | bytes 792584 | tf_op jit(solution)/shard_map/ppermute | solution.py:87
  221.6 4.6 %collective-permute-done.17 = f32[1,129,512]{2,1,0:T(8,128)} collective-permute-done((f32[1,129,512]{2,1,0:T(8,128)}, f32[1,129,512]{2,1,0:T(8,128)}, u32[]{:S(2)}, u32[]{:S(2)}) %collective-permute-start.17) | collective-permute-done | bytes 264224 | tf_op jit(solution)/shard_map/ppermute | solution.py:87
  226.2 1.6 fusion.180
  230.1 1.3 fusion.76
  231.4 2.5 collective-permute-start.18
  233.9 5.8 %collective-permute-done.18 = f32[1,128,512]{2,1,0:T(8,128)S(1)} collective-permute-done((f32[1,128,512]{2,1,0:T(8,128)S(1)}, f32[1,128,512]{2,1,0:T(8,128)S(1)}, u32[]{:S(2)}, u32[]{:S(2)}) %collective-permute-start.18) | collective-permute-done | bytes 262176 | tf_op jit(solution)/shard_map/ppermute | solution.py:111
  239.8 1.9 collective-permute-start.19
  241.7 7.8 %collective-permute-done.19 = f32[1,128,512]{2,1,0:T(8,128)S(1)} collective-permute-done((f32[1,128,512]{2,1,0:T(8,128)S(1)}, f32[1,128,512]{2,1,0:T(8,128)S(1)}, u32[]{:S(2)}, u32[]{:S(2)}) %collective-permute-start.19) | collective-permute-done | bytes 262176 | tf_op jit(solution)/shard_map/ppermute | solution.py:111
  249.6 1.9 collective-permute-start.20
  251.6 6.3 %collective-permute-done.20 = f32[1,128,512]{2,1,0:T(8,128)S(1)} collective-permute-done((f32[1,128,512]{2,1,0:T(8,128)S(1)}, f32[1,128,512]{2,1,0:T(8,128)S(1)}, u32[]{:S(2)}, u32[]{:S(2)}) %collective-permute-start.20) | collective-permute-done | bytes 262176 | tf_op jit(solution)/shard_map/ppermute | solution.py:111
  258.0 2.7 collective-permute-start.21
  260.8 8.7 %collective-permute-done.21 = f32[1,128,512]{2,1,0:T(8,128)S(1)} collective-permute-done((f32[1,128,512]{2,1,0:T(8,128)S(1)}, f32[1,128,512]{2,1,0:T(8,128)S(1)}, u32[]{:S(2)}, u32[]{:S(2)}) %collective-permute-start.21) | collective-permute-done | bytes 262176 | tf_op jit(solution)/shard_map/ppermute | solution.py:111
  269.5 3.8 collective-permute-start.22
  273.4 4.4 %collective-permute-done.22 = f32[1,128,512]{2,1,0:T(8,128)S(1)} collective-permute-done((f32[1,128,512]{2,1,0:T(8,128)S(1)}, f32[1,128,512]{2,1,0:T(8,128)S(1)}, u32[]{:S(2)}, u32[]{:S(2)}) %collective-permute-start.22) | collective-permute-done | bytes 262176 | tf_op jit(solution)/shard_map/ppermute | solution.py:111
  277.9 5.4 %collective-permute-start.23 = (f32[1,128,512]{2,1,0:T(8,128)S(1)}, f32[1,128,512]{2,1,0:T(8,128)S(1)}, u32[]{:S(2)}, u32[]{:S(2)}) collective-permute-start(f32[1,128,512]{2,1,0:T(8,128)S(1)} %select_add_fusion), channel_id=1, source_target_pairs={{0,256},{8,264},{16,272},{24,280},{32,288},{40,296},{48,304},{56,3... | collective-permute-start | bytes 786440 | tf_op jit(solution)/shard_map/ppermute | solution.py:111
  283.3 4.3 collective-permute-done.23
  292.2 75.5 %all_to_all.10 = f32[8,296,128]{2,1,0:T(8,128)S(1)} all-to-all(f32[8,296,128]{2,1,0:T(8,128)S(1)} %bitcast.475), channel_id=1, replica_groups=mesh['layer'=64,'batch'=8] {'batch'}, dimensions={0} | all-to-all | bytes 2424832 | tf_op jit(solution)/shard_map/all_to_all | solution.py:128
  367.7 1.1 broadcast_in_dim.438
  368.8 3.6 all-to-all-start.1
  374.5 60.5 %all-to-all-done.1 = f32[8,296,128]{2,1,0:T(8,128)S(1)} async-done(((f32[8,296,128]{2,1,0:T(8,128)}), f32[8,296,128]{2,1,0:T(8,128)S(1)}, u32[]{:S(2)}, u32[]{:S(2)}) %all-to-all-start.1) | async-done | bytes 1212448 | tf_op jit(solution)/shard_map/all_to_all | solution.py:130
  (223 shorter events, 35.2 us)
Async XLA Ops:
  0.6 2.2 copy-start.1
  2.5 1.1 copy-start
  4.0 0.9 copy-start.12
  5.3 10.3 %collective-permute-start = (f32[1,129,512]{2,1,0:T(8,128)S(1)}, f32[1,129,512]{2,1,0:T(8,128)S(1)}, u32[]{:S(2)}, u32[]{:S(2)}) collective-permute-start(f32[1,129,512]{2,1,0:T(8,128)S(1)} %pad_maximum_fusion.1), channel_id=1, source_target_pairs={{0,8},{8,0},{16,24},{24,16},{32,40},{40,32},{48,56},{56,48},{64,72... | collective-permute-start | bytes 792584 | tf_op jit(solution)/shard_map/ppermute | solution.py:87
  15.8 10.9 %collective-permute-start.1 = (f32[1,129,512]{2,1,0:T(8,128)S(1)}, f32[1,129,512]{2,1,0:T(8,128)S(1)}, u32[]{:S(2)}, u32[]{:S(2)}) collective-permute-start(f32[1,129,512]{2,1,0:T(8,128)S(1)} %pad_maximum_fusion.2), channel_id=1, source_target_pairs={{0,16},{8,24},{16,0},{24,8},{32,48},{40,56},{48,32},{56,40},{64,80... | collective-permute-start | bytes 792584 | tf_op jit(solution)/shard_map/ppermute | solution.py:87
  26.8 8.7 %collective-permute-start.2 = (f32[1,129,512]{2,1,0:T(8,128)S(1)}, f32[1,129,512]{2,1,0:T(8,128)S(1)}, u32[]{:S(2)}, u32[]{:S(2)}) collective-permute-start(f32[1,129,512]{2,1,0:T(8,128)S(1)} %pad_maximum_fusion.3), channel_id=1, source_target_pairs={{0,32},{8,40},{16,48},{24,56},{32,0},{40,8},{48,16},{56,24},{64,96... | collective-permute-start | bytes 792584 | tf_op jit(solution)/shard_map/ppermute | solution.py:87
  35.6 15.3 %collective-permute-start.3 = (f32[1,129,512]{2,1,0:T(8,128)S(1)}, f32[1,129,512]{2,1,0:T(8,128)S(1)}, u32[]{:S(2)}, u32[]{:S(2)}) collective-permute-start(f32[1,129,512]{2,1,0:T(8,128)S(1)} %pad_maximum_fusion.4), channel_id=1, source_target_pairs={{0,64},{8,72},{16,80},{24,88},{32,96},{40,104},{48,112},{56,120},{... | collective-permute-start | bytes 792584 | tf_op jit(solution)/shard_map/ppermute | solution.py:87
  51.0 9.7 %collective-permute-start.4 = (f32[1,129,512]{2,1,0:T(8,128)S(1)}, f32[1,129,512]{2,1,0:T(8,128)S(1)}, u32[]{:S(2)}, u32[]{:S(2)}) collective-permute-start(f32[1,129,512]{2,1,0:T(8,128)S(1)} %pad_maximum_fusion.5), channel_id=1, source_target_pairs={{0,128},{8,136},{16,144},{24,152},{32,160},{40,168},{48,176},{56,1... | collective-permute-start | bytes 792584 | tf_op jit(solution)/shard_map/ppermute | solution.py:87
  60.9 10.3 %collective-permute-start.5 = (f32[1,129,512]{2,1,0:T(8,128)S(1)}, f32[1,129,512]{2,1,0:T(8,128)S(1)}, u32[]{:S(2)}, u32[]{:S(2)}) collective-permute-start(f32[1,129,512]{2,1,0:T(8,128)S(1)} %pad_maximum_fusion.6), channel_id=1, source_target_pairs={{0,256},{8,264},{16,272},{24,280},{32,288},{40,296},{48,304},{56,3... | collective-permute-start | bytes 792584 | tf_op jit(solution)/shard_map/ppermute | solution.py:87
  71.2 0.7 copy-start.11
  75.7 8.3 %collective-permute-start.6 = (f32[1,128,512]{2,1,0:T(8,128)S(1)}, f32[1,128,512]{2,1,0:T(8,128)S(1)}, u32[]{:S(2)}, u32[]{:S(2)}) collective-permute-start(f32[1,128,512]{2,1,0:T(8,128)S(1)} %fusion.118), channel_id=1, source_target_pairs={{0,8},{8,0},{16,24},{24,16},{32,40},{40,32},{48,56},{56,48},{64,72... | collective-permute-start | bytes 786440 | tf_op jit(solution)/shard_map/ppermute | solution.py:111
  84.1 9.8 %collective-permute-start.7 = (f32[1,128,512]{2,1,0:T(8,128)S(1)}, f32[1,128,512]{2,1,0:T(8,128)S(1)}, u32[]{:S(2)}, u32[]{:S(2)}) collective-permute-start(f32[1,128,512]{2,1,0:T(8,128)S(1)} %select_add_fusion.14), channel_id=1, source_target_pairs={{0,16},{8,24},{16,0},{24,8},{32,48},{40,56},{48,32},{56,40},{64,80... | collective-permute-start | bytes 786440 | tf_op jit(solution)/shard_map/ppermute | solution.py:111
  93.9 9.0 %collective-permute-start.8 = (f32[1,128,512]{2,1,0:T(8,128)S(1)}, f32[1,128,512]{2,1,0:T(8,128)S(1)}, u32[]{:S(2)}, u32[]{:S(2)}) collective-permute-start(f32[1,128,512]{2,1,0:T(8,128)S(1)} %select_add_fusion.13), channel_id=1, source_target_pairs={{0,32},{8,40},{16,48},{24,56},{32,0},{40,8},{48,16},{56,24},{64,96... | collective-permute-start | bytes 786440 | tf_op jit(solution)/shard_map/ppermute | solution.py:111
  103.0 11.3 %collective-permute-start.9 = (f32[1,128,512]{2,1,0:T(8,128)S(1)}, f32[1,128,512]{2,1,0:T(8,128)S(1)}, u32[]{:S(2)}, u32[]{:S(2)}) collective-permute-start(f32[1,128,512]{2,1,0:T(8,128)S(1)} %select_add_fusion.12), channel_id=1, source_target_pairs={{0,64},{8,72},{16,80},{24,88},{32,96},{40,104},{48,112},{56,120},{... | collective-permute-start | bytes 786440 | tf_op jit(solution)/shard_map/ppermute | solution.py:111
  114.5 15.2 %copy-start.13 = (f32[1,128]{1,0:T(1,128)S(1)}, f32[1,128]{1,0:T(1,128)}, u32[]{:S(2)}) copy-start(f32[1,128]{1,0:T(1,128)} %param.11) | copy-start | bytes 1540
  114.5 9.3 %collective-permute-start.10 = (f32[1,128,512]{2,1,0:T(8,128)S(1)}, f32[1,128,512]{2,1,0:T(8,128)S(1)}, u32[]{:S(2)}, u32[]{:S(2)}) collective-permute-start(f32[1,128,512]{2,1,0:T(8,128)S(1)} %select_add_fusion.11), channel_id=1, source_target_pairs={{0,128},{8,136},{16,144},{24,152},{32,160},{40,168},{48,176},{56,1... | collective-permute-start | bytes 786440 | tf_op jit(solution)/shard_map/ppermute | solution.py:111
  124.6 10.1 %collective-permute-start.11 = (f32[1,128,512]{2,1,0:T(8,128)}, f32[1,128,512]{2,1,0:T(8,128)}, u32[]{:S(2)}, u32[]{:S(2)}) collective-permute-start(f32[1,128,512]{2,1,0:T(8,128)} %select_add_fusion.10), channel_id=1, source_target_pairs={{0,256},{8,264},{16,272},{24,280},{32,288},{40,296},{48,304},{56,3... | collective-permute-start | bytes 786440 | tf_op jit(solution)/shard_map/ppermute | solution.py:111
  135.9 0.9 copy-start.8
  137.2 2.4 copy-start.6
  137.2 1.0 copy-start.2
  138.6 1.0 copy-start.5
  140.0 1.0 copy-start.3
  143.7 9.4 %collective-permute-start.12 = (f32[1,129,512]{2,1,0:T(8,128)}, f32[1,129,512]{2,1,0:T(8,128)}, u32[]{:S(2)}, u32[]{:S(2)}) collective-permute-start(f32[1,129,512]{2,1,0:T(8,128)} %pad_maximum_fusion.7), channel_id=1, source_target_pairs={{0,8},{8,0},{16,24},{24,16},{32,40},{40,32},{48,56},{56,48},{64,72... | collective-permute-start | bytes 792584 | tf_op jit(solution)/shard_map/ppermute | solution.py:87
  155.0 0.7 copy-start.10
  156.4 10.3 %collective-permute-start.13 = (f32[1,129,512]{2,1,0:T(8,128)}, f32[1,129,512]{2,1,0:T(8,128)}, u32[]{:S(2)}, u32[]{:S(2)}) collective-permute-start(f32[1,129,512]{2,1,0:T(8,128)} %pad_maximum_fusion.8), channel_id=1, source_target_pairs={{0,16},{8,24},{16,0},{24,8},{32,48},{40,56},{48,32},{56,40},{64,80... | collective-permute-start | bytes 792584 | tf_op jit(solution)/shard_map/ppermute | solution.py:87
  170.8 11.2 %collective-permute-start.14 = (f32[1,129,512]{2,1,0:T(8,128)}, f32[1,129,512]{2,1,0:T(8,128)}, u32[]{:S(2)}, u32[]{:S(2)}) collective-permute-start(f32[1,129,512]{2,1,0:T(8,128)} %pad_maximum_fusion.9), channel_id=1, source_target_pairs={{0,32},{8,40},{16,48},{24,56},{32,0},{40,8},{48,16},{56,24},{64,96... | collective-permute-start | bytes 792584 | tf_op jit(solution)/shard_map/ppermute | solution.py:87
  186.2 12.6 %collective-permute-start.15 = (f32[1,129,512]{2,1,0:T(8,128)}, f32[1,129,512]{2,1,0:T(8,128)}, u32[]{:S(2)}, u32[]{:S(2)}) collective-permute-start(f32[1,129,512]{2,1,0:T(8,128)} %pad_maximum_fusion.10), channel_id=1, source_target_pairs={{0,64},{8,72},{16,80},{24,88},{32,96},{40,104},{48,112},{56,120},{... | collective-permute-start | bytes 792584 | tf_op jit(solution)/shard_map/ppermute | solution.py:87
  203.0 9.4 %collective-permute-start.16 = (f32[1,129,512]{2,1,0:T(8,128)}, f32[1,129,512]{2,1,0:T(8,128)}, u32[]{:S(2)}, u32[]{:S(2)}) collective-permute-start(f32[1,129,512]{2,1,0:T(8,128)} %pad_maximum_fusion.11), channel_id=1, source_target_pairs={{0,128},{8,136},{16,144},{24,152},{32,160},{40,168},{48,176},{56,1... | collective-permute-start | bytes 792584 | tf_op jit(solution)/shard_map/ppermute | solution.py:87
  215.1 11.1 %collective-permute-start.17 = (f32[1,129,512]{2,1,0:T(8,128)}, f32[1,129,512]{2,1,0:T(8,128)}, u32[]{:S(2)}, u32[]{:S(2)}) collective-permute-start(f32[1,129,512]{2,1,0:T(8,128)} %pad_maximum_fusion.12), channel_id=1, source_target_pairs={{0,256},{8,264},{16,272},{24,280},{32,288},{40,296},{48,304},{56,3... | collective-permute-start | bytes 792584 | tf_op jit(solution)/shard_map/ppermute | solution.py:87
  227.8 1.0 copy-start.7
  231.4 8.3 %collective-permute-start.18 = (f32[1,128,512]{2,1,0:T(8,128)S(1)}, f32[1,128,512]{2,1,0:T(8,128)S(1)}, u32[]{:S(2)}, u32[]{:S(2)}) collective-permute-start(f32[1,128,512]{2,1,0:T(8,128)S(1)} %fusion.76), channel_id=1, source_target_pairs={{0,8},{8,0},{16,24},{24,16},{32,40},{40,32},{48,56},{56,48},{64,72... | collective-permute-start | bytes 786440 | tf_op jit(solution)/shard_map/ppermute | solution.py:111
  239.8 9.8 %collective-permute-start.19 = (f32[1,128,512]{2,1,0:T(8,128)S(1)}, f32[1,128,512]{2,1,0:T(8,128)S(1)}, u32[]{:S(2)}, u32[]{:S(2)}) collective-permute-start(f32[1,128,512]{2,1,0:T(8,128)S(1)} %select_add_fusion.4), channel_id=1, source_target_pairs={{0,16},{8,24},{16,0},{24,8},{32,48},{40,56},{48,32},{56,40},{64,80... | collective-permute-start | bytes 786440 | tf_op jit(solution)/shard_map/ppermute | solution.py:111
  249.6 8.3 %collective-permute-start.20 = (f32[1,128,512]{2,1,0:T(8,128)S(1)}, f32[1,128,512]{2,1,0:T(8,128)S(1)}, u32[]{:S(2)}, u32[]{:S(2)}) collective-permute-start(f32[1,128,512]{2,1,0:T(8,128)S(1)} %select_add_fusion.3), channel_id=1, source_target_pairs={{0,32},{8,40},{16,48},{24,56},{32,0},{40,8},{48,16},{56,24},{64,96... | collective-permute-start | bytes 786440 | tf_op jit(solution)/shard_map/ppermute | solution.py:111
  258.0 11.4 %collective-permute-start.21 = (f32[1,128,512]{2,1,0:T(8,128)S(1)}, f32[1,128,512]{2,1,0:T(8,128)S(1)}, u32[]{:S(2)}, u32[]{:S(2)}) collective-permute-start(f32[1,128,512]{2,1,0:T(8,128)S(1)} %select_add_fusion.2), channel_id=1, source_target_pairs={{0,64},{8,72},{16,80},{24,88},{32,96},{40,104},{48,112},{56,120},{... | collective-permute-start | bytes 786440 | tf_op jit(solution)/shard_map/ppermute | solution.py:111
  269.5 8.3 %collective-permute-start.22 = (f32[1,128,512]{2,1,0:T(8,128)S(1)}, f32[1,128,512]{2,1,0:T(8,128)S(1)}, u32[]{:S(2)}, u32[]{:S(2)}) collective-permute-start(f32[1,128,512]{2,1,0:T(8,128)S(1)} %select_add_fusion.1), channel_id=1, source_target_pairs={{0,128},{8,136},{16,144},{24,152},{32,160},{40,168},{48,176},{56,1... | collective-permute-start | bytes 786440 | tf_op jit(solution)/shard_map/ppermute | solution.py:111
  277.9 9.8 %collective-permute-start.23 = (f32[1,128,512]{2,1,0:T(8,128)S(1)}, f32[1,128,512]{2,1,0:T(8,128)S(1)}, u32[]{:S(2)}, u32[]{:S(2)}) collective-permute-start(f32[1,128,512]{2,1,0:T(8,128)S(1)} %select_add_fusion), channel_id=1, source_target_pairs={{0,256},{8,264},{16,272},{24,280},{32,288},{40,296},{48,304},{56,3... | collective-permute-start | bytes 786440 | tf_op jit(solution)/shard_map/ppermute | solution.py:111
  289.4 1.0 copy-start.9
  368.8 66.2 %all-to-all-start.1 = ((f32[8,296,128]{2,1,0:T(8,128)}), f32[8,296,128]{2,1,0:T(8,128)S(1)}, u32[]{:S(2)}, u32[]{:S(2)}) async-start(f32[8,296,128]{2,1,0:T(8,128)} %broadcast_in_dim.438), calls=%async_computation.1 | async-start | bytes 2424832 | tf_op jit(solution)/shard_map/all_to_all | solution.py:130
  372.4 1.0 copy-start.4

commit v11 on v9

--- a/solution.py
+++ b/solution.py
@@ -87,32 +87,29 @@
         got = lax.ppermute(packed, axis, [(k, k ^ step) for k in range(count)])
         other_sum = got[:, :channels, :]
         other_gain = got[0, channels, :channels]
+        u = upper.astype(gain.dtype)
         upper_gain = jnp.where(upper, block_gain, other_gain)
-        factors.append((product, upper_gain))
-        total = jnp.where(upper, total + product[None, :, None] * other_sum, total)
+        taken = u * product
+        from_other = upper_gain * u + (1 - u)
+        from_own = upper_gain * (1 - u) + u
+        factors.append((taken, from_other, from_own))
+        total = total + taken[None, :, None] * other_sum
         product = jnp.where(upper, product * other_gain, product)
-        lower_sum = jnp.where(upper, other_sum, block_sum)
-        upper_sum = jnp.where(upper, block_sum, other_sum)
-        block_sum = upper_gain[None, :, None] * lower_sum + upper_sum
+        block_sum = from_other[None, :, None] * other_sum + from_own[None, :, None] * block_sum
         block_gain = block_gain * other_gain
         step *= 2
     return total, factors
 
 
-def butterfly_again(local, factors, axis, reverse):
+def butterfly_again(local, factors, axis):
     count = lax.axis_size(axis)
-    me = lax.axis_index(axis)
-    place = count - 1 - me if reverse else me
     total = jnp.zeros_like(local)
     block_sum = local
     step = 1
-    for product, upper_gain in factors:
-        upper = (place // step) % 2 == 1
+    for taken, from_other, from_own in factors:
         got = lax.ppermute(block_sum, axis, [(k, k ^ step) for k in range(count)])
-        total = jnp.where(upper, total + product[None, :, None] * got, total)
-        lower_sum = jnp.where(upper, got, block_sum)
-        upper_sum = jnp.where(upper, block_sum, got)
-        block_sum = upper_gain[None, :, None] * lower_sum + upper_sum
+        total = total + taken[None, :, None] * got
+        block_sum = from_other[None, :, None] * got + from_own[None, :, None] * block_sum
         step *= 2
     return total
 
@@ -174,7 +171,7 @@
         if sweep_index == 0:
             error, factors = butterfly_first(gain_row, residual, "layer", False)
         else:
-            error = butterfly_again(residual, factors, "layer", False)
+            error = butterfly_again(residual, factors, "layer")
         c_points = c_points + error
         following = following + gain_row[None, :, None] * error + residual
     ending, stored = relax_block(c_points, conv_weight, conv_bias)
@@ -186,7 +183,7 @@
         if sweep_index == 0:
             error, factors = butterfly_first(back_row, residual, "layer", True)
         else:
-            error = butterfly_again(residual, factors, "layer", True)
+            error = butterfly_again(residual, factors, "layer")
         target = target + error
         previous = previous + back_row[None, :, None] * error + residual
     adjoint = target

time: 394 us -> 395 us (level)
  the two profiles are of different devices: /device:TPU:75 before, /device:TPU:1 now
where the time goes in v11:
time: 395 us; the launch traced here: 388 us
  waiting for transfers between devices  166 us (42%)
  starting transfers between devices  164 us (42%)
  other arithmetic  39.7 us (10%)
  matrix products  7.89 us (2%)
  local copies, waits for them, and re-layouts  7.51 us (2%)
    ppermute x12, waiting for transfers between devices, butterfly_first(): got = lax.ppermute(packed, axis, [(k, k ^ step) for k in range(count)])  67.8 us
    ppermute x12, waiting for transfers between devices, butterfly_again(): got = lax.ppermute(block_sum, axis, [(k, k ^ step) for k in range(count)])  62.2 us
    ppermute x12, starting transfers between devices, butterfly_first(): got = lax.ppermute(packed, axis, [(k, k ^ step) for k in range(count)])  50.3 us
    ppermute x6, starting transfers between devices, batch_sum(): got = lax.ppermute(sent, axis, ring)  44.6 us
    ppermute x12, starting transfers between devices, butterfly_again(): got = lax.ppermute(block_sum, axis, [(k, k ^ step) for k in range(count)])  37.5 us
    ppermute x6, waiting for transfers between devices, batch_sum(): got = lax.ppermute(sent, axis, ring)  34.6 us
    ppermute x1, starting transfers between devices, batch_sum(): half = keep + lax.ppermute(give, axis, partner)  26.5 us
    unnamed x96, other arithmetic  9.1 us
  transfers between devices with their start and end apart: 32, of which 32 were waited for; matrix products, arithmetic and copies ran while one was open for 1% of the time, Pallas kernels for 0%

profile of v11, /device:TPU:1, one launch (start us, length us, event | category | flops | bytes accessed | tf_op | source)
XLA Modules:
  0.0 388.1 jit_solution(3587484149284043364)
XLA Ops:
  5.3 3.9 %collective-permute-start = (f32[1,129,512]{2,1,0:T(8,128)S(1)}, f32[1,129,512]{2,1,0:T(8,128)S(1)}, u32[]{:S(2)}, u32[]{:S(2)}) collective-permute-start(f32[1,129,512]{2,1,0:T(8,128)S(1)} %pad_maximum_fusion.1), channel_id=1, source_target_pairs={{0,8},{8,0},{16,24},{24,16},{32,40},{40,32},{48,56},{56,48},{64,72... | collective-permute-start | bytes 792584 | tf_op jit(solution)/shard_map/ppermute | solution.py:87
  9.3 3.9 %collective-permute-done = f32[1,129,512]{2,1,0:T(8,128)S(1)} collective-permute-done((f32[1,129,512]{2,1,0:T(8,128)S(1)}, f32[1,129,512]{2,1,0:T(8,128)S(1)}, u32[]{:S(2)}, u32[]{:S(2)}) %collective-permute-start) | collective-permute-done | bytes 264224 | tf_op jit(solution)/shard_map/ppermute | solution.py:87
  13.4 7.0 %collective-permute-start.1 = (f32[1,129,512]{2,1,0:T(8,128)S(1)}, f32[1,129,512]{2,1,0:T(8,128)S(1)}, u32[]{:S(2)}, u32[]{:S(2)}) collective-permute-start(f32[1,129,512]{2,1,0:T(8,128)S(1)} %pad_maximum_fusion.2), channel_id=1, source_target_pairs={{0,16},{8,24},{16,0},{24,8},{32,48},{40,56},{48,32},{56,40},{64,80... | collective-permute-start | bytes 792584 | tf_op jit(solution)/shard_map/ppermute | solution.py:87
  20.5 3.9 collective-permute-done.1
  24.5 5.0 %collective-permute-start.2 = (f32[1,129,512]{2,1,0:T(8,128)S(1)}, f32[1,129,512]{2,1,0:T(8,128)S(1)}, u32[]{:S(2)}, u32[]{:S(2)}) collective-permute-start(f32[1,129,512]{2,1,0:T(8,128)S(1)} %pad_maximum_fusion.3), channel_id=1, source_target_pairs={{0,32},{8,40},{16,48},{24,56},{32,0},{40,8},{48,16},{56,24},{64,96... | collective-permute-start | bytes 792584 | tf_op jit(solution)/shard_map/ppermute | solution.py:87
  29.4 3.9 %collective-permute-done.2 = f32[1,129,512]{2,1,0:T(8,128)S(1)} collective-permute-done((f32[1,129,512]{2,1,0:T(8,128)S(1)}, f32[1,129,512]{2,1,0:T(8,128)S(1)}, u32[]{:S(2)}, u32[]{:S(2)}) %collective-permute-start.2) | collective-permute-done | bytes 264224 | tf_op jit(solution)/shard_map/ppermute | solution.py:87
  33.5 5.4 %collective-permute-start.3 = (f32[1,129,512]{2,1,0:T(8,128)S(1)}, f32[1,129,512]{2,1,0:T(8,128)S(1)}, u32[]{:S(2)}, u32[]{:S(2)}) collective-permute-start(f32[1,129,512]{2,1,0:T(8,128)S(1)} %pad_maximum_fusion.4), channel_id=1, source_target_pairs={{0,64},{8,72},{16,80},{24,88},{32,96},{40,104},{48,112},{56,120},{... | collective-permute-start | bytes 792584 | tf_op jit(solution)/shard_map/ppermute | solution.py:87
  38.9 11.1 %collective-permute-done.3 = f32[1,129,512]{2,1,0:T(8,128)S(1)} collective-permute-done((f32[1,129,512]{2,1,0:T(8,128)S(1)}, f32[1,129,512]{2,1,0:T(8,128)S(1)}, u32[]{:S(2)}, u32[]{:S(2)}) %collective-permute-start.3) | collective-permute-done | bytes 264224 | tf_op jit(solution)/shard_map/ppermute | solution.py:87
  50.2 4.2 %collective-permute-start.4 = (f32[1,129,512]{2,1,0:T(8,128)S(1)}, f32[1,129,512]{2,1,0:T(8,128)S(1)}, u32[]{:S(2)}, u32[]{:S(2)}) collective-permute-start(f32[1,129,512]{2,1,0:T(8,128)S(1)} %pad_maximum_fusion.5), channel_id=1, source_target_pairs={{0,128},{8,136},{16,144},{24,152},{32,160},{40,168},{48,176},{56,1... | collective-permute-start | bytes 792584 | tf_op jit(solution)/shard_map/ppermute | solution.py:87
  54.5 5.1 %collective-permute-done.4 = f32[1,129,512]{2,1,0:T(8,128)S(1)} collective-permute-done((f32[1,129,512]{2,1,0:T(8,128)S(1)}, f32[1,129,512]{2,1,0:T(8,128)S(1)}, u32[]{:S(2)}, u32[]{:S(2)}) %collective-permute-start.4) | collective-permute-done | bytes 264224 | tf_op jit(solution)/shard_map/ppermute | solution.py:87
  59.8 5.3 %collective-permute-start.5 = (f32[1,129,512]{2,1,0:T(8,128)S(1)}, f32[1,129,512]{2,1,0:T(8,128)S(1)}, u32[]{:S(2)}, u32[]{:S(2)}) collective-permute-start(f32[1,129,512]{2,1,0:T(8,128)S(1)} %pad_maximum_fusion.6), channel_id=1, source_target_pairs={{0,256},{8,264},{16,272},{24,280},{32,288},{40,296},{48,304},{56,3... | collective-permute-start | bytes 792584 | tf_op jit(solution)/shard_map/ppermute | solution.py:87
  65.1 4.7 %collective-permute-done.5 = f32[1,129,512]{2,1,0:T(8,128)S(1)} collective-permute-done((f32[1,129,512]{2,1,0:T(8,128)S(1)}, f32[1,129,512]{2,1,0:T(8,128)S(1)}, u32[]{:S(2)}, u32[]{:S(2)}) %collective-permute-start.5) | collective-permute-done | bytes 264224 | tf_op jit(solution)/shard_map/ppermute | solution.py:87
  72.6 2.9 collective-permute-start.6
  75.4 4.2 %collective-permute-done.6 = f32[1,128,512]{2,1,0:T(8,128)S(1)} collective-permute-done((f32[1,128,512]{2,1,0:T(8,128)S(1)}, f32[1,128,512]{2,1,0:T(8,128)S(1)}, u32[]{:S(2)}, u32[]{:S(2)}) %collective-permute-start.6) | collective-permute-done | bytes 262176 | tf_op jit(solution)/shard_map/ppermute | solution.py:110
  79.8 4.5 %collective-permute-start.7 = (f32[1,128,512]{2,1,0:T(8,128)S(1)}, f32[1,128,512]{2,1,0:T(8,128)S(1)}, u32[]{:S(2)}, u32[]{:S(2)}) collective-permute-start(f32[1,128,512]{2,1,0:T(8,128)S(1)} %multiply_add_fusion.14), channel_id=1, source_target_pairs={{0,16},{8,24},{16,0},{24,8},{32,48},{40,56},{48,32},{56,40},{64,80... | collective-permute-start | bytes 786440 | tf_op jit(solution)/shard_map/ppermute | solution.py:110
  84.3 4.1 %collective-permute-done.7 = f32[1,128,512]{2,1,0:T(8,128)S(1)} collective-permute-done((f32[1,128,512]{2,1,0:T(8,128)S(1)}, f32[1,128,512]{2,1,0:T(8,128)S(1)}, u32[]{:S(2)}, u32[]{:S(2)}) %collective-permute-start.7) | collective-permute-done | bytes 262176 | tf_op jit(solution)/shard_map/ppermute | solution.py:110
  88.5 1.9 collective-permute-start.8
  90.4 5.2 %collective-permute-done.8 = f32[1,128,512]{2,1,0:T(8,128)S(1)} collective-permute-done((f32[1,128,512]{2,1,0:T(8,128)S(1)}, f32[1,128,512]{2,1,0:T(8,128)S(1)}, u32[]{:S(2)}, u32[]{:S(2)}) %collective-permute-start.8) | collective-permute-done | bytes 262176 | tf_op jit(solution)/shard_map/ppermute | solution.py:110
  95.7 3.1 collective-permute-start.9
  98.9 7.7 %collective-permute-done.9 = f32[1,128,512]{2,1,0:T(8,128)S(1)} collective-permute-done((f32[1,128,512]{2,1,0:T(8,128)S(1)}, f32[1,128,512]{2,1,0:T(8,128)S(1)}, u32[]{:S(2)}, u32[]{:S(2)}) %collective-permute-start.9) | collective-permute-done | bytes 262176 | tf_op jit(solution)/shard_map/ppermute | solution.py:110
  106.7 2.9 collective-permute-start.10
  109.6 4.2 %collective-permute-done.10 = f32[1,128,512]{2,1,0:T(8,128)S(1)} collective-permute-done((f32[1,128,512]{2,1,0:T(8,128)S(1)}, f32[1,128,512]{2,1,0:T(8,128)S(1)}, u32[]{:S(2)}, u32[]{:S(2)}) %collective-permute-start.10) | collective-permute-done | bytes 262176 | tf_op jit(solution)/shard_map/ppermute | solution.py:110
  114.7 4.8 %collective-permute-start.11 = (f32[1,128,512]{2,1,0:T(8,128)}, f32[1,128,512]{2,1,0:T(8,128)}, u32[]{:S(2)}, u32[]{:S(2)}) collective-permute-start(f32[1,128,512]{2,1,0:T(8,128)} %multiply_add_fusion.10), channel_id=1, source_target_pairs={{0,256},{8,264},{16,272},{24,280},{32,288},{40,296},{48,304},{56,3... | collective-permute-start | bytes 786440 | tf_op jit(solution)/shard_map/ppermute | solution.py:110
  121.9 3.6 collective-permute-done.11
  134.5 3.1 collective-permute-start.12
  137.6 4.5 %collective-permute-done.12 = f32[1,129,512]{2,1,0:T(8,128)} collective-permute-done((f32[1,129,512]{2,1,0:T(8,128)}, f32[1,129,512]{2,1,0:T(8,128)}, u32[]{:S(2)}, u32[]{:S(2)}) %collective-permute-start.12) | collective-permute-done | bytes 264224 | tf_op jit(solution)/shard_map/ppermute | solution.py:87
  142.8 1.8 multiply_add_fusion.9
  146.3 4.6 %collective-permute-start.13 = (f32[1,129,512]{2,1,0:T(8,128)}, f32[1,129,512]{2,1,0:T(8,128)}, u32[]{:S(2)}, u32[]{:S(2)}) collective-permute-start(f32[1,129,512]{2,1,0:T(8,128)} %pad_maximum_fusion.8), channel_id=1, source_target_pairs={{0,16},{8,24},{16,0},{24,8},{32,48},{40,56},{48,32},{56,40},{64,80... | collective-permute-start | bytes 792584 | tf_op jit(solution)/shard_map/ppermute | solution.py:87
  151.0 6.9 %collective-permute-done.13 = f32[1,129,512]{2,1,0:T(8,128)} collective-permute-done((f32[1,129,512]{2,1,0:T(8,128)}, f32[1,129,512]{2,1,0:T(8,128)}, u32[]{:S(2)}, u32[]{:S(2)}) %collective-permute-start.13) | collective-permute-done | bytes 264224 | tf_op jit(solution)/shard_map/ppermute | solution.py:87
  161.1 1.9 collective-permute-start.14
  163.0 5.7 %collective-permute-done.14 = f32[1,129,512]{2,1,0:T(8,128)} collective-permute-done((f32[1,129,512]{2,1,0:T(8,128)}, f32[1,129,512]{2,1,0:T(8,128)}, u32[]{:S(2)}, u32[]{:S(2)}) %collective-permute-start.14) | collective-permute-done | bytes 264224 | tf_op jit(solution)/shard_map/ppermute | solution.py:87
  172.9 3.0 collective-permute-start.15
  175.9 8.4 %collective-permute-done.15 = f32[1,129,512]{2,1,0:T(8,128)} collective-permute-done((f32[1,129,512]{2,1,0:T(8,128)}, f32[1,129,512]{2,1,0:T(8,128)}, u32[]{:S(2)}, u32[]{:S(2)}) %collective-permute-start.15) | collective-permute-done | bytes 264224 | tf_op jit(solution)/shard_map/ppermute | solution.py:87
  185.1 1.8 multiply_add_fusion.6
  188.6 2.2 collective-permute-start.16
  190.9 5.6 %collective-permute-done.16 = f32[1,129,512]{2,1,0:T(8,128)} collective-permute-done((f32[1,129,512]{2,1,0:T(8,128)}, f32[1,129,512]{2,1,0:T(8,128)}, u32[]{:S(2)}, u32[]{:S(2)}) %collective-permute-start.16) | collective-permute-done | bytes 264224 | tf_op jit(solution)/shard_map/ppermute | solution.py:87
  198.3 4.7 %collective-permute-start.17 = (f32[1,129,512]{2,1,0:T(8,128)S(1)}, f32[1,129,512]{2,1,0:T(8,128)S(1)}, u32[]{:S(2)}, u32[]{:S(2)}) collective-permute-start(f32[1,129,512]{2,1,0:T(8,128)S(1)} %pad_maximum_fusion.12), channel_id=1, source_target_pairs={{0,256},{8,264},{16,272},{24,280},{32,288},{40,296},{48,304},{56,3... | collective-permute-start | bytes 792584 | tf_op jit(solution)/shard_map/ppermute | solution.py:87
  203.0 4.1 %collective-permute-done.17 = f32[1,129,512]{2,1,0:T(8,128)S(1)} collective-permute-done((f32[1,129,512]{2,1,0:T(8,128)S(1)}, f32[1,129,512]{2,1,0:T(8,128)S(1)}, u32[]{:S(2)}, u32[]{:S(2)}) %collective-permute-start.17) | collective-permute-done | bytes 264224 | tf_op jit(solution)/shard_map/ppermute | solution.py:87
  212.3 2.4 collective-permute-start.18
  214.7 4.7 %collective-permute-done.18 = f32[1,128,512]{2,1,0:T(8,128)S(1)} collective-permute-done((f32[1,128,512]{2,1,0:T(8,128)S(1)}, f32[1,128,512]{2,1,0:T(8,128)S(1)}, u32[]{:S(2)}, u32[]{:S(2)}) %collective-permute-start.18) | collective-permute-done | bytes 262176 | tf_op jit(solution)/shard_map/ppermute | solution.py:110
  219.5 3.0 collective-permute-start.19
  222.5 5.6 %collective-permute-done.19 = f32[1,128,512]{2,1,0:T(8,128)S(1)} collective-permute-done((f32[1,128,512]{2,1,0:T(8,128)S(1)}, f32[1,128,512]{2,1,0:T(8,128)S(1)}, u32[]{:S(2)}, u32[]{:S(2)}) %collective-permute-start.19) | collective-permute-done | bytes 262176 | tf_op jit(solution)/shard_map/ppermute | solution.py:110
  228.3 2.4 collective-permute-start.20
  230.6 5.2 %collective-permute-done.20 = f32[1,128,512]{2,1,0:T(8,128)S(1)} collective-permute-done((f32[1,128,512]{2,1,0:T(8,128)S(1)}, f32[1,128,512]{2,1,0:T(8,128)S(1)}, u32[]{:S(2)}, u32[]{:S(2)}) %collective-permute-start.20) | collective-permute-done | bytes 262176 | tf_op jit(solution)/shard_map/ppermute | solution.py:110
  235.9 3.0 collective-permute-start.21
  238.9 8.1 %collective-permute-done.21 = f32[1,128,512]{2,1,0:T(8,128)S(1)} collective-permute-done((f32[1,128,512]{2,1,0:T(8,128)S(1)}, f32[1,128,512]{2,1,0:T(8,128)S(1)}, u32[]{:S(2)}, u32[]{:S(2)}) %collective-permute-start.21) | collective-permute-done | bytes 262176 | tf_op jit(solution)/shard_map/ppermute | solution.py:110
  247.2 2.3 collective-permute-start.22
  249.4 4.9 %collective-permute-done.22 = f32[1,128,512]{2,1,0:T(8,128)S(1)} collective-permute-done((f32[1,128,512]{2,1,0:T(8,128)S(1)}, f32[1,128,512]{2,1,0:T(8,128)S(1)}, u32[]{:S(2)}, u32[]{:S(2)}) %collective-permute-start.22) | collective-permute-done | bytes 262176 | tf_op jit(solution)/shard_map/ppermute | solution.py:110
  255.1 4.3 %collective-permute-start.23 = (f32[1,128,512]{2,1,0:T(8,128)}, f32[1,128,512]{2,1,0:T(8,128)}, u32[]{:S(2)}, u32[]{:S(2)}) collective-permute-start(f32[1,128,512]{2,1,0:T(8,128)} %multiply_add_fusion), channel_id=1, source_target_pairs={{0,256},{8,264},{16,272},{24,280},{32,288},{40,296},{48,304},{56,3... | collective-permute-start | bytes 786440 | tf_op jit(solution)/shard_map/ppermute | solution.py:110
  259.4 4.6 %collective-permute-done.23 = f32[1,128,512]{2,1,0:T(8,128)} collective-permute-done((f32[1,128,512]{2,1,0:T(8,128)}, f32[1,128,512]{2,1,0:T(8,128)}, u32[]{:S(2)}, u32[]{:S(2)}) %collective-permute-start.23) | collective-permute-done | bytes 262176 | tf_op jit(solution)/shard_map/ppermute | solution.py:110
  269.8 26.5 %collective-permute-start.24 = (f32[1184,128]{1,0:T(8,128)S(1)}, f32[1184,128]{1,0:T(8,128)}, u32[]{:S(2)}, u32[]{:S(2)}) collective-permute-start(f32[1184,128]{1,0:T(8,128)S(1)} %constant_dynamic-slice_fusion.3), channel_id=1, source_target_pairs={{0,1},{1,0},{2,3},{3,2},{4,5},{5,4},{6,7},{7,6},{8,9},{9,8},{10,11... | collective-permute-start | bytes 1818632 | tf_op jit(solution)/shard_map/ppermute | solution.py:133
  299.3 11.2 %collective-permute-start.25 = (f32[296,128]{1,0:T(8,128)S(1)}, f32[296,128]{1,0:T(8,128)S(1)}, u32[]{:S(2)}, u32[]{:S(2)}) collective-permute-start(f32[296,128]{1,0:T(8,128)S(1)} %get-tuple-element.31), channel_id=1, source_target_pairs={{0,2},{1,7},{2,4},{3,1},{4,6},{5,3},{6,0},{7,5},{8,10},{9,15},{10,... | collective-permute-start | bytes 454664 | tf_op jit(solution)/shard_map/ppermute | solution.py:144
  310.6 3.8 collective-permute-done.25
  314.5 9.6 %collective-permute-start.26 = (f32[296,128]{1,0:T(8,128)S(1)}, f32[296,128]{1,0:T(8,128)S(1)}, u32[]{:S(2)}, u32[]{:S(2)}) collective-permute-start(f32[296,128]{1,0:T(8,128)S(1)} %get-tuple-element.29), channel_id=1, source_target_pairs={{0,2},{1,7},{2,4},{3,1},{4,6},{5,3},{6,0},{7,5},{8,10},{9,15},{10,... | collective-permute-start | bytes 454664 | tf_op jit(solution)/shard_map/ppermute | solution.py:144
  324.2 4.7 %collective-permute-done.26 = f32[296,128]{1,0:T(8,128)S(1)} collective-permute-done((f32[296,128]{1,0:T(8,128)S(1)}, f32[296,128]{1,0:T(8,128)S(1)}, u32[]{:S(2)}, u32[]{:S(2)}) %collective-permute-start.26) | collective-permute-done | bytes 151584 | tf_op jit(solution)/shard_map/ppermute | solution.py:144
  329.0 8.0 %collective-permute-start.27 = (f32[296,128]{1,0:T(8,128)S(1)}, f32[296,128]{1,0:T(8,128)S(1)}, u32[]{:S(2)}, u32[]{:S(2)}) collective-permute-start(f32[296,128]{1,0:T(8,128)S(1)} %get-tuple-element.27), channel_id=1, source_target_pairs={{0,2},{1,7},{2,4},{3,1},{4,6},{5,3},{6,0},{7,5},{8,10},{9,15},{10,... | collective-permute-start | bytes 454664 | tf_op jit(solution)/shard_map/ppermute | solution.py:144
  337.0 6.6 %collective-permute-done.27 = f32[296,128]{1,0:T(8,128)S(1)} collective-permute-done((f32[296,128]{1,0:T(8,128)S(1)}, f32[296,128]{1,0:T(8,128)S(1)}, u32[]{:S(2)}, u32[]{:S(2)}) %collective-permute-start.27) | collective-permute-done | bytes 151584 | tf_op jit(solution)/shard_map/ppermute | solution.py:144
  343.7 7.7 %collective-permute-start.28 = (f32[296,128]{1,0:T(8,128)S(1)}, f32[296,128]{1,0:T(8,128)S(1)}, u32[]{:S(2)}, u32[]{:S(2)}) collective-permute-start(f32[296,128]{1,0:T(8,128)S(1)} %dynamic-slice_bitcast_fusion.2), channel_id=1, source_target_pairs={{0,2},{1,7},{2,4},{3,1},{4,6},{5,3},{6,0},{7,5},{8,10},{9,15},{10,... | collective-permute-start | bytes 454664 | tf_op jit(solution)/shard_map/ppermute | solution.py:150
  351.5 6.8 %collective-permute-done.28 = f32[296,128]{1,0:T(8,128)S(1)} collective-permute-done((f32[296,128]{1,0:T(8,128)S(1)}, f32[296,128]{1,0:T(8,128)S(1)}, u32[]{:S(2)}, u32[]{:S(2)}) %collective-permute-start.28) | collective-permute-done | bytes 151584 | tf_op jit(solution)/shard_map/ppermute | solution.py:150
  358.3 4.5 %collective-permute-start.29 = (f32[296,128]{1,0:T(8,128)S(1)}, f32[296,128]{1,0:T(8,128)S(1)}, u32[]{:S(2)}, u32[]{:S(2)}) collective-permute-start(f32[296,128]{1,0:T(8,128)S(1)} %dynamic-slice_bitcast_fusion.1), channel_id=1, source_target_pairs={{0,2},{1,7},{2,4},{3,1},{4,6},{5,3},{6,0},{7,5},{8,10},{9,15},{10,... | collective-permute-start | bytes 454664 | tf_op jit(solution)/shard_map/ppermute | solution.py:150
  362.9 6.5 %collective-permute-done.29 = f32[296,128]{1,0:T(8,128)S(1)} collective-permute-done((f32[296,128]{1,0:T(8,128)S(1)}, f32[296,128]{1,0:T(8,128)S(1)}, u32[]{:S(2)}, u32[]{:S(2)}) %collective-permute-start.29) | collective-permute-done | bytes 151584 | tf_op jit(solution)/shard_map/ppermute | solution.py:150
  369.4 3.6 collective-permute-start.30
  373.2 6.2 %collective-permute-done.30 = f32[296,128]{1,0:T(8,128)S(1)} collective-permute-done((f32[296,128]{1,0:T(8,128)S(1)}, f32[296,128]{1,0:T(8,128)S(1)}, u32[]{:S(2)}, u32[]{:S(2)}) %collective-permute-start.30) | collective-permute-done | bytes 151584 | tf_op jit(solution)/shard_map/ppermute | solution.py:150
  379.4 5.0 %collective-permute-start.31 = (f32[1184,128]{1,0:T(8,128)S(1)}, f32[1184,128]{1,0:T(8,128)S(1)}, u32[]{:S(2)}, u32[]{:S(2)}) collective-permute-start(f32[1184,128]{1,0:T(8,128)S(1)} %bitcast.579), channel_id=1, source_target_pairs={{0,1},{1,0},{2,3},{3,2},{4,5},{5,4},{6,7},{7,6},{8,9},{9,8},{10,11... | collective-permute-start | bytes 1818632 | tf_op jit(solution)/shard_map/ppermute | solution.py:153
  (263 shorter events, 53.0 us)
Async XLA Ops:
  0.6 2.2 copy-start.1
  2.5 1.1 copy-start
  4.0 0.9 copy-start.18
  5.3 7.9 %collective-permute-start = (f32[1,129,512]{2,1,0:T(8,128)S(1)}, f32[1,129,512]{2,1,0:T(8,128)S(1)}, u32[]{:S(2)}, u32[]{:S(2)}) collective-permute-start(f32[1,129,512]{2,1,0:T(8,128)S(1)} %pad_maximum_fusion.1), channel_id=1, source_target_pairs={{0,8},{8,0},{16,24},{24,16},{32,40},{40,32},{48,56},{56,48},{64,72... | collective-permute-start | bytes 792584 | tf_op jit(solution)/shard_map/ppermute | solution.py:87
  13.4 11.0 %collective-permute-start.1 = (f32[1,129,512]{2,1,0:T(8,128)S(1)}, f32[1,129,512]{2,1,0:T(8,128)S(1)}, u32[]{:S(2)}, u32[]{:S(2)}) collective-permute-start(f32[1,129,512]{2,1,0:T(8,128)S(1)} %pad_maximum_fusion.2), channel_id=1, source_target_pairs={{0,16},{8,24},{16,0},{24,8},{32,48},{40,56},{48,32},{56,40},{64,80... | collective-permute-start | bytes 792584 | tf_op jit(solution)/shard_map/ppermute | solution.py:87
  24.5 8.9 %collective-permute-start.2 = (f32[1,129,512]{2,1,0:T(8,128)S(1)}, f32[1,129,512]{2,1,0:T(8,128)S(1)}, u32[]{:S(2)}, u32[]{:S(2)}) collective-permute-start(f32[1,129,512]{2,1,0:T(8,128)S(1)} %pad_maximum_fusion.3), channel_id=1, source_target_pairs={{0,32},{8,40},{16,48},{24,56},{32,0},{40,8},{48,16},{56,24},{64,96... | collective-permute-start | bytes 792584 | tf_op jit(solution)/shard_map/ppermute | solution.py:87
  33.5 16.6 %collective-permute-start.3 = (f32[1,129,512]{2,1,0:T(8,128)S(1)}, f32[1,129,512]{2,1,0:T(8,128)S(1)}, u32[]{:S(2)}, u32[]{:S(2)}) collective-permute-start(f32[1,129,512]{2,1,0:T(8,128)S(1)} %pad_maximum_fusion.4), channel_id=1, source_target_pairs={{0,64},{8,72},{16,80},{24,88},{32,96},{40,104},{48,112},{56,120},{... | collective-permute-start | bytes 792584 | tf_op jit(solution)/shard_map/ppermute | solution.py:87
  50.2 9.4 %collective-permute-start.4 = (f32[1,129,512]{2,1,0:T(8,128)S(1)}, f32[1,129,512]{2,1,0:T(8,128)S(1)}, u32[]{:S(2)}, u32[]{:S(2)}) collective-permute-start(f32[1,129,512]{2,1,0:T(8,128)S(1)} %pad_maximum_fusion.5), channel_id=1, source_target_pairs={{0,128},{8,136},{16,144},{24,152},{32,160},{40,168},{48,176},{56,1... | collective-permute-start | bytes 792584 | tf_op jit(solution)/shard_map/ppermute | solution.py:87
  59.8 10.0 %collective-permute-start.5 = (f32[1,129,512]{2,1,0:T(8,128)S(1)}, f32[1,129,512]{2,1,0:T(8,128)S(1)}, u32[]{:S(2)}, u32[]{:S(2)}) collective-permute-start(f32[1,129,512]{2,1,0:T(8,128)S(1)} %pad_maximum_fusion.6), channel_id=1, source_target_pairs={{0,256},{8,264},{16,272},{24,280},{32,288},{40,296},{48,304},{56,3... | collective-permute-start | bytes 792584 | tf_op jit(solution)/shard_map/ppermute | solution.py:87
  72.6 7.1 %collective-permute-start.6 = (f32[1,128,512]{2,1,0:T(8,128)S(1)}, f32[1,128,512]{2,1,0:T(8,128)S(1)}, u32[]{:S(2)}, u32[]{:S(2)}) collective-permute-start(f32[1,128,512]{2,1,0:T(8,128)S(1)} %fusion.118), channel_id=1, source_target_pairs={{0,8},{8,0},{16,24},{24,16},{32,40},{40,32},{48,56},{56,48},{64,72... | collective-permute-start | bytes 786440 | tf_op jit(solution)/shard_map/ppermute | solution.py:110
  79.8 8.6 %collective-permute-start.7 = (f32[1,128,512]{2,1,0:T(8,128)S(1)}, f32[1,128,512]{2,1,0:T(8,128)S(1)}, u32[]{:S(2)}, u32[]{:S(2)}) collective-permute-start(f32[1,128,512]{2,1,0:T(8,128)S(1)} %multiply_add_fusion.14), channel_id=1, source_target_pairs={{0,16},{8,24},{16,0},{24,8},{32,48},{40,56},{48,32},{56,40},{64,80... | collective-permute-start | bytes 786440 | tf_op jit(solution)/shard_map/ppermute | solution.py:110
  88.5 7.1 %collective-permute-start.8 = (f32[1,128,512]{2,1,0:T(8,128)S(1)}, f32[1,128,512]{2,1,0:T(8,128)S(1)}, u32[]{:S(2)}, u32[]{:S(2)}) collective-permute-start(f32[1,128,512]{2,1,0:T(8,128)S(1)} %multiply_add_fusion.13), channel_id=1, source_target_pairs={{0,32},{8,40},{16,48},{24,56},{32,0},{40,8},{48,16},{56,24},{64,96... | collective-permute-start | bytes 786440 | tf_op jit(solution)/shard_map/ppermute | solution.py:110
  95.7 10.8 %collective-permute-start.9 = (f32[1,128,512]{2,1,0:T(8,128)S(1)}, f32[1,128,512]{2,1,0:T(8,128)S(1)}, u32[]{:S(2)}, u32[]{:S(2)}) collective-permute-start(f32[1,128,512]{2,1,0:T(8,128)S(1)} %multiply_add_fusion.12), channel_id=1, source_target_pairs={{0,64},{8,72},{16,80},{24,88},{32,96},{40,104},{48,112},{56,120},{... | collective-permute-start | bytes 786440 | tf_op jit(solution)/shard_map/ppermute | solution.py:110
  106.7 12.9 %copy-start.19 = (f32[1,128]{1,0:T(1,128)S(1)}, f32[1,128]{1,0:T(1,128)}, u32[]{:S(2)}) copy-start(f32[1,128]{1,0:T(1,128)} %param.11) | copy-start | bytes 1540
  106.7 7.2 %collective-permute-start.10 = (f32[1,128,512]{2,1,0:T(8,128)S(1)}, f32[1,128,512]{2,1,0:T(8,128)S(1)}, u32[]{:S(2)}, u32[]{:S(2)}) collective-permute-start(f32[1,128,512]{2,1,0:T(8,128)S(1)} %multiply_add_fusion.11), channel_id=1, source_target_pairs={{0,128},{8,136},{16,144},{24,152},{32,160},{40,168},{48,176},{56,1... | collective-permute-start | bytes 786440 | tf_op jit(solution)/shard_map/ppermute | solution.py:110
  114.7 10.8 %collective-permute-start.11 = (f32[1,128,512]{2,1,0:T(8,128)}, f32[1,128,512]{2,1,0:T(8,128)}, u32[]{:S(2)}, u32[]{:S(2)}) collective-permute-start(f32[1,128,512]{2,1,0:T(8,128)} %multiply_add_fusion.10), channel_id=1, source_target_pairs={{0,256},{8,264},{16,272},{24,280},{32,288},{40,296},{48,304},{56,3... | collective-permute-start | bytes 786440 | tf_op jit(solution)/shard_map/ppermute | solution.py:110
  126.6 0.9 copy-start.9
  128.0 2.4 copy-start.6
  128.0 1.0 copy-start.2
  129.4 1.0 copy-start.5
  130.8 1.0 copy-start.3
  134.5 7.6 %collective-permute-start.12 = (f32[1,129,512]{2,1,0:T(8,128)}, f32[1,129,512]{2,1,0:T(8,128)}, u32[]{:S(2)}, u32[]{:S(2)}) collective-permute-start(f32[1,129,512]{2,1,0:T(8,128)} %pad_maximum_fusion.7), channel_id=1, source_target_pairs={{0,8},{8,0},{16,24},{24,16},{32,40},{40,32},{48,56},{56,48},{64,72... | collective-permute-start | bytes 792584 | tf_op jit(solution)/shard_map/ppermute | solution.py:87
  146.3 11.5 %collective-permute-start.13 = (f32[1,129,512]{2,1,0:T(8,128)}, f32[1,129,512]{2,1,0:T(8,128)}, u32[]{:S(2)}, u32[]{:S(2)}) collective-permute-start(f32[1,129,512]{2,1,0:T(8,128)} %pad_maximum_fusion.8), channel_id=1, source_target_pairs={{0,16},{8,24},{16,0},{24,8},{32,48},{40,56},{48,32},{56,40},{64,80... | collective-permute-start | bytes 792584 | tf_op jit(solution)/shard_map/ppermute | solution.py:87
  159.6 0.7 copy-start.11
  161.1 7.6 %collective-permute-start.14 = (f32[1,129,512]{2,1,0:T(8,128)}, f32[1,129,512]{2,1,0:T(8,128)}, u32[]{:S(2)}, u32[]{:S(2)}) collective-permute-start(f32[1,129,512]{2,1,0:T(8,128)} %pad_maximum_fusion.9), channel_id=1, source_target_pairs={{0,32},{8,40},{16,48},{24,56},{32,0},{40,8},{48,16},{56,24},{64,96... | collective-permute-start | bytes 792584 | tf_op jit(solution)/shard_map/ppermute | solution.py:87
  172.9 11.5 %collective-permute-start.15 = (f32[1,129,512]{2,1,0:T(8,128)}, f32[1,129,512]{2,1,0:T(8,128)}, u32[]{:S(2)}, u32[]{:S(2)}) collective-permute-start(f32[1,129,512]{2,1,0:T(8,128)} %pad_maximum_fusion.10), channel_id=1, source_target_pairs={{0,64},{8,72},{16,80},{24,88},{32,96},{40,104},{48,112},{56,120},{... | collective-permute-start | bytes 792584 | tf_op jit(solution)/shard_map/ppermute | solution.py:87
  188.6 7.9 %collective-permute-start.16 = (f32[1,129,512]{2,1,0:T(8,128)}, f32[1,129,512]{2,1,0:T(8,128)}, u32[]{:S(2)}, u32[]{:S(2)}) collective-permute-start(f32[1,129,512]{2,1,0:T(8,128)} %pad_maximum_fusion.11), channel_id=1, source_target_pairs={{0,128},{8,136},{16,144},{24,152},{32,160},{40,168},{48,176},{56,1... | collective-permute-start | bytes 792584 | tf_op jit(solution)/shard_map/ppermute | solution.py:87
  198.3 8.8 %collective-permute-start.17 = (f32[1,129,512]{2,1,0:T(8,128)S(1)}, f32[1,129,512]{2,1,0:T(8,128)S(1)}, u32[]{:S(2)}, u32[]{:S(2)}) collective-permute-start(f32[1,129,512]{2,1,0:T(8,128)S(1)} %pad_maximum_fusion.12), channel_id=1, source_target_pairs={{0,256},{8,264},{16,272},{24,280},{32,288},{40,296},{48,304},{56,3... | collective-permute-start | bytes 792584 | tf_op jit(solution)/shard_map/ppermute | solution.py:87
  208.6 1.0 copy-start.12
  208.6 1.0 copy-start.7
  212.3 7.1 %collective-permute-start.18 = (f32[1,128,512]{2,1,0:T(8,128)S(1)}, f32[1,128,512]{2,1,0:T(8,128)S(1)}, u32[]{:S(2)}, u32[]{:S(2)}) collective-permute-start(f32[1,128,512]{2,1,0:T(8,128)S(1)} %fusion.76), channel_id=1, source_target_pairs={{0,8},{8,0},{16,24},{24,16},{32,40},{40,32},{48,56},{56,48},{64,72... | collective-permute-start | bytes 786440 | tf_op jit(solution)/shard_map/ppermute | solution.py:110
  219.5 8.6 %collective-permute-start.19 = (f32[1,128,512]{2,1,0:T(8,128)S(1)}, f32[1,128,512]{2,1,0:T(8,128)S(1)}, u32[]{:S(2)}, u32[]{:S(2)}) collective-permute-start(f32[1,128,512]{2,1,0:T(8,128)S(1)} %multiply_add_fusion.4), channel_id=1, source_target_pairs={{0,16},{8,24},{16,0},{24,8},{32,48},{40,56},{48,32},{56,40},{64,80... | collective-permute-start | bytes 786440 | tf_op jit(solution)/shard_map/ppermute | solution.py:110
  228.1 2.5 copy-start.14
  228.3 35.8 %copy-start.13 = (f32[1,128,512]{2,1,0:T(8,128)S(1)}, f32[1,128,512]{2,1,0:T(8,128)}, u32[]{:S(2)}) copy-start(f32[1,128,512]{2,1,0:T(8,128)} %copy-done.12) | copy-start | bytes 786436
  228.3 7.5 %collective-permute-start.20 = (f32[1,128,512]{2,1,0:T(8,128)S(1)}, f32[1,128,512]{2,1,0:T(8,128)S(1)}, u32[]{:S(2)}, u32[]{:S(2)}) collective-permute-start(f32[1,128,512]{2,1,0:T(8,128)S(1)} %multiply_add_fusion.3), channel_id=1, source_target_pairs={{0,32},{8,40},{16,48},{24,56},{32,0},{40,8},{48,16},{56,24},{64,96... | collective-permute-start | bytes 786440 | tf_op jit(solution)/shard_map/ppermute | solution.py:110
  235.8 19.3 %copy-start.15 = (f32[1,128,512]{2,1,0:T(8,128)}, f32[1,128,512]{2,1,0:T(8,128)S(1)}, u32[]{:S(2)}) copy-start(f32[1,128,512]{2,1,0:T(8,128)S(1)} %collective-permute-done.20) | copy-start | bytes 786436
  235.9 11.1 %collective-permute-start.21 = (f32[1,128,512]{2,1,0:T(8,128)S(1)}, f32[1,128,512]{2,1,0:T(8,128)S(1)}, u32[]{:S(2)}, u32[]{:S(2)}) collective-permute-start(f32[1,128,512]{2,1,0:T(8,128)S(1)} %multiply_add_fusion.2), channel_id=1, source_target_pairs={{0,64},{8,72},{16,80},{24,88},{32,96},{40,104},{48,112},{56,120},{... | collective-permute-start | bytes 786440 | tf_op jit(solution)/shard_map/ppermute | solution.py:110
  247.0 8.1 %copy-start.16 = (f32[1,128,512]{2,1,0:T(8,128)}, f32[1,128,512]{2,1,0:T(8,128)S(1)}, u32[]{:S(2)}) copy-start(f32[1,128,512]{2,1,0:T(8,128)S(1)} %collective-permute-done.21) | copy-start | bytes 786436
  247.2 7.1 %collective-permute-start.22 = (f32[1,128,512]{2,1,0:T(8,128)S(1)}, f32[1,128,512]{2,1,0:T(8,128)S(1)}, u32[]{:S(2)}, u32[]{:S(2)}) collective-permute-start(f32[1,128,512]{2,1,0:T(8,128)S(1)} %multiply_add_fusion.1), channel_id=1, source_target_pairs={{0,128},{8,136},{16,144},{24,152},{32,160},{40,168},{48,176},{56,1... | collective-permute-start | bytes 786440 | tf_op jit(solution)/shard_map/ppermute | solution.py:110
  254.3 0.8 copy-start.17
  255.1 8.9 %collective-permute-start.23 = (f32[1,128,512]{2,1,0:T(8,128)}, f32[1,128,512]{2,1,0:T(8,128)}, u32[]{:S(2)}, u32[]{:S(2)}) collective-permute-start(f32[1,128,512]{2,1,0:T(8,128)} %multiply_add_fusion), channel_id=1, source_target_pairs={{0,256},{8,264},{16,272},{24,280},{32,288},{40,296},{48,304},{56,3... | collective-permute-start | bytes 786440 | tf_op jit(solution)/shard_map/ppermute | solution.py:110
  267.0 1.0 copy-start.8
  267.0 1.0 copy-start.10
  269.8 28.3 %collective-permute-start.24 = (f32[1184,128]{1,0:T(8,128)S(1)}, f32[1184,128]{1,0:T(8,128)}, u32[]{:S(2)}, u32[]{:S(2)}) collective-permute-start(f32[1184,128]{1,0:T(8,128)S(1)} %constant_dynamic-slice_fusion.3), channel_id=1, source_target_pairs={{0,1},{1,0},{2,3},{3,2},{4,5},{5,4},{6,7},{7,6},{8,9},{9,8},{10,11... | collective-permute-start | bytes 1818632 | tf_op jit(solution)/shard_map/ppermute | solution.py:133
  299.3 15.1 %collective-permute-start.25 = (f32[296,128]{1,0:T(8,128)S(1)}, f32[296,128]{1,0:T(8,128)S(1)}, u32[]{:S(2)}, u32[]{:S(2)}) collective-permute-start(f32[296,128]{1,0:T(8,128)S(1)} %get-tuple-element.31), channel_id=1, source_target_pairs={{0,2},{1,7},{2,4},{3,1},{4,6},{5,3},{6,0},{7,5},{8,10},{9,15},{10,... | collective-permute-start | bytes 454664 | tf_op jit(solution)/shard_map/ppermute | solution.py:144
  314.5 14.4 %collective-permute-start.26 = (f32[296,128]{1,0:T(8,128)S(1)}, f32[296,128]{1,0:T(8,128)S(1)}, u32[]{:S(2)}, u32[]{:S(2)}) collective-permute-start(f32[296,128]{1,0:T(8,128)S(1)} %get-tuple-element.29), channel_id=1, source_target_pairs={{0,2},{1,7},{2,4},{3,1},{4,6},{5,3},{6,0},{7,5},{8,10},{9,15},{10,... | collective-permute-start | bytes 454664 | tf_op jit(solution)/shard_map/ppermute | solution.py:144
  329.0 14.6 %collective-permute-start.27 = (f32[296,128]{1,0:T(8,128)S(1)}, f32[296,128]{1,0:T(8,128)S(1)}, u32[]{:S(2)}, u32[]{:S(2)}) collective-permute-start(f32[296,128]{1,0:T(8,128)S(1)} %get-tuple-element.27), channel_id=1, source_target_pairs={{0,2},{1,7},{2,4},{3,1},{4,6},{5,3},{6,0},{7,5},{8,10},{9,15},{10,... | collective-permute-start | bytes 454664 | tf_op jit(solution)/shard_map/ppermute | solution.py:144
  343.7 14.6 %collective-permute-start.28 = (f32[296,128]{1,0:T(8,128)S(1)}, f32[296,128]{1,0:T(8,128)S(1)}, u32[]{:S(2)}, u32[]{:S(2)}) collective-permute-start(f32[296,128]{1,0:T(8,128)S(1)} %dynamic-slice_bitcast_fusion.2), channel_id=1, source_target_pairs={{0,2},{1,7},{2,4},{3,1},{4,6},{5,3},{6,0},{7,5},{8,10},{9,15},{10,... | collective-permute-start | bytes 454664 | tf_op jit(solution)/shard_map/ppermute | solution.py:150
  351.5 33.0 %copy-start.4 = (bf16[128,9,128]{0,2,1:T(8,128)(2,1)S(1)}, bf16[128,9,128]{0,2,1:T(8,128)(2,1)}, u32[]{:S(2)}) copy-start(bf16[128,9,128]{0,2,1:T(8,128)(2,1)} %copy.26) | copy-start | bytes 884740
  358.3 11.1 %collective-permute-start.29 = (f32[296,128]{1,0:T(8,128)S(1)}, f32[296,128]{1,0:T(8,128)S(1)}, u32[]{:S(2)}, u32[]{:S(2)}) collective-permute-start(f32[296,128]{1,0:T(8,128)S(1)} %dynamic-slice_bitcast_fusion.1), channel_id=1, source_target_pairs={{0,2},{1,7},{2,4},{3,1},{4,6},{5,3},{6,0},{7,5},{8,10},{9,15},{10,... | collective-permute-start | bytes 454664 | tf_op jit(solution)/shard_map/ppermute | solution.py:150
  369.4 9.9 %collective-permute-start.30 = (f32[296,128]{1,0:T(8,128)S(1)}, f32[296,128]{1,0:T(8,128)S(1)}, u32[]{:S(2)}, u32[]{:S(2)}) collective-permute-start(f32[296,128]{1,0:T(8,128)S(1)} %dynamic-slice_bitcast_fusion), channel_id=1, source_target_pairs={{0,2},{1,7},{2,4},{3,1},{4,6},{5,3},{6,0},{7,5},{8,10},{9,15},{10,... | collective-permute-start | bytes 454664 | tf_op jit(solution)/shard_map/ppermute | solution.py:150
  379.4 6.6 %collective-permute-start.31 = (f32[1184,128]{1,0:T(8,128)S(1)}, f32[1184,128]{1,0:T(8,128)S(1)}, u32[]{:S(2)}, u32[]{:S(2)}) collective-permute-start(f32[1184,128]{1,0:T(8,128)S(1)} %bitcast.579), channel_id=1, source_target_pairs={{0,1},{1,0},{2,3},{3,2},{4,5},{5,4},{6,7},{7,6},{8,9},{9,8},{10,11... | collective-permute-start | bytes 1818632 | tf_op jit(solution)/shard_map/ppermute | solution.py:153

commit v12 on v11

--- a/solution.py
+++ b/solution.py
@@ -69,36 +69,44 @@
     return adjoint
 
 
-def butterfly_first(gain, local, axis, reverse):
+def gain_factors(place, step, block_gain, other_gain, product, upper_dtype):
+    upper = (place // step) % 2 == 1
+    u = upper.astype(upper_dtype)
+    upper_gain = jnp.where(upper, block_gain, other_gain)
+    taken = u * product
+    from_other = upper_gain * u + (1 - u)
+    from_own = upper_gain * (1 - u) + u
+    product = jnp.where(upper, product * other_gain, product)
+    return (taken, from_other, from_own), product, block_gain * other_gain
+
+
+def butterfly_first(gain, local, axis, other_gain_row):
     count = lax.axis_size(axis)
     me = lax.axis_index(axis)
-    place = count - 1 - me if reverse else me
     channels, pixels = local.shape[1], local.shape[2]
     total = jnp.zeros_like(local)
-    product = jnp.ones_like(gain)
     block_sum = local
-    block_gain = gain
-    factors = []
+    states = [
+        [me, gain, jnp.ones_like(gain), []],
+        [count - 1 - me, other_gain_row, jnp.ones_like(other_gain_row), []],
+    ]
     step = 1
     while step < count:
-        upper = (place // step) % 2 == 1
-        gain_row = jnp.pad(block_gain, (0, pixels - channels))
-        packed = jnp.concatenate([block_sum, gain_row[None, None, :]], axis=1)
+        rows = [jnp.pad(state[1], (0, pixels - channels))[None, None, :] for state in states]
+        packed = jnp.concatenate([block_sum] + rows, axis=1)
         got = lax.ppermute(packed, axis, [(k, k ^ step) for k in range(count)])
         other_sum = got[:, :channels, :]
-        other_gain = got[0, channels, :channels]
-        u = upper.astype(gain.dtype)
-        upper_gain = jnp.where(upper, block_gain, other_gain)
-        taken = u * product
-        from_other = upper_gain * u + (1 - u)
-        from_own = upper_gain * (1 - u) + u
-        factors.append((taken, from_other, from_own))
+        for i, state in enumerate(states):
+            factor, state[2], new_gain = gain_factors(
+                state[0], step, state[1], got[0, channels + i, :channels], state[2], gain.dtype
+            )
+            state[1] = new_gain
+            state[3].append(factor)
+        taken, from_other, from_own = states[0][3][-1]
         total = total + taken[None, :, None] * other_sum
-        product = jnp.where(upper, product * other_gain, product)
         block_sum = from_other[None, :, None] * other_sum + from_own[None, :, None] * block_sum
-        block_gain = block_gain * other_gain
         step *= 2
-    return total, factors
+    return total, states[0][3], states[1][3]
 
 
 def butterfly_again(local, factors, axis):
@@ -169,7 +177,7 @@
         ending = relax_block(c_points, conv_weight, conv_bias)[0]
         residual = ending - following
         if sweep_index == 0:
-            error, factors = butterfly_first(gain_row, residual, "layer", False)
+            error, factors, back_factors = butterfly_first(gain_row, residual, "layer", back_row)
         else:
             error = butterfly_again(residual, factors, "layer")
         c_points = c_points + error
@@ -180,10 +188,7 @@
     for sweep_index in range(ITERS):
         start_adj = adjoint_block(target, stored, flipped_list)
         residual = start_adj - previous
-        if sweep_index == 0:
-            error, factors = butterfly_first(back_row, residual, "layer", True)
-        else:
-            error = butterfly_again(residual, factors, "layer")
+        error = butterfly_again(residual, back_factors, "layer")
         target = target + error
         previous = previous + back_row[None, :, None] * error + residual
     adjoint = target

time: 395 us -> 369 us (0.934)
  other arithmetic: 39.7 us -> 23.6 us
  waiting for transfers between devices: 166 us -> 160 us
    ppermute x12 -> x6, waiting for transfers between devices: 67.8 us -> 32 us  [butterfly_first(): got = lax.ppermute(packed, axis, [(k, k ^ step) for k in range(count)])]
    ppermute x12 -> x18, waiting for transfers between devices: 62.2 us -> 93.5 us  [butterfly_again(): got = lax.ppermute(block_sum, axis, [(k, k ^ step) for k in range(count)])]
    ppermute x12 -> x18, starting transfers between devices: 37.5 us -> 59 us  [butterfly_again(): got = lax.ppermute(block_sum, axis, [(k, k ^ step) for k in range(count)])]
    ppermute x12 -> x6, starting transfers between devices: 50.3 us -> 30.8 us  [butterfly_first(): got = lax.ppermute(packed, axis, [(k, k ^ step) for k in range(count)])]
    add x10 -> x5, other arithmetic: 8.28 us -> 0.51 us  [butterfly_first(): from_other[None, :, None] * other_sum + from_own[None, :, None] * block_sum]
    concatenate x12 -> x6, other arithmetic: 7.59 us -> 0.14 us  [butterfly_first(): packed = jnp.concatenate([block_sum] + rows, axis=1)]
where the time goes in v12:
time: 369 us; the launch traced here: 364 us
  starting transfers between devices  162 us (44%)
  waiting for transfers between devices  160 us (43%)
  other arithmetic  23.6 us (6%)
  local copies, waits for them, and re-layouts  8.22 us (2%)
  matrix products  6.25 us (2%)
    ppermute x18, waiting for transfers between devices, butterfly_again(): got = lax.ppermute(block_sum, axis, [(k, k ^ step) for k in range(count)])  93.5 us
    ppermute x18, starting transfers between devices, butterfly_again(): got = lax.ppermute(block_sum, axis, [(k, k ^ step) for k in range(count)])  59 us
    ppermute x6, starting transfers between devices, batch_sum(): got = lax.ppermute(sent, axis, ring)  43.9 us
    ppermute x6, waiting for transfers between devices, batch_sum(): got = lax.ppermute(sent, axis, ring)  32.8 us
    ppermute x6, waiting for transfers between devices, butterfly_first(): got = lax.ppermute(packed, axis, [(k, k ^ step) for k in range(count)])  32 us
    ppermute x6, starting transfers between devices, butterfly_first(): got = lax.ppermute(packed, axis, [(k, k ^ step) for k in range(count)])  30.8 us
    ppermute x1, starting transfers between devices, batch_sum(): half = keep + lax.ppermute(give, axis, partner)  24.1 us
    unnamed x96, other arithmetic  9.1 us
  transfers between devices with their start and end apart: 32, of which 32 were waited for; matrix products, arithmetic and copies ran while one was open for 1% of the time, Pallas kernels for 0%

profile of v12, /device:TPU:1, one launch (start us, length us, event | category | flops | bytes accessed | tf_op | source)
XLA Modules:
  0.0 363.7 jit_solution(5265547594314211648)
XLA Ops:
  6.6 4.0 %collective-permute-start = (f32[1,130,512]{2,1,0:T(8,128)S(1)}, f32[1,130,512]{2,1,0:T(8,128)S(1)}, u32[]{:S(2)}, u32[]{:S(2)}) collective-permute-start(f32[1,130,512]{2,1,0:T(8,128)S(1)} %pad_maximum_fusion.1), channel_id=1, source_target_pairs={{0,8},{8,0},{16,24},{24,16},{32,40},{40,32},{48,56},{56,48},{64,72... | collective-permute-start | bytes 798728 | tf_op jit(solution)/shard_map/ppermute | solution.py:97
  10.6 3.9 %collective-permute-done = f32[1,130,512]{2,1,0:T(8,128)S(1)} collective-permute-done((f32[1,130,512]{2,1,0:T(8,128)S(1)}, f32[1,130,512]{2,1,0:T(8,128)S(1)}, u32[]{:S(2)}, u32[]{:S(2)}) %collective-permute-start) | collective-permute-done | bytes 266272 | tf_op jit(solution)/shard_map/ppermute | solution.py:97
  14.7 7.0 %collective-permute-start.1 = (f32[1,130,512]{2,1,0:T(8,128)S(1)}, f32[1,130,512]{2,1,0:T(8,128)S(1)}, u32[]{:S(2)}, u32[]{:S(2)}) collective-permute-start(f32[1,130,512]{2,1,0:T(8,128)S(1)} %pad_maximum_fusion.2), channel_id=1, source_target_pairs={{0,16},{8,24},{16,0},{24,8},{32,48},{40,56},{48,32},{56,40},{64,80... | collective-permute-start | bytes 798728 | tf_op jit(solution)/shard_map/ppermute | solution.py:97
  21.9 3.8 %collective-permute-done.1 = f32[1,130,512]{2,1,0:T(8,128)S(1)} collective-permute-done((f32[1,130,512]{2,1,0:T(8,128)S(1)}, f32[1,130,512]{2,1,0:T(8,128)S(1)}, u32[]{:S(2)}, u32[]{:S(2)}) %collective-permute-start.1) | collective-permute-done | bytes 266272 | tf_op jit(solution)/shard_map/ppermute | solution.py:97
  26.4 5.0 %collective-permute-start.2 = (f32[1,130,512]{2,1,0:T(8,128)S(1)}, f32[1,130,512]{2,1,0:T(8,128)S(1)}, u32[]{:S(2)}, u32[]{:S(2)}) collective-permute-start(f32[1,130,512]{2,1,0:T(8,128)S(1)} %pad_maximum_fusion.3), channel_id=1, source_target_pairs={{0,32},{8,40},{16,48},{24,56},{32,0},{40,8},{48,16},{56,24},{64,96... | collective-permute-start | bytes 798728 | tf_op jit(solution)/shard_map/ppermute | solution.py:97
  31.4 3.9 %collective-permute-done.2 = f32[1,130,512]{2,1,0:T(8,128)S(1)} collective-permute-done((f32[1,130,512]{2,1,0:T(8,128)S(1)}, f32[1,130,512]{2,1,0:T(8,128)S(1)}, u32[]{:S(2)}, u32[]{:S(2)}) %collective-permute-start.2) | collective-permute-done | bytes 266272 | tf_op jit(solution)/shard_map/ppermute | solution.py:97
  35.5 5.4 %collective-permute-start.3 = (f32[1,130,512]{2,1,0:T(8,128)S(1)}, f32[1,130,512]{2,1,0:T(8,128)S(1)}, u32[]{:S(2)}, u32[]{:S(2)}) collective-permute-start(f32[1,130,512]{2,1,0:T(8,128)S(1)} %pad_maximum_fusion.4), channel_id=1, source_target_pairs={{0,64},{8,72},{16,80},{24,88},{32,96},{40,104},{48,112},{56,120},{... | collective-permute-start | bytes 798728 | tf_op jit(solution)/shard_map/ppermute | solution.py:97
  40.9 11.2 %collective-permute-done.3 = f32[1,130,512]{2,1,0:T(8,128)S(1)} collective-permute-done((f32[1,130,512]{2,1,0:T(8,128)S(1)}, f32[1,130,512]{2,1,0:T(8,128)S(1)}, u32[]{:S(2)}, u32[]{:S(2)}) %collective-permute-start.3) | collective-permute-done | bytes 266272 | tf_op jit(solution)/shard_map/ppermute | solution.py:97
  52.8 4.2 %collective-permute-start.4 = (f32[1,130,512]{2,1,0:T(8,128)S(1)}, f32[1,130,512]{2,1,0:T(8,128)S(1)}, u32[]{:S(2)}, u32[]{:S(2)}) collective-permute-start(f32[1,130,512]{2,1,0:T(8,128)S(1)} %pad_maximum_fusion.5), channel_id=1, source_target_pairs={{0,128},{8,136},{16,144},{24,152},{32,160},{40,168},{48,176},{56,1... | collective-permute-start | bytes 798728 | tf_op jit(solution)/shard_map/ppermute | solution.py:97
  57.7 4.5 %collective-permute-done.4 = f32[1,130,512]{2,1,0:T(8,128)S(1)} collective-permute-done((f32[1,130,512]{2,1,0:T(8,128)S(1)}, f32[1,130,512]{2,1,0:T(8,128)S(1)}, u32[]{:S(2)}, u32[]{:S(2)}) %collective-permute-start.4) | collective-permute-done | bytes 266272 | tf_op jit(solution)/shard_map/ppermute | solution.py:97
  62.9 5.3 %collective-permute-start.5 = (f32[1,130,512]{2,1,0:T(8,128)S(1)}, f32[1,130,512]{2,1,0:T(8,128)}, u32[]{:S(2)}, u32[]{:S(2)}) collective-permute-start(f32[1,130,512]{2,1,0:T(8,128)S(1)} %pad_maximum_fusion.6), channel_id=1, source_target_pairs={{0,256},{8,264},{16,272},{24,280},{32,288},{40,296},{48,304},{56,3... | collective-permute-start | bytes 798728 | tf_op jit(solution)/shard_map/ppermute | solution.py:97
  68.3 4.7 %collective-permute-done.5 = f32[1,130,512]{2,1,0:T(8,128)} collective-permute-done((f32[1,130,512]{2,1,0:T(8,128)S(1)}, f32[1,130,512]{2,1,0:T(8,128)}, u32[]{:S(2)}, u32[]{:S(2)}) %collective-permute-start.5) | collective-permute-done | bytes 266272 | tf_op jit(solution)/shard_map/ppermute | solution.py:97
  76.8 3.0 collective-permute-start.6
  79.8 4.1 %collective-permute-done.6 = f32[1,128,512]{2,1,0:T(8,128)S(1)} collective-permute-done((f32[1,128,512]{2,1,0:T(8,128)S(1)}, f32[1,128,512]{2,1,0:T(8,128)S(1)}, u32[]{:S(2)}, u32[]{:S(2)}) %collective-permute-start.6) | collective-permute-done | bytes 262176 | tf_op jit(solution)/shard_map/ppermute | solution.py:118
  84.0 4.8 %collective-permute-start.7 = (f32[1,128,512]{2,1,0:T(8,128)S(1)}, f32[1,128,512]{2,1,0:T(8,128)S(1)}, u32[]{:S(2)}, u32[]{:S(2)}) collective-permute-start(f32[1,128,512]{2,1,0:T(8,128)S(1)} %multiply_add_fusion.15), channel_id=1, source_target_pairs={{0,16},{8,24},{16,0},{24,8},{32,48},{40,56},{48,32},{56,40},{64,80... | collective-permute-start | bytes 786440 | tf_op jit(solution)/shard_map/ppermute | solution.py:118
  88.8 3.8 %collective-permute-done.7 = f32[1,128,512]{2,1,0:T(8,128)S(1)} collective-permute-done((f32[1,128,512]{2,1,0:T(8,128)S(1)}, f32[1,128,512]{2,1,0:T(8,128)S(1)}, u32[]{:S(2)}, u32[]{:S(2)}) %collective-permute-start.7) | collective-permute-done | bytes 262176 | tf_op jit(solution)/shard_map/ppermute | solution.py:118
  92.7 1.9 collective-permute-start.8
  94.6 5.2 %collective-permute-done.8 = f32[1,128,512]{2,1,0:T(8,128)S(1)} collective-permute-done((f32[1,128,512]{2,1,0:T(8,128)S(1)}, f32[1,128,512]{2,1,0:T(8,128)S(1)}, u32[]{:S(2)}, u32[]{:S(2)}) %collective-permute-start.8) | collective-permute-done | bytes 262176 | tf_op jit(solution)/shard_map/ppermute | solution.py:118
  99.9 3.1 collective-permute-start.9
  103.1 7.7 %collective-permute-done.9 = f32[1,128,512]{2,1,0:T(8,128)S(1)} collective-permute-done((f32[1,128,512]{2,1,0:T(8,128)S(1)}, f32[1,128,512]{2,1,0:T(8,128)S(1)}, u32[]{:S(2)}, u32[]{:S(2)}) %collective-permute-start.9) | collective-permute-done | bytes 262176 | tf_op jit(solution)/shard_map/ppermute | solution.py:118
  110.9 3.0 collective-permute-start.10
  113.9 4.2 %collective-permute-done.10 = f32[1,128,512]{2,1,0:T(8,128)S(1)} collective-permute-done((f32[1,128,512]{2,1,0:T(8,128)S(1)}, f32[1,128,512]{2,1,0:T(8,128)S(1)}, u32[]{:S(2)}, u32[]{:S(2)}) %collective-permute-start.10) | collective-permute-done | bytes 262176 | tf_op jit(solution)/shard_map/ppermute | solution.py:118
  118.9 4.8 %collective-permute-start.11 = (f32[1,128,512]{2,1,0:T(8,128)}, f32[1,128,512]{2,1,0:T(8,128)}, u32[]{:S(2)}, u32[]{:S(2)}) collective-permute-start(f32[1,128,512]{2,1,0:T(8,128)} %multiply_add_fusion.11), channel_id=1, source_target_pairs={{0,256},{8,264},{16,272},{24,280},{32,288},{40,296},{48,304},{56,3... | collective-permute-start | bytes 786440 | tf_op jit(solution)/shard_map/ppermute | solution.py:118
  125.4 4.3 %collective-permute-done.11 = f32[1,128,512]{2,1,0:T(8,128)} collective-permute-done((f32[1,128,512]{2,1,0:T(8,128)}, f32[1,128,512]{2,1,0:T(8,128)}, u32[]{:S(2)}, u32[]{:S(2)}) %collective-permute-start.11) | collective-permute-done | bytes 262176 | tf_op jit(solution)/shard_map/ppermute | solution.py:118
  136.4 3.2 collective-permute-start.12
  139.6 3.9 %collective-permute-done.12 = f32[1,128,512]{2,1,0:T(8,128)S(1)} collective-permute-done((f32[1,128,512]{2,1,0:T(8,128)S(1)}, f32[1,128,512]{2,1,0:T(8,128)S(1)}, u32[]{:S(2)}, u32[]{:S(2)}) %collective-permute-start.12) | collective-permute-done | bytes 262176 | tf_op jit(solution)/shard_map/ppermute | solution.py:118
  143.7 4.6 %collective-permute-start.13 = (f32[1,128,512]{2,1,0:T(8,128)S(1)}, f32[1,128,512]{2,1,0:T(8,128)S(1)}, u32[]{:S(2)}, u32[]{:S(2)}) collective-permute-start(f32[1,128,512]{2,1,0:T(8,128)S(1)} %multiply_add_fusion.10), channel_id=1, source_target_pairs={{0,16},{8,24},{16,0},{24,8},{32,48},{40,56},{48,32},{56,40},{64,80... | collective-permute-start | bytes 786440 | tf_op jit(solution)/shard_map/ppermute | solution.py:118
  148.3 4.3 %collective-permute-done.13 = f32[1,128,512]{2,1,0:T(8,128)S(1)} collective-permute-done((f32[1,128,512]{2,1,0:T(8,128)S(1)}, f32[1,128,512]{2,1,0:T(8,128)S(1)}, u32[]{:S(2)}, u32[]{:S(2)}) %collective-permute-start.13) | collective-permute-done | bytes 262176 | tf_op jit(solution)/shard_map/ppermute | solution.py:118
  152.7 1.9 collective-permute-start.14
  154.7 5.2 %collective-permute-done.14 = f32[1,128,512]{2,1,0:T(8,128)S(1)} collective-permute-done((f32[1,128,512]{2,1,0:T(8,128)S(1)}, f32[1,128,512]{2,1,0:T(8,128)S(1)}, u32[]{:S(2)}, u32[]{:S(2)}) %collective-permute-start.14) | collective-permute-done | bytes 262176 | tf_op jit(solution)/shard_map/ppermute | solution.py:118
  160.0 2.3 collective-permute-start.15
  162.3 8.2 %collective-permute-done.15 = f32[1,128,512]{2,1,0:T(8,128)S(1)} collective-permute-done((f32[1,128,512]{2,1,0:T(8,128)S(1)}, f32[1,128,512]{2,1,0:T(8,128)S(1)}, u32[]{:S(2)}, u32[]{:S(2)}) %collective-permute-start.15) | collective-permute-done | bytes 262176 | tf_op jit(solution)/shard_map/ppermute | solution.py:118
  170.6 5.3 %collective-permute-start.16 = (f32[1,128,512]{2,1,0:T(8,128)S(1)}, f32[1,128,512]{2,1,0:T(8,128)S(1)}, u32[]{:S(2)}, u32[]{:S(2)}) collective-permute-start(f32[1,128,512]{2,1,0:T(8,128)S(1)} %multiply_add_fusion.7), channel_id=1, source_target_pairs={{0,128},{8,136},{16,144},{24,152},{32,160},{40,168},{48,176},{56,1... | collective-permute-start | bytes 786440 | tf_op jit(solution)/shard_map/ppermute | solution.py:118
  176.0 3.7 %collective-permute-done.16 = f32[1,128,512]{2,1,0:T(8,128)S(1)} collective-permute-done((f32[1,128,512]{2,1,0:T(8,128)S(1)}, f32[1,128,512]{2,1,0:T(8,128)S(1)}, u32[]{:S(2)}, u32[]{:S(2)}) %collective-permute-start.16) | collective-permute-done | bytes 262176 | tf_op jit(solution)/shard_map/ppermute | solution.py:118
  179.8 2.2 collective-permute-start.17
  182.0 6.4 %collective-permute-done.17 = f32[1,128,512]{2,1,0:T(8,128)S(1)} collective-permute-done((f32[1,128,512]{2,1,0:T(8,128)S(1)}, f32[1,128,512]{2,1,0:T(8,128)S(1)}, u32[]{:S(2)}, u32[]{:S(2)}) %collective-permute-start.17) | collective-permute-done | bytes 262176 | tf_op jit(solution)/shard_map/ppermute | solution.py:118
  191.4 2.7 collective-permute-start.18
  194.1 4.4 %collective-permute-done.18 = f32[1,128,512]{2,1,0:T(8,128)S(1)} collective-permute-done((f32[1,128,512]{2,1,0:T(8,128)S(1)}, f32[1,128,512]{2,1,0:T(8,128)S(1)}, u32[]{:S(2)}, u32[]{:S(2)}) %collective-permute-start.18) | collective-permute-done | bytes 262176 | tf_op jit(solution)/shard_map/ppermute | solution.py:118
  198.6 5.9 %collective-permute-start.19 = (f32[1,128,512]{2,1,0:T(8,128)S(1)}, f32[1,128,512]{2,1,0:T(8,128)S(1)}, u32[]{:S(2)}, u32[]{:S(2)}) collective-permute-start(f32[1,128,512]{2,1,0:T(8,128)S(1)} %multiply_add_fusion.4), channel_id=1, source_target_pairs={{0,16},{8,24},{16,0},{24,8},{32,48},{40,56},{48,32},{56,40},{64,80... | collective-permute-start | bytes 786440 | tf_op jit(solution)/shard_map/ppermute | solution.py:118
  204.5 3.7 %collective-permute-done.19 = f32[1,128,512]{2,1,0:T(8,128)S(1)} collective-permute-done((f32[1,128,512]{2,1,0:T(8,128)S(1)}, f32[1,128,512]{2,1,0:T(8,128)S(1)}, u32[]{:S(2)}, u32[]{:S(2)}) %collective-permute-start.19) | collective-permute-done | bytes 262176 | tf_op jit(solution)/shard_map/ppermute | solution.py:118
  208.4 2.1 collective-permute-start.20
  210.5 5.5 %collective-permute-done.20 = f32[1,128,512]{2,1,0:T(8,128)S(1)} collective-permute-done((f32[1,128,512]{2,1,0:T(8,128)S(1)}, f32[1,128,512]{2,1,0:T(8,128)S(1)}, u32[]{:S(2)}, u32[]{:S(2)}) %collective-permute-start.20) | collective-permute-done | bytes 262176 | tf_op jit(solution)/shard_map/ppermute | solution.py:118
  216.1 2.5 collective-permute-start.21
  218.6 8.0 %collective-permute-done.21 = f32[1,128,512]{2,1,0:T(8,128)S(1)} collective-permute-done((f32[1,128,512]{2,1,0:T(8,128)S(1)}, f32[1,128,512]{2,1,0:T(8,128)S(1)}, u32[]{:S(2)}, u32[]{:S(2)}) %collective-permute-start.21) | collective-permute-done | bytes 262176 | tf_op jit(solution)/shard_map/ppermute | solution.py:118
  226.7 3.4 collective-permute-start.22
  230.1 4.0 %collective-permute-done.22 = f32[1,128,512]{2,1,0:T(8,128)S(1)} collective-permute-done((f32[1,128,512]{2,1,0:T(8,128)S(1)}, f32[1,128,512]{2,1,0:T(8,128)S(1)}, u32[]{:S(2)}, u32[]{:S(2)}) %collective-permute-start.22) | collective-permute-done | bytes 262176 | tf_op jit(solution)/shard_map/ppermute | solution.py:118
  234.9 2.3 collective-permute-start.23
  237.3 6.6 %collective-permute-done.23 = f32[1,128,512]{2,1,0:T(8,128)} collective-permute-done((f32[1,128,512]{2,1,0:T(8,128)}, f32[1,128,512]{2,1,0:T(8,128)}, u32[]{:S(2)}, u32[]{:S(2)}) %collective-permute-start.23) | collective-permute-done | bytes 262176 | tf_op jit(solution)/shard_map/ppermute | solution.py:118
  243.9 1.6 fusion.280
  250.5 24.1 %collective-permute-start.24 = (f32[1184,128]{1,0:T(8,128)}, f32[1184,128]{1,0:T(8,128)}, u32[]{:S(2)}, u32[]{:S(2)}) collective-permute-start(f32[1184,128]{1,0:T(8,128)} %constant_dynamic-slice_fusion.3), channel_id=1, source_target_pairs={{0,1},{1,0},{2,3},{3,2},{4,5},{5,4},{6,7},{7,6},{8,9},{9,8},{10,11... | collective-permute-start | bytes 1818632 | tf_op jit(solution)/shard_map/ppermute | solution.py:141
  275.1 1.6 collective-permute-done.24
  277.8 8.3 %collective-permute-start.25 = (f32[296,128]{1,0:T(8,128)S(1)}, f32[296,128]{1,0:T(8,128)S(1)}, u32[]{:S(2)}, u32[]{:S(2)}) collective-permute-start(f32[296,128]{1,0:T(8,128)S(1)} %get-tuple-element.31), channel_id=1, source_target_pairs={{0,2},{1,7},{2,4},{3,1},{4,6},{5,3},{6,0},{7,5},{8,10},{9,15},{10,... | collective-permute-start | bytes 454664 | tf_op jit(solution)/shard_map/ppermute | solution.py:152
  286.3 6.3 %collective-permute-done.25 = f32[296,128]{1,0:T(8,128)S(1)} collective-permute-done((f32[296,128]{1,0:T(8,128)S(1)}, f32[296,128]{1,0:T(8,128)S(1)}, u32[]{:S(2)}, u32[]{:S(2)}) %collective-permute-start.25) | collective-permute-done | bytes 151584 | tf_op jit(solution)/shard_map/ppermute | solution.py:152
  292.6 7.3 %collective-permute-start.26 = (f32[296,128]{1,0:T(8,128)S(1)}, f32[296,128]{1,0:T(8,128)S(1)}, u32[]{:S(2)}, u32[]{:S(2)}) collective-permute-start(f32[296,128]{1,0:T(8,128)S(1)} %get-tuple-element.29), channel_id=1, source_target_pairs={{0,2},{1,7},{2,4},{3,1},{4,6},{5,3},{6,0},{7,5},{8,10},{9,15},{10,... | collective-permute-start | bytes 454664 | tf_op jit(solution)/shard_map/ppermute | solution.py:152
  300.1 2.8 collective-permute-done.26
  303.0 11.4 %collective-permute-start.27 = (f32[296,128]{1,0:T(8,128)S(1)}, f32[296,128]{1,0:T(8,128)S(1)}, u32[]{:S(2)}, u32[]{:S(2)}) collective-permute-start(f32[296,128]{1,0:T(8,128)S(1)} %get-tuple-element.27), channel_id=1, source_target_pairs={{0,2},{1,7},{2,4},{3,1},{4,6},{5,3},{6,0},{7,5},{8,10},{9,15},{10,... | collective-permute-start | bytes 454664 | tf_op jit(solution)/shard_map/ppermute | solution.py:152
  314.4 5.2 %collective-permute-done.27 = f32[296,128]{1,0:T(8,128)S(1)} collective-permute-done((f32[296,128]{1,0:T(8,128)S(1)}, f32[296,128]{1,0:T(8,128)S(1)}, u32[]{:S(2)}, u32[]{:S(2)}) %collective-permute-start.27) | collective-permute-done | bytes 151584 | tf_op jit(solution)/shard_map/ppermute | solution.py:152
  319.7 7.8 %collective-permute-start.28 = (f32[296,128]{1,0:T(8,128)S(1)}, f32[296,128]{1,0:T(8,128)S(1)}, u32[]{:S(2)}, u32[]{:S(2)}) collective-permute-start(f32[296,128]{1,0:T(8,128)S(1)} %dynamic-slice_bitcast_fusion.2), channel_id=1, source_target_pairs={{0,2},{1,7},{2,4},{3,1},{4,6},{5,3},{6,0},{7,5},{8,10},{9,15},{10,... | collective-permute-start | bytes 454664 | tf_op jit(solution)/shard_map/ppermute | solution.py:158
  327.6 6.0 %collective-permute-done.28 = f32[296,128]{1,0:T(8,128)S(1)} collective-permute-done((f32[296,128]{1,0:T(8,128)S(1)}, f32[296,128]{1,0:T(8,128)S(1)}, u32[]{:S(2)}, u32[]{:S(2)}) %collective-permute-start.28) | collective-permute-done | bytes 151584 | tf_op jit(solution)/shard_map/ppermute | solution.py:158
  333.7 4.6 %collective-permute-start.29 = (f32[296,128]{1,0:T(8,128)S(1)}, f32[296,128]{1,0:T(8,128)S(1)}, u32[]{:S(2)}, u32[]{:S(2)}) collective-permute-start(f32[296,128]{1,0:T(8,128)S(1)} %dynamic-slice_bitcast_fusion.1), channel_id=1, source_target_pairs={{0,2},{1,7},{2,4},{3,1},{4,6},{5,3},{6,0},{7,5},{8,10},{9,15},{10,... | collective-permute-start | bytes 454664 | tf_op jit(solution)/shard_map/ppermute | solution.py:158
  338.4 6.9 %collective-permute-done.29 = f32[296,128]{1,0:T(8,128)S(1)} collective-permute-done((f32[296,128]{1,0:T(8,128)S(1)}, f32[296,128]{1,0:T(8,128)S(1)}, u32[]{:S(2)}, u32[]{:S(2)}) %collective-permute-start.29) | collective-permute-done | bytes 151584 | tf_op jit(solution)/shard_map/ppermute | solution.py:158
  345.4 4.5 %collective-permute-start.30 = (f32[296,128]{1,0:T(8,128)S(1)}, f32[296,128]{1,0:T(8,128)S(1)}, u32[]{:S(2)}, u32[]{:S(2)}) collective-permute-start(f32[296,128]{1,0:T(8,128)S(1)} %dynamic-slice_bitcast_fusion), channel_id=1, source_target_pairs={{0,2},{1,7},{2,4},{3,1},{4,6},{5,3},{6,0},{7,5},{8,10},{9,15},{10,... | collective-permute-start | bytes 454664 | tf_op jit(solution)/shard_map/ppermute | solution.py:158
  350.0 5.5 %collective-permute-done.30 = f32[296,128]{1,0:T(8,128)S(1)} collective-permute-done((f32[296,128]{1,0:T(8,128)S(1)}, f32[296,128]{1,0:T(8,128)S(1)}, u32[]{:S(2)}, u32[]{:S(2)}) %collective-permute-start.30) | collective-permute-done | bytes 151584 | tf_op jit(solution)/shard_map/ppermute | solution.py:158
  355.6 4.4 %collective-permute-start.31 = (f32[1184,128]{1,0:T(8,128)S(1)}, f32[1184,128]{1,0:T(8,128)S(1)}, u32[]{:S(2)}, u32[]{:S(2)}) collective-permute-start(f32[1184,128]{1,0:T(8,128)S(1)} %bitcast.579), channel_id=1, source_target_pairs={{0,1},{1,0},{2,3},{3,2},{4,5},{5,4},{6,7},{7,6},{8,9},{9,8},{10,11... | collective-permute-start | bytes 1818632 | tf_op jit(solution)/shard_map/ppermute | solution.py:161
  (289 shorter events, 36.8 us)
Async XLA Ops:
  0.6 3.6 copy-start.1
  3.8 1.1 copy-start
  6.2 8.3 %copy-start.19 = (f32[1,128]{1,0:T(1,128)S(1)}, f32[1,128]{1,0:T(1,128)}, u32[]{:S(2)}) copy-start(f32[1,128]{1,0:T(1,128)} %param.10) | copy-start | bytes 1540
  6.2 8.3 %copy-start.20 = (f32[1,128]{1,0:T(1,128)S(1)}, f32[1,128]{1,0:T(1,128)}, u32[]{:S(2)}) copy-start(f32[1,128]{1,0:T(1,128)} %param.11) | copy-start | bytes 1540
  6.6 7.9 %collective-permute-start = (f32[1,130,512]{2,1,0:T(8,128)S(1)}, f32[1,130,512]{2,1,0:T(8,128)S(1)}, u32[]{:S(2)}, u32[]{:S(2)}) collective-permute-start(f32[1,130,512]{2,1,0:T(8,128)S(1)} %pad_maximum_fusion.1), channel_id=1, source_target_pairs={{0,8},{8,0},{16,24},{24,16},{32,40},{40,32},{48,56},{56,48},{64,72... | collective-permute-start | bytes 798728 | tf_op jit(solution)/shard_map/ppermute | solution.py:97
  14.7 10.9 %collective-permute-start.1 = (f32[1,130,512]{2,1,0:T(8,128)S(1)}, f32[1,130,512]{2,1,0:T(8,128)S(1)}, u32[]{:S(2)}, u32[]{:S(2)}) collective-permute-start(f32[1,130,512]{2,1,0:T(8,128)S(1)} %pad_maximum_fusion.2), channel_id=1, source_target_pairs={{0,16},{8,24},{16,0},{24,8},{32,48},{40,56},{48,32},{56,40},{64,80... | collective-permute-start | bytes 798728 | tf_op jit(solution)/shard_map/ppermute | solution.py:97
  26.2 46.8 %copy-start.24 = (f32[128]{0:T(128)}, f32[128]{0:T(128)S(1)}, u32[]{:S(2)}) copy-start(f32[128]{0:T(128)S(1)} %get-tuple-element.36) | copy-start | bytes 1540
  26.2 46.8 %copy-start.26 = (f32[128]{0:T(128)}, f32[128]{0:T(128)S(1)}, u32[]{:S(2)}) copy-start(f32[128]{0:T(128)S(1)} %get-tuple-element.77) | copy-start | bytes 1540
  26.4 8.9 %collective-permute-start.2 = (f32[1,130,512]{2,1,0:T(8,128)S(1)}, f32[1,130,512]{2,1,0:T(8,128)S(1)}, u32[]{:S(2)}, u32[]{:S(2)}) collective-permute-start(f32[1,130,512]{2,1,0:T(8,128)S(1)} %pad_maximum_fusion.3), channel_id=1, source_target_pairs={{0,32},{8,40},{16,48},{24,56},{32,0},{40,8},{48,16},{56,24},{64,96... | collective-permute-start | bytes 798728 | tf_op jit(solution)/shard_map/ppermute | solution.py:97
  35.5 16.6 %collective-permute-start.3 = (f32[1,130,512]{2,1,0:T(8,128)S(1)}, f32[1,130,512]{2,1,0:T(8,128)S(1)}, u32[]{:S(2)}, u32[]{:S(2)}) collective-permute-start(f32[1,130,512]{2,1,0:T(8,128)S(1)} %pad_maximum_fusion.4), channel_id=1, source_target_pairs={{0,64},{8,72},{16,80},{24,88},{32,96},{40,104},{48,112},{56,120},{... | collective-permute-start | bytes 798728 | tf_op jit(solution)/shard_map/ppermute | solution.py:97
  52.8 9.4 %collective-permute-start.4 = (f32[1,130,512]{2,1,0:T(8,128)S(1)}, f32[1,130,512]{2,1,0:T(8,128)S(1)}, u32[]{:S(2)}, u32[]{:S(2)}) collective-permute-start(f32[1,130,512]{2,1,0:T(8,128)S(1)} %pad_maximum_fusion.5), channel_id=1, source_target_pairs={{0,128},{8,136},{16,144},{24,152},{32,160},{40,168},{48,176},{56,1... | collective-permute-start | bytes 798728 | tf_op jit(solution)/shard_map/ppermute | solution.py:97
  57.7 16.4 %copy-start.31 = (f32[128]{0:T(128)}, f32[128]{0:T(128)S(1)}, u32[]{:S(2)}) copy-start(f32[128]{0:T(128)S(1)} %get-tuple-element.34) | copy-start | bytes 1540
  57.7 16.4 %copy-start.33 = (f32[128]{0:T(128)}, f32[128]{0:T(128)S(1)}, u32[]{:S(2)}) copy-start(f32[128]{0:T(128)S(1)} %get-tuple-element.40) | copy-start | bytes 1540
  62.9 10.1 %collective-permute-start.5 = (f32[1,130,512]{2,1,0:T(8,128)S(1)}, f32[1,130,512]{2,1,0:T(8,128)}, u32[]{:S(2)}, u32[]{:S(2)}) collective-permute-start(f32[1,130,512]{2,1,0:T(8,128)S(1)} %pad_maximum_fusion.6), channel_id=1, source_target_pairs={{0,256},{8,264},{16,272},{24,280},{32,288},{40,296},{48,304},{56,3... | collective-permute-start | bytes 798728 | tf_op jit(solution)/shard_map/ppermute | solution.py:97
  68.3 5.9 %copy-start.35 = (f32[128]{0:T(128)}, f32[128]{0:T(128)S(1)}, u32[]{:S(2)}) copy-start(f32[128]{0:T(128)S(1)} %fusion.292) | copy-start | bytes 1540
  76.8 7.1 %collective-permute-start.6 = (f32[1,128,512]{2,1,0:T(8,128)S(1)}, f32[1,128,512]{2,1,0:T(8,128)S(1)}, u32[]{:S(2)}, u32[]{:S(2)}) collective-permute-start(f32[1,128,512]{2,1,0:T(8,128)S(1)} %fusion.118), channel_id=1, source_target_pairs={{0,8},{8,0},{16,24},{24,16},{32,40},{40,32},{48,56},{56,48},{64,72... | collective-permute-start | bytes 786440 | tf_op jit(solution)/shard_map/ppermute | solution.py:118
  84.0 8.6 %collective-permute-start.7 = (f32[1,128,512]{2,1,0:T(8,128)S(1)}, f32[1,128,512]{2,1,0:T(8,128)S(1)}, u32[]{:S(2)}, u32[]{:S(2)}) collective-permute-start(f32[1,128,512]{2,1,0:T(8,128)S(1)} %multiply_add_fusion.15), channel_id=1, source_target_pairs={{0,16},{8,24},{16,0},{24,8},{32,48},{40,56},{48,32},{56,40},{64,80... | collective-permute-start | bytes 786440 | tf_op jit(solution)/shard_map/ppermute | solution.py:118
  92.7 7.1 %collective-permute-start.8 = (f32[1,128,512]{2,1,0:T(8,128)S(1)}, f32[1,128,512]{2,1,0:T(8,128)S(1)}, u32[]{:S(2)}, u32[]{:S(2)}) collective-permute-start(f32[1,128,512]{2,1,0:T(8,128)S(1)} %multiply_add_fusion.14), channel_id=1, source_target_pairs={{0,32},{8,40},{16,48},{24,56},{32,0},{40,8},{48,16},{56,24},{64,96... | collective-permute-start | bytes 786440 | tf_op jit(solution)/shard_map/ppermute | solution.py:118
  99.9 10.8 %collective-permute-start.9 = (f32[1,128,512]{2,1,0:T(8,128)S(1)}, f32[1,128,512]{2,1,0:T(8,128)S(1)}, u32[]{:S(2)}, u32[]{:S(2)}) collective-permute-start(f32[1,128,512]{2,1,0:T(8,128)S(1)} %multiply_add_fusion.13), channel_id=1, source_target_pairs={{0,64},{8,72},{16,80},{24,88},{32,96},{40,104},{48,112},{56,120},{... | collective-permute-start | bytes 786440 | tf_op jit(solution)/shard_map/ppermute | solution.py:118
  110.9 7.2 %collective-permute-start.10 = (f32[1,128,512]{2,1,0:T(8,128)S(1)}, f32[1,128,512]{2,1,0:T(8,128)S(1)}, u32[]{:S(2)}, u32[]{:S(2)}) collective-permute-start(f32[1,128,512]{2,1,0:T(8,128)S(1)} %multiply_add_fusion.12), channel_id=1, source_target_pairs={{0,128},{8,136},{16,144},{24,152},{32,160},{40,168},{48,176},{56,1... | collective-permute-start | bytes 786440 | tf_op jit(solution)/shard_map/ppermute | solution.py:118
  118.1 5.7 %copy-start.10 = (f32[1,128,512]{2,1,0:T(8,128)}, f32[1,128,512]{2,1,0:T(8,128)S(1)}, u32[]{:S(2)}) copy-start(f32[1,128,512]{2,1,0:T(8,128)S(1)} %collective-permute-done.10) | copy-start | bytes 786436
  118.9 10.9 %collective-permute-start.11 = (f32[1,128,512]{2,1,0:T(8,128)}, f32[1,128,512]{2,1,0:T(8,128)}, u32[]{:S(2)}, u32[]{:S(2)}) collective-permute-start(f32[1,128,512]{2,1,0:T(8,128)} %multiply_add_fusion.11), channel_id=1, source_target_pairs={{0,256},{8,264},{16,272},{24,280},{32,288},{40,296},{48,304},{56,3... | collective-permute-start | bytes 786440 | tf_op jit(solution)/shard_map/ppermute | solution.py:118
  124.0 5.7 %copy-start.25 = (f32[128]{0:T(128)S(1)}, f32[128]{0:T(128)}, u32[]{:S(2)}) copy-start(f32[128]{0:T(128)} %copy-done.24) | copy-start | bytes 1540
  124.0 5.7 %copy-start.27 = (f32[128]{0:T(128)S(1)}, f32[128]{0:T(128)}, u32[]{:S(2)}) copy-start(f32[128]{0:T(128)} %copy-done.26) | copy-start | bytes 1540
  124.0 5.7 %copy-start.32 = (f32[128]{0:T(128)S(1)}, f32[128]{0:T(128)}, u32[]{:S(2)}) copy-start(f32[128]{0:T(128)} %copy-done.31) | copy-start | bytes 1540
  124.0 5.7 %copy-start.34 = (f32[128]{0:T(128)S(1)}, f32[128]{0:T(128)}, u32[]{:S(2)}) copy-start(f32[128]{0:T(128)} %copy-done.33) | copy-start | bytes 1540
  124.0 5.7 %copy-start.36 = (f32[128]{0:T(128)S(1)}, f32[128]{0:T(128)}, u32[]{:S(2)}) copy-start(f32[128]{0:T(128)} %copy-done.35) | copy-start | bytes 1540
  132.3 57.3 %copy-start.4 = (f32[1,512,128]{1,2,0:T(8,128)}, f32[1,512,128]{1,2,0:T(8,128)S(1)}, u32[]{:S(2)}) copy-start(f32[1,512,128]{1,2,0:T(8,128)S(1)} %get-tuple-element.99) | copy-start | bytes 786436
  132.3 1.0 copy-start.2
  133.7 1.0 copy-start.3
  136.4 7.1 %collective-permute-start.12 = (f32[1,128,512]{2,1,0:T(8,128)S(1)}, f32[1,128,512]{2,1,0:T(8,128)S(1)}, u32[]{:S(2)}, u32[]{:S(2)}) collective-permute-start(f32[1,128,512]{2,1,0:T(8,128)S(1)} %fusion.85), channel_id=1, source_target_pairs={{0,8},{8,0},{16,24},{24,16},{32,40},{40,32},{48,56},{56,48},{64,72... | collective-permute-start | bytes 786440 | tf_op jit(solution)/shard_map/ppermute | solution.py:118
  143.5 27.0 %copy-start.16 = (f32[128]{0:T(128)S(1)}, f32[128]{0:T(128)}, u32[]{:S(2)}) copy-start(f32[128]{0:T(128)} %get-tuple-element.47) | copy-start | bytes 1540
  143.7 9.0 %collective-permute-start.13 = (f32[1,128,512]{2,1,0:T(8,128)S(1)}, f32[1,128,512]{2,1,0:T(8,128)S(1)}, u32[]{:S(2)}, u32[]{:S(2)}) collective-permute-start(f32[1,128,512]{2,1,0:T(8,128)S(1)} %multiply_add_fusion.10), channel_id=1, source_target_pairs={{0,16},{8,24},{16,0},{24,8},{32,48},{40,56},{48,32},{56,40},{64,80... | collective-permute-start | bytes 786440 | tf_op jit(solution)/shard_map/ppermute | solution.py:118
  152.6 27.1 %copy-start.17 = (f32[128]{0:T(128)S(1)}, f32[128]{0:T(128)}, u32[]{:S(2)}) copy-start(f32[128]{0:T(128)} %get-tuple-element.42) | copy-start | bytes 1540
  152.6 27.1 %copy-start.18 = (f32[128]{0:T(128)S(1)}, f32[128]{0:T(128)}, u32[]{:S(2)}) copy-start(f32[128]{0:T(128)} %get-tuple-element.44) | copy-start | bytes 1540
  152.7 7.1 %collective-permute-start.14 = (f32[1,128,512]{2,1,0:T(8,128)S(1)}, f32[1,128,512]{2,1,0:T(8,128)S(1)}, u32[]{:S(2)}, u32[]{:S(2)}) collective-permute-start(f32[1,128,512]{2,1,0:T(8,128)S(1)} %multiply_add_fusion.9), channel_id=1, source_target_pairs={{0,32},{8,40},{16,48},{24,56},{32,0},{40,8},{48,16},{56,24},{64,96... | collective-permute-start | bytes 786440 | tf_op jit(solution)/shard_map/ppermute | solution.py:118
  159.9 28.6 %copy-start.22 = (f32[128]{0:T(128)S(1)}, f32[128]{0:T(128)}, u32[]{:S(2)}) copy-start(f32[128]{0:T(128)} %get-tuple-element.13) | copy-start | bytes 1540
  159.9 28.6 %copy-start.23 = (f32[128]{0:T(128)S(1)}, f32[128]{0:T(128)}, u32[]{:S(2)}) copy-start(f32[128]{0:T(128)} %get-tuple-element.72) | copy-start | bytes 1540
  159.9 28.6 %copy-start.28 = (f32[128]{0:T(128)S(1)}, f32[128]{0:T(128)}, u32[]{:S(2)}) copy-start(f32[128]{0:T(128)} %get-tuple-element.15) | copy-start | bytes 1540
  159.9 28.6 %copy-start.29 = (f32[128]{0:T(128)S(1)}, f32[128]{0:T(128)}, u32[]{:S(2)}) copy-start(f32[128]{0:T(128)} %get-tuple-element.41) | copy-start | bytes 1540
  159.9 28.6 %copy-start.30 = (f32[128]{0:T(128)S(1)}, f32[128]{0:T(128)}, u32[]{:S(2)}) copy-start(f32[128]{0:T(128)} %get-tuple-element.78) | copy-start | bytes 1540
  160.0 10.6 %collective-permute-start.15 = (f32[1,128,512]{2,1,0:T(8,128)S(1)}, f32[1,128,512]{2,1,0:T(8,128)S(1)}, u32[]{:S(2)}, u32[]{:S(2)}) collective-permute-start(f32[1,128,512]{2,1,0:T(8,128)S(1)} %multiply_add_fusion.8), channel_id=1, source_target_pairs={{0,64},{8,72},{16,80},{24,88},{32,96},{40,104},{48,112},{56,120},{... | collective-permute-start | bytes 786440 | tf_op jit(solution)/shard_map/ppermute | solution.py:118
  170.6 9.1 %collective-permute-start.16 = (f32[1,128,512]{2,1,0:T(8,128)S(1)}, f32[1,128,512]{2,1,0:T(8,128)S(1)}, u32[]{:S(2)}, u32[]{:S(2)}) collective-permute-start(f32[1,128,512]{2,1,0:T(8,128)S(1)} %multiply_add_fusion.7), channel_id=1, source_target_pairs={{0,128},{8,136},{16,144},{24,152},{32,160},{40,168},{48,176},{56,1... | collective-permute-start | bytes 786440 | tf_op jit(solution)/shard_map/ppermute | solution.py:118
  179.8 8.6 %collective-permute-start.17 = (f32[1,128,512]{2,1,0:T(8,128)S(1)}, f32[1,128,512]{2,1,0:T(8,128)S(1)}, u32[]{:S(2)}, u32[]{:S(2)}) collective-permute-start(f32[1,128,512]{2,1,0:T(8,128)S(1)} %multiply_add_fusion.6), channel_id=1, source_target_pairs={{0,256},{8,264},{16,272},{24,280},{32,288},{40,296},{48,304},{56,3... | collective-permute-start | bytes 786440 | tf_op jit(solution)/shard_map/ppermute | solution.py:118
  191.4 7.1 %collective-permute-start.18 = (f32[1,128,512]{2,1,0:T(8,128)S(1)}, f32[1,128,512]{2,1,0:T(8,128)S(1)}, u32[]{:S(2)}, u32[]{:S(2)}) collective-permute-start(f32[1,128,512]{2,1,0:T(8,128)S(1)} %fusion.76), channel_id=1, source_target_pairs={{0,8},{8,0},{16,24},{24,16},{32,40},{40,32},{48,56},{56,48},{64,72... | collective-permute-start | bytes 786440 | tf_op jit(solution)/shard_map/ppermute | solution.py:118
  198.5 6.0 %copy-start.11 = (f32[1,128,512]{2,1,0:T(8,128)}, f32[1,128,512]{2,1,0:T(8,128)S(1)}, u32[]{:S(2)}) copy-start(f32[1,128,512]{2,1,0:T(8,128)S(1)} %collective-permute-done.18) | copy-start | bytes 786436
  198.6 9.7 %collective-permute-start.19 = (f32[1,128,512]{2,1,0:T(8,128)S(1)}, f32[1,128,512]{2,1,0:T(8,128)S(1)}, u32[]{:S(2)}, u32[]{:S(2)}) collective-permute-start(f32[1,128,512]{2,1,0:T(8,128)S(1)} %multiply_add_fusion.4), channel_id=1, source_target_pairs={{0,16},{8,24},{16,0},{24,8},{32,48},{40,56},{48,32},{56,40},{64,80... | collective-permute-start | bytes 786440 | tf_op jit(solution)/shard_map/ppermute | solution.py:118
  208.3 2.2 copy-start.12
  208.4 35.5 %copy-start.9 = (f32[1,128,512]{2,1,0:T(8,128)S(1)}, f32[1,128,512]{2,1,0:T(8,128)}, u32[]{:S(2)}) copy-start(f32[1,128,512]{2,1,0:T(8,128)} %copy-done.8) | copy-start | bytes 786436
  208.4 7.5 %collective-permute-start.20 = (f32[1,128,512]{2,1,0:T(8,128)S(1)}, f32[1,128,512]{2,1,0:T(8,128)S(1)}, u32[]{:S(2)}, u32[]{:S(2)}) collective-permute-start(f32[1,128,512]{2,1,0:T(8,128)S(1)} %multiply_add_fusion.3), channel_id=1, source_target_pairs={{0,32},{8,40},{16,48},{24,56},{32,0},{40,8},{48,16},{56,24},{64,96... | collective-permute-start | bytes 786440 | tf_op jit(solution)/shard_map/ppermute | solution.py:118
  215.9 19.0 %copy-start.13 = (f32[1,128,512]{2,1,0:T(8,128)}, f32[1,128,512]{2,1,0:T(8,128)S(1)}, u32[]{:S(2)}) copy-start(f32[1,128,512]{2,1,0:T(8,128)S(1)} %collective-permute-done.20) | copy-start | bytes 786436
  216.1 10.6 %collective-permute-start.21 = (f32[1,128,512]{2,1,0:T(8,128)S(1)}, f32[1,128,512]{2,1,0:T(8,128)S(1)}, u32[]{:S(2)}, u32[]{:S(2)}) collective-permute-start(f32[1,128,512]{2,1,0:T(8,128)S(1)} %multiply_add_fusion.2), channel_id=1, source_target_pairs={{0,64},{8,72},{16,80},{24,88},{32,96},{40,104},{48,112},{56,120},{... | collective-permute-start | bytes 786440 | tf_op jit(solution)/shard_map/ppermute | solution.py:118
  226.6 8.3 %copy-start.14 = (f32[1,128,512]{2,1,0:T(8,128)}, f32[1,128,512]{2,1,0:T(8,128)S(1)}, u32[]{:S(2)}) copy-start(f32[1,128,512]{2,1,0:T(8,128)S(1)} %collective-permute-done.21) | copy-start | bytes 786436
  226.7 7.4 %collective-permute-start.22 = (f32[1,128,512]{2,1,0:T(8,128)S(1)}, f32[1,128,512]{2,1,0:T(8,128)S(1)}, u32[]{:S(2)}, u32[]{:S(2)}) collective-permute-start(f32[1,128,512]{2,1,0:T(8,128)S(1)} %multiply_add_fusion.1), channel_id=1, source_target_pairs={{0,128},{8,136},{16,144},{24,152},{32,160},{40,168},{48,176},{56,1... | collective-permute-start | bytes 786440 | tf_op jit(solution)/shard_map/ppermute | solution.py:118
  234.9 8.9 %collective-permute-start.23 = (f32[1,128,512]{2,1,0:T(8,128)}, f32[1,128,512]{2,1,0:T(8,128)}, u32[]{:S(2)}, u32[]{:S(2)}) collective-permute-start(f32[1,128,512]{2,1,0:T(8,128)} %multiply_add_fusion), channel_id=1, source_target_pairs={{0,256},{8,264},{16,272},{24,280},{32,288},{40,296},{48,304},{56,3... | collective-permute-start | bytes 786440 | tf_op jit(solution)/shard_map/ppermute | solution.py:118
  246.9 1.0 copy-start.7
  250.5 26.1 %collective-permute-start.24 = (f32[1184,128]{1,0:T(8,128)}, f32[1184,128]{1,0:T(8,128)}, u32[]{:S(2)}, u32[]{:S(2)}) collective-permute-start(f32[1184,128]{1,0:T(8,128)} %constant_dynamic-slice_fusion.3), channel_id=1, source_target_pairs={{0,1},{1,0},{2,3},{3,2},{4,5},{5,4},{6,7},{7,6},{8,9},{9,8},{10,11... | collective-permute-start | bytes 1818632 | tf_op jit(solution)/shard_map/ppermute | solution.py:141
  277.8 14.7 %collective-permute-start.25 = (f32[296,128]{1,0:T(8,128)S(1)}, f32[296,128]{1,0:T(8,128)S(1)}, u32[]{:S(2)}, u32[]{:S(2)}) collective-permute-start(f32[296,128]{1,0:T(8,128)S(1)} %get-tuple-element.31), channel_id=1, source_target_pairs={{0,2},{1,7},{2,4},{3,1},{4,6},{5,3},{6,0},{7,5},{8,10},{9,15},{10,... | collective-permute-start | bytes 454664 | tf_op jit(solution)/shard_map/ppermute | solution.py:152
  292.6 10.2 %collective-permute-start.26 = (f32[296,128]{1,0:T(8,128)S(1)}, f32[296,128]{1,0:T(8,128)S(1)}, u32[]{:S(2)}, u32[]{:S(2)}) collective-permute-start(f32[296,128]{1,0:T(8,128)S(1)} %get-tuple-element.29), channel_id=1, source_target_pairs={{0,2},{1,7},{2,4},{3,1},{4,6},{5,3},{6,0},{7,5},{8,10},{9,15},{10,... | collective-permute-start | bytes 454664 | tf_op jit(solution)/shard_map/ppermute | solution.py:152
  303.0 16.7 %collective-permute-start.27 = (f32[296,128]{1,0:T(8,128)S(1)}, f32[296,128]{1,0:T(8,128)S(1)}, u32[]{:S(2)}, u32[]{:S(2)}) collective-permute-start(f32[296,128]{1,0:T(8,128)S(1)} %get-tuple-element.27), channel_id=1, source_target_pairs={{0,2},{1,7},{2,4},{3,1},{4,6},{5,3},{6,0},{7,5},{8,10},{9,15},{10,... | collective-permute-start | bytes 454664 | tf_op jit(solution)/shard_map/ppermute | solution.py:152
  319.7 13.9 %collective-permute-start.28 = (f32[296,128]{1,0:T(8,128)S(1)}, f32[296,128]{1,0:T(8,128)S(1)}, u32[]{:S(2)}, u32[]{:S(2)}) collective-permute-start(f32[296,128]{1,0:T(8,128)S(1)} %dynamic-slice_bitcast_fusion.2), channel_id=1, source_target_pairs={{0,2},{1,7},{2,4},{3,1},{4,6},{5,3},{6,0},{7,5},{8,10},{9,15},{10,... | collective-permute-start | bytes 454664 | tf_op jit(solution)/shard_map/ppermute | solution.py:158
  333.7 11.7 %collective-permute-start.29 = (f32[296,128]{1,0:T(8,128)S(1)}, f32[296,128]{1,0:T(8,128)S(1)}, u32[]{:S(2)}, u32[]{:S(2)}) collective-permute-start(f32[296,128]{1,0:T(8,128)S(1)} %dynamic-slice_bitcast_fusion.1), channel_id=1, source_target_pairs={{0,2},{1,7},{2,4},{3,1},{4,6},{5,3},{6,0},{7,5},{8,10},{9,15},{10,... | collective-permute-start | bytes 454664 | tf_op jit(solution)/shard_map/ppermute | solution.py:158
  345.4 10.1 %collective-permute-start.30 = (f32[296,128]{1,0:T(8,128)S(1)}, f32[296,128]{1,0:T(8,128)S(1)}, u32[]{:S(2)}, u32[]{:S(2)}) collective-permute-start(f32[296,128]{1,0:T(8,128)S(1)} %dynamic-slice_bitcast_fusion), channel_id=1, source_target_pairs={{0,2},{1,7},{2,4},{3,1},{4,6},{5,3},{6,0},{7,5},{8,10},{9,15},{10,... | collective-permute-start | bytes 454664 | tf_op jit(solution)/shard_map/ppermute | solution.py:158
  355.6 6.1 %collective-permute-start.31 = (f32[1184,128]{1,0:T(8,128)S(1)}, f32[1184,128]{1,0:T(8,128)S(1)}, u32[]{:S(2)}, u32[]{:S(2)}) collective-permute-start(f32[1184,128]{1,0:T(8,128)S(1)} %bitcast.579), channel_id=1, source_target_pairs={{0,1},{1,0},{2,3},{3,2},{4,5},{5,4},{6,7},{7,6},{8,9},{9,8},{10,11... | collective-permute-start | bytes 1818632 | tf_op jit(solution)/shard_map/ppermute | solution.py:161
  (5 other events, 4.6 us)

commit v13 on v12

--- a/solution.py
+++ b/solution.py
@@ -80,33 +80,26 @@
     return (taken, from_other, from_own), product, block_gain * other_gain
 
 
-def butterfly_first(gain, local, axis, other_gain_row):
+def gain_butterfly(gains, axis):
     count = lax.axis_size(axis)
     me = lax.axis_index(axis)
-    channels, pixels = local.shape[1], local.shape[2]
-    total = jnp.zeros_like(local)
-    block_sum = local
-    states = [
-        [me, gain, jnp.ones_like(gain), []],
-        [count - 1 - me, other_gain_row, jnp.ones_like(other_gain_row), []],
-    ]
+    places = [me, count - 1 - me]
+    block = gains
+    products = [jnp.ones_like(gains[0]), jnp.ones_like(gains[1])]
+    factors = [[], []]
     step = 1
     while step < count:
-        rows = [jnp.pad(state[1], (0, pixels - channels))[None, None, :] for state in states]
-        packed = jnp.concatenate([block_sum] + rows, axis=1)
-        got = lax.ppermute(packed, axis, [(k, k ^ step) for k in range(count)])
-        other_sum = got[:, :channels, :]
-        for i, state in enumerate(states):
-            factor, state[2], new_gain = gain_factors(
-                state[0], step, state[1], got[0, channels + i, :channels], state[2], gain.dtype
+        got = lax.ppermute(block, axis, [(k, k ^ step) for k in range(count)])
+        rows = []
+        for i in range(2):
+            factor, products[i], new_gain = gain_factors(
+                places[i], step, block[i], got[i], products[i], gains.dtype
             )
-            state[1] = new_gain
-            state[3].append(factor)
-        taken, from_other, from_own = states[0][3][-1]
-        total = total + taken[None, :, None] * other_sum
-        block_sum = from_other[None, :, None] * other_sum + from_own[None, :, None] * block_sum
+            factors[i].append(factor)
+            rows.append(new_gain)
+        block = jnp.stack(rows)
         step *= 2
-    return total, states[0][3], states[1][3]
+    return factors[0], factors[1]
 
 
 def butterfly_again(local, factors, axis):
@@ -171,15 +164,13 @@
     flipped_list = [
         flip_weight(conv_weight[layer_index]) for layer_index in range(conv_weight.shape[0])
     ]
+    factors, back_factors = gain_butterfly(jnp.stack([gain_row, back_row]), "layer")
     c_points = initial_state
     following = initial_state
     for sweep_index in range(ITERS):
         ending = relax_block(c_points, conv_weight, conv_bias)[0]
         residual = ending - following
-        if sweep_index == 0:
-            error, factors, back_factors = butterfly_first(gain_row, residual, "layer", back_row)
-        else:
-            error = butterfly_again(residual, factors, "layer")
+        error = butterfly_again(residual, factors, "layer")
         c_points = c_points + error
         following = following + gain_row[None, :, None] * error + residual
     ending, stored = relax_block(c_points, conv_weight, conv_bias)

time: 369 us -> 377 us (1.022)
  starting transfers between devices: 162 us -> 192 us
  waiting for transfers between devices: 160 us -> 139 us
    ppermute x6 -> x5, waiting for transfers between devices: 32 us -> 3.94 us  [gain_butterfly(): got = lax.ppermute(block, axis, [(k, k ^ step) for k in range(count)])]
    ppermute x18 -> x24, starting transfers between devices: 59 us -> 84.9 us  [butterfly_again(): got = lax.ppermute(block_sum, axis, [(k, k ^ step) for k in range(count)])]
    ppermute x18 -> x24, waiting for transfers between devices: 93.5 us -> 109 us  [butterfly_again(): got = lax.ppermute(block_sum, axis, [(k, k ^ step) for k in range(count)])]
    ppermute x6 -> x5, starting transfers between devices: 30.8 us -> 20.1 us  [gain_butterfly(): got = lax.ppermute(block, axis, [(k, k ^ step) for k in range(count)])]
    ppermute x6, waiting for transfers between devices: 32.8 us -> 26.2 us  [batch_sum(): got = lax.ppermute(sent, axis, ring)]
    ppermute x1, starting transfers between devices: 24.1 us -> 30.5 us  [batch_sum(): half = keep + lax.ppermute(give, axis, partner)]
    unnamed x96, other arithmetic: 9.1 us -> 15.2 us
    ppermute x6, starting transfers between devices: 43.9 us -> 49.4 us  [batch_sum(): got = lax.ppermute(sent, axis, ring)]
  transfers between devices with their start and end apart: 32 -> 37, of which waited for: 32 -> 33; matrix products, arithmetic and copies ran while one was open for 1% -> 2% of each run, Pallas kernels for 0% -> 0%
where the time goes in v13:
time: 377 us; the launch traced here: 372 us
  starting transfers between devices  192 us (51%)
  waiting for transfers between devices  139 us (37%)
  other arithmetic  22.7 us (6%)
  local copies, waits for them, and re-layouts  9.04 us (2%)
  matrix products  6.57 us (2%)
    ppermute x24, waiting for transfers between devices, butterfly_again(): got = lax.ppermute(block_sum, axis, [(k, k ^ step) for k in range(count)])  109 us
    ppermute x24, starting transfers between devices, butterfly_again(): got = lax.ppermute(block_sum, axis, [(k, k ^ step) for k in range(count)])  84.9 us
    ppermute x6, starting transfers between devices, batch_sum(): got = lax.ppermute(sent, axis, ring)  49.4 us
    ppermute x1, starting transfers between devices, batch_sum(): half = keep + lax.ppermute(give, axis, partner)  30.5 us
    ppermute x6, waiting for transfers between devices, batch_sum(): got = lax.ppermute(sent, axis, ring)  26.2 us
    ppermute x5, starting transfers between devices, gain_butterfly(): got = lax.ppermute(block, axis, [(k, k ^ step) for k in range(count)])  20.1 us
    unnamed x96, other arithmetic  15.2 us
  transfers between devices with their start and end apart: 37, of which 33 were waited for; matrix products, arithmetic and copies ran while one was open for 2% of the time, Pallas kernels for 0%

profile of v13, /device:TPU:1, one launch (start us, length us, event | category | flops | bytes accessed | tf_op | source)
XLA Modules:
  0.0 371.9 jit_solution(1680023538845542543)
XLA Ops:
  6.5 4.0 %collective-permute-start = (f32[1,128,512]{1,2,0:T(8,128)S(1)}, f32[1,128,512]{1,2,0:T(8,128)S(1)}, u32[]{:S(2)}, u32[]{:S(2)}) collective-permute-start(f32[1,128,512]{1,2,0:T(8,128)S(1)} %fusion.151), channel_id=1, source_target_pairs={{0,8},{8,0},{16,24},{24,16},{32,40},{40,32},{48,56},{56,48},{64,72... | collective-permute-start | bytes 786440 | tf_op jit(solution)/shard_map/ppermute | solution.py:111
  10.5 1.9 collective-permute-start.1
  12.7 2.2 collective-permute-done.1
  14.8 6.3 %collective-permute-start.3 = (f32[2,128]{1,0:T(2,128)S(1)}, f32[2,128]{1,0:T(2,128)S(1)}, u32[]{:S(2)}, u32[]{:S(2)}) collective-permute-start(f32[2,128]{1,0:T(2,128)S(1)} %pad_maximum_fusion.2), channel_id=1, source_target_pairs={{0,16},{8,24},{16,0},{24,8},{32,48},{40,56},{48,32},{56,40},{64,80... | collective-permute-start | bytes 3080 | tf_op jit(solution)/shard_map/ppermute | solution.py:92
  22.1 3.8 %collective-permute-start.5 = (f32[2,128]{1,0:T(2,128)S(1)}, f32[2,128]{1,0:T(2,128)S(1)}, u32[]{:S(2)}, u32[]{:S(2)}) collective-permute-start(f32[2,128]{1,0:T(2,128)S(1)} %pad_maximum_fusion.3), channel_id=1, source_target_pairs={{0,32},{8,40},{16,48},{24,56},{32,0},{40,8},{48,16},{56,24},{64,96... | collective-permute-start | bytes 3080 | tf_op jit(solution)/shard_map/ppermute | solution.py:92
  26.8 4.9 %collective-permute-start.7 = (f32[2,128]{1,0:T(2,128)S(1)}, f32[2,128]{1,0:T(2,128)S(1)}, u32[]{:S(2)}, u32[]{:S(2)}) collective-permute-start(f32[2,128]{1,0:T(2,128)S(1)} %pad_maximum_fusion.4), channel_id=1, source_target_pairs={{0,64},{8,72},{16,80},{24,88},{32,96},{40,104},{48,112},{56,120},{... | collective-permute-start | bytes 3080 | tf_op jit(solution)/shard_map/ppermute | solution.py:92
  31.7 4.6 %collective-permute-start.2 = (f32[1,128,512]{1,2,0:T(8,128)S(1)}, f32[1,128,512]{1,2,0:T(8,128)S(1)}, u32[]{:S(2)}, u32[]{:S(2)}) collective-permute-start(f32[1,128,512]{1,2,0:T(8,128)S(1)} %multiply_add_fusion.21), channel_id=1, source_target_pairs={{0,16},{8,24},{16,0},{24,8},{32,48},{40,56},{48,32},{56,40},{64,80... | collective-permute-start | bytes 786440 | tf_op jit(solution)/shard_map/ppermute | solution.py:111
  36.4 3.2 collective-permute-start.9
  40.4 3.4 collective-permute-start.4
  43.8 3.7 collective-permute-done.4
  47.6 2.2 collective-permute-start.6
  49.8 7.5 %collective-permute-done.6 = f32[1,128,512]{1,2,0:T(8,128)S(1)} collective-permute-done((f32[1,128,512]{1,2,0:T(8,128)S(1)}, f32[1,128,512]{1,2,0:T(8,128)S(1)}, u32[]{:S(2)}, u32[]{:S(2)}) %collective-permute-start.6) | collective-permute-done | bytes 262176 | tf_op jit(solution)/shard_map/ppermute | solution.py:111
  57.4 4.3 %collective-permute-start.8 = (f32[1,128,512]{1,2,0:T(8,128)S(1)}, f32[1,128,512]{1,2,0:T(8,128)S(1)}, u32[]{:S(2)}, u32[]{:S(2)}) collective-permute-start(f32[1,128,512]{1,2,0:T(8,128)S(1)} %multiply_add_fusion.18), channel_id=1, source_target_pairs={{0,128},{8,136},{16,144},{24,152},{32,160},{40,168},{48,176},{56,1... | collective-permute-start | bytes 786440 | tf_op jit(solution)/shard_map/ppermute | solution.py:111
  61.7 4.0 %collective-permute-done.8 = f32[1,128,512]{1,2,0:T(8,128)S(1)} collective-permute-done((f32[1,128,512]{1,2,0:T(8,128)S(1)}, f32[1,128,512]{1,2,0:T(8,128)S(1)}, u32[]{:S(2)}, u32[]{:S(2)}) %collective-permute-start.8) | collective-permute-done | bytes 262176 | tf_op jit(solution)/shard_map/ppermute | solution.py:111
  65.8 5.0 %collective-permute-start.10 = (f32[1,128,512]{1,2,0:T(8,128)S(1)}, f32[1,128,512]{1,2,0:T(8,128)S(1)}, u32[]{:S(2)}, u32[]{:S(2)}) collective-permute-start(f32[1,128,512]{1,2,0:T(8,128)S(1)} %multiply_add_fusion.17), channel_id=1, source_target_pairs={{0,256},{8,264},{16,272},{24,280},{32,288},{40,296},{48,304},{56,3... | collective-permute-start | bytes 786440 | tf_op jit(solution)/shard_map/ppermute | solution.py:111
  70.8 5.1 %collective-permute-done.10 = f32[1,128,512]{1,2,0:T(8,128)S(1)} collective-permute-done((f32[1,128,512]{1,2,0:T(8,128)S(1)}, f32[1,128,512]{1,2,0:T(8,128)S(1)}, u32[]{:S(2)}, u32[]{:S(2)}) %collective-permute-start.10) | collective-permute-done | bytes 262176 | tf_op jit(solution)/shard_map/ppermute | solution.py:111
  80.0 3.1 collective-permute-start.11
  83.1 4.3 %collective-permute-done.11 = f32[1,128,512]{1,2,0:T(8,128)S(1)} collective-permute-done((f32[1,128,512]{1,2,0:T(8,128)S(1)}, f32[1,128,512]{1,2,0:T(8,128)S(1)}, u32[]{:S(2)}, u32[]{:S(2)}) %collective-permute-start.11) | collective-permute-done | bytes 262176 | tf_op jit(solution)/shard_map/ppermute | solution.py:111
  87.4 4.7 %collective-permute-start.12 = (f32[1,128,512]{1,2,0:T(8,128)S(1)}, f32[1,128,512]{1,2,0:T(8,128)S(1)}, u32[]{:S(2)}, u32[]{:S(2)}) collective-permute-start(f32[1,128,512]{1,2,0:T(8,128)S(1)} %multiply_add_fusion.15), channel_id=1, source_target_pairs={{0,16},{8,24},{16,0},{24,8},{32,48},{40,56},{48,32},{56,40},{64,80... | collective-permute-start | bytes 786440 | tf_op jit(solution)/shard_map/ppermute | solution.py:111
  92.1 4.0 %collective-permute-done.12 = f32[1,128,512]{1,2,0:T(8,128)S(1)} collective-permute-done((f32[1,128,512]{1,2,0:T(8,128)S(1)}, f32[1,128,512]{1,2,0:T(8,128)S(1)}, u32[]{:S(2)}, u32[]{:S(2)}) %collective-permute-start.12) | collective-permute-done | bytes 262176 | tf_op jit(solution)/shard_map/ppermute | solution.py:111
  96.1 1.9 collective-permute-start.13
  98.0 5.2 %collective-permute-done.13 = f32[1,128,512]{1,2,0:T(8,128)S(1)} collective-permute-done((f32[1,128,512]{1,2,0:T(8,128)S(1)}, f32[1,128,512]{1,2,0:T(8,128)S(1)}, u32[]{:S(2)}, u32[]{:S(2)}) %collective-permute-start.13) | collective-permute-done | bytes 262176 | tf_op jit(solution)/shard_map/ppermute | solution.py:111
  103.2 2.1 collective-permute-start.14
  105.3 8.5 %collective-permute-done.14 = f32[1,128,512]{1,2,0:T(8,128)S(1)} collective-permute-done((f32[1,128,512]{1,2,0:T(8,128)S(1)}, f32[1,128,512]{1,2,0:T(8,128)S(1)}, u32[]{:S(2)}, u32[]{:S(2)}) %collective-permute-start.14) | collective-permute-done | bytes 262176 | tf_op jit(solution)/shard_map/ppermute | solution.py:111
  113.8 2.7 collective-permute-start.15
  116.5 4.6 %collective-permute-done.15 = f32[1,128,512]{1,2,0:T(8,128)S(1)} collective-permute-done((f32[1,128,512]{1,2,0:T(8,128)S(1)}, f32[1,128,512]{1,2,0:T(8,128)S(1)}, u32[]{:S(2)}, u32[]{:S(2)}) %collective-permute-start.15) | collective-permute-done | bytes 262176 | tf_op jit(solution)/shard_map/ppermute | solution.py:111
  121.8 6.0 %collective-permute-start.16 = (f32[1,128,512]{1,2,0:T(8,128)}, f32[1,128,512]{1,2,0:T(8,128)}, u32[]{:S(2)}, u32[]{:S(2)}) collective-permute-start(f32[1,128,512]{1,2,0:T(8,128)} %multiply_add_fusion.11), channel_id=1, source_target_pairs={{0,256},{8,264},{16,272},{24,280},{32,288},{40,296},{48,304},{56,3... | collective-permute-start | bytes 786440 | tf_op jit(solution)/shard_map/ppermute | solution.py:111
  140.8 3.3 collective-permute-start.17
  144.1 4.2 %collective-permute-done.17 = f32[1,128,512]{1,2,0:T(8,128)S(1)} collective-permute-done((f32[1,128,512]{1,2,0:T(8,128)S(1)}, f32[1,128,512]{1,2,0:T(8,128)S(1)}, u32[]{:S(2)}, u32[]{:S(2)}) %collective-permute-start.17) | collective-permute-done | bytes 262176 | tf_op jit(solution)/shard_map/ppermute | solution.py:111
  148.3 5.3 %collective-permute-start.18 = (f32[1,128,512]{1,2,0:T(8,128)S(1)}, f32[1,128,512]{1,2,0:T(8,128)S(1)}, u32[]{:S(2)}, u32[]{:S(2)}) collective-permute-start(f32[1,128,512]{1,2,0:T(8,128)S(1)} %multiply_add_fusion.10), channel_id=1, source_target_pairs={{0,16},{8,24},{16,0},{24,8},{32,48},{40,56},{48,32},{56,40},{64,80... | collective-permute-start | bytes 786440 | tf_op jit(solution)/shard_map/ppermute | solution.py:111
  153.7 3.7 %collective-permute-done.18 = f32[1,128,512]{1,2,0:T(8,128)S(1)} collective-permute-done((f32[1,128,512]{1,2,0:T(8,128)S(1)}, f32[1,128,512]{1,2,0:T(8,128)S(1)}, u32[]{:S(2)}, u32[]{:S(2)}) %collective-permute-start.18) | collective-permute-done | bytes 262176 | tf_op jit(solution)/shard_map/ppermute | solution.py:111
  159.4 5.5 %collective-permute-done.19 = f32[1,128,512]{1,2,0:T(8,128)S(1)} collective-permute-done((f32[1,128,512]{1,2,0:T(8,128)S(1)}, f32[1,128,512]{1,2,0:T(8,128)S(1)}, u32[]{:S(2)}, u32[]{:S(2)}) %collective-permute-start.19) | collective-permute-done | bytes 262176 | tf_op jit(solution)/shard_map/ppermute | solution.py:111
  164.9 2.6 collective-permute-start.20
  167.5 8.2 %collective-permute-done.20 = f32[1,128,512]{1,2,0:T(8,128)S(1)} collective-permute-done((f32[1,128,512]{1,2,0:T(8,128)S(1)}, f32[1,128,512]{1,2,0:T(8,128)S(1)}, u32[]{:S(2)}, u32[]{:S(2)}) %collective-permute-start.20) | collective-permute-done | bytes 262176 | tf_op jit(solution)/shard_map/ppermute | solution.py:111
  175.7 2.8 collective-permute-start.21
  178.5 4.6 %collective-permute-done.21 = f32[1,128,512]{1,2,0:T(8,128)S(1)} collective-permute-done((f32[1,128,512]{1,2,0:T(8,128)S(1)}, f32[1,128,512]{1,2,0:T(8,128)S(1)}, u32[]{:S(2)}, u32[]{:S(2)}) %collective-permute-start.21) | collective-permute-done | bytes 262176 | tf_op jit(solution)/shard_map/ppermute | solution.py:111
  183.1 4.8 %collective-permute-start.22 = (f32[1,128,512]{1,2,0:T(8,128)S(1)}, f32[1,128,512]{1,2,0:T(8,128)S(1)}, u32[]{:S(2)}, u32[]{:S(2)}) collective-permute-start(f32[1,128,512]{1,2,0:T(8,128)S(1)} %multiply_add_fusion.6), channel_id=1, source_target_pairs={{0,256},{8,264},{16,272},{24,280},{32,288},{40,296},{48,304},{56,3... | collective-permute-start | bytes 786440 | tf_op jit(solution)/shard_map/ppermute | solution.py:111
  188.0 3.8 %collective-permute-done.22 = f32[1,128,512]{1,2,0:T(8,128)S(1)} collective-permute-done((f32[1,128,512]{1,2,0:T(8,128)S(1)}, f32[1,128,512]{1,2,0:T(8,128)S(1)}, u32[]{:S(2)}, u32[]{:S(2)}) %collective-permute-start.22) | collective-permute-done | bytes 262176 | tf_op jit(solution)/shard_map/ppermute | solution.py:111
  195.9 2.9 collective-permute-start.23
  198.8 4.5 %collective-permute-done.23 = f32[1,128,512]{1,2,0:T(8,128)S(1)} collective-permute-done((f32[1,128,512]{1,2,0:T(8,128)S(1)}, f32[1,128,512]{1,2,0:T(8,128)S(1)}, u32[]{:S(2)}, u32[]{:S(2)}) %collective-permute-start.23) | collective-permute-done | bytes 262176 | tf_op jit(solution)/shard_map/ppermute | solution.py:111
  203.3 4.9 %collective-permute-start.24 = (f32[1,128,512]{1,2,0:T(8,128)S(1)}, f32[1,128,512]{1,2,0:T(8,128)S(1)}, u32[]{:S(2)}, u32[]{:S(2)}) collective-permute-start(f32[1,128,512]{1,2,0:T(8,128)S(1)} %multiply_add_fusion.4), channel_id=1, source_target_pairs={{0,16},{8,24},{16,0},{24,8},{32,48},{40,56},{48,32},{56,40},{64,80... | collective-permute-start | bytes 786440 | tf_op jit(solution)/shard_map/ppermute | solution.py:111
  208.2 4.0 %collective-permute-done.24 = f32[1,128,512]{1,2,0:T(8,128)S(1)} collective-permute-done((f32[1,128,512]{1,2,0:T(8,128)S(1)}, f32[1,128,512]{1,2,0:T(8,128)S(1)}, u32[]{:S(2)}, u32[]{:S(2)}) %collective-permute-start.24) | collective-permute-done | bytes 262176 | tf_op jit(solution)/shard_map/ppermute | solution.py:111
  212.3 2.1 collective-permute-start.25
  214.4 5.2 %collective-permute-done.25 = f32[1,128,512]{1,2,0:T(8,128)S(1)} collective-permute-done((f32[1,128,512]{1,2,0:T(8,128)S(1)}, f32[1,128,512]{1,2,0:T(8,128)S(1)}, u32[]{:S(2)}, u32[]{:S(2)}) %collective-permute-start.25) | collective-permute-done | bytes 262176 | tf_op jit(solution)/shard_map/ppermute | solution.py:111
  219.6 2.5 collective-permute-start.26
  222.1 8.1 %collective-permute-done.26 = f32[1,128,512]{1,2,0:T(8,128)S(1)} collective-permute-done((f32[1,128,512]{1,2,0:T(8,128)S(1)}, f32[1,128,512]{1,2,0:T(8,128)S(1)}, u32[]{:S(2)}, u32[]{:S(2)}) %collective-permute-start.26) | collective-permute-done | bytes 262176 | tf_op jit(solution)/shard_map/ppermute | solution.py:111
  230.2 2.8 collective-permute-start.27
  233.0 4.3 %collective-permute-done.27 = f32[1,128,512]{1,2,0:T(8,128)S(1)} collective-permute-done((f32[1,128,512]{1,2,0:T(8,128)S(1)}, f32[1,128,512]{1,2,0:T(8,128)S(1)}, u32[]{:S(2)}, u32[]{:S(2)}) %collective-permute-start.27) | collective-permute-done | bytes 262176 | tf_op jit(solution)/shard_map/ppermute | solution.py:111
  238.1 5.1 %collective-permute-start.28 = (f32[1,128,512]{1,2,0:T(8,128)}, f32[1,128,512]{1,2,0:T(8,128)}, u32[]{:S(2)}, u32[]{:S(2)}) collective-permute-start(f32[1,128,512]{1,2,0:T(8,128)} %multiply_add_fusion), channel_id=1, source_target_pairs={{0,256},{8,264},{16,272},{24,280},{32,288},{40,296},{48,304},{56,3... | collective-permute-start | bytes 786440 | tf_op jit(solution)/shard_map/ppermute | solution.py:111
  243.2 3.8 %collective-permute-done.28 = f32[1,128,512]{1,2,0:T(8,128)} collective-permute-done((f32[1,128,512]{1,2,0:T(8,128)}, f32[1,128,512]{1,2,0:T(8,128)}, u32[]{:S(2)}, u32[]{:S(2)}) %collective-permute-start.28) | collective-permute-done | bytes 262176 | tf_op jit(solution)/shard_map/ppermute | solution.py:111
  252.3 30.5 %collective-permute-start.29 = (f32[1184,128]{1,0:T(8,128)S(1)}, f32[1184,128]{1,0:T(8,128)S(1)}, u32[]{:S(2)}, u32[]{:S(2)}) collective-permute-start(f32[1184,128]{1,0:T(8,128)S(1)} %constant_dynamic-slice_fusion.3), channel_id=1, source_target_pairs={{0,1},{1,0},{2,3},{3,2},{4,5},{5,4},{6,7},{7,6},{8,9},{9,8},{10,11... | collective-permute-start | bytes 1818632 | tf_op jit(solution)/shard_map/ppermute | solution.py:134
  284.5 10.6 %collective-permute-start.30 = (f32[296,128]{1,0:T(8,128)S(1)}, f32[296,128]{1,0:T(8,128)S(1)}, u32[]{:S(2)}, u32[]{:S(2)}) collective-permute-start(f32[296,128]{1,0:T(8,128)S(1)} %get-tuple-element.49), channel_id=1, source_target_pairs={{0,2},{1,7},{2,4},{3,1},{4,6},{5,3},{6,0},{7,5},{8,10},{9,15},{10,... | collective-permute-start | bytes 454664 | tf_op jit(solution)/shard_map/ppermute | solution.py:145
  295.3 3.7 collective-permute-done.30
  299.1 9.7 %collective-permute-start.31 = (f32[296,128]{1,0:T(8,128)S(1)}, f32[296,128]{1,0:T(8,128)S(1)}, u32[]{:S(2)}, u32[]{:S(2)}) collective-permute-start(f32[296,128]{1,0:T(8,128)S(1)} %get-tuple-element.47), channel_id=1, source_target_pairs={{0,2},{1,7},{2,4},{3,1},{4,6},{5,3},{6,0},{7,5},{8,10},{9,15},{10,... | collective-permute-start | bytes 454664 | tf_op jit(solution)/shard_map/ppermute | solution.py:145
  309.0 6.1 %collective-permute-done.31 = f32[296,128]{1,0:T(8,128)S(1)} collective-permute-done((f32[296,128]{1,0:T(8,128)S(1)}, f32[296,128]{1,0:T(8,128)S(1)}, u32[]{:S(2)}, u32[]{:S(2)}) %collective-permute-start.31) | collective-permute-done | bytes 151584 | tf_op jit(solution)/shard_map/ppermute | solution.py:145
  315.2 8.0 %collective-permute-start.32 = (f32[296,128]{1,0:T(8,128)S(1)}, f32[296,128]{1,0:T(8,128)S(1)}, u32[]{:S(2)}, u32[]{:S(2)}) collective-permute-start(f32[296,128]{1,0:T(8,128)S(1)} %get-tuple-element.45), channel_id=1, source_target_pairs={{0,2},{1,7},{2,4},{3,1},{4,6},{5,3},{6,0},{7,5},{8,10},{9,15},{10,... | collective-permute-start | bytes 454664 | tf_op jit(solution)/shard_map/ppermute | solution.py:145
  323.4 6.0 %collective-permute-done.32 = f32[296,128]{1,0:T(8,128)S(1)} collective-permute-done((f32[296,128]{1,0:T(8,128)S(1)}, f32[296,128]{1,0:T(8,128)S(1)}, u32[]{:S(2)}, u32[]{:S(2)}) %collective-permute-start.32) | collective-permute-done | bytes 151584 | tf_op jit(solution)/shard_map/ppermute | solution.py:145
  329.4 7.2 %collective-permute-start.33 = (f32[296,128]{1,0:T(8,128)S(1)}, f32[296,128]{1,0:T(8,128)S(1)}, u32[]{:S(2)}, u32[]{:S(2)}) collective-permute-start(f32[296,128]{1,0:T(8,128)S(1)} %dynamic-slice_bitcast_fusion.2), channel_id=1, source_target_pairs={{0,2},{1,7},{2,4},{3,1},{4,6},{5,3},{6,0},{7,5},{8,10},{9,15},{10,... | collective-permute-start | bytes 454664 | tf_op jit(solution)/shard_map/ppermute | solution.py:151
  336.7 4.3 %collective-permute-done.33 = f32[296,128]{1,0:T(8,128)S(1)} collective-permute-done((f32[296,128]{1,0:T(8,128)S(1)}, f32[296,128]{1,0:T(8,128)S(1)}, u32[]{:S(2)}, u32[]{:S(2)}) %collective-permute-start.33) | collective-permute-done | bytes 151584 | tf_op jit(solution)/shard_map/ppermute | solution.py:151
  341.1 7.0 %collective-permute-start.34 = (f32[296,128]{1,0:T(8,128)S(1)}, f32[296,128]{1,0:T(8,128)S(1)}, u32[]{:S(2)}, u32[]{:S(2)}) collective-permute-start(f32[296,128]{1,0:T(8,128)S(1)} %dynamic-slice_bitcast_fusion.1), channel_id=1, source_target_pairs={{0,2},{1,7},{2,4},{3,1},{4,6},{5,3},{6,0},{7,5},{8,10},{9,15},{10,... | collective-permute-start | bytes 454664 | tf_op jit(solution)/shard_map/ppermute | solution.py:151
  348.3 3.0 collective-permute-done.34
  351.3 6.8 %collective-permute-start.35 = (f32[296,128]{1,0:T(8,128)S(1)}, f32[296,128]{1,0:T(8,128)S(1)}, u32[]{:S(2)}, u32[]{:S(2)}) collective-permute-start(f32[296,128]{1,0:T(8,128)S(1)} %dynamic-slice_bitcast_fusion), channel_id=1, source_target_pairs={{0,2},{1,7},{2,4},{3,1},{4,6},{5,3},{6,0},{7,5},{8,10},{9,15},{10,... | collective-permute-start | bytes 454664 | tf_op jit(solution)/shard_map/ppermute | solution.py:151
  358.4 3.1 collective-permute-done.35
  361.4 6.8 %collective-permute-start.36 = (f32[1184,128]{1,0:T(8,128)S(1)}, f32[1184,128]{1,0:T(8,128)S(1)}, u32[]{:S(2)}, u32[]{:S(2)}) collective-permute-start(f32[1184,128]{1,0:T(8,128)S(1)} %bitcast.545), channel_id=1, source_target_pairs={{0,1},{1,0},{2,3},{3,2},{4,5},{5,4},{6,7},{7,6},{8,9},{9,8},{10,11... | collective-permute-start | bytes 1818632 | tf_op jit(solution)/shard_map/ppermute | solution.py:154
  (258 shorter events, 44.4 us)
Async XLA Ops:
  2.7 1.4 copy-start
  6.0 4.5 %copy-start.15 = (f32[1,128]{1,0:T(1,128)S(1)}, f32[1,128]{1,0:T(1,128)}, u32[]{:S(2)}) copy-start(f32[1,128]{1,0:T(1,128)} %param.10) | copy-start | bytes 1540
  6.0 4.5 %copy-start.16 = (f32[1,128]{1,0:T(1,128)S(1)}, f32[1,128]{1,0:T(1,128)}, u32[]{:S(2)}) copy-start(f32[1,128]{1,0:T(1,128)} %param.11) | copy-start | bytes 1540
  6.5 25.2 %collective-permute-start = (f32[1,128,512]{1,2,0:T(8,128)S(1)}, f32[1,128,512]{1,2,0:T(8,128)S(1)}, u32[]{:S(2)}, u32[]{:S(2)}) collective-permute-start(f32[1,128,512]{1,2,0:T(8,128)S(1)} %fusion.151), channel_id=1, source_target_pairs={{0,8},{8,0},{16,24},{24,16},{32,40},{40,32},{48,56},{56,48},{64,72... | collective-permute-start | bytes 786440 | tf_op jit(solution)/shard_map/ppermute | solution.py:111
  10.5 4.3 %collective-permute-start.1 = (f32[2,128]{1,0:T(2,128)S(1)}, f32[2,128]{1,0:T(2,128)S(1)}, u32[]{:S(2)}, u32[]{:S(2)}) collective-permute-start(f32[2,128]{1,0:T(2,128)S(1)} %pad_maximum_fusion.1), channel_id=1, source_target_pairs={{0,8},{8,0},{16,24},{24,16},{32,40},{40,32},{48,56},{56,48},{64,72... | collective-permute-start | bytes 3080 | tf_op jit(solution)/shard_map/ppermute | solution.py:92
  14.8 7.2 %collective-permute-start.3 = (f32[2,128]{1,0:T(2,128)S(1)}, f32[2,128]{1,0:T(2,128)S(1)}, u32[]{:S(2)}, u32[]{:S(2)}) collective-permute-start(f32[2,128]{1,0:T(2,128)S(1)} %pad_maximum_fusion.2), channel_id=1, source_target_pairs={{0,16},{8,24},{16,0},{24,8},{32,48},{40,56},{48,32},{56,40},{64,80... | collective-permute-start | bytes 3080 | tf_op jit(solution)/shard_map/ppermute | solution.py:92
  22.1 4.7 %collective-permute-start.5 = (f32[2,128]{1,0:T(2,128)S(1)}, f32[2,128]{1,0:T(2,128)S(1)}, u32[]{:S(2)}, u32[]{:S(2)}) collective-permute-start(f32[2,128]{1,0:T(2,128)S(1)} %pad_maximum_fusion.3), channel_id=1, source_target_pairs={{0,32},{8,40},{16,48},{24,56},{32,0},{40,8},{48,16},{56,24},{64,96... | collective-permute-start | bytes 3080 | tf_op jit(solution)/shard_map/ppermute | solution.py:92
  26.8 9.6 %collective-permute-start.7 = (f32[2,128]{1,0:T(2,128)S(1)}, f32[2,128]{1,0:T(2,128)S(1)}, u32[]{:S(2)}, u32[]{:S(2)}) collective-permute-start(f32[2,128]{1,0:T(2,128)S(1)} %pad_maximum_fusion.4), channel_id=1, source_target_pairs={{0,64},{8,72},{16,80},{24,88},{32,96},{40,104},{48,112},{56,120},{... | collective-permute-start | bytes 3080 | tf_op jit(solution)/shard_map/ppermute | solution.py:92
  31.7 8.6 %collective-permute-start.2 = (f32[1,128,512]{1,2,0:T(8,128)S(1)}, f32[1,128,512]{1,2,0:T(8,128)S(1)}, u32[]{:S(2)}, u32[]{:S(2)}) collective-permute-start(f32[1,128,512]{1,2,0:T(8,128)S(1)} %multiply_add_fusion.21), channel_id=1, source_target_pairs={{0,16},{8,24},{16,0},{24,8},{32,48},{40,56},{48,32},{56,40},{64,80... | collective-permute-start | bytes 786440 | tf_op jit(solution)/shard_map/ppermute | solution.py:111
  36.4 7.3 %collective-permute-start.9 = (f32[2,128]{1,0:T(2,128)S(1)}, f32[2,128]{1,0:T(2,128)S(1)}, u32[]{:S(2)}, u32[]{:S(2)}) collective-permute-start(f32[2,128]{1,0:T(2,128)S(1)} %pad_maximum_fusion.5), channel_id=1, source_target_pairs={{0,128},{8,136},{16,144},{24,152},{32,160},{40,168},{48,176},{56,1... | collective-permute-start | bytes 3080 | tf_op jit(solution)/shard_map/ppermute | solution.py:92
  40.4 7.1 %collective-permute-start.4 = (f32[1,128,512]{1,2,0:T(8,128)S(1)}, f32[1,128,512]{1,2,0:T(8,128)S(1)}, u32[]{:S(2)}, u32[]{:S(2)}) collective-permute-start(f32[1,128,512]{1,2,0:T(8,128)S(1)} %multiply_add_fusion.20), channel_id=1, source_target_pairs={{0,32},{8,40},{16,48},{24,56},{32,0},{40,8},{48,16},{56,24},{64,96... | collective-permute-start | bytes 786440 | tf_op jit(solution)/shard_map/ppermute | solution.py:111
  47.6 9.8 %collective-permute-start.6 = (f32[1,128,512]{1,2,0:T(8,128)S(1)}, f32[1,128,512]{1,2,0:T(8,128)S(1)}, u32[]{:S(2)}, u32[]{:S(2)}) collective-permute-start(f32[1,128,512]{1,2,0:T(8,128)S(1)} %multiply_add_fusion.19), channel_id=1, source_target_pairs={{0,64},{8,72},{16,80},{24,88},{32,96},{40,104},{48,112},{56,120},{... | collective-permute-start | bytes 786440 | tf_op jit(solution)/shard_map/ppermute | solution.py:111
  57.4 8.4 %collective-permute-start.8 = (f32[1,128,512]{1,2,0:T(8,128)S(1)}, f32[1,128,512]{1,2,0:T(8,128)S(1)}, u32[]{:S(2)}, u32[]{:S(2)}) collective-permute-start(f32[1,128,512]{1,2,0:T(8,128)S(1)} %multiply_add_fusion.18), channel_id=1, source_target_pairs={{0,128},{8,136},{16,144},{24,152},{32,160},{40,168},{48,176},{56,1... | collective-permute-start | bytes 786440 | tf_op jit(solution)/shard_map/ppermute | solution.py:111
  65.8 10.1 %collective-permute-start.10 = (f32[1,128,512]{1,2,0:T(8,128)S(1)}, f32[1,128,512]{1,2,0:T(8,128)S(1)}, u32[]{:S(2)}, u32[]{:S(2)}) collective-permute-start(f32[1,128,512]{1,2,0:T(8,128)S(1)} %multiply_add_fusion.17), channel_id=1, source_target_pairs={{0,256},{8,264},{16,272},{24,280},{32,288},{40,296},{48,304},{56,3... | collective-permute-start | bytes 786440 | tf_op jit(solution)/shard_map/ppermute | solution.py:111
  80.0 7.4 %collective-permute-start.11 = (f32[1,128,512]{1,2,0:T(8,128)S(1)}, f32[1,128,512]{1,2,0:T(8,128)S(1)}, u32[]{:S(2)}, u32[]{:S(2)}) collective-permute-start(f32[1,128,512]{1,2,0:T(8,128)S(1)} %fusion.118), channel_id=1, source_target_pairs={{0,8},{8,0},{16,24},{24,16},{32,40},{40,32},{48,56},{56,48},{64,72... | collective-permute-start | bytes 786440 | tf_op jit(solution)/shard_map/ppermute | solution.py:111
  87.4 8.6 %collective-permute-start.12 = (f32[1,128,512]{1,2,0:T(8,128)S(1)}, f32[1,128,512]{1,2,0:T(8,128)S(1)}, u32[]{:S(2)}, u32[]{:S(2)}) collective-permute-start(f32[1,128,512]{1,2,0:T(8,128)S(1)} %multiply_add_fusion.15), channel_id=1, source_target_pairs={{0,16},{8,24},{16,0},{24,8},{32,48},{40,56},{48,32},{56,40},{64,80... | collective-permute-start | bytes 786440 | tf_op jit(solution)/shard_map/ppermute | solution.py:111
  96.1 7.1 %collective-permute-start.13 = (f32[1,128,512]{1,2,0:T(8,128)S(1)}, f32[1,128,512]{1,2,0:T(8,128)S(1)}, u32[]{:S(2)}, u32[]{:S(2)}) collective-permute-start(f32[1,128,512]{1,2,0:T(8,128)S(1)} %multiply_add_fusion.14), channel_id=1, source_target_pairs={{0,32},{8,40},{16,48},{24,56},{32,0},{40,8},{48,16},{56,24},{64,96... | collective-permute-start | bytes 786440 | tf_op jit(solution)/shard_map/ppermute | solution.py:111
  103.2 10.6 %collective-permute-start.14 = (f32[1,128,512]{1,2,0:T(8,128)S(1)}, f32[1,128,512]{1,2,0:T(8,128)S(1)}, u32[]{:S(2)}, u32[]{:S(2)}) collective-permute-start(f32[1,128,512]{1,2,0:T(8,128)S(1)} %multiply_add_fusion.13), channel_id=1, source_target_pairs={{0,64},{8,72},{16,80},{24,88},{32,96},{40,104},{48,112},{56,120},{... | collective-permute-start | bytes 786440 | tf_op jit(solution)/shard_map/ppermute | solution.py:111
  113.8 14.1 %copy-start.14 = (f32[1,128,512]{2,1,0:T(8,128)S(1)}, f32[1,128,512]{2,1,0:T(8,128)}, u32[]{:S(2)}) copy-start(f32[1,128,512]{2,1,0:T(8,128)} %param.7) | copy-start | bytes 786436
  113.8 7.2 %collective-permute-start.15 = (f32[1,128,512]{1,2,0:T(8,128)S(1)}, f32[1,128,512]{1,2,0:T(8,128)S(1)}, u32[]{:S(2)}, u32[]{:S(2)}) collective-permute-start(f32[1,128,512]{1,2,0:T(8,128)S(1)} %multiply_add_fusion.12), channel_id=1, source_target_pairs={{0,128},{8,136},{16,144},{24,152},{32,160},{40,168},{48,176},{56,1... | collective-permute-start | bytes 786440 | tf_op jit(solution)/shard_map/ppermute | solution.py:111
  121.8 9.9 %collective-permute-start.16 = (f32[1,128,512]{1,2,0:T(8,128)}, f32[1,128,512]{1,2,0:T(8,128)}, u32[]{:S(2)}, u32[]{:S(2)}) collective-permute-start(f32[1,128,512]{1,2,0:T(8,128)} %multiply_add_fusion.11), channel_id=1, source_target_pairs={{0,256},{8,264},{16,272},{24,280},{32,288},{40,296},{48,304},{56,3... | collective-permute-start | bytes 786440 | tf_op jit(solution)/shard_map/ppermute | solution.py:111
  132.8 1.5 copy-start.6
  134.8 58.6 %copy-start.4 = (f32[1,512,128]{2,1,0:T(8,128)}, f32[1,512,128]{2,1,0:T(8,128)S(1)}, u32[]{:S(2)}) copy-start(f32[1,512,128]{2,1,0:T(8,128)S(1)} %get-tuple-element.104) | copy-start | bytes 786436
  136.8 1.5 copy-start.3
  138.8 1.5 copy-start.1
  140.8 7.5 %collective-permute-start.17 = (f32[1,128,512]{1,2,0:T(8,128)S(1)}, f32[1,128,512]{1,2,0:T(8,128)S(1)}, u32[]{:S(2)}, u32[]{:S(2)}) collective-permute-start(f32[1,128,512]{1,2,0:T(8,128)S(1)} %fusion.85), channel_id=1, source_target_pairs={{0,8},{8,0},{16,24},{24,16},{32,40},{40,32},{48,56},{56,48},{64,72... | collective-permute-start | bytes 786440 | tf_op jit(solution)/shard_map/ppermute | solution.py:111
  148.3 9.1 %collective-permute-start.18 = (f32[1,128,512]{1,2,0:T(8,128)S(1)}, f32[1,128,512]{1,2,0:T(8,128)S(1)}, u32[]{:S(2)}, u32[]{:S(2)}) collective-permute-start(f32[1,128,512]{1,2,0:T(8,128)S(1)} %multiply_add_fusion.10), channel_id=1, source_target_pairs={{0,16},{8,24},{16,0},{24,8},{32,48},{40,56},{48,32},{56,40},{64,80... | collective-permute-start | bytes 786440 | tf_op jit(solution)/shard_map/ppermute | solution.py:111
  157.4 7.4 %collective-permute-start.19 = (f32[1,128,512]{1,2,0:T(8,128)S(1)}, f32[1,128,512]{1,2,0:T(8,128)S(1)}, u32[]{:S(2)}, u32[]{:S(2)}) collective-permute-start(f32[1,128,512]{1,2,0:T(8,128)S(1)} %multiply_add_fusion.9), channel_id=1, source_target_pairs={{0,32},{8,40},{16,48},{24,56},{32,0},{40,8},{48,16},{56,24},{64,96... | collective-permute-start | bytes 786440 | tf_op jit(solution)/shard_map/ppermute | solution.py:111
  164.9 10.8 %collective-permute-start.20 = (f32[1,128,512]{1,2,0:T(8,128)S(1)}, f32[1,128,512]{1,2,0:T(8,128)S(1)}, u32[]{:S(2)}, u32[]{:S(2)}) collective-permute-start(f32[1,128,512]{1,2,0:T(8,128)S(1)} %multiply_add_fusion.8), channel_id=1, source_target_pairs={{0,64},{8,72},{16,80},{24,88},{32,96},{40,104},{48,112},{56,120},{... | collective-permute-start | bytes 786440 | tf_op jit(solution)/shard_map/ppermute | solution.py:111
  175.7 7.4 %collective-permute-start.21 = (f32[1,128,512]{1,2,0:T(8,128)S(1)}, f32[1,128,512]{1,2,0:T(8,128)S(1)}, u32[]{:S(2)}, u32[]{:S(2)}) collective-permute-start(f32[1,128,512]{1,2,0:T(8,128)S(1)} %multiply_add_fusion.7), channel_id=1, source_target_pairs={{0,128},{8,136},{16,144},{24,152},{32,160},{40,168},{48,176},{56,1... | collective-permute-start | bytes 786440 | tf_op jit(solution)/shard_map/ppermute | solution.py:111
  183.1 8.6 %collective-permute-start.22 = (f32[1,128,512]{1,2,0:T(8,128)S(1)}, f32[1,128,512]{1,2,0:T(8,128)S(1)}, u32[]{:S(2)}, u32[]{:S(2)}) collective-permute-start(f32[1,128,512]{1,2,0:T(8,128)S(1)} %multiply_add_fusion.6), channel_id=1, source_target_pairs={{0,256},{8,264},{16,272},{24,280},{32,288},{40,296},{48,304},{56,3... | collective-permute-start | bytes 786440 | tf_op jit(solution)/shard_map/ppermute | solution.py:111
  191.9 1.5 copy-start.8
  195.9 7.4 %collective-permute-start.23 = (f32[1,128,512]{1,2,0:T(8,128)S(1)}, f32[1,128,512]{1,2,0:T(8,128)S(1)}, u32[]{:S(2)}, u32[]{:S(2)}) collective-permute-start(f32[1,128,512]{1,2,0:T(8,128)S(1)} %fusion.76), channel_id=1, source_target_pairs={{0,8},{8,0},{16,24},{24,16},{32,40},{40,32},{48,56},{56,48},{64,72... | collective-permute-start | bytes 786440 | tf_op jit(solution)/shard_map/ppermute | solution.py:111
  203.3 8.9 %collective-permute-start.24 = (f32[1,128,512]{1,2,0:T(8,128)S(1)}, f32[1,128,512]{1,2,0:T(8,128)S(1)}, u32[]{:S(2)}, u32[]{:S(2)}) collective-permute-start(f32[1,128,512]{1,2,0:T(8,128)S(1)} %multiply_add_fusion.4), channel_id=1, source_target_pairs={{0,16},{8,24},{16,0},{24,8},{32,48},{40,56},{48,32},{56,40},{64,80... | collective-permute-start | bytes 786440 | tf_op jit(solution)/shard_map/ppermute | solution.py:111
  212.3 2.1 copy-start.10
  212.3 34.8 %copy-start.9 = (f32[1,128,512]{1,2,0:T(8,128)S(1)}, f32[1,128,512]{1,2,0:T(8,128)}, u32[]{:S(2)}) copy-start(f32[1,128,512]{1,2,0:T(8,128)} %copy-done.8) | copy-start | bytes 786436
  212.3 7.2 %collective-permute-start.25 = (f32[1,128,512]{1,2,0:T(8,128)S(1)}, f32[1,128,512]{1,2,0:T(8,128)S(1)}, u32[]{:S(2)}, u32[]{:S(2)}) collective-permute-start(f32[1,128,512]{1,2,0:T(8,128)S(1)} %multiply_add_fusion.3), channel_id=1, source_target_pairs={{0,32},{8,40},{16,48},{24,56},{32,0},{40,8},{48,16},{56,24},{64,96... | collective-permute-start | bytes 786440 | tf_op jit(solution)/shard_map/ppermute | solution.py:111
  219.6 18.6 %copy-start.11 = (f32[1,128,512]{1,2,0:T(8,128)}, f32[1,128,512]{1,2,0:T(8,128)S(1)}, u32[]{:S(2)}) copy-start(f32[1,128,512]{1,2,0:T(8,128)S(1)} %collective-permute-done.25) | copy-start | bytes 786436
  219.6 10.6 %collective-permute-start.26 = (f32[1,128,512]{1,2,0:T(8,128)S(1)}, f32[1,128,512]{1,2,0:T(8,128)S(1)}, u32[]{:S(2)}, u32[]{:S(2)}) collective-permute-start(f32[1,128,512]{1,2,0:T(8,128)S(1)} %multiply_add_fusion.2), channel_id=1, source_target_pairs={{0,64},{8,72},{16,80},{24,88},{32,96},{40,104},{48,112},{56,120},{... | collective-permute-start | bytes 786440 | tf_op jit(solution)/shard_map/ppermute | solution.py:111
  230.2 8.0 %copy-start.12 = (f32[1,128,512]{1,2,0:T(8,128)}, f32[1,128,512]{1,2,0:T(8,128)S(1)}, u32[]{:S(2)}) copy-start(f32[1,128,512]{1,2,0:T(8,128)S(1)} %collective-permute-done.26) | copy-start | bytes 786436
  230.2 7.1 %collective-permute-start.27 = (f32[1,128,512]{1,2,0:T(8,128)S(1)}, f32[1,128,512]{1,2,0:T(8,128)S(1)}, u32[]{:S(2)}, u32[]{:S(2)}) collective-permute-start(f32[1,128,512]{1,2,0:T(8,128)S(1)} %multiply_add_fusion.1), channel_id=1, source_target_pairs={{0,128},{8,136},{16,144},{24,152},{32,160},{40,168},{48,176},{56,1... | collective-permute-start | bytes 786440 | tf_op jit(solution)/shard_map/ppermute | solution.py:111
  237.3 0.8 copy-start.13
  238.1 8.9 %collective-permute-start.28 = (f32[1,128,512]{1,2,0:T(8,128)}, f32[1,128,512]{1,2,0:T(8,128)}, u32[]{:S(2)}, u32[]{:S(2)}) collective-permute-start(f32[1,128,512]{1,2,0:T(8,128)} %multiply_add_fusion), channel_id=1, source_target_pairs={{0,256},{8,264},{16,272},{24,280},{32,288},{40,296},{48,304},{56,3... | collective-permute-start | bytes 786440 | tf_op jit(solution)/shard_map/ppermute | solution.py:111
  250.2 1.0 copy-start.5
  250.3 1.0 copy-start.7
  252.3 32.1 %collective-permute-start.29 = (f32[1184,128]{1,0:T(8,128)S(1)}, f32[1184,128]{1,0:T(8,128)S(1)}, u32[]{:S(2)}, u32[]{:S(2)}) collective-permute-start(f32[1184,128]{1,0:T(8,128)S(1)} %constant_dynamic-slice_fusion.3), channel_id=1, source_target_pairs={{0,1},{1,0},{2,3},{3,2},{4,5},{5,4},{6,7},{7,6},{8,9},{9,8},{10,11... | collective-permute-start | bytes 1818632 | tf_op jit(solution)/shard_map/ppermute | solution.py:134
  284.5 14.5 %collective-permute-start.30 = (f32[296,128]{1,0:T(8,128)S(1)}, f32[296,128]{1,0:T(8,128)S(1)}, u32[]{:S(2)}, u32[]{:S(2)}) collective-permute-start(f32[296,128]{1,0:T(8,128)S(1)} %get-tuple-element.49), channel_id=1, source_target_pairs={{0,2},{1,7},{2,4},{3,1},{4,6},{5,3},{6,0},{7,5},{8,10},{9,15},{10,... | collective-permute-start | bytes 454664 | tf_op jit(solution)/shard_map/ppermute | solution.py:145
  299.1 16.0 %collective-permute-start.31 = (f32[296,128]{1,0:T(8,128)S(1)}, f32[296,128]{1,0:T(8,128)S(1)}, u32[]{:S(2)}, u32[]{:S(2)}) collective-permute-start(f32[296,128]{1,0:T(8,128)S(1)} %get-tuple-element.47), channel_id=1, source_target_pairs={{0,2},{1,7},{2,4},{3,1},{4,6},{5,3},{6,0},{7,5},{8,10},{9,15},{10,... | collective-permute-start | bytes 454664 | tf_op jit(solution)/shard_map/ppermute | solution.py:145
  315.2 14.2 %collective-permute-start.32 = (f32[296,128]{1,0:T(8,128)S(1)}, f32[296,128]{1,0:T(8,128)S(1)}, u32[]{:S(2)}, u32[]{:S(2)}) collective-permute-start(f32[296,128]{1,0:T(8,128)S(1)} %get-tuple-element.45), channel_id=1, source_target_pairs={{0,2},{1,7},{2,4},{3,1},{4,6},{5,3},{6,0},{7,5},{8,10},{9,15},{10,... | collective-permute-start | bytes 454664 | tf_op jit(solution)/shard_map/ppermute | solution.py:145
  329.4 11.7 %collective-permute-start.33 = (f32[296,128]{1,0:T(8,128)S(1)}, f32[296,128]{1,0:T(8,128)S(1)}, u32[]{:S(2)}, u32[]{:S(2)}) collective-permute-start(f32[296,128]{1,0:T(8,128)S(1)} %dynamic-slice_bitcast_fusion.2), channel_id=1, source_target_pairs={{0,2},{1,7},{2,4},{3,1},{4,6},{5,3},{6,0},{7,5},{8,10},{9,15},{10,... | collective-permute-start | bytes 454664 | tf_op jit(solution)/shard_map/ppermute | solution.py:151
  336.7 31.7 %copy-start.2 = (bf16[128,9,128]{0,2,1:T(8,128)(2,1)S(1)}, bf16[128,9,128]{0,2,1:T(8,128)(2,1)}, u32[]{:S(2)}) copy-start(bf16[128,9,128]{0,2,1:T(8,128)(2,1)} %copy.33) | copy-start | bytes 884740
  341.1 10.2 %collective-permute-start.34 = (f32[296,128]{1,0:T(8,128)S(1)}, f32[296,128]{1,0:T(8,128)S(1)}, u32[]{:S(2)}, u32[]{:S(2)}) collective-permute-start(f32[296,128]{1,0:T(8,128)S(1)} %dynamic-slice_bitcast_fusion.1), channel_id=1, source_target_pairs={{0,2},{1,7},{2,4},{3,1},{4,6},{5,3},{6,0},{7,5},{8,10},{9,15},{10,... | collective-permute-start | bytes 454664 | tf_op jit(solution)/shard_map/ppermute | solution.py:151
  351.3 10.1 %collective-permute-start.35 = (f32[296,128]{1,0:T(8,128)S(1)}, f32[296,128]{1,0:T(8,128)S(1)}, u32[]{:S(2)}, u32[]{:S(2)}) collective-permute-start(f32[296,128]{1,0:T(8,128)S(1)} %dynamic-slice_bitcast_fusion), channel_id=1, source_target_pairs={{0,2},{1,7},{2,4},{3,1},{4,6},{5,3},{6,0},{7,5},{8,10},{9,15},{10,... | collective-permute-start | bytes 454664 | tf_op jit(solution)/shard_map/ppermute | solution.py:151
  361.4 8.4 %collective-permute-start.36 = (f32[1184,128]{1,0:T(8,128)S(1)}, f32[1184,128]{1,0:T(8,128)S(1)}, u32[]{:S(2)}, u32[]{:S(2)}) collective-permute-start(f32[1184,128]{1,0:T(8,128)S(1)} %bitcast.545), channel_id=1, source_target_pairs={{0,1},{1,0},{2,3},{3,2},{4,5},{5,4},{6,7},{7,6},{8,9},{9,8},{10,11... | collective-permute-start | bytes 1818632 | tf_op jit(solution)/shard_map/ppermute | solution.py:154

commit v14 on v12

--- a/solution.py
+++ b/solution.py
@@ -147,16 +147,18 @@
     ring = [(k, following(k)) for k in range(count)]
     place = jnp.where(core == 0, chip, (chips - chip) % chips)
     pieces = half.reshape(chips, half_rows // chips, lanes)
+    doubled = jnp.concatenate([pieces, pieces], axis=0)
+    pieces = lax.dynamic_slice_in_dim(doubled, place, chips, 0)
+    slots = list(pieces)
     for t in range(chips - 1):
-        sent = lax.dynamic_index_in_dim(pieces, (place - t) % chips, 0, False)
-        got = lax.ppermute(sent, axis, ring)
-        slot = (place - t - 1 + chips) % chips
-        mine = lax.dynamic_index_in_dim(pieces, slot, 0, False)
-        pieces = lax.dynamic_update_index_in_dim(pieces, mine + got, slot, 0)
+        got = lax.ppermute(slots[(-t) % chips], axis, ring)
+        slot = (-t - 1) % chips
+        slots[slot] = slots[slot] + got
     for t in range(chips - 1):
-        sent = lax.dynamic_index_in_dim(pieces, (place + 1 - t + chips) % chips, 0, False)
-        got = lax.ppermute(sent, axis, ring)
-        pieces = lax.dynamic_update_index_in_dim(pieces, got, (place - t + chips) % chips, 0)
+        slots[(-t) % chips] = lax.ppermute(slots[(1 - t) % chips], axis, ring)
+    rotated = jnp.stack(slots)
+    doubled = jnp.concatenate([rotated, rotated], axis=0)
+    pieces = lax.dynamic_slice_in_dim(doubled, (chips - place) % chips, chips, 0)
     half = pieces.reshape(half_rows, lanes)
     other = lax.ppermute(half, axis, partner)
     whole = jnp.zeros_like(current)

time: 369 us -> 369 us (level)
  the two profiles are of different devices: /device:TPU:1 before, /device:TPU:31 now
where the time goes in v14:
time: 369 us; the launch traced here: 368 us
  waiting for transfers between devices  171 us (46%)
  starting transfers between devices  157 us (43%)
  other arithmetic  23.3 us (6%)
  local copies, waits for them, and re-layouts  7.33 us (2%)
  matrix products  6.23 us (2%)
    ppermute x18, waiting for transfers between devices, butterfly_again(): got = lax.ppermute(block_sum, axis, [(k, k ^ step) for k in range(count)])  97.3 us
    ppermute x18, starting transfers between devices, butterfly_again(): got = lax.ppermute(block_sum, axis, [(k, k ^ step) for k in range(count)])  53.2 us
    ppermute x6, waiting for transfers between devices, butterfly_first(): got = lax.ppermute(packed, axis, [(k, k ^ step) for k in range(count)])  42.3 us
    ppermute x3, starting transfers between devices, batch_sum(): got = lax.ppermute(slots[-t % chips], axis, ring)  29.5 us
    ppermute x1, starting transfers between devices, batch_sum(): half = keep + lax.ppermute(give, axis, partner)  24.2 us
    ppermute x3, starting transfers between devices, batch_sum(): slots[-t % chips] = lax.ppermute(slots[(1 - t) % chips], axis, ring)  20.1 us
    ppermute x6, starting transfers between devices, butterfly_first(): got = lax.ppermute(packed, axis, [(k, k ^ step) for k in range(count)])  19.3 us
    ppermute x3, waiting for transfers between devices, batch_sum(): slots[-t % chips] = lax.ppermute(slots[(1 - t) % chips], axis, ring)  16 us
  transfers between devices with their start and end apart: 32, of which 32 were waited for; matrix products, arithmetic and copies ran while one was open for 1% of the time, Pallas kernels for 0%

profile of v14, /device:TPU:31, one launch (start us, length us, event | category | flops | bytes accessed | tf_op | source)
XLA Modules:
  0.0 368.0 jit_solution(11645034008686633684)
XLA Ops:
  6.6 2.5 collective-permute-start
  9.1 6.9 %collective-permute-done = f32[1,130,512]{2,1,0:T(8,128)S(1)} collective-permute-done((f32[1,130,512]{2,1,0:T(8,128)S(1)}, f32[1,130,512]{2,1,0:T(8,128)S(1)}, u32[]{:S(2)}, u32[]{:S(2)}) %collective-permute-start) | collective-permute-done | bytes 266272 | tf_op jit(solution)/shard_map/ppermute | solution.py:97
  16.2 3.0 collective-permute-start.1
  19.4 6.8 %collective-permute-done.1 = f32[1,130,512]{2,1,0:T(8,128)S(1)} collective-permute-done((f32[1,130,512]{2,1,0:T(8,128)S(1)}, f32[1,130,512]{2,1,0:T(8,128)S(1)}, u32[]{:S(2)}, u32[]{:S(2)}) %collective-permute-start.1) | collective-permute-done | bytes 266272 | tf_op jit(solution)/shard_map/ppermute | solution.py:97
  26.9 3.5 collective-permute-start.2
  30.5 4.4 %collective-permute-done.2 = f32[1,130,512]{2,1,0:T(8,128)S(1)} collective-permute-done((f32[1,130,512]{2,1,0:T(8,128)S(1)}, f32[1,130,512]{2,1,0:T(8,128)S(1)}, u32[]{:S(2)}, u32[]{:S(2)}) %collective-permute-start.2) | collective-permute-done | bytes 266272 | tf_op jit(solution)/shard_map/ppermute | solution.py:97
  35.0 4.9 %collective-permute-start.3 = (f32[1,130,512]{2,1,0:T(8,128)S(1)}, f32[1,130,512]{2,1,0:T(8,128)S(1)}, u32[]{:S(2)}, u32[]{:S(2)}) collective-permute-start(f32[1,130,512]{2,1,0:T(8,128)S(1)} %pad_maximum_fusion.4), channel_id=1, source_target_pairs={{0,64},{8,72},{16,80},{24,88},{32,96},{40,104},{48,112},{56,120},{... | collective-permute-start | bytes 798728 | tf_op jit(solution)/shard_map/ppermute | solution.py:97
  40.0 12.2 %collective-permute-done.3 = f32[1,130,512]{2,1,0:T(8,128)S(1)} collective-permute-done((f32[1,130,512]{2,1,0:T(8,128)S(1)}, f32[1,130,512]{2,1,0:T(8,128)S(1)}, u32[]{:S(2)}, u32[]{:S(2)}) %collective-permute-start.3) | collective-permute-done | bytes 266272 | tf_op jit(solution)/shard_map/ppermute | solution.py:97
  52.9 2.4 collective-permute-start.4
  56.0 5.7 %collective-permute-done.4 = f32[1,130,512]{2,1,0:T(8,128)S(1)} collective-permute-done((f32[1,130,512]{2,1,0:T(8,128)S(1)}, f32[1,130,512]{2,1,0:T(8,128)S(1)}, u32[]{:S(2)}, u32[]{:S(2)}) %collective-permute-start.4) | collective-permute-done | bytes 266272 | tf_op jit(solution)/shard_map/ppermute | solution.py:97
  62.4 3.0 collective-permute-start.5
  65.5 6.4 %collective-permute-done.5 = f32[1,130,512]{2,1,0:T(8,128)} collective-permute-done((f32[1,130,512]{2,1,0:T(8,128)S(1)}, f32[1,130,512]{2,1,0:T(8,128)}, u32[]{:S(2)}, u32[]{:S(2)}) %collective-permute-start.5) | collective-permute-done | bytes 266272 | tf_op jit(solution)/shard_map/ppermute | solution.py:97
  75.6 2.8 collective-permute-start.6
  78.4 4.3 %collective-permute-done.6 = f32[1,128,512]{2,1,0:T(8,128)S(1)} collective-permute-done((f32[1,128,512]{2,1,0:T(8,128)S(1)}, f32[1,128,512]{2,1,0:T(8,128)S(1)}, u32[]{:S(2)}, u32[]{:S(2)}) %collective-permute-start.6) | collective-permute-done | bytes 262176 | tf_op jit(solution)/shard_map/ppermute | solution.py:118
  82.8 3.3 collective-permute-start.7
  86.1 5.4 %collective-permute-done.7 = f32[1,128,512]{2,1,0:T(8,128)S(1)} collective-permute-done((f32[1,128,512]{2,1,0:T(8,128)S(1)}, f32[1,128,512]{2,1,0:T(8,128)S(1)}, u32[]{:S(2)}, u32[]{:S(2)}) %collective-permute-start.7) | collective-permute-done | bytes 262176 | tf_op jit(solution)/shard_map/ppermute | solution.py:118
  91.6 1.9 collective-permute-start.8
  93.5 5.2 %collective-permute-done.8 = f32[1,128,512]{2,1,0:T(8,128)S(1)} collective-permute-done((f32[1,128,512]{2,1,0:T(8,128)S(1)}, f32[1,128,512]{2,1,0:T(8,128)S(1)}, u32[]{:S(2)}, u32[]{:S(2)}) %collective-permute-start.8) | collective-permute-done | bytes 262176 | tf_op jit(solution)/shard_map/ppermute | solution.py:118
  98.8 3.4 collective-permute-start.9
  102.2 7.4 %collective-permute-done.9 = f32[1,128,512]{2,1,0:T(8,128)S(1)} collective-permute-done((f32[1,128,512]{2,1,0:T(8,128)S(1)}, f32[1,128,512]{2,1,0:T(8,128)S(1)}, u32[]{:S(2)}, u32[]{:S(2)}) %collective-permute-start.9) | collective-permute-done | bytes 262176 | tf_op jit(solution)/shard_map/ppermute | solution.py:118
  109.7 2.4 collective-permute-start.10
  112.1 5.0 %collective-permute-done.10 = f32[1,128,512]{2,1,0:T(8,128)S(1)} collective-permute-done((f32[1,128,512]{2,1,0:T(8,128)S(1)}, f32[1,128,512]{2,1,0:T(8,128)S(1)}, u32[]{:S(2)}, u32[]{:S(2)}) %collective-permute-start.10) | collective-permute-done | bytes 262176 | tf_op jit(solution)/shard_map/ppermute | solution.py:118
  117.9 2.9 collective-permute-start.11
  122.6 5.2 %collective-permute-done.11 = f32[1,128,512]{2,1,0:T(8,128)} collective-permute-done((f32[1,128,512]{2,1,0:T(8,128)}, f32[1,128,512]{2,1,0:T(8,128)}, u32[]{:S(2)}, u32[]{:S(2)}) %collective-permute-start.11) | collective-permute-done | bytes 262176 | tf_op jit(solution)/shard_map/ppermute | solution.py:118
  134.5 2.5 collective-permute-start.12
  137.0 4.6 %collective-permute-done.12 = f32[1,128,512]{2,1,0:T(8,128)S(1)} collective-permute-done((f32[1,128,512]{2,1,0:T(8,128)S(1)}, f32[1,128,512]{2,1,0:T(8,128)S(1)}, u32[]{:S(2)}, u32[]{:S(2)}) %collective-permute-start.12) | collective-permute-done | bytes 262176 | tf_op jit(solution)/shard_map/ppermute | solution.py:118
  141.7 3.1 collective-permute-start.13
  144.8 5.7 %collective-permute-done.13 = f32[1,128,512]{2,1,0:T(8,128)S(1)} collective-permute-done((f32[1,128,512]{2,1,0:T(8,128)S(1)}, f32[1,128,512]{2,1,0:T(8,128)S(1)}, u32[]{:S(2)}, u32[]{:S(2)}) %collective-permute-start.13) | collective-permute-done | bytes 262176 | tf_op jit(solution)/shard_map/ppermute | solution.py:118
  150.6 2.1 collective-permute-start.14
  152.7 5.1 %collective-permute-done.14 = f32[1,128,512]{2,1,0:T(8,128)S(1)} collective-permute-done((f32[1,128,512]{2,1,0:T(8,128)S(1)}, f32[1,128,512]{2,1,0:T(8,128)S(1)}, u32[]{:S(2)}, u32[]{:S(2)}) %collective-permute-start.14) | collective-permute-done | bytes 262176 | tf_op jit(solution)/shard_map/ppermute | solution.py:118
  157.9 3.7 %collective-permute-start.15 = (f32[1,128,512]{2,1,0:T(8,128)S(1)}, f32[1,128,512]{2,1,0:T(8,128)S(1)}, u32[]{:S(2)}, u32[]{:S(2)}) collective-permute-start(f32[1,128,512]{2,1,0:T(8,128)S(1)} %multiply_add_fusion.8), channel_id=1, source_target_pairs={{0,64},{8,72},{16,80},{24,88},{32,96},{40,104},{48,112},{56,120},{... | collective-permute-start | bytes 786440 | tf_op jit(solution)/shard_map/ppermute | solution.py:118
  161.6 7.1 %collective-permute-done.15 = f32[1,128,512]{2,1,0:T(8,128)S(1)} collective-permute-done((f32[1,128,512]{2,1,0:T(8,128)S(1)}, f32[1,128,512]{2,1,0:T(8,128)S(1)}, u32[]{:S(2)}, u32[]{:S(2)}) %collective-permute-start.15) | collective-permute-done | bytes 262176 | tf_op jit(solution)/shard_map/ppermute | solution.py:118
  168.8 2.5 collective-permute-start.16
  171.3 4.6 %collective-permute-done.16 = f32[1,128,512]{2,1,0:T(8,128)S(1)} collective-permute-done((f32[1,128,512]{2,1,0:T(8,128)S(1)}, f32[1,128,512]{2,1,0:T(8,128)S(1)}, u32[]{:S(2)}, u32[]{:S(2)}) %collective-permute-start.16) | collective-permute-done | bytes 262176 | tf_op jit(solution)/shard_map/ppermute | solution.py:118
  176.1 7.1 %collective-permute-start.17 = (f32[1,128,512]{2,1,0:T(8,128)S(1)}, f32[1,128,512]{2,1,0:T(8,128)S(1)}, u32[]{:S(2)}, u32[]{:S(2)}) collective-permute-start(f32[1,128,512]{2,1,0:T(8,128)S(1)} %multiply_add_fusion.6), channel_id=1, source_target_pairs={{0,256},{8,264},{16,272},{24,280},{32,288},{40,296},{48,304},{56,3... | collective-permute-start | bytes 786440 | tf_op jit(solution)/shard_map/ppermute | solution.py:118
  183.2 3.6 collective-permute-done.17
  189.7 2.4 collective-permute-start.18
  192.1 4.7 %collective-permute-done.18 = f32[1,128,512]{2,1,0:T(8,128)S(1)} collective-permute-done((f32[1,128,512]{2,1,0:T(8,128)S(1)}, f32[1,128,512]{2,1,0:T(8,128)S(1)}, u32[]{:S(2)}, u32[]{:S(2)}) %collective-permute-start.18) | collective-permute-done | bytes 262176 | tf_op jit(solution)/shard_map/ppermute | solution.py:118
  196.9 1.9 collective-permute-start.19
  198.9 6.7 %collective-permute-done.19 = f32[1,128,512]{2,1,0:T(8,128)S(1)} collective-permute-done((f32[1,128,512]{2,1,0:T(8,128)S(1)}, f32[1,128,512]{2,1,0:T(8,128)S(1)}, u32[]{:S(2)}, u32[]{:S(2)}) %collective-permute-start.19) | collective-permute-done | bytes 262176 | tf_op jit(solution)/shard_map/ppermute | solution.py:118
  205.7 2.1 collective-permute-start.20
  207.7 5.5 %collective-permute-done.20 = f32[1,128,512]{2,1,0:T(8,128)S(1)} collective-permute-done((f32[1,128,512]{2,1,0:T(8,128)S(1)}, f32[1,128,512]{2,1,0:T(8,128)S(1)}, u32[]{:S(2)}, u32[]{:S(2)}) %collective-permute-start.20) | collective-permute-done | bytes 262176 | tf_op jit(solution)/shard_map/ppermute | solution.py:118
  213.3 2.2 collective-permute-start.21
  215.6 8.0 %collective-permute-done.21 = f32[1,128,512]{2,1,0:T(8,128)S(1)} collective-permute-done((f32[1,128,512]{2,1,0:T(8,128)S(1)}, f32[1,128,512]{2,1,0:T(8,128)S(1)}, u32[]{:S(2)}, u32[]{:S(2)}) %collective-permute-start.21) | collective-permute-done | bytes 262176 | tf_op jit(solution)/shard_map/ppermute | solution.py:118
  223.7 2.2 collective-permute-start.22
  225.9 5.2 %collective-permute-done.22 = f32[1,128,512]{2,1,0:T(8,128)S(1)} collective-permute-done((f32[1,128,512]{2,1,0:T(8,128)S(1)}, f32[1,128,512]{2,1,0:T(8,128)S(1)}, u32[]{:S(2)}, u32[]{:S(2)}) %collective-permute-start.22) | collective-permute-done | bytes 262176 | tf_op jit(solution)/shard_map/ppermute | solution.py:118
  231.9 4.9 %collective-permute-start.23 = (f32[1,128,512]{2,1,0:T(8,128)}, f32[1,128,512]{2,1,0:T(8,128)}, u32[]{:S(2)}, u32[]{:S(2)}) collective-permute-start(f32[1,128,512]{2,1,0:T(8,128)} %multiply_add_fusion), channel_id=1, source_target_pairs={{0,256},{8,264},{16,272},{24,280},{32,288},{40,296},{48,304},{56,3... | collective-permute-start | bytes 786440 | tf_op jit(solution)/shard_map/ppermute | solution.py:118
  236.9 4.0 %collective-permute-done.23 = f32[1,128,512]{2,1,0:T(8,128)} collective-permute-done((f32[1,128,512]{2,1,0:T(8,128)}, f32[1,128,512]{2,1,0:T(8,128)}, u32[]{:S(2)}, u32[]{:S(2)}) %collective-permute-start.23) | collective-permute-done | bytes 262176 | tf_op jit(solution)/shard_map/ppermute | solution.py:118
  240.9 1.6 fusion.284
  247.5 24.2 %collective-permute-start.24 = (f32[1184,128]{1,0:T(8,128)S(1)}, f32[1184,128]{1,0:T(8,128)S(1)}, u32[]{:S(2)}, u32[]{:S(2)}) collective-permute-start(f32[1184,128]{1,0:T(8,128)S(1)} %constant_dynamic-slice_fusion.1), channel_id=1, source_target_pairs={{0,1},{1,0},{2,3},{3,2},{4,5},{5,4},{6,7},{7,6},{8,9},{9,8},{10,11... | collective-permute-start | bytes 1818632 | tf_op jit(solution)/shard_map/ppermute | solution.py:141
  272.0 1.3 collective-permute-done.24
  273.5 11.7 %collective-permute-start.25 = (f32[296,128]{1,0:T(8,128)S(1)}, f32[296,128]{1,0:T(8,128)S(1)}, u32[]{:S(2)}, u32[]{:S(2)}) collective-permute-start(f32[296,128]{1,0:T(8,128)S(1)} %slice_bitcast_fusion), channel_id=1, source_target_pairs={{0,2},{1,7},{2,4},{3,1},{4,6},{5,3},{6,0},{7,5},{8,10},{9,15},{10,... | collective-permute-start | bytes 454664 | tf_op jit(solution)/shard_map/ppermute | solution.py:154
  285.2 3.4 collective-permute-done.25
  288.6 10.1 %collective-permute-start.26 = (f32[296,128]{1,0:T(8,128)S(1)}, f32[296,128]{1,0:T(8,128)S(1)}, u32[]{:S(2)}, u32[]{:S(2)}) collective-permute-start(f32[296,128]{1,0:T(8,128)S(1)} %fusion.182), channel_id=1, source_target_pairs={{0,2},{1,7},{2,4},{3,1},{4,6},{5,3},{6,0},{7,5},{8,10},{9,15},{10,... | collective-permute-start | bytes 454664 | tf_op jit(solution)/shard_map/ppermute | solution.py:154
  298.8 5.6 %collective-permute-done.26 = f32[296,128]{1,0:T(8,128)S(1)} collective-permute-done((f32[296,128]{1,0:T(8,128)S(1)}, f32[296,128]{1,0:T(8,128)S(1)}, u32[]{:S(2)}, u32[]{:S(2)}) %collective-permute-start.26) | collective-permute-done | bytes 151584 | tf_op jit(solution)/shard_map/ppermute | solution.py:154
  304.5 7.7 %collective-permute-start.27 = (f32[296,128]{1,0:T(8,128)S(1)}, f32[296,128]{1,0:T(8,128)S(1)}, u32[]{:S(2)}, u32[]{:S(2)}) collective-permute-start(f32[296,128]{1,0:T(8,128)S(1)} %fusion.183), channel_id=1, source_target_pairs={{0,2},{1,7},{2,4},{3,1},{4,6},{5,3},{6,0},{7,5},{8,10},{9,15},{10,... | collective-permute-start | bytes 454664 | tf_op jit(solution)/shard_map/ppermute | solution.py:154
  312.3 5.1 %collective-permute-done.27 = f32[296,128]{1,0:T(8,128)S(1)} collective-permute-done((f32[296,128]{1,0:T(8,128)S(1)}, f32[296,128]{1,0:T(8,128)S(1)}, u32[]{:S(2)}, u32[]{:S(2)}) %collective-permute-start.27) | collective-permute-done | bytes 151584 | tf_op jit(solution)/shard_map/ppermute | solution.py:154
  317.4 7.8 %collective-permute-start.28 = (f32[296,128]{1,0:T(8,128)S(1)}, f32[296,128]{1,0:T(8,128)S(1)}, u32[]{:S(2)}, u32[]{:S(2)}) collective-permute-start(f32[296,128]{1,0:T(8,128)S(1)} %fusion.184), channel_id=1, source_target_pairs={{0,2},{1,7},{2,4},{3,1},{4,6},{5,3},{6,0},{7,5},{8,10},{9,15},{10,... | collective-permute-start | bytes 454664 | tf_op jit(solution)/shard_map/ppermute | solution.py:158
  325.3 5.4 %collective-permute-done.28 = f32[296,128]{1,0:T(8,128)S(1)} collective-permute-done((f32[296,128]{1,0:T(8,128)S(1)}, f32[296,128]{1,0:T(8,128)S(1)}, u32[]{:S(2)}, u32[]{:S(2)}) %collective-permute-start.28) | collective-permute-done | bytes 151584 | tf_op jit(solution)/shard_map/ppermute | solution.py:158
  330.7 6.4 %collective-permute-start.29 = (f32[296,128]{1,0:T(8,128)S(1)}, f32[296,128]{1,0:T(8,128)S(1)}, u32[]{:S(2)}, u32[]{:S(2)}) collective-permute-start(f32[296,128]{1,0:T(8,128)S(1)} %collective-permute-done.28), channel_id=1, source_target_pairs={{0,2},{1,7},{2,4},{3,1},{4,6},{5,3},{6,0},{7,5},{8,10},{9,15},{10,... | collective-permute-start | bytes 454664 | tf_op jit(solution)/shard_map/ppermute | solution.py:158
  337.2 5.1 %collective-permute-done.29 = f32[296,128]{1,0:T(8,128)S(1)} collective-permute-done((f32[296,128]{1,0:T(8,128)S(1)}, f32[296,128]{1,0:T(8,128)S(1)}, u32[]{:S(2)}, u32[]{:S(2)}) %collective-permute-start.29) | collective-permute-done | bytes 151584 | tf_op jit(solution)/shard_map/ppermute | solution.py:158
  342.3 5.9 %collective-permute-start.30 = (f32[296,128]{1,0:T(8,128)S(1)}, f32[296,128]{1,0:T(8,128)S(1)}, u32[]{:S(2)}, u32[]{:S(2)}) collective-permute-start(f32[296,128]{1,0:T(8,128)S(1)} %collective-permute-done.29), channel_id=1, source_target_pairs={{0,2},{1,7},{2,4},{3,1},{4,6},{5,3},{6,0},{7,5},{8,10},{9,15},{10,... | collective-permute-start | bytes 454664 | tf_op jit(solution)/shard_map/ppermute | solution.py:158
  348.2 5.5 %collective-permute-done.30 = f32[296,128]{1,0:T(8,128)S(1)} collective-permute-done((f32[296,128]{1,0:T(8,128)S(1)}, f32[296,128]{1,0:T(8,128)S(1)}, u32[]{:S(2)}, u32[]{:S(2)}) %collective-permute-start.30) | collective-permute-done | bytes 151584 | tf_op jit(solution)/shard_map/ppermute | solution.py:158
  353.9 10.5 %collective-permute-start.31 = (f32[1184,128]{1,0:T(8,128)S(1)}, f32[1184,128]{1,0:T(8,128)S(1)}, u32[]{:S(2)}, u32[]{:S(2)}) collective-permute-start(f32[1184,128]{1,0:T(8,128)S(1)} %bitcast.573), channel_id=1, source_target_pairs={{0,1},{1,0},{2,3},{3,2},{4,5},{5,4},{6,7},{7,6},{8,9},{9,8},{10,11... | collective-permute-start | bytes 1818632 | tf_op jit(solution)/shard_map/ppermute | solution.py:163
  (293 shorter events, 35.5 us)
Async XLA Ops:
  0.6 3.6 copy-start.1
  3.8 1.1 copy-start
  6.2 9.9 %copy-start.20 = (f32[1,128]{1,0:T(1,128)S(1)}, f32[1,128]{1,0:T(1,128)}, u32[]{:S(2)}) copy-start(f32[1,128]{1,0:T(1,128)} %param.10) | copy-start | bytes 1540
  6.2 9.8 %copy-start.21 = (f32[1,128]{1,0:T(1,128)S(1)}, f32[1,128]{1,0:T(1,128)}, u32[]{:S(2)}) copy-start(f32[1,128]{1,0:T(1,128)} %param.11) | copy-start | bytes 1540
  6.6 9.4 %collective-permute-start = (f32[1,130,512]{2,1,0:T(8,128)S(1)}, f32[1,130,512]{2,1,0:T(8,128)S(1)}, u32[]{:S(2)}, u32[]{:S(2)}) collective-permute-start(f32[1,130,512]{2,1,0:T(8,128)S(1)} %pad_maximum_fusion.1), channel_id=1, source_target_pairs={{0,8},{8,0},{16,24},{24,16},{32,40},{40,32},{48,56},{56,48},{64,72... | collective-permute-start | bytes 798728 | tf_op jit(solution)/shard_map/ppermute | solution.py:97
  16.2 10.0 %collective-permute-start.1 = (f32[1,130,512]{2,1,0:T(8,128)S(1)}, f32[1,130,512]{2,1,0:T(8,128)S(1)}, u32[]{:S(2)}, u32[]{:S(2)}) collective-permute-start(f32[1,130,512]{2,1,0:T(8,128)S(1)} %pad_maximum_fusion.2), channel_id=1, source_target_pairs={{0,16},{8,24},{16,0},{24,8},{32,48},{40,56},{48,32},{56,40},{64,80... | collective-permute-start | bytes 798728 | tf_op jit(solution)/shard_map/ppermute | solution.py:97
  26.7 45.1 %copy-start.28 = (f32[128]{0:T(128)}, f32[128]{0:T(128)S(1)}, u32[]{:S(2)}) copy-start(f32[128]{0:T(128)S(1)} %get-tuple-element.30) | copy-start | bytes 1540
  26.7 45.1 %copy-start.30 = (f32[128]{0:T(128)}, f32[128]{0:T(128)S(1)}, u32[]{:S(2)}) copy-start(f32[128]{0:T(128)S(1)} %get-tuple-element.71) | copy-start | bytes 1540
  26.9 7.9 %collective-permute-start.2 = (f32[1,130,512]{2,1,0:T(8,128)S(1)}, f32[1,130,512]{2,1,0:T(8,128)S(1)}, u32[]{:S(2)}, u32[]{:S(2)}) collective-permute-start(f32[1,130,512]{2,1,0:T(8,128)S(1)} %pad_maximum_fusion.3), channel_id=1, source_target_pairs={{0,32},{8,40},{16,48},{24,56},{32,0},{40,8},{48,16},{56,24},{64,96... | collective-permute-start | bytes 798728 | tf_op jit(solution)/shard_map/ppermute | solution.py:97
  35.0 17.2 %collective-permute-start.3 = (f32[1,130,512]{2,1,0:T(8,128)S(1)}, f32[1,130,512]{2,1,0:T(8,128)S(1)}, u32[]{:S(2)}, u32[]{:S(2)}) collective-permute-start(f32[1,130,512]{2,1,0:T(8,128)S(1)} %pad_maximum_fusion.4), channel_id=1, source_target_pairs={{0,64},{8,72},{16,80},{24,88},{32,96},{40,104},{48,112},{56,120},{... | collective-permute-start | bytes 798728 | tf_op jit(solution)/shard_map/ppermute | solution.py:97
  52.9 8.7 %collective-permute-start.4 = (f32[1,130,512]{2,1,0:T(8,128)S(1)}, f32[1,130,512]{2,1,0:T(8,128)S(1)}, u32[]{:S(2)}, u32[]{:S(2)}) collective-permute-start(f32[1,130,512]{2,1,0:T(8,128)S(1)} %pad_maximum_fusion.5), channel_id=1, source_target_pairs={{0,128},{8,136},{16,144},{24,152},{32,160},{40,168},{48,176},{56,1... | collective-permute-start | bytes 798728 | tf_op jit(solution)/shard_map/ppermute | solution.py:97
  56.0 17.0 %copy-start.32 = (f32[128]{0:T(128)}, f32[128]{0:T(128)S(1)}, u32[]{:S(2)}) copy-start(f32[128]{0:T(128)S(1)} %get-tuple-element.28) | copy-start | bytes 1540
  56.0 17.0 %copy-start.34 = (f32[128]{0:T(128)}, f32[128]{0:T(128)S(1)}, u32[]{:S(2)}) copy-start(f32[128]{0:T(128)S(1)} %get-tuple-element.34) | copy-start | bytes 1540
  62.4 9.4 %collective-permute-start.5 = (f32[1,130,512]{2,1,0:T(8,128)S(1)}, f32[1,130,512]{2,1,0:T(8,128)}, u32[]{:S(2)}, u32[]{:S(2)}) collective-permute-start(f32[1,130,512]{2,1,0:T(8,128)S(1)} %pad_maximum_fusion.6), channel_id=1, source_target_pairs={{0,256},{8,264},{16,272},{24,280},{32,288},{40,296},{48,304},{56,3... | collective-permute-start | bytes 798728 | tf_op jit(solution)/shard_map/ppermute | solution.py:97
  65.4 7.5 %copy-start.36 = (f32[128]{0:T(128)}, f32[128]{0:T(128)S(1)}, u32[]{:S(2)}) copy-start(f32[128]{0:T(128)S(1)} %fusion.296) | copy-start | bytes 1540
  75.6 7.1 %collective-permute-start.6 = (f32[1,128,512]{2,1,0:T(8,128)S(1)}, f32[1,128,512]{2,1,0:T(8,128)S(1)}, u32[]{:S(2)}, u32[]{:S(2)}) collective-permute-start(f32[1,128,512]{2,1,0:T(8,128)S(1)} %fusion.118), channel_id=1, source_target_pairs={{0,8},{8,0},{16,24},{24,16},{32,40},{40,32},{48,56},{56,48},{64,72... | collective-permute-start | bytes 786440 | tf_op jit(solution)/shard_map/ppermute | solution.py:118
  82.8 8.6 %collective-permute-start.7 = (f32[1,128,512]{2,1,0:T(8,128)S(1)}, f32[1,128,512]{2,1,0:T(8,128)S(1)}, u32[]{:S(2)}, u32[]{:S(2)}) collective-permute-start(f32[1,128,512]{2,1,0:T(8,128)S(1)} %multiply_add_fusion.15), channel_id=1, source_target_pairs={{0,16},{8,24},{16,0},{24,8},{32,48},{40,56},{48,32},{56,40},{64,80... | collective-permute-start | bytes 786440 | tf_op jit(solution)/shard_map/ppermute | solution.py:118
  91.6 7.1 %collective-permute-start.8 = (f32[1,128,512]{2,1,0:T(8,128)S(1)}, f32[1,128,512]{2,1,0:T(8,128)S(1)}, u32[]{:S(2)}, u32[]{:S(2)}) collective-permute-start(f32[1,128,512]{2,1,0:T(8,128)S(1)} %multiply_add_fusion.14), channel_id=1, source_target_pairs={{0,32},{8,40},{16,48},{24,56},{32,0},{40,8},{48,16},{56,24},{64,96... | collective-permute-start | bytes 786440 | tf_op jit(solution)/shard_map/ppermute | solution.py:118
  98.8 10.8 %collective-permute-start.9 = (f32[1,128,512]{2,1,0:T(8,128)S(1)}, f32[1,128,512]{2,1,0:T(8,128)S(1)}, u32[]{:S(2)}, u32[]{:S(2)}) collective-permute-start(f32[1,128,512]{2,1,0:T(8,128)S(1)} %multiply_add_fusion.13), channel_id=1, source_target_pairs={{0,64},{8,72},{16,80},{24,88},{32,96},{40,104},{48,112},{56,120},{... | collective-permute-start | bytes 786440 | tf_op jit(solution)/shard_map/ppermute | solution.py:118
  109.7 7.4 %collective-permute-start.10 = (f32[1,128,512]{2,1,0:T(8,128)S(1)}, f32[1,128,512]{2,1,0:T(8,128)S(1)}, u32[]{:S(2)}, u32[]{:S(2)}) collective-permute-start(f32[1,128,512]{2,1,0:T(8,128)S(1)} %multiply_add_fusion.12), channel_id=1, source_target_pairs={{0,128},{8,136},{16,144},{24,152},{32,160},{40,168},{48,176},{56,1... | collective-permute-start | bytes 786440 | tf_op jit(solution)/shard_map/ppermute | solution.py:118
  117.1 3.8 %copy-start.11 = (f32[1,128,512]{2,1,0:T(8,128)}, f32[1,128,512]{2,1,0:T(8,128)S(1)}, u32[]{:S(2)}) copy-start(f32[1,128,512]{2,1,0:T(8,128)S(1)} %collective-permute-done.10) | copy-start | bytes 786436
  117.9 9.9 %collective-permute-start.11 = (f32[1,128,512]{2,1,0:T(8,128)}, f32[1,128,512]{2,1,0:T(8,128)}, u32[]{:S(2)}, u32[]{:S(2)}) collective-permute-start(f32[1,128,512]{2,1,0:T(8,128)} %multiply_add_fusion.11), channel_id=1, source_target_pairs={{0,256},{8,264},{16,272},{24,280},{32,288},{40,296},{48,304},{56,3... | collective-permute-start | bytes 786440 | tf_op jit(solution)/shard_map/ppermute | solution.py:118
  121.2 6.6 %copy-start.29 = (f32[128]{0:T(128)S(1)}, f32[128]{0:T(128)}, u32[]{:S(2)}) copy-start(f32[128]{0:T(128)} %copy-done.28) | copy-start | bytes 1540
  121.2 6.6 %copy-start.31 = (f32[128]{0:T(128)S(1)}, f32[128]{0:T(128)}, u32[]{:S(2)}) copy-start(f32[128]{0:T(128)} %copy-done.30) | copy-start | bytes 1540
  121.2 6.6 %copy-start.33 = (f32[128]{0:T(128)S(1)}, f32[128]{0:T(128)}, u32[]{:S(2)}) copy-start(f32[128]{0:T(128)} %copy-done.32) | copy-start | bytes 1540
  121.2 6.6 %copy-start.35 = (f32[128]{0:T(128)S(1)}, f32[128]{0:T(128)}, u32[]{:S(2)}) copy-start(f32[128]{0:T(128)} %copy-done.34) | copy-start | bytes 1540
  121.2 6.6 %copy-start.37 = (f32[128]{0:T(128)S(1)}, f32[128]{0:T(128)}, u32[]{:S(2)}) copy-start(f32[128]{0:T(128)} %copy-done.36) | copy-start | bytes 1540
  130.4 57.5 %copy-start.4 = (f32[1,512,128]{1,2,0:T(8,128)}, f32[1,512,128]{1,2,0:T(8,128)S(1)}, u32[]{:S(2)}) copy-start(f32[1,512,128]{1,2,0:T(8,128)S(1)} %get-tuple-element.93) | copy-start | bytes 786436
  130.4 1.0 copy-start.2
  134.5 7.1 %collective-permute-start.12 = (f32[1,128,512]{2,1,0:T(8,128)S(1)}, f32[1,128,512]{2,1,0:T(8,128)S(1)}, u32[]{:S(2)}, u32[]{:S(2)}) collective-permute-start(f32[1,128,512]{2,1,0:T(8,128)S(1)} %fusion.85), channel_id=1, source_target_pairs={{0,8},{8,0},{16,24},{24,16},{32,40},{40,32},{48,56},{56,48},{64,72... | collective-permute-start | bytes 786440 | tf_op jit(solution)/shard_map/ppermute | solution.py:118
  141.6 27.1 %copy-start.17 = (f32[128]{0:T(128)S(1)}, f32[128]{0:T(128)}, u32[]{:S(2)}) copy-start(f32[128]{0:T(128)} %get-tuple-element.41) | copy-start | bytes 1540
  141.7 8.8 %collective-permute-start.13 = (f32[1,128,512]{2,1,0:T(8,128)S(1)}, f32[1,128,512]{2,1,0:T(8,128)S(1)}, u32[]{:S(2)}, u32[]{:S(2)}) collective-permute-start(f32[1,128,512]{2,1,0:T(8,128)S(1)} %multiply_add_fusion.10), channel_id=1, source_target_pairs={{0,16},{8,24},{16,0},{24,8},{32,48},{40,56},{48,32},{56,40},{64,80... | collective-permute-start | bytes 786440 | tf_op jit(solution)/shard_map/ppermute | solution.py:118
  150.5 25.4 %copy-start.18 = (f32[128]{0:T(128)S(1)}, f32[128]{0:T(128)}, u32[]{:S(2)}) copy-start(f32[128]{0:T(128)} %get-tuple-element.36) | copy-start | bytes 1540
  150.5 25.4 %copy-start.19 = (f32[128]{0:T(128)S(1)}, f32[128]{0:T(128)}, u32[]{:S(2)}) copy-start(f32[128]{0:T(128)} %get-tuple-element.38) | copy-start | bytes 1540
  150.6 7.1 %collective-permute-start.14 = (f32[1,128,512]{2,1,0:T(8,128)S(1)}, f32[1,128,512]{2,1,0:T(8,128)S(1)}, u32[]{:S(2)}, u32[]{:S(2)}) collective-permute-start(f32[1,128,512]{2,1,0:T(8,128)S(1)} %multiply_add_fusion.9), channel_id=1, source_target_pairs={{0,32},{8,40},{16,48},{24,56},{32,0},{40,8},{48,16},{56,24},{64,96... | collective-permute-start | bytes 786440 | tf_op jit(solution)/shard_map/ppermute | solution.py:118
  157.7 29.0 %copy-start.23 = (f32[128]{0:T(128)S(1)}, f32[128]{0:T(128)}, u32[]{:S(2)}) copy-start(f32[128]{0:T(128)} %get-tuple-element.13) | copy-start | bytes 1540
  157.7 29.0 %copy-start.24 = (f32[128]{0:T(128)S(1)}, f32[128]{0:T(128)}, u32[]{:S(2)}) copy-start(f32[128]{0:T(128)} %get-tuple-element.66) | copy-start | bytes 1540
  157.7 29.0 %copy-start.25 = (f32[128]{0:T(128)S(1)}, f32[128]{0:T(128)}, u32[]{:S(2)}) copy-start(f32[128]{0:T(128)} %get-tuple-element.15) | copy-start | bytes 1540
  157.7 29.0 %copy-start.26 = (f32[128]{0:T(128)S(1)}, f32[128]{0:T(128)}, u32[]{:S(2)}) copy-start(f32[128]{0:T(128)} %get-tuple-element.35) | copy-start | bytes 1540
  157.7 29.0 %copy-start.27 = (f32[128]{0:T(128)S(1)}, f32[128]{0:T(128)}, u32[]{:S(2)}) copy-start(f32[128]{0:T(128)} %get-tuple-element.72) | copy-start | bytes 1540
  157.9 10.8 %collective-permute-start.15 = (f32[1,128,512]{2,1,0:T(8,128)S(1)}, f32[1,128,512]{2,1,0:T(8,128)S(1)}, u32[]{:S(2)}, u32[]{:S(2)}) collective-permute-start(f32[1,128,512]{2,1,0:T(8,128)S(1)} %multiply_add_fusion.8), channel_id=1, source_target_pairs={{0,64},{8,72},{16,80},{24,88},{32,96},{40,104},{48,112},{56,120},{... | collective-permute-start | bytes 786440 | tf_op jit(solution)/shard_map/ppermute | solution.py:118
  168.8 7.1 %collective-permute-start.16 = (f32[1,128,512]{2,1,0:T(8,128)S(1)}, f32[1,128,512]{2,1,0:T(8,128)S(1)}, u32[]{:S(2)}, u32[]{:S(2)}) collective-permute-start(f32[1,128,512]{2,1,0:T(8,128)S(1)} %multiply_add_fusion.7), channel_id=1, source_target_pairs={{0,128},{8,136},{16,144},{24,152},{32,160},{40,168},{48,176},{56,1... | collective-permute-start | bytes 786440 | tf_op jit(solution)/shard_map/ppermute | solution.py:118
  176.1 10.7 %collective-permute-start.17 = (f32[1,128,512]{2,1,0:T(8,128)S(1)}, f32[1,128,512]{2,1,0:T(8,128)S(1)}, u32[]{:S(2)}, u32[]{:S(2)}) collective-permute-start(f32[1,128,512]{2,1,0:T(8,128)S(1)} %multiply_add_fusion.6), channel_id=1, source_target_pairs={{0,256},{8,264},{16,272},{24,280},{32,288},{40,296},{48,304},{56,3... | collective-permute-start | bytes 786440 | tf_op jit(solution)/shard_map/ppermute | solution.py:118
  189.7 7.1 %collective-permute-start.18 = (f32[1,128,512]{2,1,0:T(8,128)S(1)}, f32[1,128,512]{2,1,0:T(8,128)S(1)}, u32[]{:S(2)}, u32[]{:S(2)}) collective-permute-start(f32[1,128,512]{2,1,0:T(8,128)S(1)} %fusion.76), channel_id=1, source_target_pairs={{0,8},{8,0},{16,24},{24,16},{32,40},{40,32},{48,56},{56,48},{64,72... | collective-permute-start | bytes 786440 | tf_op jit(solution)/shard_map/ppermute | solution.py:118
  196.8 2.0 copy-start.12
  196.9 8.6 %collective-permute-start.19 = (f32[1,128,512]{2,1,0:T(8,128)S(1)}, f32[1,128,512]{2,1,0:T(8,128)S(1)}, u32[]{:S(2)}, u32[]{:S(2)}) collective-permute-start(f32[1,128,512]{2,1,0:T(8,128)S(1)} %multiply_add_fusion.4), channel_id=1, source_target_pairs={{0,16},{8,24},{16,0},{24,8},{32,48},{40,56},{48,32},{56,40},{64,80... | collective-permute-start | bytes 786440 | tf_op jit(solution)/shard_map/ppermute | solution.py:118
  205.6 2.2 copy-start.13
  205.7 35.2 %copy-start.9 = (f32[1,128,512]{2,1,0:T(8,128)S(1)}, f32[1,128,512]{2,1,0:T(8,128)}, u32[]{:S(2)}) copy-start(f32[1,128,512]{2,1,0:T(8,128)} %copy-done.8) | copy-start | bytes 786436
  205.7 7.5 %collective-permute-start.20 = (f32[1,128,512]{2,1,0:T(8,128)S(1)}, f32[1,128,512]{2,1,0:T(8,128)S(1)}, u32[]{:S(2)}, u32[]{:S(2)}) collective-permute-start(f32[1,128,512]{2,1,0:T(8,128)S(1)} %multiply_add_fusion.3), channel_id=1, source_target_pairs={{0,32},{8,40},{16,48},{24,56},{32,0},{40,8},{48,16},{56,24},{64,96... | collective-permute-start | bytes 786440 | tf_op jit(solution)/shard_map/ppermute | solution.py:118
  213.2 18.7 %copy-start.14 = (f32[1,128,512]{2,1,0:T(8,128)}, f32[1,128,512]{2,1,0:T(8,128)S(1)}, u32[]{:S(2)}) copy-start(f32[1,128,512]{2,1,0:T(8,128)S(1)} %collective-permute-done.20) | copy-start | bytes 786436
  213.3 10.3 %collective-permute-start.21 = (f32[1,128,512]{2,1,0:T(8,128)S(1)}, f32[1,128,512]{2,1,0:T(8,128)S(1)}, u32[]{:S(2)}, u32[]{:S(2)}) collective-permute-start(f32[1,128,512]{2,1,0:T(8,128)S(1)} %multiply_add_fusion.2), channel_id=1, source_target_pairs={{0,64},{8,72},{16,80},{24,88},{32,96},{40,104},{48,112},{56,120},{... | collective-permute-start | bytes 786440 | tf_op jit(solution)/shard_map/ppermute | solution.py:118
  223.6 8.3 %copy-start.15 = (f32[1,128,512]{2,1,0:T(8,128)}, f32[1,128,512]{2,1,0:T(8,128)S(1)}, u32[]{:S(2)}) copy-start(f32[1,128,512]{2,1,0:T(8,128)S(1)} %collective-permute-done.21) | copy-start | bytes 786436
  223.7 7.4 %collective-permute-start.22 = (f32[1,128,512]{2,1,0:T(8,128)S(1)}, f32[1,128,512]{2,1,0:T(8,128)S(1)}, u32[]{:S(2)}, u32[]{:S(2)}) collective-permute-start(f32[1,128,512]{2,1,0:T(8,128)S(1)} %multiply_add_fusion.1), channel_id=1, source_target_pairs={{0,128},{8,136},{16,144},{24,152},{32,160},{40,168},{48,176},{56,1... | collective-permute-start | bytes 786440 | tf_op jit(solution)/shard_map/ppermute | solution.py:118
  231.9 8.9 %collective-permute-start.23 = (f32[1,128,512]{2,1,0:T(8,128)}, f32[1,128,512]{2,1,0:T(8,128)}, u32[]{:S(2)}, u32[]{:S(2)}) collective-permute-start(f32[1,128,512]{2,1,0:T(8,128)} %multiply_add_fusion), channel_id=1, source_target_pairs={{0,256},{8,264},{16,272},{24,280},{32,288},{40,296},{48,304},{56,3... | collective-permute-start | bytes 786440 | tf_op jit(solution)/shard_map/ppermute | solution.py:118
  243.9 1.0 copy-start.7
  247.4 24.2 %copy-start.10 = (bf16[1,1152,512]{2,1,0:T(8,128)(2,1)S(1)}, bf16[1,1152,512]{2,1,0:T(8,128)(2,1)}, u32[]{:S(2)}) copy-start(bf16[1,1152,512]{2,1,0:T(8,128)(2,1)} %constant_dynamic-update-slice_fusion.107) | copy-start | bytes 3538948
  247.5 25.8 %collective-permute-start.24 = (f32[1184,128]{1,0:T(8,128)S(1)}, f32[1184,128]{1,0:T(8,128)S(1)}, u32[]{:S(2)}, u32[]{:S(2)}) collective-permute-start(f32[1184,128]{1,0:T(8,128)S(1)} %constant_dynamic-slice_fusion.1), channel_id=1, source_target_pairs={{0,1},{1,0},{2,3},{3,2},{4,5},{5,4},{6,7},{7,6},{8,9},{9,8},{10,11... | collective-permute-start | bytes 1818632 | tf_op jit(solution)/shard_map/ppermute | solution.py:141
  273.5 15.1 %collective-permute-start.25 = (f32[296,128]{1,0:T(8,128)S(1)}, f32[296,128]{1,0:T(8,128)S(1)}, u32[]{:S(2)}, u32[]{:S(2)}) collective-permute-start(f32[296,128]{1,0:T(8,128)S(1)} %slice_bitcast_fusion), channel_id=1, source_target_pairs={{0,2},{1,7},{2,4},{3,1},{4,6},{5,3},{6,0},{7,5},{8,10},{9,15},{10,... | collective-permute-start | bytes 454664 | tf_op jit(solution)/shard_map/ppermute | solution.py:154
  288.6 15.8 %collective-permute-start.26 = (f32[296,128]{1,0:T(8,128)S(1)}, f32[296,128]{1,0:T(8,128)S(1)}, u32[]{:S(2)}, u32[]{:S(2)}) collective-permute-start(f32[296,128]{1,0:T(8,128)S(1)} %fusion.182), channel_id=1, source_target_pairs={{0,2},{1,7},{2,4},{3,1},{4,6},{5,3},{6,0},{7,5},{8,10},{9,15},{10,... | collective-permute-start | bytes 454664 | tf_op jit(solution)/shard_map/ppermute | solution.py:154
  304.5 12.9 %collective-permute-start.27 = (f32[296,128]{1,0:T(8,128)S(1)}, f32[296,128]{1,0:T(8,128)S(1)}, u32[]{:S(2)}, u32[]{:S(2)}) collective-permute-start(f32[296,128]{1,0:T(8,128)S(1)} %fusion.183), channel_id=1, source_target_pairs={{0,2},{1,7},{2,4},{3,1},{4,6},{5,3},{6,0},{7,5},{8,10},{9,15},{10,... | collective-permute-start | bytes 454664 | tf_op jit(solution)/shard_map/ppermute | solution.py:154
  317.4 13.3 %collective-permute-start.28 = (f32[296,128]{1,0:T(8,128)S(1)}, f32[296,128]{1,0:T(8,128)S(1)}, u32[]{:S(2)}, u32[]{:S(2)}) collective-permute-start(f32[296,128]{1,0:T(8,128)S(1)} %fusion.184), channel_id=1, source_target_pairs={{0,2},{1,7},{2,4},{3,1},{4,6},{5,3},{6,0},{7,5},{8,10},{9,15},{10,... | collective-permute-start | bytes 454664 | tf_op jit(solution)/shard_map/ppermute | solution.py:158
  330.7 11.5 %collective-permute-start.29 = (f32[296,128]{1,0:T(8,128)S(1)}, f32[296,128]{1,0:T(8,128)S(1)}, u32[]{:S(2)}, u32[]{:S(2)}) collective-permute-start(f32[296,128]{1,0:T(8,128)S(1)} %collective-permute-done.28), channel_id=1, source_target_pairs={{0,2},{1,7},{2,4},{3,1},{4,6},{5,3},{6,0},{7,5},{8,10},{9,15},{10,... | collective-permute-start | bytes 454664 | tf_op jit(solution)/shard_map/ppermute | solution.py:158
  342.3 11.5 %collective-permute-start.30 = (f32[296,128]{1,0:T(8,128)S(1)}, f32[296,128]{1,0:T(8,128)S(1)}, u32[]{:S(2)}, u32[]{:S(2)}) collective-permute-start(f32[296,128]{1,0:T(8,128)S(1)} %collective-permute-done.29), channel_id=1, source_target_pairs={{0,2},{1,7},{2,4},{3,1},{4,6},{5,3},{6,0},{7,5},{8,10},{9,15},{10,... | collective-permute-start | bytes 454664 | tf_op jit(solution)/shard_map/ppermute | solution.py:158
  353.9 12.1 %collective-permute-start.31 = (f32[1184,128]{1,0:T(8,128)S(1)}, f32[1184,128]{1,0:T(8,128)S(1)}, u32[]{:S(2)}, u32[]{:S(2)}) collective-permute-start(f32[1184,128]{1,0:T(8,128)S(1)} %bitcast.573), channel_id=1, source_target_pairs={{0,1},{1,0},{2,3},{3,2},{4,5},{5,4},{6,7},{7,6},{8,9},{9,8},{10,11... | collective-permute-start | bytes 1818632 | tf_op jit(solution)/shard_map/ppermute | solution.py:163
  (6 other events, 5.6 us)
